TPU v7x, 512 devices: a whole 4x8x8 slice. The times are simulated.
512 devices in a mesh: seq: 256 (over y_hi, z, x, core), dp: 2 (over y_lo).
Axes of the slice: x: 4, y: 8 (y_hi: 4, y_lo: 2; y = y_hi * 2 + y_lo), z: 8, core: 2. Of those that a mesh axis runs over, the one named last changes fastest.
Arguments:
- q_raw: bfloat16 [2, 32768, 2560], P('dp', 'seq'), may hold values from -33000 to 33000
- k_raw: bfloat16 [2, 32768, 2560], P('dp', 'seq'), may hold values from -19000 to 19000
- values: bfloat16 [2, 32768, 2560], P('dp', 'seq'), may hold values from -6 to 6
- cotangent: bfloat16 [2, 32768, 2560], P('dp', 'seq'), may hold values from -6 to 6
- q_gain: float32 [2560], replicated, may hold values from 0.5 to 1.5
- k_gain: float32 [2560], replicated, may hold values from 0.5 to 1.5
- key_tiles: int32 [256, 4], P('seq'), may hold values from -1 to 255, as said below
Outputs:
- q_grad: bfloat16 [2, 32768, 2560], P('dp', 'seq')
- k_grad: bfloat16 [2, 32768, 2560], P('dp', 'seq')
- v_grad: bfloat16 [2, 32768, 2560], P('dp', 'seq')
- q_gain_grad: float32 [2560], replicated
- k_gain_grad: float32 [2560], replicated
Inputs may be any that keep to these rules, and one draw needn't show every extreme that they name: `key_tiles`: row a, column 2 j + s (j below 2, s 0 or 1) holds -1 or the tile a - 2^j (s = 0) or a + 2^j (s = 1); it is -1 wherever that tile lies outside the clip.
All inputs are finite; a program needn't handle non-finite values.
Results may differ from a plain program's by a relative error of at most 0.013.
The roundings to bfloat16 on the way count: a program that leaves them out, or rounds other values in their place, can miss the bound.
Values may be sent and summed in bfloat16 or wider, within the bound.
No kernel may reach another device: no remote copies, remote signals or barrier semaphores. Data moves between devices by JAX's collectives and lax.ppermute only.
A program may use at most 128 MiB of HBM per device.

v0:
```python
import math

import jax
import jax.numpy as jnp
from jax import lax
from jax.sharding import PartitionSpec as P

HEAD = 128
LEVELS = 2


EPS = 1e-06


def from_behind(value, axis, steps):
    count = lax.axis_size(axis)
    first, last = (max(0, -steps), min(count, count - steps))
    return lax.ppermute(value, axis, [(source, source + steps) for source in range(first, last)])


def level_offsets(levels):
    return [sign * 2**level for level in range(levels) for sign in (-1, 1)]


def normalize(raw):
    numbers = raw.astype(jnp.float32)
    inverse = lax.rsqrt(jnp.mean(numbers * numbers, axis=-1, keepdims=True) + EPS)
    return (numbers * inverse, inverse)


def norm_backward(grad_norm, gain, hat, inverse):
    scaled = grad_norm * gain
    inner = jnp.mean(scaled * hat, axis=-1, keepdims=True)
    return (inverse * (scaled - hat * inner), jnp.sum(grad_norm * hat, axis=0))


def head_slice(array, index, group_width):
    return lax.dynamic_slice_in_dim(array, index * group_width, group_width, 1)


def heads_last(block):
    moved = jnp.transpose(block, (1, 0, 2, 3))
    return moved.reshape(moved.shape[0], -1)


def body(q_raw, k_raw, values, cotangent, q_gain, k_gain, key_tiles):
    tile_rows = q_raw.shape[1]
    features = q_raw.shape[2]
    heads = features // HEAD
    group_width = 4
    groups = heads // group_width
    scale = 1.0 / math.sqrt(HEAD)
    offsets = level_offsets(LEVELS)
    slots = len(offsets)
    q_hat, q_inv = normalize(q_raw[0])
    k_hat, k_inv = normalize(k_raw[0])
    q_norm = (q_hat * q_gain).astype(jnp.bfloat16).reshape(tile_rows, heads, HEAD)
    k_norm = (k_hat * k_gain).astype(jnp.bfloat16).reshape(tile_rows, heads, HEAD)
    value_rows = values[0].reshape(tile_rows, heads, HEAD)
    grad_rows = cotangent[0].reshape(tile_rows, heads, HEAD)
    entries = key_tiles[0]
    fetched = [from_behind((k_norm, value_rows), "seq", -offset) for offset in offsets]
    key_block = jnp.concatenate([k_norm] + [pair[0] for pair in fetched], axis=0)
    value_block = jnp.concatenate([value_rows] + [pair[1] for pair in fetched], axis=0)
    live = jnp.repeat(jnp.concatenate([jnp.ones((1,), bool), entries >= 0]), tile_rows)

    def attend(index):
        q_group = head_slice(q_norm, index, group_width)
        k_group = head_slice(key_block, index, group_width)
        v_group = head_slice(value_block, index, group_width)
        g_group = head_slice(grad_rows, index, group_width)
        scores = (
            jnp.einsum("qhd,khd->hqk", q_group, k_group, preferred_element_type=jnp.float32) * scale
        )
        highest = jnp.max(jnp.where(live, scores, -jnp.inf), axis=-1)
        total = jnp.sum(jnp.where(live, jnp.exp(scores - highest[:, :, None]), 0.0), axis=-1)
        log_total = highest + jnp.log(total)
        prob = jnp.where(live, jnp.exp(scores - log_total[:, :, None]), 0.0).astype(jnp.bfloat16)
        attended = jnp.einsum("hqk,khd->qhd", prob, v_group, preferred_element_type=jnp.float32)
        delta = jnp.transpose(jnp.sum(g_group.astype(jnp.float32) * attended, axis=-1))
        prob_grad = jnp.einsum("qhd,khd->hqk", g_group, v_group, preferred_element_type=jnp.float32)
        score_grad = (prob.astype(jnp.float32) * (prob_grad - delta[:, :, None]) * scale).astype(
            jnp.bfloat16
        )
        grad_q = jnp.einsum("hqk,khd->qhd", score_grad, k_group, preferred_element_type=jnp.float32)
        grad_k = jnp.einsum("hqk,qhd->khd", score_grad, q_group, preferred_element_type=jnp.float32)
        grad_v = jnp.einsum("hqk,qhd->khd", prob, g_group, preferred_element_type=jnp.float32)
        return (
            grad_q,
            grad_k[:tile_rows],
            grad_v[:tile_rows],
            grad_k[tile_rows:].astype(jnp.bfloat16),
            grad_v[tile_rows:].astype(jnp.bfloat16),
            log_total,
            delta,
        )

    results = lax.map(attend, jnp.arange(groups, dtype=jnp.int32))
    q_norm_grad = heads_last(results[0])
    k_norm_grad = heads_last(results[1])
    v_sum = heads_last(results[2])
    far_k = jnp.transpose(
        results[3].reshape(groups, slots, tile_rows, group_width, HEAD), (1, 2, 0, 3, 4)
    )
    far_v = jnp.transpose(
        results[4].reshape(groups, slots, tile_rows, group_width, HEAD), (1, 2, 0, 3, 4)
    )
    far_k = far_k.reshape(slots, tile_rows, features)
    far_v = far_v.reshape(slots, tile_rows, features)
    for slot in range(slots):
        back_k, back_v = from_behind((far_k[slot], far_v[slot]), "seq", offsets[slot])
        k_norm_grad = k_norm_grad + back_k.astype(jnp.float32)
        v_sum = v_sum + back_v.astype(jnp.float32)
    q_back, q_part = norm_backward(q_norm_grad, q_gain, q_hat, q_inv)
    k_back, k_part = norm_backward(k_norm_grad, k_gain, k_hat, k_inv)
    q_gain_grad, k_gain_grad = lax.psum((q_part, k_part), ("seq", "dp"))
    return (
        q_back.astype(jnp.bfloat16)[None],
        k_back.astype(jnp.bfloat16)[None],
        v_sum.astype(jnp.bfloat16)[None],
        q_gain_grad,
        k_gain_grad,
    )


def solution(mesh):
    return jax.shard_map(
        body,
        mesh=mesh,
        in_specs=(
            P("dp", "seq", None),
            P("dp", "seq", None),
            P("dp", "seq", None),
            P("dp", "seq", None),
            P(),
            P(),
            P("seq", None),
        ),
        out_specs=(P("dp", "seq", None), P("dp", "seq", None), P("dp", "seq", None), P(), P()),
        check_vma=False,
    )
```

profile of v0, /device:TPU:1, one launch (start us, length us, event | category | flops | bytes accessed | tf_op | source)
XLA Modules:
  0.0 367.2 jit_solution(1854530821319895498)
XLA Ops:
  3.8 4.5 %collective-permute-start = (bf16[128,20,128]{0,2,1:T(8,128)(2,1)S(1)}, bf16[128,20,128]{0,2,1:T(8,128)(2,1)}, u32[]{:S(2)}, u32[]{:S(2)}) collective-permute-start(bf16[128,20,128]{0,2,1:T(8,128)(2,1)S(1)} %get-tuple-element.152), channel_id=1, source_target_pairs={{0,2},{2,4},{4,6},{6,8},{8,10},{10,12},{12,14},{14,16},{16,18},{18... | collective-permute-start | bytes 1966088 | tf_op jit(solution)/shard_map/ppermute | solution.py:18
  8.3 6.4 %collective-permute-start.1 = (bf16[128,20,128]{0,2,1:T(8,128)(2,1)S(1)}, bf16[128,20,128]{0,2,1:T(8,128)(2,1)}, u32[]{:S(2)}, u32[]{:S(2)}) collective-permute-start(bf16[128,20,128]{0,2,1:T(8,128)(2,1)S(1)} %get-tuple-element.152), channel_id=1, source_target_pairs={{2,0},{4,2},{6,4},{8,6},{10,8},{12,10},{14,12},{16,14},{18,16},{20... | collective-permute-start | bytes 1966088 | tf_op jit(solution)/shard_map/ppermute | solution.py:18
  14.7 2.1 collective-permute-start.2
  18.5 3.5 collective-permute-start.4
  24.8 1.9 collective-permute-start.5
  27.2 2.9 collective-permute-start.6
  30.1 2.0 constant_dynamic-update-slice_fusion.4
  33.4 2.0 constant_dynamic-update-slice_fusion.3
  35.4 2.1 constant_dynamic-update-slice_fusion.2
  37.5 2.1 constant_dynamic-update-slice_fusion.1
  39.6 2.8 collective-permute-done.4
  42.4 2.1 constant_dynamic-update-slice_fusion.9
  44.4 3.2 collective-permute-done.5
  47.7 2.1 constant_dynamic-update-slice_fusion.8
  53.0 64.5 %while.19 = (s32[]{:T(128)}, f32[5,128,4,128]{1,3,2,0:T(8,128)}, f32[5,128,4,128]{1,3,2,0:T(8,128)}, f32[5,128,4,128]{1,3,2,0:T(8,128)}, bf16[5,512,4,128]{1,3,2...) while((s32[]{:T(128)}, f32[5,128,4,128]{1,3,2,0:T(8,128)}, ...), condition=%wide.region_6.7_spmd.clone, body=%wide.region_2.6_spmd.clone.sunk | while | flops 508099584 | bytes 30957784 | solution.py:98
  54.4 1.6 select_reduce_fusion.4
  56.8 1.5 fusion.69
  63.7 2.2 fusion.71
  67.3 1.6 select_reduce_fusion.4
  69.7 1.5 fusion.69
  76.5 2.2 fusion.71
  80.2 1.6 select_reduce_fusion.4
  82.6 1.5 fusion.69
  84.1 1.5 fusion.70
  89.4 2.2 fusion.71
  93.0 1.6 select_reduce_fusion.4
  95.4 1.5 fusion.69
  97.0 1.5 fusion.70
  102.3 2.2 fusion.71
  106.0 1.6 select_reduce_fusion.4
  108.4 1.5 fusion.69
  109.9 1.5 fusion.70
  115.3 2.2 fusion.71
  117.6 2.5 bitcast_bitcast_fusion
  120.1 1.5 fusion.35
  122.9 6.0 %collective-permute-start.11 = (bf16[128,2560]{0,1:T(8,128)(2,1)}, bf16[128,2560]{0,1:T(8,128)(2,1)}, u32[]{:S(2)}, u32[]{:S(2)}) collective-permute-start(bf16[128,2560]{0,1:T(8,128)(2,1)} %bitcast.17), channel_id=1, source_target_pairs={{0,4},{2,6},{4,8},{6,10},{8,12},{10,14},{12,16},{14,18},{16,20},{1... | collective-permute-start | bytes 1966088 | tf_op jit(solution)/shard_map/ppermute | solution.py:18
  128.9 6.0 %collective-permute-start.8 = (bf16[128,2560]{0,1:T(8,128)(2,1)}, bf16[128,2560]{0,1:T(8,128)(2,1)}, u32[]{:S(2)}, u32[]{:S(2)}) collective-permute-start(bf16[128,2560]{0,1:T(8,128)(2,1)} %bitcast.14), channel_id=1, source_target_pairs={{2,0},{4,2},{6,4},{8,6},{10,8},{12,10},{14,12},{16,14},{18,16},{20... | collective-permute-start | bytes 1966088 | tf_op jit(solution)/shard_map/ppermute | solution.py:18
  134.9 1.9 collective-permute-start.9
  136.8 2.2 fusion.27
  139.0 2.6 fusion.34
  142.7 3.2 collective-permute-start.12
  149.2 1.8 copy.48
  151.1 1.7 multiply_convert_fusion.1
  153.9 2.3 collective-permute-start.13
  157.7 6.2 %collective-permute-start.15 = (bf16[128,2560]{1,0:T(8,128)(2,1)}, bf16[128,2560]{1,0:T(8,128)(2,1)}, u32[]{:S(2)}, u32[]{:S(2)}) collective-permute-start(bf16[128,2560]{1,0:T(8,128)(2,1)} %squeeze.36), channel_id=1, source_target_pairs={{0,4},{2,6},{4,8},{6,10},{8,12},{10,14},{12,16},{14,18},{16,20},{1... | collective-permute-start | bytes 1966088 | tf_op jit(solution)/shard_map/ppermute | solution.py:18
  163.9 3.1 multiply_reduce_fusion
  168.5 195.9 %all-reduce = (f32[2560]{0:T(1024)}, f32[2560]{0:T(1024)}) all-reduce(f32[2560]{0:T(1024)S(1)} %reduce_sum.79, f32[2560]{0:T(1024)S(1)} %get-tuple-element.122), channel_id=1, replica_groups=mesh['seq'=256,'dp'=2] {'seq','dp'}, use_global_device_ids=true, to_apply=%region_10.11 | all-reduce | flops 5120 | bytes 40960 | tf_op jit(solution)/shard_map/psum | solution.py:116
  364.5 2.7 fusion.32
  (187 shorter events, 52.0 us)
Async XLA Ops:
  0.6 1.8 copy-start.13
  2.1 1.8 copy-start
  2.1 16.1 %copy-start.10 = (bf16[1,128,2560]{2,1,0:T(8,128)(2,1)S(1)}, bf16[1,128,2560]{2,1,0:T(8,128)(2,1)}, u32[]{:S(2)}) copy-start(bf16[1,128,2560]{2,1,0:T(8,128)(2,1)} %param.11) | copy-start | bytes 1966084
  2.5 19.6 %copy-start.11 = (bf16[1,128,2560]{2,1,0:T(8,128)(2,1)S(1)}, bf16[1,128,2560]{2,1,0:T(8,128)(2,1)}, u32[]{:S(2)}) copy-start(bf16[1,128,2560]{2,1,0:T(8,128)(2,1)} %param.9) | copy-start | bytes 1966084
  3.8 21.0 %collective-permute-start = (bf16[128,20,128]{0,2,1:T(8,128)(2,1)S(1)}, bf16[128,20,128]{0,2,1:T(8,128)(2,1)}, u32[]{:S(2)}, u32[]{:S(2)}) collective-permute-start(bf16[128,20,128]{0,2,1:T(8,128)(2,1)S(1)} %get-tuple-element.152), channel_id=1, source_target_pairs={{0,2},{2,4},{4,6},{6,8},{8,10},{10,12},{12,14},{14,16},{16,18},{18... | collective-permute-start | bytes 1966088 | tf_op jit(solution)/shard_map/ppermute | solution.py:18
  8.3 18.8 %collective-permute-start.1 = (bf16[128,20,128]{0,2,1:T(8,128)(2,1)S(1)}, bf16[128,20,128]{0,2,1:T(8,128)(2,1)}, u32[]{:S(2)}, u32[]{:S(2)}) collective-permute-start(bf16[128,20,128]{0,2,1:T(8,128)(2,1)S(1)} %get-tuple-element.152), channel_id=1, source_target_pairs={{2,0},{4,2},{6,4},{8,6},{10,8},{12,10},{14,12},{16,14},{18,16},{20... | collective-permute-start | bytes 1966088 | tf_op jit(solution)/shard_map/ppermute | solution.py:18
  14.7 17.4 %collective-permute-start.2 = (bf16[128,20,128]{0,2,1:T(8,128)(2,1)S(1)}, bf16[128,20,128]{0,2,1:T(8,128)(2,1)}, u32[]{:S(2)}, u32[]{:S(2)}) collective-permute-start(bf16[128,20,128]{0,2,1:T(8,128)(2,1)S(1)} %get-tuple-element.152), channel_id=1, source_target_pairs={{0,4},{2,6},{4,8},{6,10},{8,12},{10,14},{12,16},{14,18},{16,20},{1... | collective-permute-start | bytes 1966088 | tf_op jit(solution)/shard_map/ppermute | solution.py:18
  16.9 20.6 %collective-permute-start.3 = (bf16[128,20,128]{0,2,1:T(8,128)(2,1)S(1)}, bf16[128,20,128]{0,2,1:T(8,128)(2,1)}, u32[]{:S(2)}, u32[]{:S(2)}) collective-permute-start(bf16[128,20,128]{0,2,1:T(8,128)(2,1)S(1)} %get-tuple-element.152), channel_id=1, source_target_pairs={{4,0},{6,2},{8,4},{10,6},{12,8},{14,10},{16,12},{18,14},{20,16},{2... | collective-permute-start | bytes 1966088 | tf_op jit(solution)/shard_map/ppermute | solution.py:18
  18.5 23.9 %collective-permute-start.4 = (bf16[128,20,128]{0,2,1:T(8,128)(2,1)S(1)}, bf16[128,20,128]{0,2,1:T(8,128)(2,1)}, u32[]{:S(2)}, u32[]{:S(2)}) collective-permute-start(bf16[128,20,128]{0,2,1:T(8,128)(2,1)S(1)} %bitcast.145), channel_id=1, source_target_pairs={{0,2},{2,4},{4,6},{6,8},{8,10},{10,12},{12,14},{14,16},{16,18},{18... | collective-permute-start | bytes 1966088 | tf_op jit(solution)/shard_map/ppermute | solution.py:18
  22.4 0.8 copy-start.4
  22.4 0.8 copy-start.14
  23.2 1.6 copy-start.2
  23.2 0.7 copy-start.15
  23.2 3.6 copy-start.12
  24.8 22.8 %collective-permute-start.5 = (bf16[128,20,128]{0,2,1:T(8,128)(2,1)S(1)}, bf16[128,20,128]{0,2,1:T(8,128)(2,1)}, u32[]{:S(2)}, u32[]{:S(2)}) collective-permute-start(bf16[128,20,128]{0,2,1:T(8,128)(2,1)S(1)} %bitcast.147), channel_id=1, source_target_pairs={{2,0},{4,2},{6,4},{8,6},{10,8},{12,10},{14,12},{16,14},{18,16},{20... | collective-permute-start | bytes 1966088 | tf_op jit(solution)/shard_map/ppermute | solution.py:18
  27.2 24.0 %collective-permute-start.6 = (bf16[128,20,128]{0,2,1:T(8,128)(2,1)S(1)}, bf16[128,20,128]{0,2,1:T(8,128)(2,1)S(1)}, u32[]{:S(2)}, u32[]{:S(2)}) collective-permute-start(bf16[128,20,128]{0,2,1:T(8,128)(2,1)S(1)} %bitcast.148), channel_id=1, source_target_pairs={{0,4},{2,6},{4,8},{6,10},{8,12},{10,14},{12,16},{14,18},{16,20},{1... | collective-permute-start | bytes 1966088 | tf_op jit(solution)/shard_map/ppermute | solution.py:18
  32.1 20.0 %collective-permute-start.7 = (bf16[128,20,128]{0,2,1:T(8,128)(2,1)S(1)}, bf16[128,20,128]{0,2,1:T(8,128)(2,1)S(1)}, u32[]{:S(2)}, u32[]{:S(2)}) collective-permute-start(bf16[128,20,128]{0,2,1:T(8,128)(2,1)S(1)} %bitcast.149), channel_id=1, source_target_pairs={{4,0},{6,2},{8,4},{10,6},{12,8},{14,10},{16,12},{18,14},{20,16},{2... | collective-permute-start | bytes 1966088 | tf_op jit(solution)/shard_map/ppermute | solution.py:18
  53.0 3.6 copy-start.8
  53.0 6.8 %copy-start.6 = (bf16[128,20,128]{0,2,1:T(8,128)(2,1)}, bf16[128,20,128]{0,2,1:T(8,128)(2,1)S(1)}, u32[]{:S(2)}) copy-start(bf16[128,20,128]{0,2,1:T(8,128)(2,1)S(1)} %get-tuple-element.286) | copy-start | bytes 1966084 | tf_op jit(solution)/shard_map/while
  62.8 3.1 copy-start.7
  63.7 2.2 copy-start.9
  65.9 3.6 copy-start.8
  65.9 6.9 %copy-start.6 = (bf16[128,20,128]{0,2,1:T(8,128)(2,1)}, bf16[128,20,128]{0,2,1:T(8,128)(2,1)S(1)}, u32[]{:S(2)}) copy-start(bf16[128,20,128]{0,2,1:T(8,128)(2,1)S(1)} %get-tuple-element.286) | copy-start | bytes 1966084 | tf_op jit(solution)/shard_map/while
  75.7 3.1 copy-start.7
  76.5 2.2 copy-start.9
  78.8 3.6 copy-start.8
  78.8 6.9 %copy-start.6 = (bf16[128,20,128]{0,2,1:T(8,128)(2,1)}, bf16[128,20,128]{0,2,1:T(8,128)(2,1)S(1)}, u32[]{:S(2)}) copy-start(bf16[128,20,128]{0,2,1:T(8,128)(2,1)S(1)} %get-tuple-element.286) | copy-start | bytes 1966084 | tf_op jit(solution)/shard_map/while
  88.5 3.1 copy-start.7
  89.4 2.2 copy-start.9
  91.6 3.6 copy-start.8
  91.6 6.9 %copy-start.6 = (bf16[128,20,128]{0,2,1:T(8,128)(2,1)}, bf16[128,20,128]{0,2,1:T(8,128)(2,1)S(1)}, u32[]{:S(2)}) copy-start(bf16[128,20,128]{0,2,1:T(8,128)(2,1)S(1)} %get-tuple-element.286) | copy-start | bytes 1966084 | tf_op jit(solution)/shard_map/while
  101.4 3.2 copy-start.7
  102.3 2.2 copy-start.9
  104.6 3.6 copy-start.8
  104.6 6.9 %copy-start.6 = (bf16[128,20,128]{0,2,1:T(8,128)(2,1)}, bf16[128,20,128]{0,2,1:T(8,128)(2,1)S(1)}, u32[]{:S(2)}) copy-start(bf16[128,20,128]{0,2,1:T(8,128)(2,1)S(1)} %get-tuple-element.286) | copy-start | bytes 1966084 | tf_op jit(solution)/shard_map/while
  114.4 3.2 copy-start.7
  115.3 2.2 copy-start.9
  120.1 16.8 %copy-start.3 = (f32[1,128,2560]{1,2,0:T(8,128)S(1)}, f32[1,128,2560]{1,2,0:T(8,128)}, u32[]{:S(2)}) copy-start(f32[1,128,2560]{1,2,0:T(8,128)} %copy-done.2) | copy-start | bytes 3932164
  121.6 32.3 %collective-permute-start.10 = (bf16[128,2560]{0,1:T(8,128)(2,1)}, bf16[128,2560]{0,1:T(8,128)(2,1)}, u32[]{:S(2)}, u32[]{:S(2)}) collective-permute-start(bf16[128,2560]{0,1:T(8,128)(2,1)} %bitcast.16), channel_id=1, source_target_pairs={{4,0},{6,2},{8,4},{10,6},{12,8},{14,10},{16,12},{18,14},{20,16},{2... | collective-permute-start | bytes 1966088 | tf_op jit(solution)/shard_map/ppermute | solution.py:18
  122.9 33.3 %collective-permute-start.11 = (bf16[128,2560]{0,1:T(8,128)(2,1)}, bf16[128,2560]{0,1:T(8,128)(2,1)}, u32[]{:S(2)}, u32[]{:S(2)}) collective-permute-start(bf16[128,2560]{0,1:T(8,128)(2,1)} %bitcast.17), channel_id=1, source_target_pairs={{0,4},{2,6},{4,8},{6,10},{8,12},{10,14},{12,16},{14,18},{16,20},{1... | collective-permute-start | bytes 1966088 | tf_op jit(solution)/shard_map/ppermute | solution.py:18
  128.9 28.8 %collective-permute-start.8 = (bf16[128,2560]{0,1:T(8,128)(2,1)}, bf16[128,2560]{0,1:T(8,128)(2,1)}, u32[]{:S(2)}, u32[]{:S(2)}) collective-permute-start(bf16[128,2560]{0,1:T(8,128)(2,1)} %bitcast.14), channel_id=1, source_target_pairs={{2,0},{4,2},{6,4},{8,6},{10,8},{12,10},{14,12},{16,14},{18,16},{20... | collective-permute-start | bytes 1966088 | tf_op jit(solution)/shard_map/ppermute | solution.py:18
  134.9 29.0 %collective-permute-start.9 = (bf16[128,2560]{0,1:T(8,128)(2,1)}, bf16[128,2560]{0,1:T(8,128)(2,1)}, u32[]{:S(2)}, u32[]{:S(2)}) collective-permute-start(bf16[128,2560]{0,1:T(8,128)(2,1)} %bitcast.15), channel_id=1, source_target_pairs={{0,2},{2,4},{4,6},{6,8},{8,10},{10,12},{12,14},{14,16},{16,18},{18... | collective-permute-start | bytes 1966088 | tf_op jit(solution)/shard_map/ppermute | solution.py:18
  142.7 221.8 %collective-permute-start.12 = (bf16[128,2560]{1,0:T(8,128)(2,1)}, bf16[128,2560]{1,0:T(8,128)(2,1)S(1)}, u32[]{:S(2)}, u32[]{:S(2)}) collective-permute-start(bf16[128,2560]{1,0:T(8,128)(2,1)} %squeeze.33), channel_id=1, source_target_pairs={{2,0},{4,2},{6,4},{8,6},{10,8},{12,10},{14,12},{16,14},{18,16},{20... | collective-permute-start | bytes 1966088 | tf_op jit(solution)/shard_map/ppermute | solution.py:18
  149.2 1.8 copy-start.5
  152.8 11.1 %copy-start.1 = (bf16[1,128,2560]{1,2,0:T(8,128)(2,1)S(1)}, bf16[1,128,2560]{1,2,0:T(8,128)(2,1)}, u32[]{:S(2)}) copy-start(bf16[1,128,2560]{1,2,0:T(8,128)(2,1)} %copy-done) | copy-start | bytes 1966084
  153.9 210.6 %collective-permute-start.13 = (bf16[128,2560]{1,0:T(8,128)(2,1)}, bf16[128,2560]{1,0:T(8,128)(2,1)}, u32[]{:S(2)}, u32[]{:S(2)}) collective-permute-start(bf16[128,2560]{1,0:T(8,128)(2,1)} %squeeze.34), channel_id=1, source_target_pairs={{0,2},{2,4},{4,6},{6,8},{8,10},{10,12},{12,14},{14,16},{16,18},{18... | collective-permute-start | bytes 1966088 | tf_op jit(solution)/shard_map/ppermute | solution.py:18
  156.2 208.3 %collective-permute-start.14 = (bf16[128,2560]{1,0:T(8,128)(2,1)}, bf16[128,2560]{1,0:T(8,128)(2,1)}, u32[]{:S(2)}, u32[]{:S(2)}) collective-permute-start(bf16[128,2560]{1,0:T(8,128)(2,1)} %squeeze.35), channel_id=1, source_target_pairs={{4,0},{6,2},{8,4},{10,6},{12,8},{14,10},{16,12},{18,14},{20,16},{2... | collective-permute-start | bytes 1966088 | tf_op jit(solution)/shard_map/ppermute | solution.py:18
  157.7 206.8 %collective-permute-start.15 = (bf16[128,2560]{1,0:T(8,128)(2,1)}, bf16[128,2560]{1,0:T(8,128)(2,1)}, u32[]{:S(2)}, u32[]{:S(2)}) collective-permute-start(bf16[128,2560]{1,0:T(8,128)(2,1)} %squeeze.36), channel_id=1, source_target_pairs={{0,4},{2,6},{4,8},{6,10},{8,12},{10,14},{12,16},{14,18},{16,20},{1... | collective-permute-start | bytes 1966088 | tf_op jit(solution)/shard_map/ppermute | solution.py:18
where the time goes:
time: 369 us; the launch traced here: 367 us
  blocking collectives  196 us (53%)
  local copies, waits for them, and re-layouts  53.3 us (14%)
  starting transfers between devices  52.3 us (14%)
  matrix products  37.4 us (10%)
  other arithmetic  16 us (4%)
  waiting for transfers between devices  7.49 us (2%)
  loops' own time  3.72 us (1%)
    psum x1, blocking collectives, body(): q_gain_grad, k_gain_grad = lax.psum((q_part, k_part), ('seq', 'dp'))  196 us
    ppermute x16, starting transfers between devices, from_behind(): lax.ppermute(value, axis, [(source, source + steps) for source in range(f...  52.3 us
    unnamed x37, local copies, waits for them, and re-layouts  17.3 us
    dynamic_update_slice x20, local copies, waits for them, and re-layouts, body(): results = lax.map(attend, jnp.arange(groups, dtype=jnp.int32))  15.3 us
    dot_general x5, matrix products, attend(): jnp.einsum('hqk,khd->qhd', score_grad, k_group, preferred_element_type=jn...  11.1 us
    dot_general x5, matrix products, attend(): jnp.einsum('qhd,khd->hqk', q_group, k_group, preferred_element_type=jnp.f...  7.78 us
    dot_general x5, matrix products, attend(): jnp.einsum('hqk,khd->qhd', prob, v_group, preferred_element_type=jnp.floa...  7.71 us
    dot_general x5, matrix products, attend(): jnp.einsum('qhd,khd->hqk', g_group, v_group, preferred_element_type=jnp.f...  7.53 us
  transfers between devices with their start and end apart: 16, of which 3 were waited for; matrix products, arithmetic and copies ran while one was open for 9% of the time, Pallas kernels for 0%

commit v1 on v0

--- a/solution.py
+++ b/solution.py
@@ -16,6 +16,16 @@
     count = lax.axis_size(axis)
     first, last = (max(0, -steps), min(count, count - steps))
     return lax.ppermute(value, axis, [(source, source + steps) for source in range(first, last)])
+
+
+def all_sum(value, axes):
+    for axis in axes:
+        count = lax.axis_size(axis)
+        bit = 1
+        while bit < count:
+            value = value + lax.ppermute(value, axis, [(i, i ^ bit) for i in range(count)])
+            bit *= 2
+    return value
 
 
 def level_offsets(levels):
@@ -113,7 +123,8 @@
         v_sum = v_sum + back_v.astype(jnp.float32)
     q_back, q_part = norm_backward(q_norm_grad, q_gain, q_hat, q_inv)
     k_back, k_part = norm_backward(k_norm_grad, k_gain, k_hat, k_inv)
-    q_gain_grad, k_gain_grad = lax.psum((q_part, k_part), ("seq", "dp"))
+    gain_grads = all_sum(jnp.concatenate([q_part, k_part]), ("dp", "seq"))
+    q_gain_grad, k_gain_grad = gain_grads[:features], gain_grads[features:]
     return (
         q_back.astype(jnp.bfloat16)[None],
         k_back.astype(jnp.bfloat16)[None],

time: 369 us -> 329 us (0.89)
  blocking collectives: 196 us -> 0 us
  starting transfers between devices: 52.3 us -> 180 us
  waiting for transfers between devices: 7.49 us -> 30.9 us
    psum x1 -> x0, blocking collectives: 196 us -> none  [body(): q_gain_grad, k_gain_grad = lax.psum((q_part, k_part), ('seq', 'dp'))]
    ppermute x0 -> x9, starting transfers between devices: none -> 129 us  [all_sum(): lax.ppermute(value, axis, [(i, i ^ bit) for i in range(count)])]
    ppermute x0 -> x9, waiting for transfers between devices: none -> 12.7 us  [all_sum(): lax.ppermute(value, axis, [(i, i ^ bit) for i in range(count)])]
    ppermute x16, waiting for transfers between devices: 7.49 us -> 18.3 us  [from_behind(): lax.ppermute(value, axis, [(source, source + steps) for source in range(f...]
    unnamed x37 -> x41, local copies, waits for them, and re-layouts: 17.3 us -> 18.5 us
  transfers between devices with their start and end apart: 16 -> 25, of which waited for: 3 -> 10; matrix products, arithmetic and copies ran while one was open for 9% -> 12% of each run, Pallas kernels for 0% -> 0%
where the time goes in v1:
time: 329 us; the launch traced here: 327 us
  starting transfers between devices  180 us (55%)
  local copies, waits for them, and re-layouts  56.8 us (17%)
  matrix products  37.4 us (11%)
  waiting for transfers between devices  30.9 us (9%)
  other arithmetic  16.8 us (5%)
  loops' own time  3.72 us (1%)
    ppermute x9, starting transfers between devices, all_sum(): lax.ppermute(value, axis, [(i, i ^ bit) for i in range(count)])  129 us
    ppermute x16, starting transfers between devices, from_behind(): lax.ppermute(value, axis, [(source, source + steps) for source in range(f...  51.6 us
    unnamed x41, local copies, waits for them, and re-layouts  18.5 us
    ppermute x16, waiting for transfers between devices, from_behind(): lax.ppermute(value, axis, [(source, source + steps) for source in range(f...  18.3 us
    dynamic_update_slice x20, local copies, waits for them, and re-layouts, body(): results = lax.map(attend, jnp.arange(groups, dtype=jnp.int32))  15.3 us
    ppermute x9, waiting for transfers between devices, all_sum(): lax.ppermute(value, axis, [(i, i ^ bit) for i in range(count)])  12.7 us
    dot_general x5, matrix products, attend(): jnp.einsum('hqk,khd->qhd', score_grad, k_group, preferred_element_type=jn...  11.1 us
    dot_general x5, matrix products, attend(): jnp.einsum('qhd,khd->hqk', q_group, k_group, preferred_element_type=jnp.f...  7.78 us
  transfers between devices with their start and end apart: 25, of which 10 were waited for; matrix products, arithmetic and copies ran while one was open for 12% of the time, Pallas kernels for 0%

profile of v1, /device:TPU:1, one launch (start us, length us, event | category | flops | bytes accessed | tf_op | source)
XLA Modules:
  0.0 327.3 jit_solution(15184064526731721080)
XLA Ops:
  3.8 4.5 %collective-permute-start = (bf16[128,20,128]{0,2,1:T(8,128)(2,1)S(1)}, bf16[128,20,128]{0,2,1:T(8,128)(2,1)}, u32[]{:S(2)}, u32[]{:S(2)}) collective-permute-start(bf16[128,20,128]{0,2,1:T(8,128)(2,1)S(1)} %get-tuple-element.150), channel_id=1, source_target_pairs={{0,2},{2,4},{4,6},{6,8},{8,10},{10,12},{12,14},{14,16},{16,18},{18... | collective-permute-start | bytes 1966088 | tf_op jit(solution)/shard_map/ppermute | solution.py:18
  8.3 6.4 %collective-permute-start.1 = (bf16[128,20,128]{0,2,1:T(8,128)(2,1)S(1)}, bf16[128,20,128]{0,2,1:T(8,128)(2,1)}, u32[]{:S(2)}, u32[]{:S(2)}) collective-permute-start(bf16[128,20,128]{0,2,1:T(8,128)(2,1)S(1)} %get-tuple-element.150), channel_id=1, source_target_pairs={{2,0},{4,2},{6,4},{8,6},{10,8},{12,10},{14,12},{16,14},{18,16},{20... | collective-permute-start | bytes 1966088 | tf_op jit(solution)/shard_map/ppermute | solution.py:18
  14.7 2.1 collective-permute-start.2
  18.4 3.5 %collective-permute-start.4 = (bf16[128,20,128]{0,2,1:T(8,128)(2,1)S(1)}, bf16[128,20,128]{0,2,1:T(8,128)(2,1)}, u32[]{:S(2)}, u32[]{:S(2)}) collective-permute-start(bf16[128,20,128]{0,2,1:T(8,128)(2,1)S(1)} %bitcast.145), channel_id=1, source_target_pairs={{0,2},{2,4},{4,6},{6,8},{8,10},{10,12},{12,14},{14,16},{16,18},{18... | collective-permute-start | bytes 1966088 | tf_op jit(solution)/shard_map/ppermute | solution.py:18
  24.8 1.9 collective-permute-start.5
  27.1 2.9 collective-permute-start.6
  30.0 2.1 constant_dynamic-update-slice_fusion.4
  33.4 2.1 constant_dynamic-update-slice_fusion.3
  35.5 2.1 constant_dynamic-update-slice_fusion.2
  37.5 2.1 constant_dynamic-update-slice_fusion.1
  39.6 2.7 collective-permute-done.4
  42.3 2.0 constant_dynamic-update-slice_fusion.9
  44.4 3.2 collective-permute-done.5
  47.6 2.0 constant_dynamic-update-slice_fusion.8
  53.0 64.5 %while.19 = (s32[]{:T(128)}, f32[5,128,4,128]{1,3,2,0:T(8,128)}, f32[5,128,4,128]{1,3,2,0:T(8,128)}, f32[5,128,4,128]{1,3,2,0:T(8,128)}, bf16[5,512,4,128]{1,3,2...) while((s32[]{:T(128)}, f32[5,128,4,128]{1,3,2,0:T(8,128)}, ...), condition=%wide.region_6.7_spmd.clone, body=%wide.region_2.6_spmd.clone.sunk | while | flops 508099584 | bytes 30957784 | solution.py:108
  63.7 2.2 fusion.73
  76.6 2.2 fusion.73
  89.5 2.2 fusion.73
  102.4 2.2 fusion.73
  115.3 2.2 fusion.73
  117.6 2.5 bitcast_bitcast_fusion
  120.1 1.6 fusion.35
  122.9 6.1 %collective-permute-start.11 = (bf16[128,2560]{0,1:T(8,128)(2,1)}, bf16[128,2560]{0,1:T(8,128)(2,1)}, u32[]{:S(2)}, u32[]{:S(2)}) collective-permute-start(bf16[128,2560]{0,1:T(8,128)(2,1)} %bitcast.17), channel_id=1, source_target_pairs={{0,4},{2,6},{4,8},{6,10},{8,12},{10,14},{12,16},{14,18},{16,20},{1... | collective-permute-start | bytes 1966088 | tf_op jit(solution)/shard_map/ppermute | solution.py:18
  129.0 6.0 %collective-permute-start.8 = (bf16[128,2560]{0,1:T(8,128)(2,1)}, bf16[128,2560]{0,1:T(8,128)(2,1)}, u32[]{:S(2)}, u32[]{:S(2)}) collective-permute-start(bf16[128,2560]{0,1:T(8,128)(2,1)} %bitcast.14), channel_id=1, source_target_pairs={{2,0},{4,2},{6,4},{8,6},{10,8},{12,10},{14,12},{16,14},{18,16},{20... | collective-permute-start | bytes 1966088 | tf_op jit(solution)/shard_map/ppermute | solution.py:18
  134.9 1.9 collective-permute-start.9
  136.9 2.2 fusion.27
  139.2 9.3 %collective-permute-done.8 = bf16[128,2560]{0,1:T(8,128)(2,1)} collective-permute-done((bf16[128,2560]{0,1:T(8,128)(2,1)}, bf16[128,2560]{0,1:T(8,128)(2,1)}, u32[]{:S(2)}, u32[]{:S(2)}) %collective-permute-start.8) | collective-permute-done | bytes 655392 | tf_op jit(solution)/shard_map/ppermute | solution.py:18
  150.0 2.8 multiply_reduce_fusion
  152.8 3.2 collective-permute-start.16
  157.4 1.9 collective-permute-start.17
  160.4 5.3 %collective-permute-start.18 = (f32[5120]{0:T(1024)S(1)}, f32[5120]{0:T(1024)S(1)}, u32[]{:S(2)}, u32[]{:S(2)}) collective-permute-start(f32[5120]{0:T(1024)S(1)} %add.94), channel_id=1, source_target_pairs={{0,4},{2,6},{4,0},{6,2},{8,12},{10,14},{12,8},{14,10},{16,20},{18,... | collective-permute-start | bytes 61448 | tf_op jit(solution)/shard_map/ppermute | solution.py:26
  166.9 6.1 %collective-permute-start.19 = (f32[5120]{0:T(1024)S(1)}, f32[5120]{0:T(1024)S(1)}, u32[]{:S(2)}, u32[]{:S(2)}) collective-permute-start(f32[5120]{0:T(1024)S(1)} %add.95), channel_id=1, source_target_pairs={{0,8},{2,10},{4,12},{6,14},{8,0},{10,2},{12,4},{14,6},{16,24},{18,... | collective-permute-start | bytes 61448 | tf_op jit(solution)/shard_map/ppermute | solution.py:26
  173.0 2.0 fusion.34
  174.9 2.3 squeeze.33
  177.2 3.2 collective-permute-start.12
  181.5 3.1 collective-permute-start.13
  184.7 2.3 squeeze.35
  189.4 4.8 %collective-permute-start.15 = (bf16[128,2560]{1,0:T(8,128)(2,1)}, bf16[128,2560]{1,0:T(8,128)(2,1)}, u32[]{:S(2)}, u32[]{:S(2)}) collective-permute-start(bf16[128,2560]{1,0:T(8,128)(2,1)} %squeeze.36), channel_id=1, source_target_pairs={{0,4},{2,6},{4,8},{6,10},{8,12},{10,14},{12,16},{14,18},{16,20},{1... | collective-permute-start | bytes 1966088 | tf_op jit(solution)/shard_map/ppermute | solution.py:18
  194.2 5.6 %collective-permute-start.20 = (f32[5120]{0:T(1024)S(1)}, f32[5120]{0:T(1024)S(1)}, u32[]{:S(2)}, u32[]{:S(2)}) collective-permute-start(f32[5120]{0:T(1024)S(1)} %add.96), channel_id=1, source_target_pairs={{0,16},{2,18},{4,20},{6,22},{8,24},{10,26},{12,28},{14,30},{16,0},... | collective-permute-start | bytes 61448 | tf_op jit(solution)/shard_map/ppermute | solution.py:26
  199.9 7.9 %collective-permute-done.20 = f32[5120]{0:T(1024)S(1)} collective-permute-done((f32[5120]{0:T(1024)S(1)}, f32[5120]{0:T(1024)S(1)}, u32[]{:S(2)}, u32[]{:S(2)}) %collective-permute-start.20) | collective-permute-done | bytes 20512 | tf_op jit(solution)/shard_map/ppermute | solution.py:26
  207.8 7.9 %collective-permute-start.21 = (f32[5120]{0:T(1024)S(1)}, f32[5120]{0:T(1024)S(1)}, u32[]{:S(2)}, u32[]{:S(2)}) collective-permute-start(f32[5120]{0:T(1024)S(1)} %add.97), channel_id=1, source_target_pairs={{0,32},{2,34},{4,36},{6,38},{8,40},{10,42},{12,44},{14,46},{16,48}... | collective-permute-start | bytes 61448 | tf_op jit(solution)/shard_map/ppermute | solution.py:26
  215.7 2.6 multiply_convert_fusion.1
  218.3 1.7 copy.48
  220.0 2.2 copy.41
  222.2 64.2 %collective-permute-start.22 = (f32[5120]{0:T(1024)S(1)}, f32[5120]{0:T(1024)S(1)}, u32[]{:S(2)}, u32[]{:S(2)}) collective-permute-start(f32[5120]{0:T(1024)S(1)} %add.98), channel_id=1, source_target_pairs={{0,64},{2,66},{4,68},{6,70},{8,72},{10,74},{12,76},{14,78},{16,80}... | collective-permute-start | bytes 61448 | tf_op jit(solution)/shard_map/ppermute | solution.py:26
  286.5 2.9 fusion.32
  289.4 10.5 %collective-permute-start.23 = (f32[5120]{0:T(1024)S(1)}, f32[5120]{0:T(1024)S(1)}, u32[]{:S(2)}, u32[]{:S(2)}) collective-permute-start(f32[5120]{0:T(1024)S(1)} %add.99), channel_id=1, source_target_pairs={{0,128},{2,130},{4,132},{6,134},{8,136},{10,138},{12,140},{14,142}... | collective-permute-start | bytes 61448 | tf_op jit(solution)/shard_map/ppermute | solution.py:26
  301.1 24.1 %collective-permute-start.24 = (f32[5120]{0:T(1024)S(1)}, f32[5120]{0:T(1024)S(1)}, u32[]{:S(2)}, u32[]{:S(2)}) collective-permute-start(f32[5120]{0:T(1024)S(1)} %add.100), channel_id=1, source_target_pairs={{0,256},{2,258},{4,260},{6,262},{8,264},{10,266},{12,268},{14,270}... | collective-permute-start | bytes 61448 | tf_op jit(solution)/shard_map/ppermute | solution.py:26
  (219 shorter events, 75.4 us)
Async XLA Ops:
  2.1 16.0 %copy-start.12 = (bf16[1,128,2560]{2,1,0:T(8,128)(2,1)S(1)}, bf16[1,128,2560]{2,1,0:T(8,128)(2,1)}, u32[]{:S(2)}) copy-start(bf16[1,128,2560]{2,1,0:T(8,128)(2,1)} %param.11) | copy-start | bytes 1966084
  2.5 19.5 %copy-start.13 = (bf16[1,128,2560]{2,1,0:T(8,128)(2,1)S(1)}, bf16[1,128,2560]{2,1,0:T(8,128)(2,1)}, u32[]{:S(2)}) copy-start(bf16[1,128,2560]{2,1,0:T(8,128)(2,1)} %param.9) | copy-start | bytes 1966084
  3.8 21.0 %collective-permute-start = (bf16[128,20,128]{0,2,1:T(8,128)(2,1)S(1)}, bf16[128,20,128]{0,2,1:T(8,128)(2,1)}, u32[]{:S(2)}, u32[]{:S(2)}) collective-permute-start(bf16[128,20,128]{0,2,1:T(8,128)(2,1)S(1)} %get-tuple-element.150), channel_id=1, source_target_pairs={{0,2},{2,4},{4,6},{6,8},{8,10},{10,12},{12,14},{14,16},{16,18},{18... | collective-permute-start | bytes 1966088 | tf_op jit(solution)/shard_map/ppermute | solution.py:18
  8.3 18.8 %collective-permute-start.1 = (bf16[128,20,128]{0,2,1:T(8,128)(2,1)S(1)}, bf16[128,20,128]{0,2,1:T(8,128)(2,1)}, u32[]{:S(2)}, u32[]{:S(2)}) collective-permute-start(bf16[128,20,128]{0,2,1:T(8,128)(2,1)S(1)} %get-tuple-element.150), channel_id=1, source_target_pairs={{2,0},{4,2},{6,4},{8,6},{10,8},{12,10},{14,12},{16,14},{18,16},{20... | collective-permute-start | bytes 1966088 | tf_op jit(solution)/shard_map/ppermute | solution.py:18
  14.7 17.4 %collective-permute-start.2 = (bf16[128,20,128]{0,2,1:T(8,128)(2,1)S(1)}, bf16[128,20,128]{0,2,1:T(8,128)(2,1)}, u32[]{:S(2)}, u32[]{:S(2)}) collective-permute-start(bf16[128,20,128]{0,2,1:T(8,128)(2,1)S(1)} %get-tuple-element.150), channel_id=1, source_target_pairs={{0,4},{2,6},{4,8},{6,10},{8,12},{10,14},{12,16},{14,18},{16,20},{1... | collective-permute-start | bytes 1966088 | tf_op jit(solution)/shard_map/ppermute | solution.py:18
  16.8 20.7 %collective-permute-start.3 = (bf16[128,20,128]{0,2,1:T(8,128)(2,1)S(1)}, bf16[128,20,128]{0,2,1:T(8,128)(2,1)}, u32[]{:S(2)}, u32[]{:S(2)}) collective-permute-start(bf16[128,20,128]{0,2,1:T(8,128)(2,1)S(1)} %get-tuple-element.150), channel_id=1, source_target_pairs={{4,0},{6,2},{8,4},{10,6},{12,8},{14,10},{16,12},{18,14},{20,16},{2... | collective-permute-start | bytes 1966088 | tf_op jit(solution)/shard_map/ppermute | solution.py:18
  18.4 23.9 %collective-permute-start.4 = (bf16[128,20,128]{0,2,1:T(8,128)(2,1)S(1)}, bf16[128,20,128]{0,2,1:T(8,128)(2,1)}, u32[]{:S(2)}, u32[]{:S(2)}) collective-permute-start(bf16[128,20,128]{0,2,1:T(8,128)(2,1)S(1)} %bitcast.145), channel_id=1, source_target_pairs={{0,2},{2,4},{4,6},{6,8},{8,10},{10,12},{12,14},{14,16},{16,18},{18... | collective-permute-start | bytes 1966088 | tf_op jit(solution)/shard_map/ppermute | solution.py:18
  23.2 3.6 %copy-start.14 = (bf16[1,128,2560]{2,1,0:T(8,128)(2,1)S(1)}, bf16[1,128,2560]{2,1,0:T(8,128)(2,1)}, u32[]{:S(2)}) copy-start(bf16[1,128,2560]{2,1,0:T(8,128)(2,1)} %param.12) | copy-start | bytes 1966084
  24.8 22.8 %collective-permute-start.5 = (bf16[128,20,128]{0,2,1:T(8,128)(2,1)S(1)}, bf16[128,20,128]{0,2,1:T(8,128)(2,1)}, u32[]{:S(2)}, u32[]{:S(2)}) collective-permute-start(bf16[128,20,128]{0,2,1:T(8,128)(2,1)S(1)} %bitcast.147), channel_id=1, source_target_pairs={{2,0},{4,2},{6,4},{8,6},{10,8},{12,10},{14,12},{16,14},{18,16},{20... | collective-permute-start | bytes 1966088 | tf_op jit(solution)/shard_map/ppermute | solution.py:18
  27.1 24.0 %collective-permute-start.6 = (bf16[128,20,128]{0,2,1:T(8,128)(2,1)S(1)}, bf16[128,20,128]{0,2,1:T(8,128)(2,1)S(1)}, u32[]{:S(2)}, u32[]{:S(2)}) collective-permute-start(bf16[128,20,128]{0,2,1:T(8,128)(2,1)S(1)} %bitcast.148), channel_id=1, source_target_pairs={{0,4},{2,6},{4,8},{6,10},{8,12},{10,14},{12,16},{14,18},{16,20},{1... | collective-permute-start | bytes 1966088 | tf_op jit(solution)/shard_map/ppermute | solution.py:18
  32.1 20.0 %collective-permute-start.7 = (bf16[128,20,128]{0,2,1:T(8,128)(2,1)S(1)}, bf16[128,20,128]{0,2,1:T(8,128)(2,1)S(1)}, u32[]{:S(2)}, u32[]{:S(2)}) collective-permute-start(bf16[128,20,128]{0,2,1:T(8,128)(2,1)S(1)} %bitcast.149), channel_id=1, source_target_pairs={{4,0},{6,2},{8,4},{10,6},{12,8},{14,10},{16,12},{18,14},{20,16},{2... | collective-permute-start | bytes 1966088 | tf_op jit(solution)/shard_map/ppermute | solution.py:18
  53.0 3.6 %copy-start.9 = (bf16[128,20,128]{0,2,1:T(8,128)(2,1)}, bf16[128,20,128]{0,2,1:T(8,128)(2,1)S(1)}, u32[]{:S(2)}) copy-start(bf16[128,20,128]{0,2,1:T(8,128)(2,1)S(1)} %get-tuple-element.287) | copy-start | bytes 1966084 | tf_op jit(solution)/shard_map/while
  53.0 6.9 %copy-start.6 = (bf16[128,20,128]{0,2,1:T(8,128)(2,1)}, bf16[128,20,128]{0,2,1:T(8,128)(2,1)S(1)}, u32[]{:S(2)}) copy-start(bf16[128,20,128]{0,2,1:T(8,128)(2,1)S(1)} %get-tuple-element.286) | copy-start | bytes 1966084 | tf_op jit(solution)/shard_map/while
  62.8 3.1 copy-start.7
  65.9 3.6 %copy-start.9 = (bf16[128,20,128]{0,2,1:T(8,128)(2,1)}, bf16[128,20,128]{0,2,1:T(8,128)(2,1)S(1)}, u32[]{:S(2)}) copy-start(bf16[128,20,128]{0,2,1:T(8,128)(2,1)S(1)} %get-tuple-element.287) | copy-start | bytes 1966084 | tf_op jit(solution)/shard_map/while
  65.9 6.9 %copy-start.6 = (bf16[128,20,128]{0,2,1:T(8,128)(2,1)}, bf16[128,20,128]{0,2,1:T(8,128)(2,1)S(1)}, u32[]{:S(2)}) copy-start(bf16[128,20,128]{0,2,1:T(8,128)(2,1)S(1)} %get-tuple-element.286) | copy-start | bytes 1966084 | tf_op jit(solution)/shard_map/while
  75.7 3.1 copy-start.7
  78.8 3.6 %copy-start.9 = (bf16[128,20,128]{0,2,1:T(8,128)(2,1)}, bf16[128,20,128]{0,2,1:T(8,128)(2,1)S(1)}, u32[]{:S(2)}) copy-start(bf16[128,20,128]{0,2,1:T(8,128)(2,1)S(1)} %get-tuple-element.287) | copy-start | bytes 1966084 | tf_op jit(solution)/shard_map/while
  78.8 6.9 %copy-start.6 = (bf16[128,20,128]{0,2,1:T(8,128)(2,1)}, bf16[128,20,128]{0,2,1:T(8,128)(2,1)S(1)}, u32[]{:S(2)}) copy-start(bf16[128,20,128]{0,2,1:T(8,128)(2,1)S(1)} %get-tuple-element.286) | copy-start | bytes 1966084 | tf_op jit(solution)/shard_map/while
  88.6 3.1 copy-start.7
  91.7 3.6 %copy-start.9 = (bf16[128,20,128]{0,2,1:T(8,128)(2,1)}, bf16[128,20,128]{0,2,1:T(8,128)(2,1)S(1)}, u32[]{:S(2)}) copy-start(bf16[128,20,128]{0,2,1:T(8,128)(2,1)S(1)} %get-tuple-element.287) | copy-start | bytes 1966084 | tf_op jit(solution)/shard_map/while
  91.7 6.9 %copy-start.6 = (bf16[128,20,128]{0,2,1:T(8,128)(2,1)}, bf16[128,20,128]{0,2,1:T(8,128)(2,1)S(1)}, u32[]{:S(2)}) copy-start(bf16[128,20,128]{0,2,1:T(8,128)(2,1)S(1)} %get-tuple-element.286) | copy-start | bytes 1966084 | tf_op jit(solution)/shard_map/while
  101.5 3.1 copy-start.7
  104.7 3.6 %copy-start.9 = (bf16[128,20,128]{0,2,1:T(8,128)(2,1)}, bf16[128,20,128]{0,2,1:T(8,128)(2,1)S(1)}, u32[]{:S(2)}) copy-start(bf16[128,20,128]{0,2,1:T(8,128)(2,1)S(1)} %get-tuple-element.287) | copy-start | bytes 1966084 | tf_op jit(solution)/shard_map/while
  104.7 6.9 %copy-start.6 = (bf16[128,20,128]{0,2,1:T(8,128)(2,1)}, bf16[128,20,128]{0,2,1:T(8,128)(2,1)S(1)}, u32[]{:S(2)}) copy-start(bf16[128,20,128]{0,2,1:T(8,128)(2,1)S(1)} %get-tuple-element.286) | copy-start | bytes 1966084 | tf_op jit(solution)/shard_map/while
  114.4 3.1 copy-start.7
  120.1 16.8 %copy-start.3 = (f32[1,128,2560]{1,2,0:T(8,128)S(1)}, f32[1,128,2560]{1,2,0:T(8,128)}, u32[]{:S(2)}) copy-start(f32[1,128,2560]{1,2,0:T(8,128)} %copy-done.2) | copy-start | bytes 3932164
  121.6 17.5 %collective-permute-start.10 = (bf16[128,2560]{0,1:T(8,128)(2,1)}, bf16[128,2560]{0,1:T(8,128)(2,1)}, u32[]{:S(2)}, u32[]{:S(2)}) collective-permute-start(bf16[128,2560]{0,1:T(8,128)(2,1)} %bitcast.16), channel_id=1, source_target_pairs={{4,0},{6,2},{8,4},{10,6},{12,8},{14,10},{16,12},{18,14},{20,16},{2... | collective-permute-start | bytes 1966088 | tf_op jit(solution)/shard_map/ppermute | solution.py:18
  122.9 16.3 %collective-permute-start.11 = (bf16[128,2560]{0,1:T(8,128)(2,1)}, bf16[128,2560]{0,1:T(8,128)(2,1)}, u32[]{:S(2)}, u32[]{:S(2)}) collective-permute-start(bf16[128,2560]{0,1:T(8,128)(2,1)} %bitcast.17), channel_id=1, source_target_pairs={{0,4},{2,6},{4,8},{6,10},{8,12},{10,14},{12,16},{14,18},{16,20},{1... | collective-permute-start | bytes 1966088 | tf_op jit(solution)/shard_map/ppermute | solution.py:18
  129.0 19.5 %collective-permute-start.8 = (bf16[128,2560]{0,1:T(8,128)(2,1)}, bf16[128,2560]{0,1:T(8,128)(2,1)}, u32[]{:S(2)}, u32[]{:S(2)}) collective-permute-start(bf16[128,2560]{0,1:T(8,128)(2,1)} %bitcast.14), channel_id=1, source_target_pairs={{2,0},{4,2},{6,4},{8,6},{10,8},{12,10},{14,12},{16,14},{18,16},{20... | collective-permute-start | bytes 1966088 | tf_op jit(solution)/shard_map/ppermute | solution.py:18
  134.9 15.1 %collective-permute-start.9 = (bf16[128,2560]{0,1:T(8,128)(2,1)}, bf16[128,2560]{0,1:T(8,128)(2,1)}, u32[]{:S(2)}, u32[]{:S(2)}) collective-permute-start(bf16[128,2560]{0,1:T(8,128)(2,1)} %bitcast.15), channel_id=1, source_target_pairs={{0,2},{2,4},{4,6},{6,8},{8,10},{10,12},{12,14},{14,16},{16,18},{18... | collective-permute-start | bytes 1966088 | tf_op jit(solution)/shard_map/ppermute | solution.py:18
  136.9 13.1 %copy-start.1 = (bf16[1,128,2560]{1,2,0:T(8,128)(2,1)S(1)}, bf16[1,128,2560]{1,2,0:T(8,128)(2,1)}, u32[]{:S(2)}) copy-start(bf16[1,128,2560]{1,2,0:T(8,128)(2,1)} %copy-done) | copy-start | bytes 1966084
  136.9 13.1 %copy-start.11 = (f32[5,128,4,128]{1,3,2,0:T(8,128)S(1)}, f32[5,128,4,128]{1,3,2,0:T(8,128)}, u32[]{:S(2)}) copy-start(f32[5,128,4,128]{1,3,2,0:T(8,128)} %get-tuple-element.72) | copy-start | bytes 3932164
  150.0 23.0 %copy-start.8 = (bf16[5,512,4,128]{3,2,0,1:T(4,128)(2,1)S(1)}, bf16[5,512,4,128]{3,2,0,1:T(4,128)(2,1)}, u32[]{:S(2)}) copy-start(bf16[5,512,4,128]{3,2,0,1:T(4,128)(2,1)} %get-tuple-element.75) | copy-start | bytes 7864324
  152.8 4.5 %collective-permute-start.16 = (f32[5120]{0:T(1024)S(1)}, f32[5120]{0:T(1024)S(1)}, u32[]{:S(2)}, u32[]{:S(2)}) collective-permute-start(f32[5120]{0:T(1024)S(1)} %pad_maximum_fusion), channel_id=1, source_target_pairs={{0,1},{1,0},{2,3},{3,2},{4,5},{5,4},{6,7},{7,6},{8,9},{9,8},{10,11... | collective-permute-start | bytes 61448 | tf_op jit(solution)/shard_map/ppermute | solution.py:26
  157.4 3.1 collective-permute-start.17
  160.4 6.5 %collective-permute-start.18 = (f32[5120]{0:T(1024)S(1)}, f32[5120]{0:T(1024)S(1)}, u32[]{:S(2)}, u32[]{:S(2)}) collective-permute-start(f32[5120]{0:T(1024)S(1)} %add.94), channel_id=1, source_target_pairs={{0,4},{2,6},{4,0},{6,2},{8,12},{10,14},{12,8},{14,10},{16,20},{18,... | collective-permute-start | bytes 61448 | tf_op jit(solution)/shard_map/ppermute | solution.py:26
  166.9 27.3 %collective-permute-start.19 = (f32[5120]{0:T(1024)S(1)}, f32[5120]{0:T(1024)S(1)}, u32[]{:S(2)}, u32[]{:S(2)}) collective-permute-start(f32[5120]{0:T(1024)S(1)} %add.95), channel_id=1, source_target_pairs={{0,8},{2,10},{4,12},{6,14},{8,0},{10,2},{12,4},{14,6},{16,24},{18,... | collective-permute-start | bytes 61448 | tf_op jit(solution)/shard_map/ppermute | solution.py:26
  177.2 109.2 %collective-permute-start.12 = (bf16[128,2560]{1,0:T(8,128)(2,1)}, bf16[128,2560]{1,0:T(8,128)(2,1)}, u32[]{:S(2)}, u32[]{:S(2)}) collective-permute-start(bf16[128,2560]{1,0:T(8,128)(2,1)} %squeeze.33), channel_id=1, source_target_pairs={{2,0},{4,2},{6,4},{8,6},{10,8},{12,10},{14,12},{16,14},{18,16},{20... | collective-permute-start | bytes 1966088 | tf_op jit(solution)/shard_map/ppermute | solution.py:18
  181.5 104.9 %collective-permute-start.13 = (bf16[128,2560]{1,0:T(8,128)(2,1)}, bf16[128,2560]{1,0:T(8,128)(2,1)}, u32[]{:S(2)}, u32[]{:S(2)}) collective-permute-start(bf16[128,2560]{1,0:T(8,128)(2,1)} %squeeze.34), channel_id=1, source_target_pairs={{0,2},{2,4},{4,6},{6,8},{8,10},{10,12},{12,14},{14,16},{16,18},{18... | collective-permute-start | bytes 1966088 | tf_op jit(solution)/shard_map/ppermute | solution.py:18
  184.7 31.1 %copy-start.5 = (bf16[1,128,2560]{1,2,0:T(8,128)(2,1)S(1)}, bf16[1,128,2560]{1,2,0:T(8,128)(2,1)}, u32[]{:S(2)}) copy-start(bf16[1,128,2560]{1,2,0:T(8,128)(2,1)} %copy-done.4) | copy-start | bytes 1966084
  187.0 99.5 %collective-permute-start.14 = (bf16[128,2560]{1,0:T(8,128)(2,1)}, bf16[128,2560]{1,0:T(8,128)(2,1)}, u32[]{:S(2)}, u32[]{:S(2)}) collective-permute-start(bf16[128,2560]{1,0:T(8,128)(2,1)} %squeeze.35), channel_id=1, source_target_pairs={{4,0},{6,2},{8,4},{10,6},{12,8},{14,10},{16,12},{18,14},{20,16},{2... | collective-permute-start | bytes 1966088 | tf_op jit(solution)/shard_map/ppermute | solution.py:18
  189.4 97.1 %collective-permute-start.15 = (bf16[128,2560]{1,0:T(8,128)(2,1)}, bf16[128,2560]{1,0:T(8,128)(2,1)}, u32[]{:S(2)}, u32[]{:S(2)}) collective-permute-start(bf16[128,2560]{1,0:T(8,128)(2,1)} %squeeze.36), channel_id=1, source_target_pairs={{0,4},{2,6},{4,8},{6,10},{8,12},{10,14},{12,16},{14,18},{16,20},{1... | collective-permute-start | bytes 1966088 | tf_op jit(solution)/shard_map/ppermute | solution.py:18
  194.2 13.5 %collective-permute-start.20 = (f32[5120]{0:T(1024)S(1)}, f32[5120]{0:T(1024)S(1)}, u32[]{:S(2)}, u32[]{:S(2)}) collective-permute-start(f32[5120]{0:T(1024)S(1)} %add.96), channel_id=1, source_target_pairs={{0,16},{2,18},{4,20},{6,22},{8,24},{10,26},{12,28},{14,30},{16,0},... | collective-permute-start | bytes 61448 | tf_op jit(solution)/shard_map/ppermute | solution.py:26
  207.8 14.4 %collective-permute-start.21 = (f32[5120]{0:T(1024)S(1)}, f32[5120]{0:T(1024)S(1)}, u32[]{:S(2)}, u32[]{:S(2)}) collective-permute-start(f32[5120]{0:T(1024)S(1)} %add.97), channel_id=1, source_target_pairs={{0,32},{2,34},{4,36},{6,38},{8,40},{10,42},{12,44},{14,46},{16,48}... | collective-permute-start | bytes 61448 | tf_op jit(solution)/shard_map/ppermute | solution.py:26
  222.2 67.2 %collective-permute-start.22 = (f32[5120]{0:T(1024)S(1)}, f32[5120]{0:T(1024)S(1)}, u32[]{:S(2)}, u32[]{:S(2)}) collective-permute-start(f32[5120]{0:T(1024)S(1)} %add.98), channel_id=1, source_target_pairs={{0,64},{2,66},{4,68},{6,70},{8,72},{10,74},{12,76},{14,78},{16,80}... | collective-permute-start | bytes 61448 | tf_op jit(solution)/shard_map/ppermute | solution.py:26
  289.4 11.7 %collective-permute-start.23 = (f32[5120]{0:T(1024)S(1)}, f32[5120]{0:T(1024)S(1)}, u32[]{:S(2)}, u32[]{:S(2)}) collective-permute-start(f32[5120]{0:T(1024)S(1)} %add.99), channel_id=1, source_target_pairs={{0,128},{2,130},{4,132},{6,134},{8,136},{10,138},{12,140},{14,142}... | collective-permute-start | bytes 61448 | tf_op jit(solution)/shard_map/ppermute | solution.py:26
  301.1 25.6 %collective-permute-start.24 = (f32[5120]{0:T(1024)S(1)}, f32[5120]{0:T(1024)S(1)}, u32[]{:S(2)}, u32[]{:S(2)}) collective-permute-start(f32[5120]{0:T(1024)S(1)} %add.100), channel_id=1, source_target_pairs={{0,256},{2,258},{4,260},{6,262},{8,264},{10,266},{12,268},{14,270}... | collective-permute-start | bytes 61448 | tf_op jit(solution)/shard_map/ppermute | solution.py:26
  (11 other events, 18.7 us)

commit v2 on v1

v2 whole, which is shorter than its diff:
```python
import functools
import math

import jax
import jax.numpy as jnp
from jax import lax
from jax.experimental import pallas as pl
from jax.experimental.pallas import tpu as pltpu
from jax.sharding import PartitionSpec as P

HEAD = 128
LEVELS = 2
HEADS_PER_STEP = 4


EPS = 1e-06

NT = (((1,), (1,)), ((), ()))
TN = (((0,), (0,)), ((), ()))


def from_behind(value, axis, steps):
    count = lax.axis_size(axis)
    first, last = (max(0, -steps), min(count, count - steps))
    return lax.ppermute(value, axis, [(source, source + steps) for source in range(first, last)])


def all_sum(value, axes):
    for axis in axes:
        count = lax.axis_size(axis)
        bit = 1
        while bit < count:
            value = value + lax.ppermute(value, axis, [(i, i ^ bit) for i in range(count)])
            bit *= 2
    return value


def level_offsets(levels):
    return [sign * 2**level for level in range(levels) for sign in (-1, 1)]


def normalize(raw):
    numbers = raw.astype(jnp.float32)
    inverse = lax.rsqrt(jnp.mean(numbers * numbers, axis=-1, keepdims=True) + EPS)
    return (numbers * inverse, inverse)


def norm_backward(grad_norm, gain, hat, inverse):
    scaled = grad_norm * gain
    inner = jnp.mean(scaled * hat, axis=-1, keepdims=True)
    return (inverse * (scaled - hat * inner), jnp.sum(grad_norm * hat, axis=0))


def attention_kernel(live_ref, q_ref, k_ref, v_ref, g_ref, *refs):
    slots = (len(refs) - 3) // 2
    fetched = refs[:slots]
    dq_ref, dk_ref, dv_ref = refs[slots:slots + 3]
    far = refs[slots + 3:]
    rows = q_ref.shape[0]
    scale = 1.0 / math.sqrt(HEAD)
    live = live_ref[...] > 0
    for h in range(q_ref.shape[1] // HEAD):
        cols = pl.ds(h * HEAD, HEAD)
        q = q_ref[:, cols]
        g = g_ref[:, cols]
        keys = jnp.concatenate([k_ref[:, cols]] + [r[0, :, cols] for r in fetched], axis=0)
        vals = jnp.concatenate([v_ref[:, cols]] + [r[1, :, cols] for r in fetched], axis=0)
        scores = lax.dot_general(q, keys, NT, preferred_element_type=jnp.float32) * scale
        highest = jnp.max(jnp.where(live, scores, -jnp.inf), axis=1, keepdims=True)
        total = jnp.sum(jnp.where(live, jnp.exp(scores - highest), 0.0), axis=1, keepdims=True)
        log_total = highest + jnp.log(total)
        prob = jnp.where(live, jnp.exp(scores - log_total), 0.0).astype(jnp.bfloat16)
        attended = jnp.dot(prob, vals, preferred_element_type=jnp.float32)
        delta = jnp.sum(g.astype(jnp.float32) * attended, axis=1, keepdims=True)
        prob_grad = lax.dot_general(g, vals, NT, preferred_element_type=jnp.float32)
        score_grad = (prob.astype(jnp.float32) * (prob_grad - delta) * scale).astype(jnp.bfloat16)
        dq_ref[:, cols] = jnp.dot(score_grad, keys, preferred_element_type=jnp.float32)
        grad_k = lax.dot_general(score_grad, q, TN, preferred_element_type=jnp.float32)
        grad_v = lax.dot_general(prob, g, TN, preferred_element_type=jnp.float32)
        dk_ref[:, cols] = grad_k[:rows]
        dv_ref[:, cols] = grad_v[:rows]
        for slot in range(slots):
            part = slice((slot + 1) * rows, (slot + 2) * rows)
            far[slot][0, :, cols] = grad_k[part].astype(jnp.bfloat16)
            far[slot][1, :, cols] = grad_v[part].astype(jnp.bfloat16)


def attention(live, q_norm, k_norm, value_rows, grad_rows, fetched):
    rows, features = q_norm.shape
    width = HEADS_PER_STEP * HEAD
    slots = len(fetched)
    tile = pl.BlockSpec((rows, width), lambda h: (0, h))
    pair = pl.BlockSpec((2, rows, width), lambda h: (0, 0, h))
    f32 = jax.ShapeDtypeStruct((rows, features), jnp.float32)
    bf16_pair = jax.ShapeDtypeStruct((2, rows, features), jnp.bfloat16)
    keys = rows * (slots + 1)
    flops = 2 * rows * keys * features * 6
    return pl.pallas_call(
        attention_kernel,
        grid=(features // width,),
        in_specs=[pl.BlockSpec(live.shape, lambda h: (0, 0))] + [tile] * 4 + [pair] * slots,
        out_specs=[tile] * 3 + [pair] * slots,
        out_shape=[f32] * 3 + [bf16_pair] * slots,
        cost_estimate=pl.CostEstimate(
            flops=flops,
            transcendentals=2 * rows * keys * (features // HEAD),
            bytes_accessed=2 * rows * features * (4 + 4 * slots) + 12 * rows * features,
        ),
    )(live, q_norm, k_norm, value_rows, grad_rows, *fetched)


def body(q_raw, k_raw, values, cotangent, q_gain, k_gain, key_tiles):
    tile_rows = q_raw.shape[1]
    features = q_raw.shape[2]
    offsets = level_offsets(LEVELS)
    q_hat, q_inv = normalize(q_raw[0])
    k_hat, k_inv = normalize(k_raw[0])
    q_norm = (q_hat * q_gain).astype(jnp.bfloat16)
    k_norm = (k_hat * k_gain).astype(jnp.bfloat16)
    value_rows = values[0]
    grad_rows = cotangent[0]
    entries = key_tiles[0]
    stacked = jnp.stack([k_norm, value_rows])
    fetched = [from_behind(stacked, "seq", -offset) for offset in offsets]
    live = jnp.repeat(
        jnp.concatenate([jnp.ones((1,), jnp.int32), (entries >= 0).astype(jnp.int32)]), tile_rows
    )[None, :]
    q_norm_grad, k_norm_grad, v_sum, *far = attention(
        live, q_norm, k_norm, value_rows, grad_rows, fetched
    )
    for slot, offset in enumerate(offsets):
        back = from_behind(far[slot], "seq", offset)
        k_norm_grad = k_norm_grad + back[0].astype(jnp.float32)
        v_sum = v_sum + back[1].astype(jnp.float32)
    q_back, q_part = norm_backward(q_norm_grad, q_gain, q_hat, q_inv)
    k_back, k_part = norm_backward(k_norm_grad, k_gain, k_hat, k_inv)
    gain_grads = all_sum(jnp.concatenate([q_part, k_part]), ("dp", "seq"))
    q_gain_grad, k_gain_grad = gain_grads[:features], gain_grads[features:]
    return (
        q_back.astype(jnp.bfloat16)[None],
        k_back.astype(jnp.bfloat16)[None],
        v_sum.astype(jnp.bfloat16)[None],
        q_gain_grad,
        k_gain_grad,
    )


def solution(mesh):
    return jax.shard_map(
        body,
        mesh=mesh,
        in_specs=(
            P("dp", "seq", None),
            P("dp", "seq", None),
            P("dp", "seq", None),
            P("dp", "seq", None),
            P(),
            P(),
            P("seq", None),
        ),
        out_specs=(P("dp", "seq", None), P("dp", "seq", None), P("dp", "seq", None), P(), P()),
        check_vma=False,
    )
```

time: 329 us -> 293 us (0.89)
  the two profiles are of different devices: /device:TPU:1 before, /device:TPU:32 now
where the time goes in v2:
time: 293 us; the launch traced here: 292 us
  waiting for transfers between devices  194 us (66%)
  starting transfers between devices  62.7 us (21%)
  Pallas kernels  20.1 us (7%)
  other arithmetic  12.2 us (4%)
    ppermute x8, waiting for transfers between devices, from_behind(): lax.ppermute(value, axis, [(source, source + steps) for source in range(f...  155 us
    ppermute x9, waiting for transfers between devices, all_sum(): lax.ppermute(value, axis, [(i, i ^ bit) for i in range(count)])  39.1 us
    ppermute x8, starting transfers between devices, from_behind(): lax.ppermute(value, axis, [(source, source + steps) for source in range(f...  36.3 us
    ppermute x9, starting transfers between devices, all_sum(): lax.ppermute(value, axis, [(i, i ^ bit) for i in range(count)])  26.4 us
    pallas_call x1, Pallas kernels, attention(): pl.pallas_call(attention_kernel, grid=(features // width,), in_specs=[pl....  20.1 us
  transfers between devices with their start and end apart: 17, of which 14 were waited for; matrix products, arithmetic and copies ran while one was open for 2% of the time, Pallas kernels for 0%

profile of v2, /device:TPU:32, one launch (start us, length us, event | category | flops | bytes accessed | tf_op | source)
XLA Modules:
  0.0 292.1 jit_solution(14934803246334527317)
XLA Ops:
  0.6 0.0 copy-start.4
  0.6 1.4 fusion.16
  2.0 1.3 fusion.18
  3.3 0.0 copy-start.11
  3.4 0.1 pad_maximum_fusion
  3.5 13.0 %collective-permute-start.3 = (bf16[2,128,2560]{2,1,0:T(8,128)(2,1)S(1)}, bf16[2,128,2560]{2,1,0:T(8,128)(2,1)S(1)}, u32[]{:S(2)}, u32[]{:S(2)}) collective-permute-start(bf16[2,128,2560]{2,1,0:T(8,128)(2,1)S(1)} %pad_maximum_fusion), channel_id=1, source_target_pairs={{4,0},{6,2},{8,4},{10,6},{12,8},{14,10},{16,12},{18,14},{20,16},{2... | collective-permute-start | bytes 3932168 | tf_op jit(solution)/shard_map/ppermute | solution.py:25
  16.6 1.9 collective-permute-start.2
  18.5 9.1 %collective-permute-start.1 = (bf16[2,128,2560]{2,1,0:T(8,128)(2,1)S(1)}, bf16[2,128,2560]{2,1,0:T(8,128)(2,1)S(1)}, u32[]{:S(2)}, u32[]{:S(2)}) collective-permute-start(bf16[2,128,2560]{2,1,0:T(8,128)(2,1)S(1)} %pad_maximum_fusion), channel_id=1, source_target_pairs={{2,0},{4,2},{6,4},{8,6},{10,8},{12,10},{14,12},{16,14},{18,16},{20... | collective-permute-start | bytes 3932168 | tf_op jit(solution)/shard_map/ppermute | solution.py:25
  27.7 1.9 collective-permute-start
  29.6 0.1 add_convert_fusion
  29.7 0.1 broadcast_bitcast_fusion
  29.8 0.6 copy.14
  30.3 0.2 fusion.25
  30.6 1.4 fusion.10
  32.0 54.7 %collective-permute-done.3.refs_3_ = bf16[2,128,2560]{2,1,0:T(8,128)(2,1)S(1)} collective-permute-done((bf16[2,128,2560]{2,1,0:T(8,128)(2,1)S(1)}, bf16[2,128,2560]{2,1,0:T(8,128)(2,1)S(1)}, u32[]{:S(2)}, u32[]{:S(2)}) %collective-permute-start.3) | collective-permute-done | bytes 1310752 | tf_op jit(solution)/shard_map/ppermute | solution.py:25
  86.7 14.0 %collective-permute-done.1.refs_1_ = bf16[2,128,2560]{2,1,0:T(8,128)(2,1)S(1)} collective-permute-done((bf16[2,128,2560]{2,1,0:T(8,128)(2,1)S(1)}, bf16[2,128,2560]{2,1,0:T(8,128)(2,1)S(1)}, u32[]{:S(2)}, u32[]{:S(2)}) %collective-permute-start.1) | collective-permute-done | bytes 1310752 | tf_op jit(solution)/shard_map/ppermute | solution.py:25
  100.8 10.5 %collective-permute-done.refs_0_ = bf16[2,128,2560]{2,1,0:T(8,128)(2,1)S(1)} collective-permute-done((bf16[2,128,2560]{2,1,0:T(8,128)(2,1)S(1)}, bf16[2,128,2560]{2,1,0:T(8,128)(2,1)S(1)}, u32[]{:S(2)}, u32[]{:S(2)}) %collective-permute-start) | collective-permute-done | bytes 1310752 | tf_op jit(solution)/shard_map/ppermute | solution.py:25
  111.3 1.1 copy-done.10
  112.3 20.1 %shard_map.110 = (f32[128,2560]{1,0:T(8,128)}, f32[128,2560]{1,0:T(8,128)}, f32[128,2560]{1,0:T(8,128)}, bf16[2,128,2560]{2,1,0:T(8,128)(2,1)}, bf16[2,128,2560]...) custom-call(s32[1,640]{1,0:T(1,128)} %bitcast.98, ...), custom_call_target="tpu_custom_call" | custom-call | flops 2516582400 | bytes 17039360 | tf_op jit(solution)/shard_map/pallas_call | solution.py:98
  132.5 2.1 collective-permute-start.4
  134.6 2.4 collective-permute-start.5
  137.0 1.9 collective-permute-start.6
  138.9 3.9 %collective-permute-start.7 = (bf16[2,128,2560]{2,1,0:T(8,128)(2,1)}, bf16[2,128,2560]{2,1,0:T(8,128)(2,1)S(1)}, u32[]{:S(2)}, u32[]{:S(2)}) collective-permute-start(bf16[2,128,2560]{2,1,0:T(8,128)(2,1)} %get-tuple-element.17), channel_id=1, source_target_pairs={{0,4},{2,6},{4,8},{6,10},{8,12},{10,14},{12,16},{14,18},{16,20},{1... | collective-permute-start | bytes 3932168 | tf_op jit(solution)/shard_map/ppermute | solution.py:25
  142.8 1.8 fusion.24
  144.6 61.1 %collective-permute-done.4 = bf16[2,128,2560]{2,1,0:T(8,128)(2,1)S(1)} collective-permute-done((bf16[2,128,2560]{2,1,0:T(8,128)(2,1)}, bf16[2,128,2560]{2,1,0:T(8,128)(2,1)S(1)}, u32[]{:S(2)}, u32[]{:S(2)}) %collective-permute-start.4) | collective-permute-done | bytes 1310752 | tf_op jit(solution)/shard_map/ppermute | solution.py:25
  205.7 14.1 %collective-permute-done.6 = bf16[2,128,2560]{2,1,0:T(8,128)(2,1)S(1)} collective-permute-done((bf16[2,128,2560]{2,1,0:T(8,128)(2,1)}, bf16[2,128,2560]{2,1,0:T(8,128)(2,1)S(1)}, u32[]{:S(2)}, u32[]{:S(2)}) %collective-permute-start.6) | collective-permute-done | bytes 1310752 | tf_op jit(solution)/shard_map/ppermute | solution.py:25
  219.9 3.4 %fusion.15 = (f32[2560]{0:T(1024)S(1)}, f32[128]{0:T(128)S(1)}, f32[128,2560]{1,0:T(8,128)S(1)}, bf16[1,128,2560]{2,1,0:T(8,128)(2,1)}) fusion(bf16[1,128,2560]{2,1,0:T(8,128)(2,1)S(1)} %copy-done, f32[128]{0:T(128)S(1)} %add_rsqrt_fusion, f32[2560]{0:T(1024)S(1)} %copy-done.5, bf16[2,128,2560]{2,1,0:T(8,128)(2,1)S(1)} %collective-permute-done.7, ...), kind=kLoop, calls=%fused_computation.19 | loop fusion | flops 7861632 | bytes 10507264 | tf_op jit(solution)/shard_map/reduce_sum | solution.py:51
  223.3 1.9 collective-permute-start.8
  225.2 3.7 %collective-permute-done.8 = f32[5120]{0:T(1024)S(1)} collective-permute-done((f32[5120]{0:T(1024)S(1)}, f32[5120]{0:T(1024)S(1)}, u32[]{:S(2)}, u32[]{:S(2)}) %collective-permute-start.8) | collective-permute-done | bytes 20512 | tf_op jit(solution)/shard_map/ppermute | solution.py:33
  229.0 10.9 %collective-permute-start.9 = (f32[5120]{0:T(1024)S(1)}, f32[5120]{0:T(1024)S(1)}, u32[]{:S(2)}, u32[]{:S(2)}) collective-permute-start(f32[5120]{0:T(1024)S(1)} %fusion.31), channel_id=1, source_target_pairs={{0,2},{2,0},{4,6},{6,4},{8,10},{10,8},{12,14},{14,12},{16,18},{18,... | collective-permute-start | bytes 61448 | tf_op jit(solution)/shard_map/ppermute | solution.py:33
  239.9 0.8 collective-permute-done.9
  240.7 1.9 collective-permute-start.10
  242.6 3.7 %collective-permute-done.10 = f32[5120]{0:T(1024)S(1)} collective-permute-done((f32[5120]{0:T(1024)S(1)}, f32[5120]{0:T(1024)S(1)}, u32[]{:S(2)}, u32[]{:S(2)}) %collective-permute-start.10) | collective-permute-done | bytes 20512 | tf_op jit(solution)/shard_map/ppermute | solution.py:33
  246.3 1.9 collective-permute-start.11
  248.3 5.3 %collective-permute-done.11 = f32[5120]{0:T(1024)S(1)} collective-permute-done((f32[5120]{0:T(1024)S(1)}, f32[5120]{0:T(1024)S(1)}, u32[]{:S(2)}, u32[]{:S(2)}) %collective-permute-start.11) | collective-permute-done | bytes 20512 | tf_op jit(solution)/shard_map/ppermute | solution.py:33
  253.5 1.9 collective-permute-start.12
  255.4 3.7 %collective-permute-done.12 = f32[5120]{0:T(1024)S(1)} collective-permute-done((f32[5120]{0:T(1024)S(1)}, f32[5120]{0:T(1024)S(1)}, u32[]{:S(2)}, u32[]{:S(2)}) %collective-permute-start.12) | collective-permute-done | bytes 20512 | tf_op jit(solution)/shard_map/ppermute | solution.py:33
  259.2 1.9 collective-permute-start.13
  261.1 4.6 %collective-permute-done.13 = f32[5120]{0:T(1024)S(1)} collective-permute-done((f32[5120]{0:T(1024)S(1)}, f32[5120]{0:T(1024)S(1)}, u32[]{:S(2)}, u32[]{:S(2)}) %collective-permute-start.13) | collective-permute-done | bytes 20512 | tf_op jit(solution)/shard_map/ppermute | solution.py:33
  265.8 1.9 collective-permute-start.14
  267.7 1.2 fusion.28
  268.9 6.4 %collective-permute-done.14 = f32[5120]{0:T(1024)S(1)} collective-permute-done((f32[5120]{0:T(1024)S(1)}, f32[5120]{0:T(1024)S(1)}, u32[]{:S(2)}, u32[]{:S(2)}) %collective-permute-start.14) | collective-permute-done | bytes 20512 | tf_op jit(solution)/shard_map/ppermute | solution.py:33
  275.3 2.2 collective-permute-start.15
  277.5 4.4 %collective-permute-done.15 = f32[5120]{0:T(1024)S(1)} collective-permute-done((f32[5120]{0:T(1024)S(1)}, f32[5120]{0:T(1024)S(1)}, u32[]{:S(2)}, u32[]{:S(2)}) %collective-permute-start.15) | collective-permute-done | bytes 20512 | tf_op jit(solution)/shard_map/ppermute | solution.py:33
  281.9 1.9 collective-permute-start.16
  283.8 1.2 fusion.29
  285.1 6.4 %collective-permute-done.16 = f32[5120]{0:T(1024)S(1)} collective-permute-done((f32[5120]{0:T(1024)S(1)}, f32[5120]{0:T(1024)S(1)}, u32[]{:S(2)}, u32[]{:S(2)}) %collective-permute-start.16) | collective-permute-done | bytes 20512 | tf_op jit(solution)/shard_map/ppermute | solution.py:33
  291.5 0.6 fusion.30
  (39 shorter events, 0.1 us)
Async XLA Ops:
  0.6 2.7 copy-start.4
  3.3 26.2 %copy-start.11 = (s32[1,4]{1,0:T(1,128)S(1)}, s32[1,4]{1,0:T(1,128)}, u32[]{:S(2)}) copy-start(s32[1,4]{1,0:T(1,128)} %param.13) | copy-start | bytes 52
  3.4 27.0 %copy-start.1 = (bf16[1,128,2560]{2,1,0:T(8,128)(2,1)S(1)}, bf16[1,128,2560]{2,1,0:T(8,128)(2,1)}, u32[]{:S(2)}) copy-start(bf16[1,128,2560]{2,1,0:T(8,128)(2,1)} %param.7) | copy-start | bytes 1966084
  3.4 27.2 %copy-start = (bf16[1,128,2560]{2,1,0:T(8,128)(2,1)S(1)}, bf16[1,128,2560]{2,1,0:T(8,128)(2,1)}, u32[]{:S(2)}) copy-start(bf16[1,128,2560]{2,1,0:T(8,128)(2,1)} %param.8) | copy-start | bytes 1966084
  3.4 27.2 %copy-start.5 = (f32[2560]{0:T(1024)S(1)}, f32[2560]{0:T(1024)}, u32[]{:S(2)}) copy-start(f32[2560]{0:T(1024)} %param.12) | copy-start | bytes 30724
  3.4 27.2 %copy-start.6 = (f32[2560]{0:T(1024)S(1)}, f32[2560]{0:T(1024)}, u32[]{:S(2)}) copy-start(f32[2560]{0:T(1024)} %param.11) | copy-start | bytes 30724
  3.5 83.2 %collective-permute-start.3 = (bf16[2,128,2560]{2,1,0:T(8,128)(2,1)S(1)}, bf16[2,128,2560]{2,1,0:T(8,128)(2,1)S(1)}, u32[]{:S(2)}, u32[]{:S(2)}) collective-permute-start(bf16[2,128,2560]{2,1,0:T(8,128)(2,1)S(1)} %pad_maximum_fusion), channel_id=1, source_target_pairs={{4,0},{6,2},{8,4},{10,6},{12,8},{14,10},{16,12},{18,14},{20,16},{2... | collective-permute-start | bytes 3932168 | tf_op jit(solution)/shard_map/ppermute | solution.py:25
  16.6 70.2 %collective-permute-start.2 = (bf16[2,128,2560]{2,1,0:T(8,128)(2,1)S(1)}, bf16[2,128,2560]{2,1,0:T(8,128)(2,1)S(1)}, u32[]{:S(2)}, u32[]{:S(2)}) collective-permute-start(bf16[2,128,2560]{2,1,0:T(8,128)(2,1)S(1)} %pad_maximum_fusion), channel_id=1, source_target_pairs={{0,4},{2,6},{4,8},{6,10},{8,12},{10,14},{12,16},{14,18},{16,20},{1... | collective-permute-start | bytes 3932168 | tf_op jit(solution)/shard_map/ppermute | solution.py:25
  18.5 82.3 %collective-permute-start.1 = (bf16[2,128,2560]{2,1,0:T(8,128)(2,1)S(1)}, bf16[2,128,2560]{2,1,0:T(8,128)(2,1)S(1)}, u32[]{:S(2)}, u32[]{:S(2)}) collective-permute-start(bf16[2,128,2560]{2,1,0:T(8,128)(2,1)S(1)} %pad_maximum_fusion), channel_id=1, source_target_pairs={{2,0},{4,2},{6,4},{8,6},{10,8},{12,10},{14,12},{16,14},{18,16},{20... | collective-permute-start | bytes 3932168 | tf_op jit(solution)/shard_map/ppermute | solution.py:25
  27.7 83.6 %collective-permute-start = (bf16[2,128,2560]{2,1,0:T(8,128)(2,1)S(1)}, bf16[2,128,2560]{2,1,0:T(8,128)(2,1)S(1)}, u32[]{:S(2)}, u32[]{:S(2)}) collective-permute-start(bf16[2,128,2560]{2,1,0:T(8,128)(2,1)S(1)} %pad_maximum_fusion), channel_id=1, source_target_pairs={{0,2},{2,4},{4,6},{6,8},{8,10},{10,12},{12,14},{14,16},{16,18},{18... | collective-permute-start | bytes 3932168 | tf_op jit(solution)/shard_map/ppermute | solution.py:25
  86.7 25.6 %copy-start.7 = (bf16[2,128,2560]{2,1,0:T(8,128)(2,1)}, bf16[2,128,2560]{2,1,0:T(8,128)(2,1)S(1)}, u32[]{:S(2)}) copy-start(bf16[2,128,2560]{2,1,0:T(8,128)(2,1)S(1)} %collective-permute-done.3.refs_3_) | copy-start | bytes 3932164
  86.7 24.5 %copy-start.8 = (bf16[2,128,2560]{2,1,0:T(8,128)(2,1)}, bf16[2,128,2560]{2,1,0:T(8,128)(2,1)S(1)}, u32[]{:S(2)}) copy-start(bf16[2,128,2560]{2,1,0:T(8,128)(2,1)S(1)} %collective-permute-done.2.refs_2_) | copy-start | bytes 3932164
  100.8 10.5 %copy-start.9 = (bf16[2,128,2560]{2,1,0:T(8,128)(2,1)}, bf16[2,128,2560]{2,1,0:T(8,128)(2,1)S(1)}, u32[]{:S(2)}) copy-start(bf16[2,128,2560]{2,1,0:T(8,128)(2,1)S(1)} %collective-permute-done.1.refs_1_) | copy-start | bytes 3932164
  111.3 1.1 copy-start.10
  132.5 87.4 %copy-start.3 = (f32[128,2560]{1,0:T(8,128)S(1)}, f32[128,2560]{1,0:T(8,128)}, u32[]{:S(2)}) copy-start(f32[128,2560]{1,0:T(8,128)} %get-tuple-element.13) | copy-start | bytes 3932164
  132.5 73.2 %collective-permute-start.4 = (bf16[2,128,2560]{2,1,0:T(8,128)(2,1)}, bf16[2,128,2560]{2,1,0:T(8,128)(2,1)S(1)}, u32[]{:S(2)}, u32[]{:S(2)}) collective-permute-start(bf16[2,128,2560]{2,1,0:T(8,128)(2,1)} %get-tuple-element.14), channel_id=1, source_target_pairs={{2,0},{4,2},{6,4},{8,6},{10,8},{12,10},{14,12},{16,14},{18,16},{20... | collective-permute-start | bytes 3932168 | tf_op jit(solution)/shard_map/ppermute | solution.py:25
  134.6 71.2 %collective-permute-start.5 = (bf16[2,128,2560]{2,1,0:T(8,128)(2,1)}, bf16[2,128,2560]{2,1,0:T(8,128)(2,1)S(1)}, u32[]{:S(2)}, u32[]{:S(2)}) collective-permute-start(bf16[2,128,2560]{2,1,0:T(8,128)(2,1)} %get-tuple-element.15), channel_id=1, source_target_pairs={{0,2},{2,4},{4,6},{6,8},{8,10},{10,12},{12,14},{14,16},{16,18},{18... | collective-permute-start | bytes 3932168 | tf_op jit(solution)/shard_map/ppermute | solution.py:25
  137.0 82.9 %collective-permute-start.6 = (bf16[2,128,2560]{2,1,0:T(8,128)(2,1)}, bf16[2,128,2560]{2,1,0:T(8,128)(2,1)S(1)}, u32[]{:S(2)}, u32[]{:S(2)}) collective-permute-start(bf16[2,128,2560]{2,1,0:T(8,128)(2,1)} %get-tuple-element.16), channel_id=1, source_target_pairs={{4,0},{6,2},{8,4},{10,6},{12,8},{14,10},{16,12},{18,14},{20,16},{2... | collective-permute-start | bytes 3932168 | tf_op jit(solution)/shard_map/ppermute | solution.py:25
  138.9 81.0 %collective-permute-start.7 = (bf16[2,128,2560]{2,1,0:T(8,128)(2,1)}, bf16[2,128,2560]{2,1,0:T(8,128)(2,1)S(1)}, u32[]{:S(2)}, u32[]{:S(2)}) collective-permute-start(bf16[2,128,2560]{2,1,0:T(8,128)(2,1)} %get-tuple-element.17), channel_id=1, source_target_pairs={{0,4},{2,6},{4,8},{6,10},{8,12},{10,14},{12,16},{14,18},{16,20},{1... | collective-permute-start | bytes 3932168 | tf_op jit(solution)/shard_map/ppermute | solution.py:25
  219.9 47.8 %copy-start.2 = (f32[128,2560]{1,0:T(8,128)S(1)}, f32[128,2560]{1,0:T(8,128)}, u32[]{:S(2)}) copy-start(f32[128,2560]{1,0:T(8,128)} %get-tuple-element.12) | copy-start | bytes 3932164
  223.3 5.7 %collective-permute-start.8 = (f32[5120]{0:T(1024)S(1)}, f32[5120]{0:T(1024)S(1)}, u32[]{:S(2)}, u32[]{:S(2)}) collective-permute-start(f32[5120]{0:T(1024)S(1)} %pad_maximum_fusion.1), channel_id=1, source_target_pairs={{0,1},{1,0},{2,3},{3,2},{4,5},{5,4},{6,7},{7,6},{8,9},{9,8},{10,11... | collective-permute-start | bytes 61448 | tf_op jit(solution)/shard_map/ppermute | solution.py:33
  229.0 11.7 %collective-permute-start.9 = (f32[5120]{0:T(1024)S(1)}, f32[5120]{0:T(1024)S(1)}, u32[]{:S(2)}, u32[]{:S(2)}) collective-permute-start(f32[5120]{0:T(1024)S(1)} %fusion.31), channel_id=1, source_target_pairs={{0,2},{2,0},{4,6},{6,4},{8,10},{10,8},{12,14},{14,12},{16,18},{18,... | collective-permute-start | bytes 61448 | tf_op jit(solution)/shard_map/ppermute | solution.py:33
  240.7 5.7 %collective-permute-start.10 = (f32[5120]{0:T(1024)S(1)}, f32[5120]{0:T(1024)S(1)}, u32[]{:S(2)}, u32[]{:S(2)}) collective-permute-start(f32[5120]{0:T(1024)S(1)} %add.78), channel_id=1, source_target_pairs={{0,4},{2,6},{4,0},{6,2},{8,12},{10,14},{12,8},{14,10},{16,20},{18,... | collective-permute-start | bytes 61448 | tf_op jit(solution)/shard_map/ppermute | solution.py:33
  246.3 7.2 %collective-permute-start.11 = (f32[5120]{0:T(1024)S(1)}, f32[5120]{0:T(1024)S(1)}, u32[]{:S(2)}, u32[]{:S(2)}) collective-permute-start(f32[5120]{0:T(1024)S(1)} %add.79), channel_id=1, source_target_pairs={{0,8},{2,10},{4,12},{6,14},{8,0},{10,2},{12,4},{14,6},{16,24},{18,... | collective-permute-start | bytes 61448 | tf_op jit(solution)/shard_map/ppermute | solution.py:33
  253.5 5.7 %collective-permute-start.12 = (f32[5120]{0:T(1024)S(1)}, f32[5120]{0:T(1024)S(1)}, u32[]{:S(2)}, u32[]{:S(2)}) collective-permute-start(f32[5120]{0:T(1024)S(1)} %add.80), channel_id=1, source_target_pairs={{0,16},{2,18},{4,20},{6,22},{8,24},{10,26},{12,28},{14,30},{16,0},... | collective-permute-start | bytes 61448 | tf_op jit(solution)/shard_map/ppermute | solution.py:33
  259.2 6.6 %collective-permute-start.13 = (f32[5120]{0:T(1024)S(1)}, f32[5120]{0:T(1024)S(1)}, u32[]{:S(2)}, u32[]{:S(2)}) collective-permute-start(f32[5120]{0:T(1024)S(1)} %add.81), channel_id=1, source_target_pairs={{0,32},{2,34},{4,36},{6,38},{8,40},{10,42},{12,44},{14,46},{16,48}... | collective-permute-start | bytes 61448 | tf_op jit(solution)/shard_map/ppermute | solution.py:33
  265.8 9.6 %collective-permute-start.14 = (f32[5120]{0:T(1024)S(1)}, f32[5120]{0:T(1024)S(1)}, u32[]{:S(2)}, u32[]{:S(2)}) collective-permute-start(f32[5120]{0:T(1024)S(1)} %add.82), channel_id=1, source_target_pairs={{0,64},{2,66},{4,68},{6,70},{8,72},{10,74},{12,76},{14,78},{16,80}... | collective-permute-start | bytes 61448 | tf_op jit(solution)/shard_map/ppermute | solution.py:33
  275.3 6.6 %collective-permute-start.15 = (f32[5120]{0:T(1024)S(1)}, f32[5120]{0:T(1024)S(1)}, u32[]{:S(2)}, u32[]{:S(2)}) collective-permute-start(f32[5120]{0:T(1024)S(1)} %add.83), channel_id=1, source_target_pairs={{0,128},{2,130},{4,132},{6,134},{8,136},{10,138},{12,140},{14,142}... | collective-permute-start | bytes 61448 | tf_op jit(solution)/shard_map/ppermute | solution.py:33
  281.9 9.6 %collective-permute-start.16 = (f32[5120]{0:T(1024)S(1)}, f32[5120]{0:T(1024)S(1)}, u32[]{:S(2)}, u32[]{:S(2)}) collective-permute-start(f32[5120]{0:T(1024)S(1)} %add.84), channel_id=1, source_target_pairs={{0,256},{2,258},{4,260},{6,262},{8,264},{10,266},{12,268},{14,270}... | collective-permute-start | bytes 61448 | tf_op jit(solution)/shard_map/ppermute | solution.py:33

commit v3 on v2

--- a/solution.py
+++ b/solution.py
@@ -23,6 +23,28 @@
     count = lax.axis_size(axis)
     first, last = (max(0, -steps), min(count, count - steps))
     return lax.ppermute(value, axis, [(source, source + steps) for source in range(first, last)])
+
+
+def pairs_permute(value, axis, pairs):
+    count = lax.axis_size(axis)
+    return lax.ppermute(value, axis, [(i, j) for i, j in pairs if 0 <= j < count])
+
+
+def fetch_neighbours(value, axis):
+    count = lax.axis_size(axis)
+    behind = from_behind(value, axis, 1)
+    ahead = from_behind(value, axis, -1)
+    far_behind = pairs_permute(value, axis, [(i, i + 2) for i in range(0, count, 2)])
+    far_ahead = pairs_permute(value, axis, [(i, i - 2) for i in range(1, count, 2)])
+    relay_behind = pairs_permute(behind, axis, [(i, i + 1) for i in range(0, count, 2)])
+    relay_ahead = pairs_permute(ahead, axis, [(i, i - 1) for i in range(1, count, 2)])
+    odd = lax.axis_index(axis) % 2 == 1
+    return [
+        behind,
+        ahead,
+        jnp.where(odd, relay_behind, far_behind),
+        jnp.where(odd, far_ahead, relay_ahead),
+    ]
 
 
 def all_sum(value, axes):
@@ -121,7 +143,7 @@
     grad_rows = cotangent[0]
     entries = key_tiles[0]
     stacked = jnp.stack([k_norm, value_rows])
-    fetched = [from_behind(stacked, "seq", -offset) for offset in offsets]
+    fetched = fetch_neighbours(stacked, "seq")
     live = jnp.repeat(
         jnp.concatenate([jnp.ones((1,), jnp.int32), (entries >= 0).astype(jnp.int32)]), tile_rows
     )[None, :]

time: 293 us -> 270 us (0.922)
  the two profiles are of different devices: /device:TPU:32 before, /device:TPU:48 now
where the time goes in v3:
time: 270 us; the launch traced here: 269 us
  waiting for transfers between devices  165 us (61%)
  starting transfers between devices  65.5 us (24%)
  Pallas kernels  20.2 us (7%)
  other arithmetic  16 us (6%)
    ppermute x6, waiting for transfers between devices, from_behind(): lax.ppermute(value, axis, [(source, source + steps) for source in range(f...  126 us
    ppermute x9, waiting for transfers between devices, all_sum(): lax.ppermute(value, axis, [(i, i ^ bit) for i in range(count)])  37.8 us
    ppermute x6, starting transfers between devices, from_behind(): lax.ppermute(value, axis, [(source, source + steps) for source in range(f...  30.1 us
    ppermute x9, starting transfers between devices, all_sum(): lax.ppermute(value, axis, [(i, i ^ bit) for i in range(count)])  27.3 us
    pallas_call x1, Pallas kernels, attention(): pl.pallas_call(attention_kernel, grid=(features // width,), in_specs=[pl....  20.2 us
    ppermute x4, starting transfers between devices, pairs_permute(): lax.ppermute(value, axis, [(i, j) for i, j in pairs if 0 <= j < count])  8.1 us
  transfers between devices with their start and end apart: 19, of which 13 were waited for; matrix products, arithmetic and copies ran while one was open for 3% of the time, Pallas kernels for 0%

profile of v3, /device:TPU:48, one launch (start us, length us, event | category | flops | bytes accessed | tf_op | source)
XLA Modules:
  0.0 269.5 jit_solution(3577779578860169600)
XLA Ops:
  0.6 1.4 fusion.16
  2.0 1.3 fusion.18
  3.4 0.1 pad_maximum_fusion
  3.5 14.3 %collective-permute-start.1 = (bf16[2,128,2560]{2,1,0:T(8,128)(2,1)S(1)}, bf16[2,128,2560]{2,1,0:T(8,128)(2,1)}, u32[]{:S(2)}, u32[]{:S(2)}) collective-permute-start(bf16[2,128,2560]{2,1,0:T(8,128)(2,1)S(1)} %pad_maximum_fusion), channel_id=1, source_target_pairs={{2,0},{4,2},{6,4},{8,6},{10,8},{12,10},{14,12},{16,14},{18,16},{20... | collective-permute-start | bytes 3932168 | tf_op jit(solution)/shard_map/ppermute | solution.py:25
  17.8 1.9 collective-permute-start
  19.8 1.7 collective-permute-start.4
  21.5 1.9 collective-permute-start.3
  23.4 0.1 add_convert_fusion
  23.5 51.3 %collective-permute-done.1.refs_1_ = bf16[2,128,2560]{2,1,0:T(8,128)(2,1)} collective-permute-done((bf16[2,128,2560]{2,1,0:T(8,128)(2,1)S(1)}, bf16[2,128,2560]{2,1,0:T(8,128)(2,1)}, u32[]{:S(2)}, u32[]{:S(2)}) %collective-permute-start.1) | collective-permute-done | bytes 1310752 | tf_op jit(solution)/shard_map/ppermute | solution.py:25
  74.9 1.3 collective-permute-start.5
  76.1 0.1 broadcast_bitcast_fusion
  76.2 0.6 copy.14
  76.8 0.2 fusion.25
  77.0 3.2 %collective-permute-start.2 = (bf16[2,128,2560]{2,1,0:T(8,128)(2,1)}, bf16[2,128,2560]{2,1,0:T(8,128)(2,1)S(1)}, u32[]{:S(2)}, u32[]{:S(2)}) collective-permute-start(bf16[2,128,2560]{2,1,0:T(8,128)(2,1)} %collective-permute-done.refs_0_), channel_id=1, source_target_pairs={{0,2},{4,6},{8,10},{12,14},{16,18},{20,22},{24,26},{28,30},{32,34}... | collective-permute-start | bytes 3932168 | tf_op jit(solution)/shard_map/ppermute | solution.py:30
  80.3 1.4 fusion.10
  81.7 1.2 broadcast_select_fusion.refs_3_
  82.9 1.2 collective-permute-done.3
  84.2 2.5 broadcast_select_fusion.1.refs_2_
  86.7 20.2 %shard_map.110 = (f32[128,2560]{1,0:T(8,128)}, f32[128,2560]{1,0:T(8,128)}, f32[128,2560]{1,0:T(8,128)}, bf16[2,128,2560]{2,1,0:T(8,128)(2,1)}, bf16[2,128,2560]...) custom-call(s32[1,640]{1,0:T(1,128)} %bitcast.98, ...), custom_call_target="tpu_custom_call" | custom-call | flops 2516582400 | bytes 17039360 | tf_op jit(solution)/shard_map/pallas_call | solution.py:120
  106.9 6.1 %collective-permute-start.6 = (bf16[2,128,2560]{2,1,0:T(8,128)(2,1)}, bf16[2,128,2560]{2,1,0:T(8,128)(2,1)S(1)}, u32[]{:S(2)}, u32[]{:S(2)}) collective-permute-start(bf16[2,128,2560]{2,1,0:T(8,128)(2,1)} %get-tuple-element.14), channel_id=1, source_target_pairs={{2,0},{4,2},{6,4},{8,6},{10,8},{12,10},{14,12},{16,14},{18,16},{20... | collective-permute-start | bytes 3932168 | tf_op jit(solution)/shard_map/ppermute | solution.py:25
  113.1 1.9 collective-permute-start.7
  115.0 3.6 %collective-permute-start.8 = (bf16[2,128,2560]{2,1,0:T(8,128)(2,1)}, bf16[2,128,2560]{2,1,0:T(8,128)(2,1)S(1)}, u32[]{:S(2)}, u32[]{:S(2)}) collective-permute-start(bf16[2,128,2560]{2,1,0:T(8,128)(2,1)} %get-tuple-element.16), channel_id=1, source_target_pairs={{4,0},{6,2},{8,4},{10,6},{12,8},{14,10},{16,12},{18,14},{20,16},{2... | collective-permute-start | bytes 3932168 | tf_op jit(solution)/shard_map/ppermute | solution.py:25
  118.6 2.3 collective-permute-start.9
  120.9 1.8 fusion.24
  122.6 60.9 %collective-permute-done.6 = bf16[2,128,2560]{2,1,0:T(8,128)(2,1)S(1)} collective-permute-done((bf16[2,128,2560]{2,1,0:T(8,128)(2,1)}, bf16[2,128,2560]{2,1,0:T(8,128)(2,1)S(1)}, u32[]{:S(2)}, u32[]{:S(2)}) %collective-permute-start.6) | collective-permute-done | bytes 1310752 | tf_op jit(solution)/shard_map/ppermute | solution.py:25
  183.5 14.1 %collective-permute-done.8 = bf16[2,128,2560]{2,1,0:T(8,128)(2,1)S(1)} collective-permute-done((bf16[2,128,2560]{2,1,0:T(8,128)(2,1)}, bf16[2,128,2560]{2,1,0:T(8,128)(2,1)S(1)}, u32[]{:S(2)}, u32[]{:S(2)}) %collective-permute-start.8) | collective-permute-done | bytes 1310752 | tf_op jit(solution)/shard_map/ppermute | solution.py:25
  197.7 3.4 %fusion.15 = (f32[2560]{0:T(1024)S(1)}, f32[128]{0:T(128)S(1)}, f32[128,2560]{1,0:T(8,128)S(1)}, bf16[1,128,2560]{2,1,0:T(8,128)(2,1)}) fusion(bf16[1,128,2560]{2,1,0:T(8,128)(2,1)S(1)} %copy-done, f32[128]{0:T(128)S(1)} %add_rsqrt_fusion, f32[2560]{0:T(1024)S(1)} %copy-done.5, bf16[2,128,2560]{2,1,0:T(8,128)(2,1)S(1)} %collective-permute-done.9, ...), kind=kLoop, calls=%fused_computation.19 | loop fusion | flops 7861632 | bytes 10507264 | tf_op jit(solution)/shard_map/reduce_sum | solution.py:73
  201.1 1.9 collective-permute-start.10
  203.0 3.7 %collective-permute-done.10 = f32[5120]{0:T(1024)S(1)} collective-permute-done((f32[5120]{0:T(1024)S(1)}, f32[5120]{0:T(1024)S(1)}, u32[]{:S(2)}, u32[]{:S(2)}) %collective-permute-start.10) | collective-permute-done | bytes 20512 | tf_op jit(solution)/shard_map/ppermute | solution.py:55
  206.8 10.4 %collective-permute-start.11 = (f32[5120]{0:T(1024)S(1)}, f32[5120]{0:T(1024)S(1)}, u32[]{:S(2)}, u32[]{:S(2)}) collective-permute-start(f32[5120]{0:T(1024)S(1)} %fusion.31), channel_id=1, source_target_pairs={{0,2},{2,0},{4,6},{6,4},{8,10},{10,8},{12,14},{14,12},{16,18},{18,... | collective-permute-start | bytes 61448 | tf_op jit(solution)/shard_map/ppermute | solution.py:55
  217.2 0.8 collective-permute-done.11
  218.0 1.9 collective-permute-start.12
  220.0 3.7 %collective-permute-done.12 = f32[5120]{0:T(1024)S(1)} collective-permute-done((f32[5120]{0:T(1024)S(1)}, f32[5120]{0:T(1024)S(1)}, u32[]{:S(2)}, u32[]{:S(2)}) %collective-permute-start.12) | collective-permute-done | bytes 20512 | tf_op jit(solution)/shard_map/ppermute | solution.py:55
  223.7 1.9 collective-permute-start.13
  225.6 5.3 %collective-permute-done.13 = f32[5120]{0:T(1024)S(1)} collective-permute-done((f32[5120]{0:T(1024)S(1)}, f32[5120]{0:T(1024)S(1)}, u32[]{:S(2)}, u32[]{:S(2)}) %collective-permute-start.13) | collective-permute-done | bytes 20512 | tf_op jit(solution)/shard_map/ppermute | solution.py:55
  230.9 1.9 collective-permute-start.14
  232.8 3.7 %collective-permute-done.14 = f32[5120]{0:T(1024)S(1)} collective-permute-done((f32[5120]{0:T(1024)S(1)}, f32[5120]{0:T(1024)S(1)}, u32[]{:S(2)}, u32[]{:S(2)}) %collective-permute-start.14) | collective-permute-done | bytes 20512 | tf_op jit(solution)/shard_map/ppermute | solution.py:55
  236.6 1.9 collective-permute-start.15
  238.5 4.6 %collective-permute-done.15 = f32[5120]{0:T(1024)S(1)} collective-permute-done((f32[5120]{0:T(1024)S(1)}, f32[5120]{0:T(1024)S(1)}, u32[]{:S(2)}, u32[]{:S(2)}) %collective-permute-start.15) | collective-permute-done | bytes 20512 | tf_op jit(solution)/shard_map/ppermute | solution.py:55
  243.1 1.9 collective-permute-start.16
  245.1 1.2 fusion.28
  246.3 6.4 %collective-permute-done.16 = f32[5120]{0:T(1024)S(1)} collective-permute-done((f32[5120]{0:T(1024)S(1)}, f32[5120]{0:T(1024)S(1)}, u32[]{:S(2)}, u32[]{:S(2)}) %collective-permute-start.16) | collective-permute-done | bytes 20512 | tf_op jit(solution)/shard_map/ppermute | solution.py:55
  252.7 3.5 %collective-permute-start.17 = (f32[5120]{0:T(1024)S(1)}, f32[5120]{0:T(1024)S(1)}, u32[]{:S(2)}, u32[]{:S(2)}) collective-permute-start(f32[5120]{0:T(1024)S(1)} %add.88), channel_id=1, source_target_pairs={{0,128},{2,130},{4,132},{6,134},{8,136},{10,138},{12,140},{14,142}... | collective-permute-start | bytes 61448 | tf_op jit(solution)/shard_map/ppermute | solution.py:55
  256.3 3.0 %collective-permute-done.17 = f32[5120]{0:T(1024)S(1)} collective-permute-done((f32[5120]{0:T(1024)S(1)}, f32[5120]{0:T(1024)S(1)}, u32[]{:S(2)}, u32[]{:S(2)}) %collective-permute-start.17) | collective-permute-done | bytes 20512 | tf_op jit(solution)/shard_map/ppermute | solution.py:55
  259.3 1.9 collective-permute-start.18
  261.2 1.2 fusion.29
  262.4 6.4 %collective-permute-done.18 = f32[5120]{0:T(1024)S(1)} collective-permute-done((f32[5120]{0:T(1024)S(1)}, f32[5120]{0:T(1024)S(1)}, u32[]{:S(2)}, u32[]{:S(2)}) %collective-permute-start.18) | collective-permute-done | bytes 20512 | tf_op jit(solution)/shard_map/ppermute | solution.py:55
  268.9 0.6 fusion.30
  (37 shorter events, 0.1 us)
Async XLA Ops:
  0.6 2.7 %copy-start.4 = (bf16[1,128,2560]{2,1,0:T(8,128)(2,1)S(1)}, bf16[1,128,2560]{2,1,0:T(8,128)(2,1)}, u32[]{:S(2)}) copy-start(bf16[1,128,2560]{2,1,0:T(8,128)(2,1)} %param.9) | copy-start | bytes 1966084
  3.3 20.1 %copy-start.7 = (s32[1,4]{1,0:T(1,128)S(1)}, s32[1,4]{1,0:T(1,128)}, u32[]{:S(2)}) copy-start(s32[1,4]{1,0:T(1,128)} %param.13) | copy-start | bytes 52
  3.4 73.4 %copy-start.1 = (bf16[1,128,2560]{2,1,0:T(8,128)(2,1)S(1)}, bf16[1,128,2560]{2,1,0:T(8,128)(2,1)}, u32[]{:S(2)}) copy-start(bf16[1,128,2560]{2,1,0:T(8,128)(2,1)} %param.7) | copy-start | bytes 1966084
  3.4 76.9 %copy-start = (bf16[1,128,2560]{2,1,0:T(8,128)(2,1)S(1)}, bf16[1,128,2560]{2,1,0:T(8,128)(2,1)}, u32[]{:S(2)}) copy-start(bf16[1,128,2560]{2,1,0:T(8,128)(2,1)} %param.8) | copy-start | bytes 1966084
  3.4 76.9 %copy-start.5 = (f32[2560]{0:T(1024)S(1)}, f32[2560]{0:T(1024)}, u32[]{:S(2)}) copy-start(f32[2560]{0:T(1024)} %param.12) | copy-start | bytes 30724
  3.4 76.9 %copy-start.6 = (f32[2560]{0:T(1024)S(1)}, f32[2560]{0:T(1024)}, u32[]{:S(2)}) copy-start(f32[2560]{0:T(1024)} %param.11) | copy-start | bytes 30724
  3.5 71.3 %collective-permute-start.1 = (bf16[2,128,2560]{2,1,0:T(8,128)(2,1)S(1)}, bf16[2,128,2560]{2,1,0:T(8,128)(2,1)}, u32[]{:S(2)}, u32[]{:S(2)}) collective-permute-start(bf16[2,128,2560]{2,1,0:T(8,128)(2,1)S(1)} %pad_maximum_fusion), channel_id=1, source_target_pairs={{2,0},{4,2},{6,4},{8,6},{10,8},{12,10},{14,12},{16,14},{18,16},{20... | collective-permute-start | bytes 3932168 | tf_op jit(solution)/shard_map/ppermute | solution.py:25
  17.8 59.2 %collective-permute-start = (bf16[2,128,2560]{2,1,0:T(8,128)(2,1)S(1)}, bf16[2,128,2560]{2,1,0:T(8,128)(2,1)}, u32[]{:S(2)}, u32[]{:S(2)}) collective-permute-start(bf16[2,128,2560]{2,1,0:T(8,128)(2,1)S(1)} %pad_maximum_fusion), channel_id=1, source_target_pairs={{0,2},{2,4},{4,6},{6,8},{8,10},{10,12},{12,14},{14,16},{16,18},{18... | collective-permute-start | bytes 3932168 | tf_op jit(solution)/shard_map/ppermute | solution.py:25
  19.8 61.9 %collective-permute-start.4 = (bf16[2,128,2560]{2,1,0:T(8,128)(2,1)S(1)}, bf16[2,128,2560]{2,1,0:T(8,128)(2,1)}, u32[]{:S(2)}, u32[]{:S(2)}) collective-permute-start(bf16[2,128,2560]{2,1,0:T(8,128)(2,1)S(1)} %pad_maximum_fusion), channel_id=1, source_target_pairs={{6,2},{10,6},{14,10},{18,14},{22,18},{26,22},{30,26},{34,30},{38,3... | collective-permute-start | bytes 3932168 | tf_op jit(solution)/shard_map/ppermute | solution.py:30
  21.5 62.7 %collective-permute-start.3 = (bf16[2,128,2560]{2,1,0:T(8,128)(2,1)S(1)}, bf16[2,128,2560]{2,1,0:T(8,128)(2,1)}, u32[]{:S(2)}, u32[]{:S(2)}) collective-permute-start(bf16[2,128,2560]{2,1,0:T(8,128)(2,1)S(1)} %pad_maximum_fusion), channel_id=1, source_target_pairs={{0,4},{4,8},{8,12},{12,16},{16,20},{20,24},{24,28},{28,32},{32,36}... | collective-permute-start | bytes 3932168 | tf_op jit(solution)/shard_map/ppermute | solution.py:30
  74.9 6.8 %collective-permute-start.5 = (bf16[2,128,2560]{2,1,0:T(8,128)(2,1)}, bf16[2,128,2560]{2,1,0:T(8,128)(2,1)S(1)}, u32[]{:S(2)}, u32[]{:S(2)}) collective-permute-start(bf16[2,128,2560]{2,1,0:T(8,128)(2,1)} %collective-permute-done.1.refs_1_), channel_id=1, source_target_pairs={{2,0},{6,4},{10,8},{14,12},{18,16},{22,20},{26,24},{30,28},{34,32}... | collective-permute-start | bytes 3932168 | tf_op jit(solution)/shard_map/ppermute | solution.py:30
  77.0 7.1 %collective-permute-start.2 = (bf16[2,128,2560]{2,1,0:T(8,128)(2,1)}, bf16[2,128,2560]{2,1,0:T(8,128)(2,1)S(1)}, u32[]{:S(2)}, u32[]{:S(2)}) collective-permute-start(bf16[2,128,2560]{2,1,0:T(8,128)(2,1)} %collective-permute-done.refs_0_), channel_id=1, source_target_pairs={{0,2},{4,6},{8,10},{12,14},{16,18},{20,22},{24,26},{28,30},{32,34}... | collective-permute-start | bytes 3932168 | tf_op jit(solution)/shard_map/ppermute | solution.py:30
  106.9 90.7 %copy-start.3 = (f32[128,2560]{1,0:T(8,128)S(1)}, f32[128,2560]{1,0:T(8,128)}, u32[]{:S(2)}) copy-start(f32[128,2560]{1,0:T(8,128)} %get-tuple-element.13) | copy-start | bytes 3932164
  106.9 76.6 %collective-permute-start.6 = (bf16[2,128,2560]{2,1,0:T(8,128)(2,1)}, bf16[2,128,2560]{2,1,0:T(8,128)(2,1)S(1)}, u32[]{:S(2)}, u32[]{:S(2)}) collective-permute-start(bf16[2,128,2560]{2,1,0:T(8,128)(2,1)} %get-tuple-element.14), channel_id=1, source_target_pairs={{2,0},{4,2},{6,4},{8,6},{10,8},{12,10},{14,12},{16,14},{18,16},{20... | collective-permute-start | bytes 3932168 | tf_op jit(solution)/shard_map/ppermute | solution.py:25
  113.1 70.5 %collective-permute-start.7 = (bf16[2,128,2560]{2,1,0:T(8,128)(2,1)}, bf16[2,128,2560]{2,1,0:T(8,128)(2,1)S(1)}, u32[]{:S(2)}, u32[]{:S(2)}) collective-permute-start(bf16[2,128,2560]{2,1,0:T(8,128)(2,1)} %get-tuple-element.15), channel_id=1, source_target_pairs={{0,2},{2,4},{4,6},{6,8},{8,10},{10,12},{12,14},{14,16},{16,18},{18... | collective-permute-start | bytes 3932168 | tf_op jit(solution)/shard_map/ppermute | solution.py:25
  115.0 82.7 %collective-permute-start.8 = (bf16[2,128,2560]{2,1,0:T(8,128)(2,1)}, bf16[2,128,2560]{2,1,0:T(8,128)(2,1)S(1)}, u32[]{:S(2)}, u32[]{:S(2)}) collective-permute-start(bf16[2,128,2560]{2,1,0:T(8,128)(2,1)} %get-tuple-element.16), channel_id=1, source_target_pairs={{4,0},{6,2},{8,4},{10,6},{12,8},{14,10},{16,12},{18,14},{20,16},{2... | collective-permute-start | bytes 3932168 | tf_op jit(solution)/shard_map/ppermute | solution.py:25
  118.6 79.1 %collective-permute-start.9 = (bf16[2,128,2560]{2,1,0:T(8,128)(2,1)}, bf16[2,128,2560]{2,1,0:T(8,128)(2,1)S(1)}, u32[]{:S(2)}, u32[]{:S(2)}) collective-permute-start(bf16[2,128,2560]{2,1,0:T(8,128)(2,1)} %get-tuple-element.17), channel_id=1, source_target_pairs={{0,4},{2,6},{4,8},{6,10},{8,12},{10,14},{12,16},{14,18},{16,20},{1... | collective-permute-start | bytes 3932168 | tf_op jit(solution)/shard_map/ppermute | solution.py:25
  197.7 47.4 %copy-start.2 = (f32[128,2560]{1,0:T(8,128)S(1)}, f32[128,2560]{1,0:T(8,128)}, u32[]{:S(2)}) copy-start(f32[128,2560]{1,0:T(8,128)} %get-tuple-element.12) | copy-start | bytes 3932164
  201.1 5.7 %collective-permute-start.10 = (f32[5120]{0:T(1024)S(1)}, f32[5120]{0:T(1024)S(1)}, u32[]{:S(2)}, u32[]{:S(2)}) collective-permute-start(f32[5120]{0:T(1024)S(1)} %pad_maximum_fusion.1), channel_id=1, source_target_pairs={{0,1},{1,0},{2,3},{3,2},{4,5},{5,4},{6,7},{7,6},{8,9},{9,8},{10,11... | collective-permute-start | bytes 61448 | tf_op jit(solution)/shard_map/ppermute | solution.py:55
  206.8 11.3 %collective-permute-start.11 = (f32[5120]{0:T(1024)S(1)}, f32[5120]{0:T(1024)S(1)}, u32[]{:S(2)}, u32[]{:S(2)}) collective-permute-start(f32[5120]{0:T(1024)S(1)} %fusion.31), channel_id=1, source_target_pairs={{0,2},{2,0},{4,6},{6,4},{8,10},{10,8},{12,14},{14,12},{16,18},{18,... | collective-permute-start | bytes 61448 | tf_op jit(solution)/shard_map/ppermute | solution.py:55
  218.0 5.7 %collective-permute-start.12 = (f32[5120]{0:T(1024)S(1)}, f32[5120]{0:T(1024)S(1)}, u32[]{:S(2)}, u32[]{:S(2)}) collective-permute-start(f32[5120]{0:T(1024)S(1)} %add.83), channel_id=1, source_target_pairs={{0,4},{2,6},{4,0},{6,2},{8,12},{10,14},{12,8},{14,10},{16,20},{18,... | collective-permute-start | bytes 61448 | tf_op jit(solution)/shard_map/ppermute | solution.py:55
  223.7 7.2 %collective-permute-start.13 = (f32[5120]{0:T(1024)S(1)}, f32[5120]{0:T(1024)S(1)}, u32[]{:S(2)}, u32[]{:S(2)}) collective-permute-start(f32[5120]{0:T(1024)S(1)} %add.84), channel_id=1, source_target_pairs={{0,8},{2,10},{4,12},{6,14},{8,0},{10,2},{12,4},{14,6},{16,24},{18,... | collective-permute-start | bytes 61448 | tf_op jit(solution)/shard_map/ppermute | solution.py:55
  230.9 5.7 %collective-permute-start.14 = (f32[5120]{0:T(1024)S(1)}, f32[5120]{0:T(1024)S(1)}, u32[]{:S(2)}, u32[]{:S(2)}) collective-permute-start(f32[5120]{0:T(1024)S(1)} %add.85), channel_id=1, source_target_pairs={{0,16},{2,18},{4,20},{6,22},{8,24},{10,26},{12,28},{14,30},{16,0},... | collective-permute-start | bytes 61448 | tf_op jit(solution)/shard_map/ppermute | solution.py:55
  236.6 6.6 %collective-permute-start.15 = (f32[5120]{0:T(1024)S(1)}, f32[5120]{0:T(1024)S(1)}, u32[]{:S(2)}, u32[]{:S(2)}) collective-permute-start(f32[5120]{0:T(1024)S(1)} %add.86), channel_id=1, source_target_pairs={{0,32},{2,34},{4,36},{6,38},{8,40},{10,42},{12,44},{14,46},{16,48}... | collective-permute-start | bytes 61448 | tf_op jit(solution)/shard_map/ppermute | solution.py:55
  243.1 9.6 %collective-permute-start.16 = (f32[5120]{0:T(1024)S(1)}, f32[5120]{0:T(1024)S(1)}, u32[]{:S(2)}, u32[]{:S(2)}) collective-permute-start(f32[5120]{0:T(1024)S(1)} %add.87), channel_id=1, source_target_pairs={{0,64},{2,66},{4,68},{6,70},{8,72},{10,74},{12,76},{14,78},{16,80}... | collective-permute-start | bytes 61448 | tf_op jit(solution)/shard_map/ppermute | solution.py:55
  252.7 6.6 %collective-permute-start.17 = (f32[5120]{0:T(1024)S(1)}, f32[5120]{0:T(1024)S(1)}, u32[]{:S(2)}, u32[]{:S(2)}) collective-permute-start(f32[5120]{0:T(1024)S(1)} %add.88), channel_id=1, source_target_pairs={{0,128},{2,130},{4,132},{6,134},{8,136},{10,138},{12,140},{14,142}... | collective-permute-start | bytes 61448 | tf_op jit(solution)/shard_map/ppermute | solution.py:55
  259.3 9.6 %collective-permute-start.18 = (f32[5120]{0:T(1024)S(1)}, f32[5120]{0:T(1024)S(1)}, u32[]{:S(2)}, u32[]{:S(2)}) collective-permute-start(f32[5120]{0:T(1024)S(1)} %add.89), channel_id=1, source_target_pairs={{0,256},{2,258},{4,260},{6,262},{8,264},{10,266},{12,268},{14,270}... | collective-permute-start | bytes 61448 | tf_op jit(solution)/shard_map/ppermute | solution.py:55

commit v4 on v3

--- a/solution.py
+++ b/solution.py
@@ -45,6 +45,24 @@
         jnp.where(odd, relay_behind, far_behind),
         jnp.where(odd, far_ahead, relay_ahead),
     ]
+
+
+def return_parts(far, axis):
+    count = lax.axis_size(axis)
+    behind, ahead, far_behind, far_ahead = far
+    odd = lax.axis_index(axis) % 2 == 1
+    swapped = pairs_permute(
+        jnp.where(odd, far_behind, far_ahead), axis, [(i, i ^ 1) for i in range(count)]
+    )
+
+    def joined(own):
+        return (own.astype(jnp.float32) + swapped.astype(jnp.float32)).astype(jnp.bfloat16)
+
+    to_next = from_behind(jnp.where(odd, joined(ahead), ahead), axis, 1)
+    to_previous = from_behind(jnp.where(odd, behind, joined(behind)), axis, -1)
+    two_ahead = pairs_permute(far_ahead, axis, [(i, i + 2) for i in range(1, count, 2)])
+    two_behind = pairs_permute(far_behind, axis, [(i, i - 2) for i in range(0, count, 2)])
+    return [to_next, to_previous, two_ahead, two_behind]
 
 
 def all_sum(value, axes):
@@ -150,8 +168,7 @@
     q_norm_grad, k_norm_grad, v_sum, *far = attention(
         live, q_norm, k_norm, value_rows, grad_rows, fetched
     )
-    for slot, offset in enumerate(offsets):
-        back = from_behind(far[slot], "seq", offset)
+    for back in return_parts(far, "seq"):
         k_norm_grad = k_norm_grad + back[0].astype(jnp.float32)
         v_sum = v_sum + back[1].astype(jnp.float32)
     q_back, q_part = norm_backward(q_norm_grad, q_gain, q_hat, q_inv)

time: 270 us -> 241 us (0.89)
  the two profiles are of different devices: /device:TPU:48 before, /device:TPU:32 now
where the time goes in v4:
time: 241 us
  waiting for transfers between devices  140 us (58%)
  starting transfers between devices  60.6 us (25%)
  Pallas kernels  20.2 us (8%)
  other arithmetic  17.6 us (7%)
    ppermute x4, waiting for transfers between devices, from_behind(): lax.ppermute(value, axis, [(source, source + steps) for source in range(f...  70.9 us
    ppermute x9, waiting for transfers between devices, all_sum(): lax.ppermute(value, axis, [(i, i ^ bit) for i in range(count)])  39.6 us
    ppermute x7, waiting for transfers between devices, pairs_permute(): lax.ppermute(value, axis, [(i, j) for i, j in pairs if 0 <= j < count])  29.4 us
    ppermute x4, starting transfers between devices, from_behind(): lax.ppermute(value, axis, [(source, source + steps) for source in range(f...  26.4 us
    pallas_call x1, Pallas kernels, attention(): pl.pallas_call(attention_kernel, grid=(features // width,), in_specs=[pl....  20.2 us
    ppermute x9, starting transfers between devices, all_sum(): lax.ppermute(value, axis, [(i, i ^ bit) for i in range(count)])  17.3 us
    ppermute x7, starting transfers between devices, pairs_permute(): lax.ppermute(value, axis, [(i, j) for i, j in pairs if 0 <= j < count])  16.9 us
  transfers between devices with their start and end apart: 20, of which 13 were waited for; matrix products, arithmetic and copies ran while one was open for 4% of the time, Pallas kernels for 0%

profile of v4, /device:TPU:32, one launch (start us, length us, event | category | flops | bytes accessed | tf_op | source)
XLA Modules:
  0.0 240.7 jit_solution(10189895761854938595)
XLA Ops:
  0.6 1.4 fusion.20
  2.0 1.3 fusion.22
  3.5 12.5 %collective-permute-start.1 = (bf16[2,128,2560]{2,1,0:T(8,128)(2,1)S(1)}, bf16[2,128,2560]{2,1,0:T(8,128)(2,1)}, u32[]{:S(2)}, u32[]{:S(2)}) collective-permute-start(bf16[2,128,2560]{2,1,0:T(8,128)(2,1)S(1)} %pad_maximum_fusion), channel_id=1, source_target_pairs={{2,0},{4,2},{6,4},{8,6},{10,8},{12,10},{14,12},{16,14},{18,16},{20... | collective-permute-start | bytes 3932168 | tf_op jit(solution)/shard_map/ppermute | solution.py:25
  16.0 1.9 collective-permute-start
  18.0 1.7 collective-permute-start.4
  19.7 1.9 collective-permute-start.3
  21.7 50.3 %collective-permute-done.1.refs_1_ = bf16[2,128,2560]{2,1,0:T(8,128)(2,1)} collective-permute-done((bf16[2,128,2560]{2,1,0:T(8,128)(2,1)S(1)}, bf16[2,128,2560]{2,1,0:T(8,128)(2,1)}, u32[]{:S(2)}, u32[]{:S(2)}) %collective-permute-start.1) | collective-permute-done | bytes 1310752 | tf_op jit(solution)/shard_map/ppermute | solution.py:25
  72.0 1.3 collective-permute-start.5
  73.4 0.6 copy.14
  73.9 0.2 fusion.29
  74.2 3.2 %collective-permute-start.2 = (bf16[2,128,2560]{2,1,0:T(8,128)(2,1)}, bf16[2,128,2560]{2,1,0:T(8,128)(2,1)S(1)}, u32[]{:S(2)}, u32[]{:S(2)}) collective-permute-start(bf16[2,128,2560]{2,1,0:T(8,128)(2,1)} %collective-permute-done.refs_0_), channel_id=1, source_target_pairs={{0,2},{4,6},{8,10},{12,14},{16,18},{20,22},{24,26},{28,30},{32,34}... | collective-permute-start | bytes 3932168 | tf_op jit(solution)/shard_map/ppermute | solution.py:30
  77.4 1.4 fusion.14
  78.8 1.2 broadcast_select_fusion.1.refs_3_
  80.1 3.5 %collective-permute-done.3 = bf16[2,128,2560]{2,1,0:T(8,128)(2,1)} collective-permute-done((bf16[2,128,2560]{2,1,0:T(8,128)(2,1)S(1)}, bf16[2,128,2560]{2,1,0:T(8,128)(2,1)}, u32[]{:S(2)}, u32[]{:S(2)}) %collective-permute-start.3) | collective-permute-done | bytes 1310752 | tf_op jit(solution)/shard_map/ppermute | solution.py:30
  83.6 2.5 %broadcast_select_fusion.2.refs_2_ = bf16[2,128,2560]{2,1,0:T(8,128)(2,1)} fusion(bf16[2,128,2560]{2,1,0:T(8,128)(2,1)S(1)} %collective-permute-done.2, bf16[2,128,2560]{2,1,0:T(8,128)(2,1)} %collective-permute-done.3, pred[]{:T(512)S(6)} %eq.7), kind=kLoop, calls=%fused_computation.48 | loop fusion | flops 655360 | bytes 3932161 | tf_op jit(solution)/shard_map/jit(_where)/select_n | solution.py:45
  86.1 20.2 %shard_map.110 = (f32[128,2560]{1,0:T(8,128)}, f32[128,2560]{1,0:T(8,128)}, f32[128,2560]{1,0:T(8,128)}, bf16[2,128,2560]{2,1,0:T(8,128)(2,1)}, bf16[2,128,2560]...) custom-call(s32[1,640]{1,0:T(1,128)} %bitcast.98, ...), custom_call_target="tpu_custom_call" | custom-call | flops 2516582400 | bytes 17039360 | tf_op jit(solution)/shard_map/pallas_call | solution.py:138
  106.4 1.6 broadcast_select_fusion
  108.0 1.9 collective-permute-start.6
  109.9 6.1 %collective-permute-start.10 = (bf16[2,128,2560]{2,1,0:T(8,128)(2,1)S(1)}, bf16[2,128,2560]{2,1,0:T(8,128)(2,1)S(1)}, u32[]{:S(2)}, u32[]{:S(2)}) collective-permute-start(bf16[2,128,2560]{2,1,0:T(8,128)(2,1)S(1)} %copy-done.6), channel_id=1, source_target_pairs={{4,0},{8,4},{12,8},{16,12},{20,16},{24,20},{28,24},{32,28},{36,32}... | collective-permute-start | bytes 3932168 | tf_op jit(solution)/shard_map/ppermute | solution.py:30
  116.0 0.7 collective-permute-start.9
  116.8 2.6 %fusion.3 = (bf16[2,128,2560]{2,1,0:T(8,128)(2,1)S(1)}, bf16[2,128,2560]{2,1,0:T(8,128)(2,1)S(1)}) fusion(bf16[2,128,2560]{2,1,0:T(8,128)(2,1)} %get-tuple-element.14, bf16[2,128,2560]{2,1,0:T(8,128)(2,1)S(1)} %collective-permute-done.6, pred[]{:T(512)S(6)} %eq.7, bf16[2,128,2560]{2,1,0:T(8,128)(2,1)S(1)} %copy-done.7), kind=kLoop, calls=%fused_computation.5 | loop fusion | flops 5898240 | bytes 6553601 | tf_op jit(solution)/shard_map/jit(_where)/select_n | solution.py:61
  119.5 2.1 collective-permute-start.7
  121.5 10.0 %collective-permute-start.8 = (bf16[2,128,2560]{2,1,0:T(8,128)(2,1)S(1)}, bf16[2,128,2560]{2,1,0:T(8,128)(2,1)S(1)}, u32[]{:S(2)}, u32[]{:S(2)}) collective-permute-start(bf16[2,128,2560]{2,1,0:T(8,128)(2,1)S(1)} %get-tuple-element.26), channel_id=1, source_target_pairs={{2,0},{4,2},{6,4},{8,6},{10,8},{12,10},{14,12},{16,14},{18,16},{20... | collective-permute-start | bytes 3932168 | tf_op jit(solution)/shard_map/ppermute | solution.py:25
  131.5 0.5 fusion.28
  132.0 25.9 %collective-permute-done.10 = bf16[2,128,2560]{2,1,0:T(8,128)(2,1)S(1)} collective-permute-done((bf16[2,128,2560]{2,1,0:T(8,128)(2,1)S(1)}, bf16[2,128,2560]{2,1,0:T(8,128)(2,1)S(1)}, u32[]{:S(2)}, u32[]{:S(2)}) %collective-permute-start.10) | collective-permute-done | bytes 1310752 | tf_op jit(solution)/shard_map/ppermute | solution.py:30
  157.8 20.6 %collective-permute-done.7 = bf16[2,128,2560]{2,1,0:T(8,128)(2,1)S(1)} collective-permute-done((bf16[2,128,2560]{2,1,0:T(8,128)(2,1)S(1)}, bf16[2,128,2560]{2,1,0:T(8,128)(2,1)S(1)}, u32[]{:S(2)}, u32[]{:S(2)}) %collective-permute-start.7) | collective-permute-done | bytes 1310752 | tf_op jit(solution)/shard_map/ppermute | solution.py:25
  178.5 2.0 fusion.19
  180.5 1.9 collective-permute-start.11
  182.4 3.7 %collective-permute-done.11 = f32[5120]{0:T(1024)S(1)} collective-permute-done((f32[5120]{0:T(1024)S(1)}, f32[5120]{0:T(1024)S(1)}, u32[]{:S(2)}, u32[]{:S(2)}) %collective-permute-start.11) | collective-permute-done | bytes 20512 | tf_op jit(solution)/shard_map/ppermute | solution.py:73
  186.2 1.9 collective-permute-start.12
  188.1 1.2 collective-permute-done.12
  189.2 1.9 collective-permute-start.13
  191.2 3.7 %collective-permute-done.13 = f32[5120]{0:T(1024)S(1)} collective-permute-done((f32[5120]{0:T(1024)S(1)}, f32[5120]{0:T(1024)S(1)}, u32[]{:S(2)}, u32[]{:S(2)}) %collective-permute-start.13) | collective-permute-done | bytes 20512 | tf_op jit(solution)/shard_map/ppermute | solution.py:73
  194.9 1.9 collective-permute-start.14
  196.8 5.3 %collective-permute-done.14 = f32[5120]{0:T(1024)S(1)} collective-permute-done((f32[5120]{0:T(1024)S(1)}, f32[5120]{0:T(1024)S(1)}, u32[]{:S(2)}, u32[]{:S(2)}) %collective-permute-start.14) | collective-permute-done | bytes 20512 | tf_op jit(solution)/shard_map/ppermute | solution.py:73
  202.1 1.9 collective-permute-start.15
  204.0 3.7 %collective-permute-done.15 = f32[5120]{0:T(1024)S(1)} collective-permute-done((f32[5120]{0:T(1024)S(1)}, f32[5120]{0:T(1024)S(1)}, u32[]{:S(2)}, u32[]{:S(2)}) %collective-permute-start.15) | collective-permute-done | bytes 20512 | tf_op jit(solution)/shard_map/ppermute | solution.py:73
  207.8 1.9 collective-permute-start.16
  209.7 4.6 %collective-permute-done.16 = f32[5120]{0:T(1024)S(1)} collective-permute-done((f32[5120]{0:T(1024)S(1)}, f32[5120]{0:T(1024)S(1)}, u32[]{:S(2)}, u32[]{:S(2)}) %collective-permute-start.16) | collective-permute-done | bytes 20512 | tf_op jit(solution)/shard_map/ppermute | solution.py:73
  214.3 1.9 collective-permute-start.17
  216.2 1.2 fusion.32
  217.5 6.4 %collective-permute-done.17 = f32[5120]{0:T(1024)S(1)} collective-permute-done((f32[5120]{0:T(1024)S(1)}, f32[5120]{0:T(1024)S(1)}, u32[]{:S(2)}, u32[]{:S(2)}) %collective-permute-start.17) | collective-permute-done | bytes 20512 | tf_op jit(solution)/shard_map/ppermute | solution.py:73
  223.9 2.1 collective-permute-start.18
  226.0 4.5 %collective-permute-done.18 = f32[5120]{0:T(1024)S(1)} collective-permute-done((f32[5120]{0:T(1024)S(1)}, f32[5120]{0:T(1024)S(1)}, u32[]{:S(2)}, u32[]{:S(2)}) %collective-permute-start.18) | collective-permute-done | bytes 20512 | tf_op jit(solution)/shard_map/ppermute | solution.py:73
  230.5 1.9 collective-permute-start.19
  232.4 1.2 fusion.33
  233.6 6.4 %collective-permute-done.19 = f32[5120]{0:T(1024)S(1)} collective-permute-done((f32[5120]{0:T(1024)S(1)}, f32[5120]{0:T(1024)S(1)}, u32[]{:S(2)}, u32[]{:S(2)}) %collective-permute-start.19) | collective-permute-done | bytes 20512 | tf_op jit(solution)/shard_map/ppermute | solution.py:73
  240.1 0.6 fusion.34
  (49 shorter events, 0.4 us)
Async XLA Ops:
  0.6 2.7 %copy-start.8 = (bf16[1,128,2560]{2,1,0:T(8,128)(2,1)S(1)}, bf16[1,128,2560]{2,1,0:T(8,128)(2,1)}, u32[]{:S(2)}) copy-start(bf16[1,128,2560]{2,1,0:T(8,128)(2,1)} %param.9) | copy-start | bytes 1966084
  3.3 18.3 %copy-start.11 = (s32[1,4]{1,0:T(1,128)S(1)}, s32[1,4]{1,0:T(1,128)}, u32[]{:S(2)}) copy-start(s32[1,4]{1,0:T(1,128)} %param.13) | copy-start | bytes 52
  3.4 70.6 %copy-start.1 = (bf16[1,128,2560]{2,1,0:T(8,128)(2,1)S(1)}, bf16[1,128,2560]{2,1,0:T(8,128)(2,1)}, u32[]{:S(2)}) copy-start(bf16[1,128,2560]{2,1,0:T(8,128)(2,1)} %param.7) | copy-start | bytes 1966084
  3.4 74.0 %copy-start = (bf16[1,128,2560]{2,1,0:T(8,128)(2,1)S(1)}, bf16[1,128,2560]{2,1,0:T(8,128)(2,1)}, u32[]{:S(2)}) copy-start(bf16[1,128,2560]{2,1,0:T(8,128)(2,1)} %param.8) | copy-start | bytes 1966084
  3.4 74.0 %copy-start.9 = (f32[2560]{0:T(1024)S(1)}, f32[2560]{0:T(1024)}, u32[]{:S(2)}) copy-start(f32[2560]{0:T(1024)} %param.12) | copy-start | bytes 30724
  3.4 74.0 %copy-start.10 = (f32[2560]{0:T(1024)S(1)}, f32[2560]{0:T(1024)}, u32[]{:S(2)}) copy-start(f32[2560]{0:T(1024)} %param.11) | copy-start | bytes 30724
  3.5 68.5 %collective-permute-start.1 = (bf16[2,128,2560]{2,1,0:T(8,128)(2,1)S(1)}, bf16[2,128,2560]{2,1,0:T(8,128)(2,1)}, u32[]{:S(2)}, u32[]{:S(2)}) collective-permute-start(bf16[2,128,2560]{2,1,0:T(8,128)(2,1)S(1)} %pad_maximum_fusion), channel_id=1, source_target_pairs={{2,0},{4,2},{6,4},{8,6},{10,8},{12,10},{14,12},{16,14},{18,16},{20... | collective-permute-start | bytes 3932168 | tf_op jit(solution)/shard_map/ppermute | solution.py:25
  16.0 58.1 %collective-permute-start = (bf16[2,128,2560]{2,1,0:T(8,128)(2,1)S(1)}, bf16[2,128,2560]{2,1,0:T(8,128)(2,1)}, u32[]{:S(2)}, u32[]{:S(2)}) collective-permute-start(bf16[2,128,2560]{2,1,0:T(8,128)(2,1)S(1)} %pad_maximum_fusion), channel_id=1, source_target_pairs={{0,2},{2,4},{4,6},{6,8},{8,10},{10,12},{12,14},{14,16},{16,18},{18... | collective-permute-start | bytes 3932168 | tf_op jit(solution)/shard_map/ppermute | solution.py:25
  18.0 60.9 %collective-permute-start.4 = (bf16[2,128,2560]{2,1,0:T(8,128)(2,1)S(1)}, bf16[2,128,2560]{2,1,0:T(8,128)(2,1)}, u32[]{:S(2)}, u32[]{:S(2)}) collective-permute-start(bf16[2,128,2560]{2,1,0:T(8,128)(2,1)S(1)} %pad_maximum_fusion), channel_id=1, source_target_pairs={{6,2},{10,6},{14,10},{18,14},{22,18},{26,22},{30,26},{34,30},{38,3... | collective-permute-start | bytes 3932168 | tf_op jit(solution)/shard_map/ppermute | solution.py:30
  19.7 63.9 %collective-permute-start.3 = (bf16[2,128,2560]{2,1,0:T(8,128)(2,1)S(1)}, bf16[2,128,2560]{2,1,0:T(8,128)(2,1)}, u32[]{:S(2)}, u32[]{:S(2)}) collective-permute-start(bf16[2,128,2560]{2,1,0:T(8,128)(2,1)S(1)} %pad_maximum_fusion), channel_id=1, source_target_pairs={{0,4},{4,8},{8,12},{12,16},{16,20},{20,24},{24,28},{28,32},{32,36}... | collective-permute-start | bytes 3932168 | tf_op jit(solution)/shard_map/ppermute | solution.py:30
  72.0 6.8 %collective-permute-start.5 = (bf16[2,128,2560]{2,1,0:T(8,128)(2,1)}, bf16[2,128,2560]{2,1,0:T(8,128)(2,1)S(1)}, u32[]{:S(2)}, u32[]{:S(2)}) collective-permute-start(bf16[2,128,2560]{2,1,0:T(8,128)(2,1)} %collective-permute-done.1.refs_1_), channel_id=1, source_target_pairs={{2,0},{6,4},{10,8},{14,12},{18,16},{22,20},{26,24},{30,28},{34,32}... | collective-permute-start | bytes 3932168 | tf_op jit(solution)/shard_map/ppermute | solution.py:30
  74.2 9.4 %collective-permute-start.2 = (bf16[2,128,2560]{2,1,0:T(8,128)(2,1)}, bf16[2,128,2560]{2,1,0:T(8,128)(2,1)S(1)}, u32[]{:S(2)}, u32[]{:S(2)}) collective-permute-start(bf16[2,128,2560]{2,1,0:T(8,128)(2,1)} %collective-permute-done.refs_0_), channel_id=1, source_target_pairs={{0,2},{4,6},{8,10},{12,14},{16,18},{20,22},{24,26},{28,30},{32,34}... | collective-permute-start | bytes 3932168 | tf_op jit(solution)/shard_map/ppermute | solution.py:30
  106.3 3.6 %copy-start.6 = (bf16[2,128,2560]{2,1,0:T(8,128)(2,1)S(1)}, bf16[2,128,2560]{2,1,0:T(8,128)(2,1)}, u32[]{:S(2)}) copy-start(bf16[2,128,2560]{2,1,0:T(8,128)(2,1)} %get-tuple-element.15) | copy-start | bytes 3932164
  106.3 9.7 %copy-start.5 = (bf16[2,128,2560]{2,1,0:T(8,128)(2,1)S(1)}, bf16[2,128,2560]{2,1,0:T(8,128)(2,1)}, u32[]{:S(2)}) copy-start(bf16[2,128,2560]{2,1,0:T(8,128)(2,1)} %get-tuple-element.16) | copy-start | bytes 3932164
  106.4 10.4 %copy-start.7 = (bf16[2,128,2560]{2,1,0:T(8,128)(2,1)S(1)}, bf16[2,128,2560]{2,1,0:T(8,128)(2,1)}, u32[]{:S(2)}) copy-start(bf16[2,128,2560]{2,1,0:T(8,128)(2,1)} %get-tuple-element.17) | copy-start | bytes 3932164
  108.0 8.8 %collective-permute-start.6 = (bf16[2,128,2560]{2,1,0:T(8,128)(2,1)S(1)}, bf16[2,128,2560]{2,1,0:T(8,128)(2,1)S(1)}, u32[]{:S(2)}, u32[]{:S(2)}) collective-permute-start(bf16[2,128,2560]{2,1,0:T(8,128)(2,1)S(1)} %broadcast_select_fusion), channel_id=1, source_target_pairs={{0,2},{2,0},{4,6},{6,4},{8,10},{10,8},{12,14},{14,12},{16,18},{18,... | collective-permute-start | bytes 3932168 | tf_op jit(solution)/shard_map/ppermute | solution.py:30
  109.9 47.9 %collective-permute-start.10 = (bf16[2,128,2560]{2,1,0:T(8,128)(2,1)S(1)}, bf16[2,128,2560]{2,1,0:T(8,128)(2,1)S(1)}, u32[]{:S(2)}, u32[]{:S(2)}) collective-permute-start(bf16[2,128,2560]{2,1,0:T(8,128)(2,1)S(1)} %copy-done.6), channel_id=1, source_target_pairs={{4,0},{8,4},{12,8},{16,12},{20,16},{24,20},{28,24},{32,28},{36,32}... | collective-permute-start | bytes 3932168 | tf_op jit(solution)/shard_map/ppermute | solution.py:30
  116.0 41.8 %collective-permute-start.9 = (bf16[2,128,2560]{2,1,0:T(8,128)(2,1)S(1)}, bf16[2,128,2560]{2,1,0:T(8,128)(2,1)S(1)}, u32[]{:S(2)}, u32[]{:S(2)}) collective-permute-start(bf16[2,128,2560]{2,1,0:T(8,128)(2,1)S(1)} %copy-done.5), channel_id=1, source_target_pairs={{2,6},{6,10},{10,14},{14,18},{18,22},{22,26},{26,30},{30,34},{34,3... | collective-permute-start | bytes 3932168 | tf_op jit(solution)/shard_map/ppermute | solution.py:30
  116.8 14.7 %copy-start.2 = (f32[128,2560]{1,0:T(8,128)S(1)}, f32[128,2560]{1,0:T(8,128)}, u32[]{:S(2)}) copy-start(f32[128,2560]{1,0:T(8,128)} %get-tuple-element.12) | copy-start | bytes 3932164
  116.8 61.6 %copy-start.4 = (f32[128,2560]{1,0:T(8,128)S(1)}, f32[128,2560]{1,0:T(8,128)}, u32[]{:S(2)}) copy-start(f32[128,2560]{1,0:T(8,128)} %get-tuple-element.18) | copy-start | bytes 3932164
  119.5 59.0 %copy-start.3 = (f32[128,2560]{1,0:T(8,128)S(1)}, f32[128,2560]{1,0:T(8,128)}, u32[]{:S(2)}) copy-start(f32[128,2560]{1,0:T(8,128)} %get-tuple-element.13) | copy-start | bytes 3932164
  119.5 59.0 %collective-permute-start.7 = (bf16[2,128,2560]{2,1,0:T(8,128)(2,1)S(1)}, bf16[2,128,2560]{2,1,0:T(8,128)(2,1)S(1)}, u32[]{:S(2)}, u32[]{:S(2)}) collective-permute-start(bf16[2,128,2560]{2,1,0:T(8,128)(2,1)S(1)} %get-tuple-element.25), channel_id=1, source_target_pairs={{0,2},{2,4},{4,6},{6,8},{8,10},{10,12},{12,14},{14,16},{16,18},{18... | collective-permute-start | bytes 3932168 | tf_op jit(solution)/shard_map/ppermute | solution.py:25
  121.5 56.9 %collective-permute-start.8 = (bf16[2,128,2560]{2,1,0:T(8,128)(2,1)S(1)}, bf16[2,128,2560]{2,1,0:T(8,128)(2,1)S(1)}, u32[]{:S(2)}, u32[]{:S(2)}) collective-permute-start(bf16[2,128,2560]{2,1,0:T(8,128)(2,1)S(1)} %get-tuple-element.26), channel_id=1, source_target_pairs={{2,0},{4,2},{6,4},{8,6},{10,8},{12,10},{14,12},{16,14},{18,16},{20... | collective-permute-start | bytes 3932168 | tf_op jit(solution)/shard_map/ppermute | solution.py:25
  180.5 5.7 %collective-permute-start.11 = (f32[5120]{0:T(1024)S(1)}, f32[5120]{0:T(1024)S(1)}, u32[]{:S(2)}, u32[]{:S(2)}) collective-permute-start(f32[5120]{0:T(1024)S(1)} %pad_maximum_fusion.1), channel_id=1, source_target_pairs={{0,1},{1,0},{2,3},{3,2},{4,5},{5,4},{6,7},{7,6},{8,9},{9,8},{10,11... | collective-permute-start | bytes 61448 | tf_op jit(solution)/shard_map/ppermute | solution.py:73
  186.2 3.1 %collective-permute-start.12 = (f32[5120]{0:T(1024)S(1)}, f32[5120]{0:T(1024)S(1)}, u32[]{:S(2)}, u32[]{:S(2)}) collective-permute-start(f32[5120]{0:T(1024)S(1)} %fusion.35), channel_id=1, source_target_pairs={{0,2},{2,0},{4,6},{6,4},{8,10},{10,8},{12,14},{14,12},{16,18},{18,... | collective-permute-start | bytes 61448 | tf_op jit(solution)/shard_map/ppermute | solution.py:73
  189.2 5.7 %collective-permute-start.13 = (f32[5120]{0:T(1024)S(1)}, f32[5120]{0:T(1024)S(1)}, u32[]{:S(2)}, u32[]{:S(2)}) collective-permute-start(f32[5120]{0:T(1024)S(1)} %add.92), channel_id=1, source_target_pairs={{0,4},{2,6},{4,0},{6,2},{8,12},{10,14},{12,8},{14,10},{16,20},{18,... | collective-permute-start | bytes 61448 | tf_op jit(solution)/shard_map/ppermute | solution.py:73
  194.9 7.2 %collective-permute-start.14 = (f32[5120]{0:T(1024)S(1)}, f32[5120]{0:T(1024)S(1)}, u32[]{:S(2)}, u32[]{:S(2)}) collective-permute-start(f32[5120]{0:T(1024)S(1)} %add.93), channel_id=1, source_target_pairs={{0,8},{2,10},{4,12},{6,14},{8,0},{10,2},{12,4},{14,6},{16,24},{18,... | collective-permute-start | bytes 61448 | tf_op jit(solution)/shard_map/ppermute | solution.py:73
  202.1 5.7 %collective-permute-start.15 = (f32[5120]{0:T(1024)S(1)}, f32[5120]{0:T(1024)S(1)}, u32[]{:S(2)}, u32[]{:S(2)}) collective-permute-start(f32[5120]{0:T(1024)S(1)} %add.94), channel_id=1, source_target_pairs={{0,16},{2,18},{4,20},{6,22},{8,24},{10,26},{12,28},{14,30},{16,0},... | collective-permute-start | bytes 61448 | tf_op jit(solution)/shard_map/ppermute | solution.py:73
  207.8 6.6 %collective-permute-start.16 = (f32[5120]{0:T(1024)S(1)}, f32[5120]{0:T(1024)S(1)}, u32[]{:S(2)}, u32[]{:S(2)}) collective-permute-start(f32[5120]{0:T(1024)S(1)} %add.95), channel_id=1, source_target_pairs={{0,32},{2,34},{4,36},{6,38},{8,40},{10,42},{12,44},{14,46},{16,48}... | collective-permute-start | bytes 61448 | tf_op jit(solution)/shard_map/ppermute | solution.py:73
  214.3 9.6 %collective-permute-start.17 = (f32[5120]{0:T(1024)S(1)}, f32[5120]{0:T(1024)S(1)}, u32[]{:S(2)}, u32[]{:S(2)}) collective-permute-start(f32[5120]{0:T(1024)S(1)} %add.96), channel_id=1, source_target_pairs={{0,64},{2,66},{4,68},{6,70},{8,72},{10,74},{12,76},{14,78},{16,80}... | collective-permute-start | bytes 61448 | tf_op jit(solution)/shard_map/ppermute | solution.py:73
  223.9 6.6 %collective-permute-start.18 = (f32[5120]{0:T(1024)S(1)}, f32[5120]{0:T(1024)S(1)}, u32[]{:S(2)}, u32[]{:S(2)}) collective-permute-start(f32[5120]{0:T(1024)S(1)} %add.97), channel_id=1, source_target_pairs={{0,128},{2,130},{4,132},{6,134},{8,136},{10,138},{12,140},{14,142}... | collective-permute-start | bytes 61448 | tf_op jit(solution)/shard_map/ppermute | solution.py:73
  230.5 9.6 %collective-permute-start.19 = (f32[5120]{0:T(1024)S(1)}, f32[5120]{0:T(1024)S(1)}, u32[]{:S(2)}, u32[]{:S(2)}) collective-permute-start(f32[5120]{0:T(1024)S(1)} %add.98), channel_id=1, source_target_pairs={{0,256},{2,258},{4,260},{6,262},{8,264},{10,266},{12,268},{14,270}... | collective-permute-start | bytes 61448 | tf_op jit(solution)/shard_map/ppermute | solution.py:73

commit v5 on v4

--- a/solution.py
+++ b/solution.py
@@ -38,13 +38,7 @@
     far_ahead = pairs_permute(value, axis, [(i, i - 2) for i in range(1, count, 2)])
     relay_behind = pairs_permute(behind, axis, [(i, i + 1) for i in range(0, count, 2)])
     relay_ahead = pairs_permute(ahead, axis, [(i, i - 1) for i in range(1, count, 2)])
-    odd = lax.axis_index(axis) % 2 == 1
-    return [
-        behind,
-        ahead,
-        jnp.where(odd, relay_behind, far_behind),
-        jnp.where(odd, far_ahead, relay_ahead),
-    ]
+    return [behind, ahead, far_behind, relay_behind, far_ahead, relay_ahead]
 
 
 def return_parts(far, axis):
@@ -91,25 +85,38 @@
     return (inverse * (scaled - hat * inner), jnp.sum(grad_norm * hat, axis=0))
 
 
-def attention_kernel(live_ref, q_ref, k_ref, v_ref, g_ref, *refs):
-    slots = (len(refs) - 3) // 2
-    fetched = refs[:slots]
-    dq_ref, dk_ref, dv_ref = refs[slots:slots + 3]
-    far = refs[slots + 3:]
+def attention_kernel(odd_ref, bias_ref, q_ref, k_ref, v_ref, g_ref, *refs):
+    behind, ahead, far_behind, relay_behind, far_ahead, relay_ahead = refs[:6]
+    dq_ref, dk_ref, dv_ref = refs[6:9]
+    far = refs[9:]
+    slots = len(far)
     rows = q_ref.shape[0]
     scale = 1.0 / math.sqrt(HEAD)
-    live = live_ref[...] > 0
+    odd = odd_ref[0] == 1
+    bias = bias_ref[...]
     for h in range(q_ref.shape[1] // HEAD):
         cols = pl.ds(h * HEAD, HEAD)
+
+        def pick(which, cols=cols):
+            return jnp.concatenate(
+                [
+                    behind[which, :, cols],
+                    ahead[which, :, cols],
+                    jnp.where(odd, relay_behind[which, :, cols], far_behind[which, :, cols]),
+                    jnp.where(odd, far_ahead[which, :, cols], relay_ahead[which, :, cols]),
+                ],
+                axis=0,
+            )
+
         q = q_ref[:, cols]
         g = g_ref[:, cols]
-        keys = jnp.concatenate([k_ref[:, cols]] + [r[0, :, cols] for r in fetched], axis=0)
-        vals = jnp.concatenate([v_ref[:, cols]] + [r[1, :, cols] for r in fetched], axis=0)
-        scores = lax.dot_general(q, keys, NT, preferred_element_type=jnp.float32) * scale
-        highest = jnp.max(jnp.where(live, scores, -jnp.inf), axis=1, keepdims=True)
-        total = jnp.sum(jnp.where(live, jnp.exp(scores - highest), 0.0), axis=1, keepdims=True)
+        keys = jnp.concatenate([k_ref[:, cols], pick(0)], axis=0)
+        vals = jnp.concatenate([v_ref[:, cols], pick(1)], axis=0)
+        scores = lax.dot_general(q, keys, NT, preferred_element_type=jnp.float32) * scale + bias
+        highest = jnp.max(scores, axis=1, keepdims=True)
+        total = jnp.sum(jnp.exp(scores - highest), axis=1, keepdims=True)
         log_total = highest + jnp.log(total)
-        prob = jnp.where(live, jnp.exp(scores - log_total), 0.0).astype(jnp.bfloat16)
+        prob = jnp.exp(scores - log_total).astype(jnp.bfloat16)
         attended = jnp.dot(prob, vals, preferred_element_type=jnp.float32)
         delta = jnp.sum(g.astype(jnp.float32) * attended, axis=1, keepdims=True)
         prob_grad = lax.dot_general(g, vals, NT, preferred_element_type=jnp.float32)
@@ -125,28 +132,32 @@
             far[slot][1, :, cols] = grad_v[part].astype(jnp.bfloat16)
 
 
-def attention(live, q_norm, k_norm, value_rows, grad_rows, fetched):
+def attention(odd, bias, q_norm, k_norm, value_rows, grad_rows, fetched):
     rows, features = q_norm.shape
     width = HEADS_PER_STEP * HEAD
-    slots = len(fetched)
-    tile = pl.BlockSpec((rows, width), lambda h: (0, h))
-    pair = pl.BlockSpec((2, rows, width), lambda h: (0, 0, h))
+    slots = 4
+    tile = pl.BlockSpec((rows, width), lambda h, odd: (0, h))
+    pair = pl.BlockSpec((2, rows, width), lambda h, odd: (0, 0, h))
     f32 = jax.ShapeDtypeStruct((rows, features), jnp.float32)
     bf16_pair = jax.ShapeDtypeStruct((2, rows, features), jnp.bfloat16)
     keys = rows * (slots + 1)
     flops = 2 * rows * keys * features * 6
+    grid_spec = pltpu.PrefetchScalarGridSpec(
+        num_scalar_prefetch=1,
+        grid=(features // width,),
+        in_specs=[pl.BlockSpec(bias.shape, lambda h, odd: (0, 0))] + [tile] * 4 + [pair] * len(fetched),
+        out_specs=[tile] * 3 + [pair] * slots,
+    )
     return pl.pallas_call(
         attention_kernel,
-        grid=(features // width,),
-        in_specs=[pl.BlockSpec(live.shape, lambda h: (0, 0))] + [tile] * 4 + [pair] * slots,
-        out_specs=[tile] * 3 + [pair] * slots,
+        grid_spec=grid_spec,
         out_shape=[f32] * 3 + [bf16_pair] * slots,
         cost_estimate=pl.CostEstimate(
             flops=flops,
             transcendentals=2 * rows * keys * (features // HEAD),
-            bytes_accessed=2 * rows * features * (4 + 4 * slots) + 12 * rows * features,
+            bytes_accessed=2 * rows * features * (4 + 2 * len(fetched)) + 12 * rows * features,
         ),
-    )(live, q_norm, k_norm, value_rows, grad_rows, *fetched)
+    )(odd, bias, q_norm, k_norm, value_rows, grad_rows, *fetched)
 
 
 def body(q_raw, k_raw, values, cotangent, q_gain, k_gain, key_tiles):
@@ -162,11 +173,11 @@
     entries = key_tiles[0]
     stacked = jnp.stack([k_norm, value_rows])
     fetched = fetch_neighbours(stacked, "seq")
-    live = jnp.repeat(
-        jnp.concatenate([jnp.ones((1,), jnp.int32), (entries >= 0).astype(jnp.int32)]), tile_rows
-    )[None, :]
+    live = jnp.concatenate([jnp.ones((1,), bool), entries >= 0])
+    bias = jnp.repeat(jnp.where(live, 0.0, -jnp.inf).astype(jnp.float32), tile_rows)[None, :]
+    odd = (lax.axis_index("seq") % 2).astype(jnp.int32)[None]
     q_norm_grad, k_norm_grad, v_sum, *far = attention(
-        live, q_norm, k_norm, value_rows, grad_rows, fetched
+        odd, bias, q_norm, k_norm, value_rows, grad_rows, fetched
     )
     for back in return_parts(far, "seq"):
         k_norm_grad = k_norm_grad + back[0].astype(jnp.float32)

time: 241 us -> 237 us (0.983)
  the two profiles are of different devices: /device:TPU:32 before, /device:TPU:48 now
where the time goes in v5:
time: 237 us
  waiting for transfers between devices  136 us (57%)
  starting transfers between devices  63.3 us (27%)
  Pallas kernels  19.9 us (8%)
  other arithmetic  15 us (6%)
    ppermute x4, waiting for transfers between devices, from_behind(): lax.ppermute(value, axis, [(source, source + steps) for source in range(f...  72.8 us
    ppermute x9, waiting for transfers between devices, all_sum(): lax.ppermute(value, axis, [(i, i ^ bit) for i in range(count)])  39.4 us
    ppermute x4, starting transfers between devices, from_behind(): lax.ppermute(value, axis, [(source, source + steps) for source in range(f...  26.9 us
    ppermute x7, waiting for transfers between devices, pairs_permute(): lax.ppermute(value, axis, [(i, j) for i, j in pairs if 0 <= j < count])  23.9 us
    pallas_call x1, Pallas kernels, attention(): pl.pallas_call(attention_kernel, grid_spec=grid_spec, out_shape=[f32] * 3...  19.9 us
    ppermute x7, starting transfers between devices, pairs_permute(): lax.ppermute(value, axis, [(i, j) for i, j in pairs if 0 <= j < count])  18.7 us
    ppermute x9, starting transfers between devices, all_sum(): lax.ppermute(value, axis, [(i, i ^ bit) for i in range(count)])  17.7 us
  transfers between devices with their start and end apart: 20, of which 14 were waited for; matrix products, arithmetic and copies ran while one was open for 3% of the time, Pallas kernels for 0%

profile of v5, /device:TPU:48, one launch (start us, length us, event | category | flops | bytes accessed | tf_op | source)
XLA Modules:
  0.0 236.6 jit_solution(8268792562261090801)
XLA Ops:
  0.6 1.4 fusion.20
  2.0 1.3 fusion.22
  3.4 1.3 pad_maximum_fusion
  4.7 1.9 collective-permute-start
  6.6 14.2 %collective-permute-start.1 = (bf16[2,128,2560]{2,1,0:T(8,128)(2,1)}, bf16[2,128,2560]{2,1,0:T(8,128)(2,1)}, u32[]{:S(2)}, u32[]{:S(2)}) collective-permute-start(bf16[2,128,2560]{2,1,0:T(8,128)(2,1)} %pad_maximum_fusion), channel_id=1, source_target_pairs={{2,0},{4,2},{6,4},{8,6},{10,8},{12,10},{14,12},{16,14},{18,16},{20... | collective-permute-start | bytes 3932168 | tf_op jit(solution)/shard_map/ppermute | solution.py:25
  20.7 1.9 collective-permute-start.2
  22.7 1.8 collective-permute-start.4
  24.5 12.7 %collective-permute-done.refs_0_ = bf16[2,128,2560]{2,1,0:T(8,128)(2,1)S(1)} collective-permute-done((bf16[2,128,2560]{2,1,0:T(8,128)(2,1)}, bf16[2,128,2560]{2,1,0:T(8,128)(2,1)S(1)}, u32[]{:S(2)}, u32[]{:S(2)}) %collective-permute-start) | collective-permute-done | bytes 1310752 | tf_op jit(solution)/shard_map/ppermute | solution.py:25
  37.3 2.3 collective-permute-start.3
  39.6 38.5 %collective-permute-done.1.refs_1_ = bf16[2,128,2560]{2,1,0:T(8,128)(2,1)} collective-permute-done((bf16[2,128,2560]{2,1,0:T(8,128)(2,1)}, bf16[2,128,2560]{2,1,0:T(8,128)(2,1)}, u32[]{:S(2)}, u32[]{:S(2)}) %collective-permute-start.1) | collective-permute-done | bytes 1310752 | tf_op jit(solution)/shard_map/ppermute | solution.py:25
  78.1 1.3 collective-permute-start.5
  79.4 0.6 copy.14
  80.0 0.2 fusion.29
  80.3 1.4 fusion.14
  81.7 1.6 collective-permute-done.5.refs_5_
  83.3 19.9 %shard_map.110 = (f32[128,2560]{1,0:T(8,128)}, f32[128,2560]{1,0:T(8,128)}, f32[128,2560]{1,0:T(8,128)}, bf16[2,128,2560]{2,1,0:T(8,128)(2,1)}, bf16[2,128,2560]...) custom-call(s32[1]{0:T(128)} %bitcast.1.odd_ref, f32[1,640]{1,0:T(1,128)} %bitcast.100, ...), custom_call_target="tpu_custom_call" | custom-call | flops 2516582400 | bytes 14417920 | tf_op jit(solution)/shard_map/pallas_call | solution.py:151
  103.3 1.6 broadcast_select_fusion
  104.9 2.5 %collective-permute-start.6 = (bf16[2,128,2560]{2,1,0:T(8,128)(2,1)S(1)}, bf16[2,128,2560]{2,1,0:T(8,128)(2,1)S(1)}, u32[]{:S(2)}, u32[]{:S(2)}) collective-permute-start(bf16[2,128,2560]{2,1,0:T(8,128)(2,1)S(1)} %broadcast_select_fusion), channel_id=1, source_target_pairs={{0,2},{2,0},{4,6},{6,4},{8,10},{10,8},{12,14},{14,12},{16,18},{18,... | collective-permute-start | bytes 3932168 | tf_op jit(solution)/shard_map/ppermute | solution.py:30
  107.4 8.2 %collective-permute-start.10 = (bf16[2,128,2560]{2,1,0:T(8,128)(2,1)S(1)}, bf16[2,128,2560]{2,1,0:T(8,128)(2,1)S(1)}, u32[]{:S(2)}, u32[]{:S(2)}) collective-permute-start(bf16[2,128,2560]{2,1,0:T(8,128)(2,1)S(1)} %copy-done.8), channel_id=1, source_target_pairs={{4,0},{8,4},{12,8},{16,12},{20,16},{24,20},{28,24},{32,28},{36,32}... | collective-permute-start | bytes 3932168 | tf_op jit(solution)/shard_map/ppermute | solution.py:30
  115.6 0.7 collective-permute-start.9
  116.4 2.7 %fusion.3 = (bf16[2,128,2560]{2,1,0:T(8,128)(2,1)S(1)}, bf16[2,128,2560]{2,1,0:T(8,128)(2,1)S(1)}) fusion(bf16[2,128,2560]{2,1,0:T(8,128)(2,1)} %get-tuple-element.14, bf16[2,128,2560]{2,1,0:T(8,128)(2,1)S(1)} %collective-permute-done.6, pred[]{:T(512)S(6)} %eq.6, bf16[2,128,2560]{2,1,0:T(8,128)(2,1)S(1)} %copy-done.9), kind=kLoop, calls=%fused_computation.5 | loop fusion | flops 5898240 | bytes 6553601 | tf_op jit(solution)/shard_map/jit(_where)/select_n | solution.py:55
  119.1 2.1 collective-permute-start.7
  121.2 8.8 %collective-permute-start.8 = (bf16[2,128,2560]{2,1,0:T(8,128)(2,1)S(1)}, bf16[2,128,2560]{2,1,0:T(8,128)(2,1)S(1)}, u32[]{:S(2)}, u32[]{:S(2)}) collective-permute-start(bf16[2,128,2560]{2,1,0:T(8,128)(2,1)S(1)} %get-tuple-element.26), channel_id=1, source_target_pairs={{2,0},{4,2},{6,4},{8,6},{10,8},{12,10},{14,12},{16,14},{18,16},{20... | collective-permute-start | bytes 3932168 | tf_op jit(solution)/shard_map/ppermute | solution.py:25
  130.0 0.5 fusion.28
  130.4 22.3 %collective-permute-done.10 = bf16[2,128,2560]{2,1,0:T(8,128)(2,1)S(1)} collective-permute-done((bf16[2,128,2560]{2,1,0:T(8,128)(2,1)S(1)}, bf16[2,128,2560]{2,1,0:T(8,128)(2,1)S(1)}, u32[]{:S(2)}, u32[]{:S(2)}) %collective-permute-start.10) | collective-permute-done | bytes 1310752 | tf_op jit(solution)/shard_map/ppermute | solution.py:30
  152.7 21.6 %collective-permute-done.7 = bf16[2,128,2560]{2,1,0:T(8,128)(2,1)S(1)} collective-permute-done((bf16[2,128,2560]{2,1,0:T(8,128)(2,1)S(1)}, bf16[2,128,2560]{2,1,0:T(8,128)(2,1)S(1)}, u32[]{:S(2)}, u32[]{:S(2)}) %collective-permute-start.7) | collective-permute-done | bytes 1310752 | tf_op jit(solution)/shard_map/ppermute | solution.py:25
  174.3 2.0 fusion.19
  176.3 1.9 collective-permute-start.11
  178.2 3.7 %collective-permute-done.11 = f32[5120]{0:T(1024)S(1)} collective-permute-done((f32[5120]{0:T(1024)S(1)}, f32[5120]{0:T(1024)S(1)}, u32[]{:S(2)}, u32[]{:S(2)}) %collective-permute-start.11) | collective-permute-done | bytes 20512 | tf_op jit(solution)/shard_map/ppermute | solution.py:67
  182.0 1.9 collective-permute-start.12
  183.9 1.2 collective-permute-done.12
  185.0 1.9 collective-permute-start.13
  187.0 3.7 %collective-permute-done.13 = f32[5120]{0:T(1024)S(1)} collective-permute-done((f32[5120]{0:T(1024)S(1)}, f32[5120]{0:T(1024)S(1)}, u32[]{:S(2)}, u32[]{:S(2)}) %collective-permute-start.13) | collective-permute-done | bytes 20512 | tf_op jit(solution)/shard_map/ppermute | solution.py:67
  190.7 1.9 collective-permute-start.14
  192.6 5.3 %collective-permute-done.14 = f32[5120]{0:T(1024)S(1)} collective-permute-done((f32[5120]{0:T(1024)S(1)}, f32[5120]{0:T(1024)S(1)}, u32[]{:S(2)}, u32[]{:S(2)}) %collective-permute-start.14) | collective-permute-done | bytes 20512 | tf_op jit(solution)/shard_map/ppermute | solution.py:67
  197.9 1.9 collective-permute-start.15
  199.8 3.7 %collective-permute-done.15 = f32[5120]{0:T(1024)S(1)} collective-permute-done((f32[5120]{0:T(1024)S(1)}, f32[5120]{0:T(1024)S(1)}, u32[]{:S(2)}, u32[]{:S(2)}) %collective-permute-start.15) | collective-permute-done | bytes 20512 | tf_op jit(solution)/shard_map/ppermute | solution.py:67
  203.6 1.9 collective-permute-start.16
  205.5 4.6 %collective-permute-done.16 = f32[5120]{0:T(1024)S(1)} collective-permute-done((f32[5120]{0:T(1024)S(1)}, f32[5120]{0:T(1024)S(1)}, u32[]{:S(2)}, u32[]{:S(2)}) %collective-permute-start.16) | collective-permute-done | bytes 20512 | tf_op jit(solution)/shard_map/ppermute | solution.py:67
  210.1 1.9 collective-permute-start.17
  212.0 1.2 fusion.32
  213.3 6.4 %collective-permute-done.17 = f32[5120]{0:T(1024)S(1)} collective-permute-done((f32[5120]{0:T(1024)S(1)}, f32[5120]{0:T(1024)S(1)}, u32[]{:S(2)}, u32[]{:S(2)}) %collective-permute-start.17) | collective-permute-done | bytes 20512 | tf_op jit(solution)/shard_map/ppermute | solution.py:67
  219.7 2.4 %collective-permute-start.18 = (f32[5120]{0:T(1024)S(1)}, f32[5120]{0:T(1024)S(1)}, u32[]{:S(2)}, u32[]{:S(2)}) collective-permute-start(f32[5120]{0:T(1024)S(1)} %add.97), channel_id=1, source_target_pairs={{0,128},{2,130},{4,132},{6,134},{8,136},{10,138},{12,140},{14,142}... | collective-permute-start | bytes 61448 | tf_op jit(solution)/shard_map/ppermute | solution.py:67
  222.1 4.2 %collective-permute-done.18 = f32[5120]{0:T(1024)S(1)} collective-permute-done((f32[5120]{0:T(1024)S(1)}, f32[5120]{0:T(1024)S(1)}, u32[]{:S(2)}, u32[]{:S(2)}) %collective-permute-start.18) | collective-permute-done | bytes 20512 | tf_op jit(solution)/shard_map/ppermute | solution.py:67
  226.3 1.9 collective-permute-start.19
  228.2 1.2 fusion.33
  229.4 6.5 %collective-permute-done.19 = f32[5120]{0:T(1024)S(1)} collective-permute-done((f32[5120]{0:T(1024)S(1)}, f32[5120]{0:T(1024)S(1)}, u32[]{:S(2)}, u32[]{:S(2)}) %collective-permute-start.19) | collective-permute-done | bytes 20512 | tf_op jit(solution)/shard_map/ppermute | solution.py:67
  236.0 0.6 fusion.34
  (49 shorter events, 0.3 us)
Async XLA Ops:
  0.6 2.7 %copy-start.3 = (bf16[1,128,2560]{2,1,0:T(8,128)(2,1)S(1)}, bf16[1,128,2560]{2,1,0:T(8,128)(2,1)}, u32[]{:S(2)}) copy-start(bf16[1,128,2560]{2,1,0:T(8,128)(2,1)} %param.9) | copy-start | bytes 1966084
  3.3 21.1 %copy-start.12 = (s32[1,4]{1,0:T(1,128)S(1)}, s32[1,4]{1,0:T(1,128)}, u32[]{:S(2)}) copy-start(s32[1,4]{1,0:T(1,128)} %param.13) | copy-start | bytes 52
  3.4 76.7 %copy-start.1 = (bf16[1,128,2560]{2,1,0:T(8,128)(2,1)S(1)}, bf16[1,128,2560]{2,1,0:T(8,128)(2,1)}, u32[]{:S(2)}) copy-start(bf16[1,128,2560]{2,1,0:T(8,128)(2,1)} %param.7) | copy-start | bytes 1966084
  3.4 76.9 %copy-start = (bf16[1,128,2560]{2,1,0:T(8,128)(2,1)S(1)}, bf16[1,128,2560]{2,1,0:T(8,128)(2,1)}, u32[]{:S(2)}) copy-start(bf16[1,128,2560]{2,1,0:T(8,128)(2,1)} %param.8) | copy-start | bytes 1966084
  3.4 76.9 %copy-start.10 = (f32[2560]{0:T(1024)S(1)}, f32[2560]{0:T(1024)}, u32[]{:S(2)}) copy-start(f32[2560]{0:T(1024)} %param.12) | copy-start | bytes 30724
  3.4 76.9 %copy-start.11 = (f32[2560]{0:T(1024)S(1)}, f32[2560]{0:T(1024)}, u32[]{:S(2)}) copy-start(f32[2560]{0:T(1024)} %param.11) | copy-start | bytes 30724
  4.7 32.6 %collective-permute-start = (bf16[2,128,2560]{2,1,0:T(8,128)(2,1)}, bf16[2,128,2560]{2,1,0:T(8,128)(2,1)S(1)}, u32[]{:S(2)}, u32[]{:S(2)}) collective-permute-start(bf16[2,128,2560]{2,1,0:T(8,128)(2,1)} %pad_maximum_fusion), channel_id=1, source_target_pairs={{0,2},{2,4},{4,6},{6,8},{8,10},{10,12},{12,14},{14,16},{16,18},{18... | collective-permute-start | bytes 3932168 | tf_op jit(solution)/shard_map/ppermute | solution.py:25
  6.6 71.5 %collective-permute-start.1 = (bf16[2,128,2560]{2,1,0:T(8,128)(2,1)}, bf16[2,128,2560]{2,1,0:T(8,128)(2,1)}, u32[]{:S(2)}, u32[]{:S(2)}) collective-permute-start(bf16[2,128,2560]{2,1,0:T(8,128)(2,1)} %pad_maximum_fusion), channel_id=1, source_target_pairs={{2,0},{4,2},{6,4},{8,6},{10,8},{12,10},{14,12},{16,14},{18,16},{20... | collective-permute-start | bytes 3932168 | tf_op jit(solution)/shard_map/ppermute | solution.py:25
  20.7 61.0 %collective-permute-start.2 = (bf16[2,128,2560]{2,1,0:T(8,128)(2,1)}, bf16[2,128,2560]{2,1,0:T(8,128)(2,1)}, u32[]{:S(2)}, u32[]{:S(2)}) collective-permute-start(bf16[2,128,2560]{2,1,0:T(8,128)(2,1)} %pad_maximum_fusion), channel_id=1, source_target_pairs={{0,4},{4,8},{8,12},{12,16},{16,20},{20,24},{24,28},{28,32},{32,36}... | collective-permute-start | bytes 3932168 | tf_op jit(solution)/shard_map/ppermute | solution.py:30
  22.7 59.0 %collective-permute-start.4 = (bf16[2,128,2560]{2,1,0:T(8,128)(2,1)}, bf16[2,128,2560]{2,1,0:T(8,128)(2,1)}, u32[]{:S(2)}, u32[]{:S(2)}) collective-permute-start(bf16[2,128,2560]{2,1,0:T(8,128)(2,1)} %pad_maximum_fusion), channel_id=1, source_target_pairs={{6,2},{10,6},{14,10},{18,14},{22,18},{26,22},{30,26},{34,30},{38,3... | collective-permute-start | bytes 3932168 | tf_op jit(solution)/shard_map/ppermute | solution.py:30
  37.3 44.4 %copy-start.4 = (bf16[2,128,2560]{2,1,0:T(8,128)(2,1)}, bf16[2,128,2560]{2,1,0:T(8,128)(2,1)S(1)}, u32[]{:S(2)}) copy-start(bf16[2,128,2560]{2,1,0:T(8,128)(2,1)S(1)} %collective-permute-done.refs_0_) | copy-start | bytes 3932164
  37.3 44.4 %collective-permute-start.3 = (bf16[2,128,2560]{2,1,0:T(8,128)(2,1)S(1)}, bf16[2,128,2560]{2,1,0:T(8,128)(2,1)}, u32[]{:S(2)}, u32[]{:S(2)}) collective-permute-start(bf16[2,128,2560]{2,1,0:T(8,128)(2,1)S(1)} %collective-permute-done.refs_0_), channel_id=1, source_target_pairs={{0,2},{4,6},{8,10},{12,14},{16,18},{20,22},{24,26},{28,30},{32,34}... | collective-permute-start | bytes 3932168 | tf_op jit(solution)/shard_map/ppermute | solution.py:30
  78.1 5.3 %collective-permute-start.5 = (bf16[2,128,2560]{2,1,0:T(8,128)(2,1)}, bf16[2,128,2560]{2,1,0:T(8,128)(2,1)}, u32[]{:S(2)}, u32[]{:S(2)}) collective-permute-start(bf16[2,128,2560]{2,1,0:T(8,128)(2,1)} %collective-permute-done.1.refs_1_), channel_id=1, source_target_pairs={{2,0},{6,4},{10,8},{14,12},{18,16},{22,20},{26,24},{30,28},{34,32}... | collective-permute-start | bytes 3932168 | tf_op jit(solution)/shard_map/ppermute | solution.py:30
  103.3 4.2 %copy-start.8 = (bf16[2,128,2560]{2,1,0:T(8,128)(2,1)S(1)}, bf16[2,128,2560]{2,1,0:T(8,128)(2,1)}, u32[]{:S(2)}) copy-start(bf16[2,128,2560]{2,1,0:T(8,128)(2,1)} %get-tuple-element.15) | copy-start | bytes 3932164
  103.3 12.4 %copy-start.7 = (bf16[2,128,2560]{2,1,0:T(8,128)(2,1)S(1)}, bf16[2,128,2560]{2,1,0:T(8,128)(2,1)}, u32[]{:S(2)}) copy-start(bf16[2,128,2560]{2,1,0:T(8,128)(2,1)} %get-tuple-element.16) | copy-start | bytes 3932164
  103.3 13.1 %copy-start.9 = (bf16[2,128,2560]{2,1,0:T(8,128)(2,1)S(1)}, bf16[2,128,2560]{2,1,0:T(8,128)(2,1)}, u32[]{:S(2)}) copy-start(bf16[2,128,2560]{2,1,0:T(8,128)(2,1)} %get-tuple-element.17) | copy-start | bytes 3932164
  104.9 11.5 %collective-permute-start.6 = (bf16[2,128,2560]{2,1,0:T(8,128)(2,1)S(1)}, bf16[2,128,2560]{2,1,0:T(8,128)(2,1)S(1)}, u32[]{:S(2)}, u32[]{:S(2)}) collective-permute-start(bf16[2,128,2560]{2,1,0:T(8,128)(2,1)S(1)} %broadcast_select_fusion), channel_id=1, source_target_pairs={{0,2},{2,0},{4,6},{6,4},{8,10},{10,8},{12,14},{14,12},{16,18},{18,... | collective-permute-start | bytes 3932168 | tf_op jit(solution)/shard_map/ppermute | solution.py:30
  107.4 45.2 %collective-permute-start.10 = (bf16[2,128,2560]{2,1,0:T(8,128)(2,1)S(1)}, bf16[2,128,2560]{2,1,0:T(8,128)(2,1)S(1)}, u32[]{:S(2)}, u32[]{:S(2)}) collective-permute-start(bf16[2,128,2560]{2,1,0:T(8,128)(2,1)S(1)} %copy-done.8), channel_id=1, source_target_pairs={{4,0},{8,4},{12,8},{16,12},{20,16},{24,20},{28,24},{32,28},{36,32}... | collective-permute-start | bytes 3932168 | tf_op jit(solution)/shard_map/ppermute | solution.py:30
  115.6 37.0 %collective-permute-start.9 = (bf16[2,128,2560]{2,1,0:T(8,128)(2,1)S(1)}, bf16[2,128,2560]{2,1,0:T(8,128)(2,1)S(1)}, u32[]{:S(2)}, u32[]{:S(2)}) collective-permute-start(bf16[2,128,2560]{2,1,0:T(8,128)(2,1)S(1)} %copy-done.7), channel_id=1, source_target_pairs={{2,6},{6,10},{10,14},{14,18},{18,22},{22,26},{26,30},{30,34},{34,3... | collective-permute-start | bytes 3932168 | tf_op jit(solution)/shard_map/ppermute | solution.py:30
  116.4 13.5 %copy-start.2 = (f32[128,2560]{1,0:T(8,128)S(1)}, f32[128,2560]{1,0:T(8,128)}, u32[]{:S(2)}) copy-start(f32[128,2560]{1,0:T(8,128)} %get-tuple-element.12) | copy-start | bytes 3932164
  116.4 57.8 %copy-start.6 = (f32[128,2560]{1,0:T(8,128)S(1)}, f32[128,2560]{1,0:T(8,128)}, u32[]{:S(2)}) copy-start(f32[128,2560]{1,0:T(8,128)} %get-tuple-element.18) | copy-start | bytes 3932164
  119.1 55.1 %copy-start.5 = (f32[128,2560]{1,0:T(8,128)S(1)}, f32[128,2560]{1,0:T(8,128)}, u32[]{:S(2)}) copy-start(f32[128,2560]{1,0:T(8,128)} %get-tuple-element.13) | copy-start | bytes 3932164
  119.1 55.1 %collective-permute-start.7 = (bf16[2,128,2560]{2,1,0:T(8,128)(2,1)S(1)}, bf16[2,128,2560]{2,1,0:T(8,128)(2,1)S(1)}, u32[]{:S(2)}, u32[]{:S(2)}) collective-permute-start(bf16[2,128,2560]{2,1,0:T(8,128)(2,1)S(1)} %get-tuple-element.25), channel_id=1, source_target_pairs={{0,2},{2,4},{4,6},{6,8},{8,10},{10,12},{12,14},{14,16},{16,18},{18... | collective-permute-start | bytes 3932168 | tf_op jit(solution)/shard_map/ppermute | solution.py:25
  121.2 53.1 %collective-permute-start.8 = (bf16[2,128,2560]{2,1,0:T(8,128)(2,1)S(1)}, bf16[2,128,2560]{2,1,0:T(8,128)(2,1)S(1)}, u32[]{:S(2)}, u32[]{:S(2)}) collective-permute-start(bf16[2,128,2560]{2,1,0:T(8,128)(2,1)S(1)} %get-tuple-element.26), channel_id=1, source_target_pairs={{2,0},{4,2},{6,4},{8,6},{10,8},{12,10},{14,12},{16,14},{18,16},{20... | collective-permute-start | bytes 3932168 | tf_op jit(solution)/shard_map/ppermute | solution.py:25
  176.3 5.7 %collective-permute-start.11 = (f32[5120]{0:T(1024)S(1)}, f32[5120]{0:T(1024)S(1)}, u32[]{:S(2)}, u32[]{:S(2)}) collective-permute-start(f32[5120]{0:T(1024)S(1)} %pad_maximum_fusion.1), channel_id=1, source_target_pairs={{0,1},{1,0},{2,3},{3,2},{4,5},{5,4},{6,7},{7,6},{8,9},{9,8},{10,11... | collective-permute-start | bytes 61448 | tf_op jit(solution)/shard_map/ppermute | solution.py:67
  182.0 3.1 %collective-permute-start.12 = (f32[5120]{0:T(1024)S(1)}, f32[5120]{0:T(1024)S(1)}, u32[]{:S(2)}, u32[]{:S(2)}) collective-permute-start(f32[5120]{0:T(1024)S(1)} %fusion.35), channel_id=1, source_target_pairs={{0,2},{2,0},{4,6},{6,4},{8,10},{10,8},{12,14},{14,12},{16,18},{18,... | collective-permute-start | bytes 61448 | tf_op jit(solution)/shard_map/ppermute | solution.py:67
  185.0 5.7 %collective-permute-start.13 = (f32[5120]{0:T(1024)S(1)}, f32[5120]{0:T(1024)S(1)}, u32[]{:S(2)}, u32[]{:S(2)}) collective-permute-start(f32[5120]{0:T(1024)S(1)} %add.92), channel_id=1, source_target_pairs={{0,4},{2,6},{4,0},{6,2},{8,12},{10,14},{12,8},{14,10},{16,20},{18,... | collective-permute-start | bytes 61448 | tf_op jit(solution)/shard_map/ppermute | solution.py:67
  190.7 7.2 %collective-permute-start.14 = (f32[5120]{0:T(1024)S(1)}, f32[5120]{0:T(1024)S(1)}, u32[]{:S(2)}, u32[]{:S(2)}) collective-permute-start(f32[5120]{0:T(1024)S(1)} %add.93), channel_id=1, source_target_pairs={{0,8},{2,10},{4,12},{6,14},{8,0},{10,2},{12,4},{14,6},{16,24},{18,... | collective-permute-start | bytes 61448 | tf_op jit(solution)/shard_map/ppermute | solution.py:67
  197.9 5.7 %collective-permute-start.15 = (f32[5120]{0:T(1024)S(1)}, f32[5120]{0:T(1024)S(1)}, u32[]{:S(2)}, u32[]{:S(2)}) collective-permute-start(f32[5120]{0:T(1024)S(1)} %add.94), channel_id=1, source_target_pairs={{0,16},{2,18},{4,20},{6,22},{8,24},{10,26},{12,28},{14,30},{16,0},... | collective-permute-start | bytes 61448 | tf_op jit(solution)/shard_map/ppermute | solution.py:67
  203.6 6.6 %collective-permute-start.16 = (f32[5120]{0:T(1024)S(1)}, f32[5120]{0:T(1024)S(1)}, u32[]{:S(2)}, u32[]{:S(2)}) collective-permute-start(f32[5120]{0:T(1024)S(1)} %add.95), channel_id=1, source_target_pairs={{0,32},{2,34},{4,36},{6,38},{8,40},{10,42},{12,44},{14,46},{16,48}... | collective-permute-start | bytes 61448 | tf_op jit(solution)/shard_map/ppermute | solution.py:67
  210.1 9.6 %collective-permute-start.17 = (f32[5120]{0:T(1024)S(1)}, f32[5120]{0:T(1024)S(1)}, u32[]{:S(2)}, u32[]{:S(2)}) collective-permute-start(f32[5120]{0:T(1024)S(1)} %add.96), channel_id=1, source_target_pairs={{0,64},{2,66},{4,68},{6,70},{8,72},{10,74},{12,76},{14,78},{16,80}... | collective-permute-start | bytes 61448 | tf_op jit(solution)/shard_map/ppermute | solution.py:67
  219.7 6.6 %collective-permute-start.18 = (f32[5120]{0:T(1024)S(1)}, f32[5120]{0:T(1024)S(1)}, u32[]{:S(2)}, u32[]{:S(2)}) collective-permute-start(f32[5120]{0:T(1024)S(1)} %add.97), channel_id=1, source_target_pairs={{0,128},{2,130},{4,132},{6,134},{8,136},{10,138},{12,140},{14,142}... | collective-permute-start | bytes 61448 | tf_op jit(solution)/shard_map/ppermute | solution.py:67
  226.3 9.7 %collective-permute-start.19 = (f32[5120]{0:T(1024)S(1)}, f32[5120]{0:T(1024)S(1)}, u32[]{:S(2)}, u32[]{:S(2)}) collective-permute-start(f32[5120]{0:T(1024)S(1)} %add.98), channel_id=1, source_target_pairs={{0,256},{2,258},{4,260},{6,262},{8,264},{10,266},{12,268},{14,270}... | collective-permute-start | bytes 61448 | tf_op jit(solution)/shard_map/ppermute | solution.py:67

commit v6 on v5

--- a/solution.py
+++ b/solution.py
@@ -10,7 +10,8 @@
 
 HEAD = 128
 LEVELS = 2
-HEADS_PER_STEP = 4
+HEADS_PER_STEP = 2
+CHUNKS = 2
 
 
 EPS = 1e-06
@@ -132,10 +133,12 @@
             far[slot][1, :, cols] = grad_v[part].astype(jnp.bfloat16)
 
 
-def attention(odd, bias, q_norm, k_norm, value_rows, grad_rows, fetched):
-    rows, features = q_norm.shape
+def attention(odd, bias, q_norm, k_norm, value_rows, grad_rows, fetched, first=0):
+    rows = q_norm.shape[0]
+    features = fetched[0].shape[2]
     width = HEADS_PER_STEP * HEAD
     slots = 4
+    own = pl.BlockSpec((rows, width), lambda h, odd: (0, h + first))
     tile = pl.BlockSpec((rows, width), lambda h, odd: (0, h))
     pair = pl.BlockSpec((2, rows, width), lambda h, odd: (0, 0, h))
     f32 = jax.ShapeDtypeStruct((rows, features), jnp.float32)
@@ -145,7 +148,7 @@
     grid_spec = pltpu.PrefetchScalarGridSpec(
         num_scalar_prefetch=1,
         grid=(features // width,),
-        in_specs=[pl.BlockSpec(bias.shape, lambda h, odd: (0, 0))] + [tile] * 4 + [pair] * len(fetched),
+        in_specs=[pl.BlockSpec(bias.shape, lambda h, odd: (0, 0))] + [own] * 4 + [pair] * len(fetched),
         out_specs=[tile] * 3 + [pair] * slots,
     )
     return pl.pallas_call(
@@ -171,17 +174,28 @@
     value_rows = values[0]
     grad_rows = cotangent[0]
     entries = key_tiles[0]
-    stacked = jnp.stack([k_norm, value_rows])
-    fetched = fetch_neighbours(stacked, "seq")
     live = jnp.concatenate([jnp.ones((1,), bool), entries >= 0])
     bias = jnp.repeat(jnp.where(live, 0.0, -jnp.inf).astype(jnp.float32), tile_rows)[None, :]
     odd = (lax.axis_index("seq") % 2).astype(jnp.int32)[None]
-    q_norm_grad, k_norm_grad, v_sum, *far = attention(
-        odd, bias, q_norm, k_norm, value_rows, grad_rows, fetched
-    )
-    for back in return_parts(far, "seq"):
-        k_norm_grad = k_norm_grad + back[0].astype(jnp.float32)
-        v_sum = v_sum + back[1].astype(jnp.float32)
+    chunk = features // CHUNKS
+    pieces = []
+    fetched = None
+    for c in range(CHUNKS):
+        cols = slice(c * chunk, (c + 1) * chunk)
+        stacked = jnp.stack([k_norm[:, cols], value_rows[:, cols]])
+        if fetched is not None:
+            stacked, _ = lax.optimization_barrier((stacked, fetched))
+        fetched = fetch_neighbours(stacked, "seq")
+        q_grad_c, k_grad_c, v_sum_c, *far = attention(
+            odd, bias, q_norm, k_norm, value_rows, grad_rows, fetched, c * chunk // (HEADS_PER_STEP * HEAD)
+        )
+        for back in return_parts(far, "seq"):
+            k_grad_c = k_grad_c + back[0].astype(jnp.float32)
+            v_sum_c = v_sum_c + back[1].astype(jnp.float32)
+        pieces.append((q_grad_c, k_grad_c, v_sum_c))
+    q_norm_grad, k_norm_grad, v_sum = (
+        jnp.concatenate([p[i] for p in pieces], axis=1) for i in range(3)
+    )
     q_back, q_part = norm_backward(q_norm_grad, q_gain, q_hat, q_inv)
     k_back, k_part = norm_backward(k_norm_grad, k_gain, k_hat, k_inv)
     gain_grads = all_sum(jnp.concatenate([q_part, k_part]), ("dp", "seq"))

time: 237 us -> 232 us (0.979)
  the two profiles are of different devices: /device:TPU:48 before, /device:TPU:24 now
where the time goes in v6:
time: 232 us; the launch traced here: 231 us
  waiting for transfers between devices  107 us (46%)
  starting transfers between devices  79.5 us (34%)
  Pallas kernels  22.5 us (10%)
  other arithmetic  17.3 us (7%)
  local copies, waits for them, and re-layouts  3.68 us (2%)
    ppermute x8, waiting for transfers between devices, from_behind(): lax.ppermute(value, axis, [(source, source + steps) for source in range(f...  67.9 us
    ppermute x9, waiting for transfers between devices, all_sum(): lax.ppermute(value, axis, [(i, i ^ bit) for i in range(count)])  37.8 us
    ppermute x8, starting transfers between devices, from_behind(): lax.ppermute(value, axis, [(source, source + steps) for source in range(f...  33.8 us
    ppermute x14, starting transfers between devices, pairs_permute(): lax.ppermute(value, axis, [(i, j) for i, j in pairs if 0 <= j < count])  27.4 us
    pallas_call x2, Pallas kernels, attention(): pl.pallas_call(attention_kernel, grid_spec=grid_spec, out_shape=[f32] * 3...  22.5 us
    ppermute x9, starting transfers between devices, all_sum(): lax.ppermute(value, axis, [(i, i ^ bit) for i in range(count)])  18.3 us
  transfers between devices with their start and end apart: 31, of which 15 were waited for; matrix products, arithmetic and copies ran while one was open for 6% of the time, Pallas kernels for 10%

profile of v6, /device:TPU:24, one launch (start us, length us, event | category | flops | bytes accessed | tf_op | source)
XLA Modules:
  0.0 231.0 jit_solution(8690994913163455296)
XLA Ops:
  0.6 1.4 fusion.25
  2.0 1.3 fusion.22.k_ref
  5.1 2.0 collective-permute-start
  7.1 12.4 %collective-permute-start.1 = (bf16[2,128,1280]{2,1,0:T(8,128)(2,1)}, bf16[2,128,1280]{2,1,0:T(8,128)(2,1)S(1)}, u32[]{:S(2)}, u32[]{:S(2)}) collective-permute-start(bf16[2,128,1280]{2,1,0:T(8,128)(2,1)} %pad_maximum_fusion.1), channel_id=1, source_target_pairs={{2,0},{4,2},{6,4},{8,6},{10,8},{12,10},{14,12},{16,14},{18,16},{20... | collective-permute-start | bytes 1966088 | tf_op jit(solution)/shard_map/ppermute | solution.py:26
  19.5 1.9 collective-permute-start.2
  21.4 1.5 collective-permute-start.4
  23.0 19.8 %collective-permute-done.refs_0_ = bf16[2,128,1280]{2,1,0:T(8,128)(2,1)S(1)} collective-permute-done((bf16[2,128,1280]{2,1,0:T(8,128)(2,1)}, bf16[2,128,1280]{2,1,0:T(8,128)(2,1)S(1)}, u32[]{:S(2)}, u32[]{:S(2)}) %collective-permute-start) | collective-permute-done | bytes 655392 | tf_op jit(solution)/shard_map/ppermute | solution.py:26
  42.8 2.1 collective-permute-start.3
  49.1 2.8 %collective-permute-start.7 = (bf16[2,128,1280]{2,1,0:T(8,128)(2,1)}, bf16[2,128,1280]{2,1,0:T(8,128)(2,1)}, u32[]{:S(2)}, u32[]{:S(2)}) collective-permute-start(bf16[2,128,1280]{2,1,0:T(8,128)(2,1)} %pad_maximum_fusion.2), channel_id=1, source_target_pairs={{2,0},{4,2},{6,4},{8,6},{10,8},{12,10},{14,12},{16,14},{18,16},{20... | collective-permute-start | bytes 1966088 | tf_op jit(solution)/shard_map/ppermute | solution.py:26
  51.9 2.0 collective-permute-start.6
  54.9 1.5 collective-permute-start.10
  56.5 3.5 %collective-permute-start.8 = (bf16[2,128,1280]{2,1,0:T(8,128)(2,1)}, bf16[2,128,1280]{2,1,0:T(8,128)(2,1)}, u32[]{:S(2)}, u32[]{:S(2)}) collective-permute-start(bf16[2,128,1280]{2,1,0:T(8,128)(2,1)} %pad_maximum_fusion.2), channel_id=1, source_target_pairs={{0,4},{4,8},{8,12},{12,16},{16,20},{20,24},{24,28},{28,32},{32,36}... | collective-permute-start | bytes 1966088 | tf_op jit(solution)/shard_map/ppermute | solution.py:31
  60.0 11.2 %shard_map.110 = (f32[128,1280]{1,0:T(8,128)}, f32[128,1280]{1,0:T(8,128)}, f32[128,1280]{1,0:T(8,128)}, bf16[2,128,1280]{2,1,0:T(8,128)(2,1)}, bf16[2,128,1280]...) custom-call(s32[1]{0:T(128)} %bitcast.1.odd_ref, f32[1,640]{1,0:T(1,128)} %bitcast.156, ...), custom_call_target="tpu_custom_call" | custom-call | flops 1258291200 | bytes 7208960 | tf_op jit(solution)/shard_map/pallas_call | solution.py:154
  71.3 1.4 collective-permute-start.11
  72.7 12.5 %collective-permute-done.6.refs_0_ = bf16[2,128,1280]{2,1,0:T(8,128)(2,1)} collective-permute-done((bf16[2,128,1280]{2,1,0:T(8,128)(2,1)}, bf16[2,128,1280]{2,1,0:T(8,128)(2,1)}, u32[]{:S(2)}, u32[]{:S(2)}) %collective-permute-start.6) | collective-permute-done | bytes 655392 | tf_op jit(solution)/shard_map/ppermute | solution.py:26
  85.2 2.1 collective-permute-start.9
  87.4 2.0 broadcast_select_fusion.1
  89.4 1.9 collective-permute-start.12
  92.1 1.9 collective-permute-start.16
  94.1 11.3 %shard_map.111 = (f32[128,1280]{1,0:T(8,128)}, f32[128,1280]{1,0:T(8,128)}, f32[128,1280]{1,0:T(8,128)}, bf16[2,128,1280]{2,1,0:T(8,128)(2,1)}, bf16[2,128,1280]...) custom-call(s32[1]{0:T(128)} %bitcast.1.odd_ref, f32[1,640]{1,0:T(1,128)} %bitcast.157, ...), custom_call_target="tpu_custom_call" | custom-call | flops 1258291200 | bytes 7208960 | tf_op jit(solution)/shard_map/pallas_call | solution.py:154
  106.6 3.1 %collective-permute-start.17 = (bf16[2,128,1280]{2,1,0:T(8,128)(2,1)S(1)}, bf16[2,128,1280]{2,1,0:T(8,128)(2,1)S(1)}, u32[]{:S(2)}, u32[]{:S(2)}) collective-permute-start(bf16[2,128,1280]{2,1,0:T(8,128)(2,1)S(1)} %broadcast_select_fusion), channel_id=1, source_target_pairs={{0,2},{2,0},{4,6},{6,4},{8,10},{10,8},{12,14},{14,12},{16,18},{18,... | collective-permute-start | bytes 1966088 | tf_op jit(solution)/shard_map/ppermute | solution.py:31
  109.8 1.5 fusion.33
  111.4 2.1 collective-permute-start.13
  113.4 8.8 %collective-permute-start.14 = (bf16[2,128,1280]{2,1,0:T(8,128)(2,1)S(1)}, bf16[2,128,1280]{2,1,0:T(8,128)(2,1)S(1)}, u32[]{:S(2)}, u32[]{:S(2)}) collective-permute-start(bf16[2,128,1280]{2,1,0:T(8,128)(2,1)S(1)} %get-tuple-element.44), channel_id=1, source_target_pairs={{2,0},{4,2},{6,4},{8,6},{10,8},{12,10},{14,12},{16,14},{18,16},{20... | collective-permute-start | bytes 1966088 | tf_op jit(solution)/shard_map/ppermute | solution.py:26
  124.1 3.6 %collective-permute-start.21 = (bf16[2,128,1280]{2,1,0:T(8,128)(2,1)S(1)}, bf16[2,128,1280]{2,1,0:T(8,128)(2,1)S(1)}, u32[]{:S(2)}, u32[]{:S(2)}) collective-permute-start(bf16[2,128,1280]{2,1,0:T(8,128)(2,1)S(1)} %copy-done.13), channel_id=1, source_target_pairs={{4,0},{8,4},{12,8},{16,12},{20,16},{24,20},{28,24},{32,28},{36,32}... | collective-permute-start | bytes 1966088 | tf_op jit(solution)/shard_map/ppermute | solution.py:31
  127.8 1.9 collective-permute-start.18
  129.7 20.0 %collective-permute-done.13 = bf16[2,128,1280]{2,1,0:T(8,128)(2,1)S(1)} collective-permute-done((bf16[2,128,1280]{2,1,0:T(8,128)(2,1)S(1)}, bf16[2,128,1280]{2,1,0:T(8,128)(2,1)S(1)}, u32[]{:S(2)}, u32[]{:S(2)}) %collective-permute-start.13) | collective-permute-done | bytes 655392 | tf_op jit(solution)/shard_map/ppermute | solution.py:26
  149.7 1.9 collective-permute-start.19
  152.1 1.6 fusion.36
  153.8 10.0 %collective-permute-done.18 = bf16[2,128,1280]{2,1,0:T(8,128)(2,1)S(1)} collective-permute-done((bf16[2,128,1280]{2,1,0:T(8,128)(2,1)S(1)}, bf16[2,128,1280]{2,1,0:T(8,128)(2,1)S(1)}, u32[]{:S(2)}, u32[]{:S(2)}) %collective-permute-start.18) | collective-permute-done | bytes 655392 | tf_op jit(solution)/shard_map/ppermute | solution.py:26
  163.8 5.5 %collective-permute-done.19 = bf16[2,128,1280]{2,1,0:T(8,128)(2,1)S(1)} collective-permute-done((bf16[2,128,1280]{2,1,0:T(8,128)(2,1)S(1)}, bf16[2,128,1280]{2,1,0:T(8,128)(2,1)S(1)}, u32[]{:S(2)}, u32[]{:S(2)}) %collective-permute-start.19) | collective-permute-done | bytes 655392 | tf_op jit(solution)/shard_map/ppermute | solution.py:26
  170.8 1.9 collective-permute-start.22
  172.8 3.7 %collective-permute-done.22 = f32[5120]{0:T(1024)S(1)} collective-permute-done((f32[5120]{0:T(1024)S(1)}, f32[5120]{0:T(1024)S(1)}, u32[]{:S(2)}, u32[]{:S(2)}) %collective-permute-start.22) | collective-permute-done | bytes 20512 | tf_op jit(solution)/shard_map/ppermute | solution.py:68
  176.5 1.9 collective-permute-start.23
  179.6 1.9 collective-permute-start.24
  181.5 3.7 %collective-permute-done.24 = f32[5120]{0:T(1024)S(1)} collective-permute-done((f32[5120]{0:T(1024)S(1)}, f32[5120]{0:T(1024)S(1)}, u32[]{:S(2)}, u32[]{:S(2)}) %collective-permute-start.24) | collective-permute-done | bytes 20512 | tf_op jit(solution)/shard_map/ppermute | solution.py:68
  185.3 1.9 collective-permute-start.25
  187.2 5.3 %collective-permute-done.25 = f32[5120]{0:T(1024)S(1)} collective-permute-done((f32[5120]{0:T(1024)S(1)}, f32[5120]{0:T(1024)S(1)}, u32[]{:S(2)}, u32[]{:S(2)}) %collective-permute-start.25) | collective-permute-done | bytes 20512 | tf_op jit(solution)/shard_map/ppermute | solution.py:68
  192.4 1.9 collective-permute-start.26
  194.4 3.7 %collective-permute-done.26 = f32[5120]{0:T(1024)S(1)} collective-permute-done((f32[5120]{0:T(1024)S(1)}, f32[5120]{0:T(1024)S(1)}, u32[]{:S(2)}, u32[]{:S(2)}) %collective-permute-start.26) | collective-permute-done | bytes 20512 | tf_op jit(solution)/shard_map/ppermute | solution.py:68
  198.1 1.9 collective-permute-start.27
  201.2 3.4 %collective-permute-done.27 = f32[5120]{0:T(1024)S(1)} collective-permute-done((f32[5120]{0:T(1024)S(1)}, f32[5120]{0:T(1024)S(1)}, u32[]{:S(2)}, u32[]{:S(2)}) %collective-permute-start.27) | collective-permute-done | bytes 20512 | tf_op jit(solution)/shard_map/ppermute | solution.py:68
  204.7 1.9 collective-permute-start.28
  206.6 7.6 %collective-permute-done.28 = f32[5120]{0:T(1024)S(1)} collective-permute-done((f32[5120]{0:T(1024)S(1)}, f32[5120]{0:T(1024)S(1)}, u32[]{:S(2)}, u32[]{:S(2)}) %collective-permute-start.28) | collective-permute-done | bytes 20512 | tf_op jit(solution)/shard_map/ppermute | solution.py:68
  214.2 1.9 collective-permute-start.29
  217.4 3.4 %collective-permute-done.29 = f32[5120]{0:T(1024)S(1)} collective-permute-done((f32[5120]{0:T(1024)S(1)}, f32[5120]{0:T(1024)S(1)}, u32[]{:S(2)}, u32[]{:S(2)}) %collective-permute-start.29) | collective-permute-done | bytes 20512 | tf_op jit(solution)/shard_map/ppermute | solution.py:68
  220.8 3.0 %collective-permute-start.30 = (f32[5120]{0:T(1024)S(1)}, f32[5120]{0:T(1024)S(1)}, u32[]{:S(2)}, u32[]{:S(2)}) collective-permute-start(f32[5120]{0:T(1024)S(1)} %add.139), channel_id=1, source_target_pairs={{0,256},{2,258},{4,260},{6,262},{8,264},{10,266},{12,268},{14,270}... | collective-permute-start | bytes 61448 | tf_op jit(solution)/shard_map/ppermute | solution.py:68
  224.7 5.7 %collective-permute-done.30 = f32[5120]{0:T(1024)S(1)} collective-permute-done((f32[5120]{0:T(1024)S(1)}, f32[5120]{0:T(1024)S(1)}, u32[]{:S(2)}, u32[]{:S(2)}) %collective-permute-start.30) | collective-permute-done | bytes 20512 | tf_op jit(solution)/shard_map/ppermute | solution.py:68
  (99 shorter events, 18.0 us)
Async XLA Ops:
  4.2 18.7 %copy-start.21 = (s32[1,4]{1,0:T(1,128)S(1)}, s32[1,4]{1,0:T(1,128)}, u32[]{:S(2)}) copy-start(s32[1,4]{1,0:T(1,128)} %param.13) | copy-start | bytes 52
  4.2 42.7 %copy-start.1 = (bf16[1,128,2560]{2,1,0:T(8,128)(2,1)S(1)}, bf16[1,128,2560]{2,1,0:T(8,128)(2,1)}, u32[]{:S(2)}) copy-start(bf16[1,128,2560]{2,1,0:T(8,128)(2,1)} %param.7) | copy-start | bytes 1966084
  5.1 48.8 %copy-start.19 = (f32[2560]{0:T(1024)S(1)}, f32[2560]{0:T(1024)}, u32[]{:S(2)}) copy-start(f32[2560]{0:T(1024)} %param.11) | copy-start | bytes 30724
  5.1 37.7 %collective-permute-start = (bf16[2,128,1280]{2,1,0:T(8,128)(2,1)}, bf16[2,128,1280]{2,1,0:T(8,128)(2,1)S(1)}, u32[]{:S(2)}, u32[]{:S(2)}) collective-permute-start(bf16[2,128,1280]{2,1,0:T(8,128)(2,1)} %pad_maximum_fusion.1), channel_id=1, source_target_pairs={{0,2},{2,4},{4,6},{6,8},{8,10},{10,12},{12,14},{14,16},{16,18},{18... | collective-permute-start | bytes 1966088 | tf_op jit(solution)/shard_map/ppermute | solution.py:26
  7.1 37.8 %collective-permute-start.1 = (bf16[2,128,1280]{2,1,0:T(8,128)(2,1)}, bf16[2,128,1280]{2,1,0:T(8,128)(2,1)S(1)}, u32[]{:S(2)}, u32[]{:S(2)}) collective-permute-start(bf16[2,128,1280]{2,1,0:T(8,128)(2,1)} %pad_maximum_fusion.1), channel_id=1, source_target_pairs={{2,0},{4,2},{6,4},{8,6},{10,8},{12,10},{14,12},{16,14},{18,16},{20... | collective-permute-start | bytes 1966088 | tf_op jit(solution)/shard_map/ppermute | solution.py:26
  19.5 28.5 %collective-permute-start.2 = (bf16[2,128,1280]{2,1,0:T(8,128)(2,1)}, bf16[2,128,1280]{2,1,0:T(8,128)(2,1)S(1)}, u32[]{:S(2)}, u32[]{:S(2)}) collective-permute-start(bf16[2,128,1280]{2,1,0:T(8,128)(2,1)} %pad_maximum_fusion.1), channel_id=1, source_target_pairs={{0,4},{4,8},{8,12},{12,16},{16,20},{20,24},{24,28},{28,32},{32,36}... | collective-permute-start | bytes 1966088 | tf_op jit(solution)/shard_map/ppermute | solution.py:31
  21.4 26.6 %collective-permute-start.4 = (bf16[2,128,1280]{2,1,0:T(8,128)(2,1)}, bf16[2,128,1280]{2,1,0:T(8,128)(2,1)}, u32[]{:S(2)}, u32[]{:S(2)}) collective-permute-start(bf16[2,128,1280]{2,1,0:T(8,128)(2,1)} %pad_maximum_fusion.1), channel_id=1, source_target_pairs={{6,2},{10,6},{14,10},{18,14},{22,18},{26,22},{30,26},{34,30},{38,3... | collective-permute-start | bytes 1966088 | tf_op jit(solution)/shard_map/ppermute | solution.py:31
  42.8 12.1 %copy-start.10 = (bf16[2,128,1280]{2,1,0:T(8,128)(2,1)}, bf16[2,128,1280]{2,1,0:T(8,128)(2,1)S(1)}, u32[]{:S(2)}) copy-start(bf16[2,128,1280]{2,1,0:T(8,128)(2,1)S(1)} %collective-permute-done.refs_0_) | copy-start | bytes 1966084
  42.8 5.2 %collective-permute-start.3 = (bf16[2,128,1280]{2,1,0:T(8,128)(2,1)S(1)}, bf16[2,128,1280]{2,1,0:T(8,128)(2,1)}, u32[]{:S(2)}, u32[]{:S(2)}) collective-permute-start(bf16[2,128,1280]{2,1,0:T(8,128)(2,1)S(1)} %collective-permute-done.refs_0_), channel_id=1, source_target_pairs={{0,2},{4,6},{8,10},{12,14},{16,18},{20,22},{24,26},{28,30},{32,34}... | collective-permute-start | bytes 1966088 | tf_op jit(solution)/shard_map/ppermute | solution.py:31
  44.9 10.0 %copy-start.11 = (bf16[2,128,1280]{2,1,0:T(8,128)(2,1)}, bf16[2,128,1280]{2,1,0:T(8,128)(2,1)S(1)}, u32[]{:S(2)}) copy-start(bf16[2,128,1280]{2,1,0:T(8,128)(2,1)S(1)} %collective-permute-done.1.refs_1_) | copy-start | bytes 1966084
  44.9 4.1 %collective-permute-start.5 = (bf16[2,128,1280]{2,1,0:T(8,128)(2,1)S(1)}, bf16[2,128,1280]{2,1,0:T(8,128)(2,1)}, u32[]{:S(2)}, u32[]{:S(2)}) collective-permute-start(bf16[2,128,1280]{2,1,0:T(8,128)(2,1)S(1)} %collective-permute-done.1.refs_1_), channel_id=1, source_target_pairs={{2,0},{6,4},{10,8},{14,12},{18,16},{22,20},{26,24},{30,28},{34,32}... | collective-permute-start | bytes 1966088 | tf_op jit(solution)/shard_map/ppermute | solution.py:31
  48.0 12.0 %copy-start.12 = (bf16[2,128,1280]{2,1,0:T(8,128)(2,1)}, bf16[2,128,1280]{2,1,0:T(8,128)(2,1)S(1)}, u32[]{:S(2)}) copy-start(bf16[2,128,1280]{2,1,0:T(8,128)(2,1)S(1)} %collective-permute-done.2.refs_2_) | copy-start | bytes 1966084
  49.1 22.2 %collective-permute-start.7 = (bf16[2,128,1280]{2,1,0:T(8,128)(2,1)}, bf16[2,128,1280]{2,1,0:T(8,128)(2,1)}, u32[]{:S(2)}, u32[]{:S(2)}) collective-permute-start(bf16[2,128,1280]{2,1,0:T(8,128)(2,1)} %pad_maximum_fusion.2), channel_id=1, source_target_pairs={{2,0},{4,2},{6,4},{8,6},{10,8},{12,10},{14,12},{16,14},{18,16},{20... | collective-permute-start | bytes 1966088 | tf_op jit(solution)/shard_map/ppermute | solution.py:26
  51.9 33.4 %collective-permute-start.6 = (bf16[2,128,1280]{2,1,0:T(8,128)(2,1)}, bf16[2,128,1280]{2,1,0:T(8,128)(2,1)}, u32[]{:S(2)}, u32[]{:S(2)}) collective-permute-start(bf16[2,128,1280]{2,1,0:T(8,128)(2,1)} %pad_maximum_fusion.2), channel_id=1, source_target_pairs={{0,2},{2,4},{4,6},{6,8},{8,10},{10,12},{12,14},{14,16},{16,18},{18... | collective-permute-start | bytes 1966088 | tf_op jit(solution)/shard_map/ppermute | solution.py:26
  54.9 36.4 %collective-permute-start.10 = (bf16[2,128,1280]{2,1,0:T(8,128)(2,1)}, bf16[2,128,1280]{2,1,0:T(8,128)(2,1)}, u32[]{:S(2)}, u32[]{:S(2)}) collective-permute-start(bf16[2,128,1280]{2,1,0:T(8,128)(2,1)} %pad_maximum_fusion.2), channel_id=1, source_target_pairs={{6,2},{10,6},{14,10},{18,14},{22,18},{26,22},{30,26},{34,30},{38,3... | collective-permute-start | bytes 1966088 | tf_op jit(solution)/shard_map/ppermute | solution.py:31
  56.5 35.6 %collective-permute-start.8 = (bf16[2,128,1280]{2,1,0:T(8,128)(2,1)}, bf16[2,128,1280]{2,1,0:T(8,128)(2,1)}, u32[]{:S(2)}, u32[]{:S(2)}) collective-permute-start(bf16[2,128,1280]{2,1,0:T(8,128)(2,1)} %pad_maximum_fusion.2), channel_id=1, source_target_pairs={{0,4},{4,8},{8,12},{12,16},{16,20},{20,24},{24,28},{28,32},{32,36}... | collective-permute-start | bytes 1966088 | tf_op jit(solution)/shard_map/ppermute | solution.py:31
  71.3 20.0 %copy-start.4 = (f32[128,1280]{1,0:T(8,128)S(1)}, f32[128,1280]{1,0:T(8,128)}, u32[]{:S(2)}) copy-start(f32[128,1280]{1,0:T(8,128)} %get-tuple-element.20) | copy-start | bytes 1966084
  71.3 22.8 %collective-permute-start.11 = (bf16[2,128,1280]{2,1,0:T(8,128)(2,1)}, bf16[2,128,1280]{2,1,0:T(8,128)(2,1)}, u32[]{:S(2)}, u32[]{:S(2)}) collective-permute-start(bf16[2,128,1280]{2,1,0:T(8,128)(2,1)} %collective-permute-done.7.refs_1_), channel_id=1, source_target_pairs={{2,0},{6,4},{10,8},{14,12},{18,16},{22,20},{26,24},{30,28},{34,32}... | collective-permute-start | bytes 1966088 | tf_op jit(solution)/shard_map/ppermute | solution.py:31
  85.2 8.8 %collective-permute-start.9 = (bf16[2,128,1280]{2,1,0:T(8,128)(2,1)}, bf16[2,128,1280]{2,1,0:T(8,128)(2,1)}, u32[]{:S(2)}, u32[]{:S(2)}) collective-permute-start(bf16[2,128,1280]{2,1,0:T(8,128)(2,1)} %collective-permute-done.6.refs_0_), channel_id=1, source_target_pairs={{0,2},{4,6},{8,10},{12,14},{16,18},{20,22},{24,26},{28,30},{32,34}... | collective-permute-start | bytes 1966088 | tf_op jit(solution)/shard_map/ppermute | solution.py:31
  89.4 20.4 %collective-permute-start.12 = (bf16[2,128,1280]{2,1,0:T(8,128)(2,1)}, bf16[2,128,1280]{2,1,0:T(8,128)(2,1)}, u32[]{:S(2)}, u32[]{:S(2)}) collective-permute-start(bf16[2,128,1280]{2,1,0:T(8,128)(2,1)} %broadcast_select_fusion.1), channel_id=1, source_target_pairs={{0,2},{2,0},{4,6},{6,4},{8,10},{10,8},{12,14},{14,12},{16,18},{18,... | collective-permute-start | bytes 1966088 | tf_op jit(solution)/shard_map/ppermute | solution.py:31
  91.4 32.0 %collective-permute-start.15 = (bf16[2,128,1280]{2,1,0:T(8,128)(2,1)}, bf16[2,128,1280]{2,1,0:T(8,128)(2,1)S(1)}, u32[]{:S(2)}, u32[]{:S(2)}) collective-permute-start(bf16[2,128,1280]{2,1,0:T(8,128)(2,1)} %get-tuple-element.26), channel_id=1, source_target_pairs={{2,6},{6,10},{10,14},{14,18},{18,22},{22,26},{26,30},{30,34},{34,3... | collective-permute-start | bytes 1966088 | tf_op jit(solution)/shard_map/ppermute | solution.py:31
  92.1 35.7 %collective-permute-start.16 = (bf16[2,128,1280]{2,1,0:T(8,128)(2,1)}, bf16[2,128,1280]{2,1,0:T(8,128)(2,1)}, u32[]{:S(2)}, u32[]{:S(2)}) collective-permute-start(bf16[2,128,1280]{2,1,0:T(8,128)(2,1)} %get-tuple-element.25), channel_id=1, source_target_pairs={{4,0},{8,4},{12,8},{16,12},{20,16},{24,20},{28,24},{32,28},{36,32}... | collective-permute-start | bytes 1966088 | tf_op jit(solution)/shard_map/ppermute | solution.py:31
  105.3 4.5 %copy-start.15 = (bf16[2,128,1280]{2,1,0:T(8,128)(2,1)S(1)}, bf16[2,128,1280]{2,1,0:T(8,128)(2,1)}, u32[]{:S(2)}) copy-start(bf16[2,128,1280]{2,1,0:T(8,128)(2,1)} %get-tuple-element.27) | copy-start | bytes 1966084
  105.3 4.5 %copy-start.16 = (bf16[2,128,1280]{2,1,0:T(8,128)(2,1)S(1)}, bf16[2,128,1280]{2,1,0:T(8,128)(2,1)}, u32[]{:S(2)}) copy-start(bf16[2,128,1280]{2,1,0:T(8,128)(2,1)} %get-tuple-element.24) | copy-start | bytes 1966084
  106.6 15.7 %collective-permute-start.17 = (bf16[2,128,1280]{2,1,0:T(8,128)(2,1)S(1)}, bf16[2,128,1280]{2,1,0:T(8,128)(2,1)S(1)}, u32[]{:S(2)}, u32[]{:S(2)}) collective-permute-start(bf16[2,128,1280]{2,1,0:T(8,128)(2,1)S(1)} %broadcast_select_fusion), channel_id=1, source_target_pairs={{0,2},{2,0},{4,6},{6,4},{8,10},{10,8},{12,14},{14,12},{16,18},{18,... | collective-permute-start | bytes 1966088 | tf_op jit(solution)/shard_map/ppermute | solution.py:31
  109.8 12.4 %copy-start.5 = (f32[128,1280]{1,0:T(8,128)S(1)}, f32[128,1280]{1,0:T(8,128)}, u32[]{:S(2)}) copy-start(f32[128,1280]{1,0:T(8,128)} %get-tuple-element.22) | copy-start | bytes 1966084
  109.8 13.2 %copy-start.18 = (bf16[2,128,1280]{2,1,0:T(8,128)(2,1)S(1)}, bf16[2,128,1280]{2,1,0:T(8,128)(2,1)}, u32[]{:S(2)}) copy-start(bf16[2,128,1280]{2,1,0:T(8,128)(2,1)} %get-tuple-element.29) | copy-start | bytes 1966084
  111.4 10.9 %copy-start.14 = (bf16[2,128,1280]{2,1,0:T(8,128)(2,1)S(1)}, bf16[2,128,1280]{2,1,0:T(8,128)(2,1)}, u32[]{:S(2)}) copy-start(bf16[2,128,1280]{2,1,0:T(8,128)(2,1)} %get-tuple-element.31) | copy-start | bytes 1966084
  111.4 11.7 %copy-start.17 = (bf16[2,128,1280]{2,1,0:T(8,128)(2,1)S(1)}, bf16[2,128,1280]{2,1,0:T(8,128)(2,1)}, u32[]{:S(2)}) copy-start(bf16[2,128,1280]{2,1,0:T(8,128)(2,1)} %get-tuple-element.32) | copy-start | bytes 1966084
  111.4 38.4 %collective-permute-start.13 = (bf16[2,128,1280]{2,1,0:T(8,128)(2,1)S(1)}, bf16[2,128,1280]{2,1,0:T(8,128)(2,1)S(1)}, u32[]{:S(2)}, u32[]{:S(2)}) collective-permute-start(bf16[2,128,1280]{2,1,0:T(8,128)(2,1)S(1)} %get-tuple-element.43), channel_id=1, source_target_pairs={{0,2},{2,4},{4,6},{6,8},{8,10},{10,12},{12,14},{14,16},{16,18},{18... | collective-permute-start | bytes 1966088 | tf_op jit(solution)/shard_map/ppermute | solution.py:26
  113.4 38.7 %collective-permute-start.14 = (bf16[2,128,1280]{2,1,0:T(8,128)(2,1)S(1)}, bf16[2,128,1280]{2,1,0:T(8,128)(2,1)S(1)}, u32[]{:S(2)}, u32[]{:S(2)}) collective-permute-start(bf16[2,128,1280]{2,1,0:T(8,128)(2,1)S(1)} %get-tuple-element.44), channel_id=1, source_target_pairs={{2,0},{4,2},{6,4},{8,6},{10,8},{12,10},{14,12},{16,14},{18,16},{20... | collective-permute-start | bytes 1966088 | tf_op jit(solution)/shard_map/ppermute | solution.py:26
  122.3 31.4 %collective-permute-start.20 = (bf16[2,128,1280]{2,1,0:T(8,128)(2,1)S(1)}, bf16[2,128,1280]{2,1,0:T(8,128)(2,1)S(1)}, u32[]{:S(2)}, u32[]{:S(2)}) collective-permute-start(bf16[2,128,1280]{2,1,0:T(8,128)(2,1)S(1)} %copy-done.14), channel_id=1, source_target_pairs={{2,6},{6,10},{10,14},{14,18},{18,22},{22,26},{26,30},{30,34},{34,3... | collective-permute-start | bytes 1966088 | tf_op jit(solution)/shard_map/ppermute | solution.py:31
  123.4 28.7 %copy-start.6 = (f32[128,1280]{1,0:T(8,128)S(1)}, f32[128,1280]{1,0:T(8,128)}, u32[]{:S(2)}) copy-start(f32[128,1280]{1,0:T(8,128)} %get-tuple-element.23) | copy-start | bytes 1966084
  123.4 28.7 %copy-start.7 = (f32[128,1280]{1,0:T(8,128)S(1)}, f32[128,1280]{1,0:T(8,128)}, u32[]{:S(2)}) copy-start(f32[128,1280]{1,0:T(8,128)} %get-tuple-element.33) | copy-start | bytes 1966084
  124.1 29.6 %collective-permute-start.21 = (bf16[2,128,1280]{2,1,0:T(8,128)(2,1)S(1)}, bf16[2,128,1280]{2,1,0:T(8,128)(2,1)S(1)}, u32[]{:S(2)}, u32[]{:S(2)}) collective-permute-start(bf16[2,128,1280]{2,1,0:T(8,128)(2,1)S(1)} %copy-done.13), channel_id=1, source_target_pairs={{4,0},{8,4},{12,8},{16,12},{20,16},{24,20},{28,24},{32,28},{36,32}... | collective-permute-start | bytes 1966088 | tf_op jit(solution)/shard_map/ppermute | solution.py:31
  127.8 36.0 %collective-permute-start.18 = (bf16[2,128,1280]{2,1,0:T(8,128)(2,1)S(1)}, bf16[2,128,1280]{2,1,0:T(8,128)(2,1)S(1)}, u32[]{:S(2)}, u32[]{:S(2)}) collective-permute-start(bf16[2,128,1280]{2,1,0:T(8,128)(2,1)S(1)} %get-tuple-element.45), channel_id=1, source_target_pairs={{0,2},{2,4},{4,6},{6,8},{8,10},{10,12},{12,14},{14,16},{16,18},{18... | collective-permute-start | bytes 1966088 | tf_op jit(solution)/shard_map/ppermute | solution.py:26
  149.7 19.5 %collective-permute-start.19 = (bf16[2,128,1280]{2,1,0:T(8,128)(2,1)S(1)}, bf16[2,128,1280]{2,1,0:T(8,128)(2,1)S(1)}, u32[]{:S(2)}, u32[]{:S(2)}) collective-permute-start(bf16[2,128,1280]{2,1,0:T(8,128)(2,1)S(1)} %get-tuple-element.46), channel_id=1, source_target_pairs={{2,0},{4,2},{6,4},{8,6},{10,8},{12,10},{14,12},{16,14},{18,16},{20... | collective-permute-start | bytes 1966088 | tf_op jit(solution)/shard_map/ppermute | solution.py:26
  152.1 17.2 %copy-start.8 = (f32[128,1280]{1,0:T(8,128)S(1)}, f32[128,1280]{1,0:T(8,128)}, u32[]{:S(2)}) copy-start(f32[128,1280]{1,0:T(8,128)} %get-tuple-element.28) | copy-start | bytes 1966084
  152.1 17.1 %copy-start.9 = (f32[128,1280]{1,0:T(8,128)S(1)}, f32[128,1280]{1,0:T(8,128)}, u32[]{:S(2)}) copy-start(f32[128,1280]{1,0:T(8,128)} %get-tuple-element.34) | copy-start | bytes 1966084
  170.8 5.7 %collective-permute-start.22 = (f32[5120]{0:T(1024)S(1)}, f32[5120]{0:T(1024)S(1)}, u32[]{:S(2)}, u32[]{:S(2)}) collective-permute-start(f32[5120]{0:T(1024)S(1)} %pad_maximum_fusion.4), channel_id=1, source_target_pairs={{0,1},{1,0},{2,3},{3,2},{4,5},{5,4},{6,7},{7,6},{8,9},{9,8},{10,11... | collective-permute-start | bytes 61448 | tf_op jit(solution)/shard_map/ppermute | solution.py:68
  176.5 3.1 %collective-permute-start.23 = (f32[5120]{0:T(1024)S(1)}, f32[5120]{0:T(1024)S(1)}, u32[]{:S(2)}, u32[]{:S(2)}) collective-permute-start(f32[5120]{0:T(1024)S(1)} %fusion.39), channel_id=1, source_target_pairs={{0,2},{2,0},{4,6},{6,4},{8,10},{10,8},{12,14},{14,12},{16,18},{18,... | collective-permute-start | bytes 61448 | tf_op jit(solution)/shard_map/ppermute | solution.py:68
  179.6 5.7 %collective-permute-start.24 = (f32[5120]{0:T(1024)S(1)}, f32[5120]{0:T(1024)S(1)}, u32[]{:S(2)}, u32[]{:S(2)}) collective-permute-start(f32[5120]{0:T(1024)S(1)} %add.133), channel_id=1, source_target_pairs={{0,4},{2,6},{4,0},{6,2},{8,12},{10,14},{12,8},{14,10},{16,20},{18,... | collective-permute-start | bytes 61448 | tf_op jit(solution)/shard_map/ppermute | solution.py:68
  185.3 7.2 %collective-permute-start.25 = (f32[5120]{0:T(1024)S(1)}, f32[5120]{0:T(1024)S(1)}, u32[]{:S(2)}, u32[]{:S(2)}) collective-permute-start(f32[5120]{0:T(1024)S(1)} %add.134), channel_id=1, source_target_pairs={{0,8},{2,10},{4,12},{6,14},{8,0},{10,2},{12,4},{14,6},{16,24},{18,... | collective-permute-start | bytes 61448 | tf_op jit(solution)/shard_map/ppermute | solution.py:68
  192.4 5.7 %collective-permute-start.26 = (f32[5120]{0:T(1024)S(1)}, f32[5120]{0:T(1024)S(1)}, u32[]{:S(2)}, u32[]{:S(2)}) collective-permute-start(f32[5120]{0:T(1024)S(1)} %add.135), channel_id=1, source_target_pairs={{0,16},{2,18},{4,20},{6,22},{8,24},{10,26},{12,28},{14,30},{16,0},... | collective-permute-start | bytes 61448 | tf_op jit(solution)/shard_map/ppermute | solution.py:68
  198.1 6.6 %collective-permute-start.27 = (f32[5120]{0:T(1024)S(1)}, f32[5120]{0:T(1024)S(1)}, u32[]{:S(2)}, u32[]{:S(2)}) collective-permute-start(f32[5120]{0:T(1024)S(1)} %add.136), channel_id=1, source_target_pairs={{0,32},{2,34},{4,36},{6,38},{8,40},{10,42},{12,44},{14,46},{16,48}... | collective-permute-start | bytes 61448 | tf_op jit(solution)/shard_map/ppermute | solution.py:68
  204.7 9.6 %collective-permute-start.28 = (f32[5120]{0:T(1024)S(1)}, f32[5120]{0:T(1024)S(1)}, u32[]{:S(2)}, u32[]{:S(2)}) collective-permute-start(f32[5120]{0:T(1024)S(1)} %add.137), channel_id=1, source_target_pairs={{0,64},{2,66},{4,68},{6,70},{8,72},{10,74},{12,76},{14,78},{16,80}... | collective-permute-start | bytes 61448 | tf_op jit(solution)/shard_map/ppermute | solution.py:68
  214.2 6.6 %collective-permute-start.29 = (f32[5120]{0:T(1024)S(1)}, f32[5120]{0:T(1024)S(1)}, u32[]{:S(2)}, u32[]{:S(2)}) collective-permute-start(f32[5120]{0:T(1024)S(1)} %add.138), channel_id=1, source_target_pairs={{0,128},{2,130},{4,132},{6,134},{8,136},{10,138},{12,140},{14,142}... | collective-permute-start | bytes 61448 | tf_op jit(solution)/shard_map/ppermute | solution.py:68
  220.8 9.6 %collective-permute-start.30 = (f32[5120]{0:T(1024)S(1)}, f32[5120]{0:T(1024)S(1)}, u32[]{:S(2)}, u32[]{:S(2)}) collective-permute-start(f32[5120]{0:T(1024)S(1)} %add.139), channel_id=1, source_target_pairs={{0,256},{2,258},{4,260},{6,262},{8,264},{10,266},{12,268},{14,270}... | collective-permute-start | bytes 61448 | tf_op jit(solution)/shard_map/ppermute | solution.py:68
  (5 other events, 6.8 us)

commit v7 on v6

--- a/solution.py
+++ b/solution.py
@@ -10,8 +10,8 @@
 
 HEAD = 128
 LEVELS = 2
-HEADS_PER_STEP = 2
-CHUNKS = 2
+HEADS_PER_STEP = 5
+CHUNKS = 4
 
 
 EPS = 1e-06

time: 232 us -> 299 us (1.29)
  the two profiles are of different devices: /device:TPU:24 before, /device:TPU:32 now
where the time goes in v7:
time: 299 us; the launch traced here: 297 us
  starting transfers between devices  171 us (57%)
  waiting for transfers between devices  65.3 us (22%)
  Pallas kernels  29 us (10%)
  other arithmetic  25.6 us (9%)
  local copies, waits for them, and re-layouts  4.6 us (2%)
    ppermute x16, starting transfers between devices, from_behind(): lax.ppermute(value, axis, [(source, source + steps) for source in range(f...  96.5 us
    ppermute x28, starting transfers between devices, pairs_permute(): lax.ppermute(value, axis, [(i, j) for i, j in pairs if 0 <= j < count])  56.9 us
    ppermute x9, waiting for transfers between devices, all_sum(): lax.ppermute(value, axis, [(i, i ^ bit) for i in range(count)])  38.8 us
    pallas_call x4, Pallas kernels, attention(): pl.pallas_call(attention_kernel, grid_spec=grid_spec, out_shape=[f32] * 3...  29 us
    ppermute x9, starting transfers between devices, all_sum(): lax.ppermute(value, axis, [(i, i ^ bit) for i in range(count)])  17.2 us
    ppermute x16, waiting for transfers between devices, from_behind(): lax.ppermute(value, axis, [(source, source + steps) for source in range(f...  13.8 us
    ppermute x28, waiting for transfers between devices, pairs_permute(): lax.ppermute(value, axis, [(i, j) for i, j in pairs if 0 <= j < count])  12.8 us
    concatenate x5, other arithmetic, body(): jnp.concatenate([p[i] for p in pieces], axis=1)  6.1 us
  transfers between devices with their start and end apart: 53, of which 17 were waited for; matrix products, arithmetic and copies ran while one was open for 7% of the time, Pallas kernels for 10%

profile of v7, /device:TPU:32, one launch (start us, length us, event | category | flops | bytes accessed | tf_op | source)
XLA Modules:
  0.0 297.1 jit_solution(8250633717036031235)
XLA Ops:
  6.9 12.4 %collective-permute-start.1 = (bf16[2,128,640]{2,1,0:T(8,128)(2,1)}, bf16[2,128,640]{2,1,0:T(8,128)(2,1)S(1)}, u32[]{:S(2)}, u32[]{:S(2)}) collective-permute-start(bf16[2,128,640]{2,1,0:T(8,128)(2,1)} %pad_maximum_fusion.2), channel_id=1, source_target_pairs={{2,0},{4,2},{6,4},{8,6},{10,8},{12,10},{14,12},{16,14},{18,16},{20... | collective-permute-start | bytes 983048 | tf_op jit(solution)/shard_map/ppermute | solution.py:26
  19.2 1.9 collective-permute-start.2
  23.2 2.6 collective-permute-done.refs_0_
  27.1 6.2 %collective-permute-done.1.refs_1_ = bf16[2,128,640]{2,1,0:T(8,128)(2,1)S(1)} collective-permute-done((bf16[2,128,640]{2,1,0:T(8,128)(2,1)}, bf16[2,128,640]{2,1,0:T(8,128)(2,1)S(1)}, u32[]{:S(2)}, u32[]{:S(2)}) %collective-permute-start.1) | collective-permute-done | bytes 327712 | tf_op jit(solution)/shard_map/ppermute | solution.py:26
  36.1 2.2 collective-permute-done.2.refs_2_
  39.1 8.6 %collective-permute-start.7 = (bf16[2,128,640]{2,1,0:T(8,128)(2,1)}, bf16[2,128,640]{2,1,0:T(8,128)(2,1)S(1)}, u32[]{:S(2)}, u32[]{:S(2)}) collective-permute-start(bf16[2,128,640]{2,1,0:T(8,128)(2,1)} %pad_maximum_fusion.3), channel_id=1, source_target_pairs={{2,0},{4,2},{6,4},{8,6},{10,8},{12,10},{14,12},{16,14},{18,16},{20... | collective-permute-start | bytes 983048 | tf_op jit(solution)/shard_map/ppermute | solution.py:26
  47.7 1.9 collective-permute-start.6
  49.6 7.2 %shard_map.110 = (f32[128,640]{1,0:T(8,128)}, f32[128,640]{1,0:T(8,128)}, f32[128,640]{1,0:T(8,128)}, bf16[2,128,640]{2,1,0:T(8,128)(2,1)}, bf16[2,128,640]{2,1,...) custom-call(s32[1]{0:T(128)} %bitcast.1.odd_ref, f32[1,640]{1,0:T(1,128)} %bitcast.260, ...), custom_call_target="tpu_custom_call" | custom-call | flops 629145600 | bytes 3604480 | tf_op jit(solution)/shard_map/pallas_call | solution.py:154
  57.9 1.9 collective-permute-start.24
  63.8 10.1 %collective-permute-start.9 = (bf16[2,128,640]{2,1,0:T(8,128)(2,1)S(1)}, bf16[2,128,640]{2,1,0:T(8,128)(2,1)S(1)}, u32[]{:S(2)}, u32[]{:S(2)}) collective-permute-start(bf16[2,128,640]{2,1,0:T(8,128)(2,1)S(1)} %collective-permute-done.6.refs_0_), channel_id=1, source_target_pairs={{0,2},{4,6},{8,10},{12,14},{16,18},{20,22},{24,26},{28,30},{32,34}... | collective-permute-start | bytes 983048 | tf_op jit(solution)/shard_map/ppermute | solution.py:31
  75.4 3.3 %collective-permute-start.28 = (bf16[2,128,640]{2,1,0:T(8,128)(2,1)}, bf16[2,128,640]{2,1,0:T(8,128)(2,1)}, u32[]{:S(2)}, u32[]{:S(2)}) collective-permute-start(bf16[2,128,640]{2,1,0:T(8,128)(2,1)} %get-tuple-element.45), channel_id=1, source_target_pairs={{4,0},{8,4},{12,8},{16,12},{20,16},{24,20},{28,24},{32,28},{36,32}... | collective-permute-start | bytes 983048 | tf_op jit(solution)/shard_map/ppermute | solution.py:31
  79.8 2.3 collective-permute-start.25
  82.1 9.9 %collective-permute-start.26 = (bf16[2,128,640]{2,1,0:T(8,128)(2,1)}, bf16[2,128,640]{2,1,0:T(8,128)(2,1)}, u32[]{:S(2)}, u32[]{:S(2)}) collective-permute-start(bf16[2,128,640]{2,1,0:T(8,128)(2,1)} %get-tuple-element.88), channel_id=1, source_target_pairs={{2,0},{4,2},{6,4},{8,6},{10,8},{12,10},{14,12},{16,14},{18,16},{20... | collective-permute-start | bytes 983048 | tf_op jit(solution)/shard_map/ppermute | solution.py:26
  92.9 7.3 %shard_map.111 = (f32[128,640]{1,0:T(8,128)}, f32[128,640]{1,0:T(8,128)}, f32[128,640]{1,0:T(8,128)}, bf16[2,128,640]{2,1,0:T(8,128)(2,1)}, bf16[2,128,640]{2,1,...) custom-call(s32[1]{0:T(128)} %bitcast.1.odd_ref, f32[1,640]{1,0:T(1,128)} %bitcast.261, ...), custom_call_target="tpu_custom_call" | custom-call | flops 629145600 | bytes 3604480 | tf_op jit(solution)/shard_map/pallas_call | solution.py:154
  101.3 1.9 collective-permute-start.29
  103.2 2.4 collective-permute-start.12
  105.7 9.6 %collective-permute-start.13 = (bf16[2,128,640]{2,1,0:T(8,128)(2,1)}, bf16[2,128,640]{2,1,0:T(8,128)(2,1)S(1)}, u32[]{:S(2)}, u32[]{:S(2)}) collective-permute-start(bf16[2,128,640]{2,1,0:T(8,128)(2,1)} %pad_maximum_fusion.4), channel_id=1, source_target_pairs={{2,0},{4,2},{6,4},{8,6},{10,8},{12,10},{14,12},{16,14},{18,16},{20... | collective-permute-start | bytes 983048 | tf_op jit(solution)/shard_map/ppermute | solution.py:26
  117.0 1.9 collective-permute-start.14
  119.6 3.9 %collective-permute-start.15 = (bf16[2,128,640]{2,1,0:T(8,128)(2,1)S(1)}, bf16[2,128,640]{2,1,0:T(8,128)(2,1)S(1)}, u32[]{:S(2)}, u32[]{:S(2)}) collective-permute-start(bf16[2,128,640]{2,1,0:T(8,128)(2,1)S(1)} %collective-permute-done.12.refs_0_), channel_id=1, source_target_pairs={{0,2},{4,6},{8,10},{12,14},{16,18},{20,22},{24,26},{28,30},{32,34}... | collective-permute-start | bytes 983048 | tf_op jit(solution)/shard_map/ppermute | solution.py:31
  127.4 4.8 %collective-permute-done.14.refs_2_ = bf16[2,128,640]{2,1,0:T(8,128)(2,1)S(1)} collective-permute-done((bf16[2,128,640]{2,1,0:T(8,128)(2,1)S(1)}, bf16[2,128,640]{2,1,0:T(8,128)(2,1)S(1)}, u32[]{:S(2)}, u32[]{:S(2)}) %collective-permute-start.14) | collective-permute-done | bytes 327712 | tf_op jit(solution)/shard_map/ppermute | solution.py:31
  132.3 2.9 collective-permute-start.33
  135.2 1.9 collective-permute-start.30
  137.1 10.0 %collective-permute-start.31 = (bf16[2,128,640]{2,1,0:T(8,128)(2,1)}, bf16[2,128,640]{2,1,0:T(8,128)(2,1)}, u32[]{:S(2)}, u32[]{:S(2)}) collective-permute-start(bf16[2,128,640]{2,1,0:T(8,128)(2,1)} %get-tuple-element.90), channel_id=1, source_target_pairs={{2,0},{4,2},{6,4},{8,6},{10,8},{12,10},{14,12},{16,14},{18,16},{20... | collective-permute-start | bytes 983048 | tf_op jit(solution)/shard_map/ppermute | solution.py:26
  149.1 10.2 %collective-permute-start.19 = (bf16[2,128,640]{2,1,0:T(8,128)(2,1)}, bf16[2,128,640]{2,1,0:T(8,128)(2,1)}, u32[]{:S(2)}, u32[]{:S(2)}) collective-permute-start(bf16[2,128,640]{2,1,0:T(8,128)(2,1)} %pad_maximum_fusion.5), channel_id=1, source_target_pairs={{2,0},{4,2},{6,4},{8,6},{10,8},{12,10},{14,12},{16,14},{18,16},{20... | collective-permute-start | bytes 983048 | tf_op jit(solution)/shard_map/ppermute | solution.py:26
  159.3 7.3 %shard_map.112 = (f32[128,640]{1,0:T(8,128)}, f32[128,640]{1,0:T(8,128)}, f32[128,640]{1,0:T(8,128)}, bf16[2,128,640]{2,1,0:T(8,128)(2,1)}, bf16[2,128,640]{2,1,...) custom-call(s32[1]{0:T(128)} %bitcast.1.odd_ref, f32[1,640]{1,0:T(1,128)} %bitcast.262, ...), custom_call_target="tpu_custom_call" | custom-call | flops 629145600 | bytes 3604480 | tf_op jit(solution)/shard_map/pallas_call | solution.py:154
  168.4 2.0 collective-permute-start.20
  171.1 2.0 collective-permute-start.34
  173.2 2.3 collective-permute-start.21
  176.8 2.3 fusion.47
  179.2 5.6 %collective-permute-done.20.refs_2_ = bf16[2,128,640]{2,1,0:T(8,128)(2,1)S(1)} collective-permute-done((bf16[2,128,640]{2,1,0:T(8,128)(2,1)}, bf16[2,128,640]{2,1,0:T(8,128)(2,1)S(1)}, u32[]{:S(2)}, u32[]{:S(2)}) %collective-permute-start.20) | collective-permute-done | bytes 327712 | tf_op jit(solution)/shard_map/ppermute | solution.py:31
  185.6 4.6 %collective-permute-start.38 = (bf16[2,128,640]{2,1,0:T(8,128)(2,1)}, bf16[2,128,640]{2,1,0:T(8,128)(2,1)}, u32[]{:S(2)}, u32[]{:S(2)}) collective-permute-start(bf16[2,128,640]{2,1,0:T(8,128)(2,1)} %get-tuple-element.55), channel_id=1, source_target_pairs={{4,0},{8,4},{12,8},{16,12},{20,16},{24,20},{28,24},{32,28},{36,32}... | collective-permute-start | bytes 983048 | tf_op jit(solution)/shard_map/ppermute | solution.py:31
  191.0 7.2 %shard_map.113 = (f32[128,640]{1,0:T(8,128)}, f32[128,640]{1,0:T(8,128)}, f32[128,640]{1,0:T(8,128)}, bf16[2,128,640]{2,1,0:T(8,128)(2,1)}, bf16[2,128,640]{2,1,...) custom-call(s32[1]{0:T(128)} %bitcast.1.odd_ref, f32[1,640]{1,0:T(1,128)} %bitcast.263, ...), custom_call_target="tpu_custom_call" | custom-call | flops 629145600 | bytes 3604480 | tf_op jit(solution)/shard_map/pallas_call | solution.py:154
  199.3 2.1 collective-permute-start.39
  203.0 2.5 collective-permute-start.35
  205.5 9.5 %collective-permute-start.36 = (bf16[2,128,640]{2,1,0:T(8,128)(2,1)S(1)}, bf16[2,128,640]{2,1,0:T(8,128)(2,1)S(1)}, u32[]{:S(2)}, u32[]{:S(2)}) collective-permute-start(bf16[2,128,640]{2,1,0:T(8,128)(2,1)S(1)} %get-tuple-element.92), channel_id=1, source_target_pairs={{2,0},{4,2},{6,4},{8,6},{10,8},{12,10},{14,12},{16,14},{18,16},{20... | collective-permute-start | bytes 983048 | tf_op jit(solution)/shard_map/ppermute | solution.py:26
  216.0 2.1 collective-permute-start.43
  218.1 1.9 collective-permute-start.40
  220.5 9.5 %collective-permute-start.41 = (bf16[2,128,640]{2,1,0:T(8,128)(2,1)S(1)}, bf16[2,128,640]{2,1,0:T(8,128)(2,1)S(1)}, u32[]{:S(2)}, u32[]{:S(2)}) collective-permute-start(bf16[2,128,640]{2,1,0:T(8,128)(2,1)S(1)} %get-tuple-element.94), channel_id=1, source_target_pairs={{2,0},{4,2},{6,4},{8,6},{10,8},{12,10},{14,12},{16,14},{18,16},{20... | collective-permute-start | bytes 983048 | tf_op jit(solution)/shard_map/ppermute | solution.py:26
  232.9 3.3 %collective-permute-done.41 = bf16[2,128,640]{2,1,0:T(8,128)(2,1)S(1)} collective-permute-done((bf16[2,128,640]{2,1,0:T(8,128)(2,1)S(1)}, bf16[2,128,640]{2,1,0:T(8,128)(2,1)S(1)}, u32[]{:S(2)}, u32[]{:S(2)}) %collective-permute-start.41) | collective-permute-done | bytes 327712 | tf_op jit(solution)/shard_map/ppermute | solution.py:26
  237.0 1.9 collective-permute-start.44
  238.9 3.7 %collective-permute-done.44 = f32[5120]{0:T(1024)S(1)} collective-permute-done((f32[5120]{0:T(1024)S(1)}, f32[5120]{0:T(1024)S(1)}, u32[]{:S(2)}, u32[]{:S(2)}) %collective-permute-start.44) | collective-permute-done | bytes 20512 | tf_op jit(solution)/shard_map/ppermute | solution.py:68
  247.6 3.7 %collective-permute-done.46 = f32[5120]{0:T(1024)S(1)} collective-permute-done((f32[5120]{0:T(1024)S(1)}, f32[5120]{0:T(1024)S(1)}, u32[]{:S(2)}, u32[]{:S(2)}) %collective-permute-start.46) | collective-permute-done | bytes 20512 | tf_op jit(solution)/shard_map/ppermute | solution.py:68
  253.3 5.3 %collective-permute-done.47 = f32[5120]{0:T(1024)S(1)} collective-permute-done((f32[5120]{0:T(1024)S(1)}, f32[5120]{0:T(1024)S(1)}, u32[]{:S(2)}, u32[]{:S(2)}) %collective-permute-start.47) | collective-permute-done | bytes 20512 | tf_op jit(solution)/shard_map/ppermute | solution.py:68
  260.5 3.7 %collective-permute-done.48 = f32[5120]{0:T(1024)S(1)} collective-permute-done((f32[5120]{0:T(1024)S(1)}, f32[5120]{0:T(1024)S(1)}, u32[]{:S(2)}, u32[]{:S(2)}) %collective-permute-start.48) | collective-permute-done | bytes 20512 | tf_op jit(solution)/shard_map/ppermute | solution.py:68
  267.4 3.4 %collective-permute-done.49 = f32[5120]{0:T(1024)S(1)} collective-permute-done((f32[5120]{0:T(1024)S(1)}, f32[5120]{0:T(1024)S(1)}, u32[]{:S(2)}, u32[]{:S(2)}) %collective-permute-start.49) | collective-permute-done | bytes 20512 | tf_op jit(solution)/shard_map/ppermute | solution.py:68
  272.7 7.6 %collective-permute-done.50 = f32[5120]{0:T(1024)S(1)} collective-permute-done((f32[5120]{0:T(1024)S(1)}, f32[5120]{0:T(1024)S(1)}, u32[]{:S(2)}, u32[]{:S(2)}) %collective-permute-start.50) | collective-permute-done | bytes 20512 | tf_op jit(solution)/shard_map/ppermute | solution.py:68
  283.6 3.4 %collective-permute-done.51 = f32[5120]{0:T(1024)S(1)} collective-permute-done((f32[5120]{0:T(1024)S(1)}, f32[5120]{0:T(1024)S(1)}, u32[]{:S(2)}, u32[]{:S(2)}) %collective-permute-start.51) | collective-permute-done | bytes 20512 | tf_op jit(solution)/shard_map/ppermute | solution.py:68
  289.8 6.8 %collective-permute-done.52 = f32[5120]{0:T(1024)S(1)} collective-permute-done((f32[5120]{0:T(1024)S(1)}, f32[5120]{0:T(1024)S(1)}, u32[]{:S(2)}, u32[]{:S(2)}) %collective-permute-start.52) | collective-permute-done | bytes 20512 | tf_op jit(solution)/shard_map/ppermute | solution.py:68
  (223 shorter events, 63.7 us)
Async XLA Ops:
  5.0 20.9 %collective-permute-start = (bf16[2,128,640]{2,1,0:T(8,128)(2,1)}, bf16[2,128,640]{2,1,0:T(8,128)(2,1)S(1)}, u32[]{:S(2)}, u32[]{:S(2)}) collective-permute-start(bf16[2,128,640]{2,1,0:T(8,128)(2,1)} %pad_maximum_fusion.2), channel_id=1, source_target_pairs={{0,2},{2,4},{4,6},{6,8},{8,10},{10,12},{12,14},{14,16},{16,18},{18... | collective-permute-start | bytes 983048 | tf_op jit(solution)/shard_map/ppermute | solution.py:26
  6.9 26.5 %collective-permute-start.1 = (bf16[2,128,640]{2,1,0:T(8,128)(2,1)}, bf16[2,128,640]{2,1,0:T(8,128)(2,1)S(1)}, u32[]{:S(2)}, u32[]{:S(2)}) collective-permute-start(bf16[2,128,640]{2,1,0:T(8,128)(2,1)} %pad_maximum_fusion.2), channel_id=1, source_target_pairs={{2,0},{4,2},{6,4},{8,6},{10,8},{12,10},{14,12},{16,14},{18,16},{20... | collective-permute-start | bytes 983048 | tf_op jit(solution)/shard_map/ppermute | solution.py:26
  19.2 19.1 %collective-permute-start.2 = (bf16[2,128,640]{2,1,0:T(8,128)(2,1)}, bf16[2,128,640]{2,1,0:T(8,128)(2,1)S(1)}, u32[]{:S(2)}, u32[]{:S(2)}) collective-permute-start(bf16[2,128,640]{2,1,0:T(8,128)(2,1)} %pad_maximum_fusion.2), channel_id=1, source_target_pairs={{0,4},{4,8},{8,12},{12,16},{16,20},{20,24},{24,28},{28,32},{32,36}... | collective-permute-start | bytes 983048 | tf_op jit(solution)/shard_map/ppermute | solution.py:31
  21.2 17.1 %collective-permute-start.4 = (bf16[2,128,640]{2,1,0:T(8,128)(2,1)}, bf16[2,128,640]{2,1,0:T(8,128)(2,1)S(1)}, u32[]{:S(2)}, u32[]{:S(2)}) collective-permute-start(bf16[2,128,640]{2,1,0:T(8,128)(2,1)} %pad_maximum_fusion.2), channel_id=1, source_target_pairs={{6,2},{10,6},{14,10},{18,14},{22,18},{26,22},{30,26},{34,30},{38,3... | collective-permute-start | bytes 983048 | tf_op jit(solution)/shard_map/ppermute | solution.py:31
  25.8 12.5 %collective-permute-start.3 = (bf16[2,128,640]{2,1,0:T(8,128)(2,1)S(1)}, bf16[2,128,640]{2,1,0:T(8,128)(2,1)S(1)}, u32[]{:S(2)}, u32[]{:S(2)}) collective-permute-start(bf16[2,128,640]{2,1,0:T(8,128)(2,1)S(1)} %collective-permute-done.refs_0_), channel_id=1, source_target_pairs={{0,2},{4,6},{8,10},{12,14},{16,18},{20,22},{24,26},{28,30},{32,34}... | collective-permute-start | bytes 983048 | tf_op jit(solution)/shard_map/ppermute | solution.py:31
  39.1 23.4 %collective-permute-start.7 = (bf16[2,128,640]{2,1,0:T(8,128)(2,1)}, bf16[2,128,640]{2,1,0:T(8,128)(2,1)S(1)}, u32[]{:S(2)}, u32[]{:S(2)}) collective-permute-start(bf16[2,128,640]{2,1,0:T(8,128)(2,1)} %pad_maximum_fusion.3), channel_id=1, source_target_pairs={{2,0},{4,2},{6,4},{8,6},{10,8},{12,10},{14,12},{16,14},{18,16},{20... | collective-permute-start | bytes 983048 | tf_op jit(solution)/shard_map/ppermute | solution.py:26
  47.7 16.1 %collective-permute-start.6 = (bf16[2,128,640]{2,1,0:T(8,128)(2,1)}, bf16[2,128,640]{2,1,0:T(8,128)(2,1)S(1)}, u32[]{:S(2)}, u32[]{:S(2)}) collective-permute-start(bf16[2,128,640]{2,1,0:T(8,128)(2,1)} %pad_maximum_fusion.3), channel_id=1, source_target_pairs={{0,2},{2,4},{4,6},{6,8},{8,10},{10,12},{12,14},{14,16},{16,18},{18... | collective-permute-start | bytes 983048 | tf_op jit(solution)/shard_map/ppermute | solution.py:26
  57.9 16.8 %collective-permute-start.24 = (bf16[2,128,640]{2,1,0:T(8,128)(2,1)S(1)}, bf16[2,128,640]{2,1,0:T(8,128)(2,1)S(1)}, u32[]{:S(2)}, u32[]{:S(2)}) collective-permute-start(bf16[2,128,640]{2,1,0:T(8,128)(2,1)S(1)} %broadcast_select_fusion.3), channel_id=1, source_target_pairs={{0,2},{2,0},{4,6},{6,4},{8,10},{10,8},{12,14},{14,12},{16,18},{18,... | collective-permute-start | bytes 983048 | tf_op jit(solution)/shard_map/ppermute | solution.py:31
  59.9 15.5 %collective-permute-start.10 = (bf16[2,128,640]{2,1,0:T(8,128)(2,1)}, bf16[2,128,640]{2,1,0:T(8,128)(2,1)S(1)}, u32[]{:S(2)}, u32[]{:S(2)}) collective-permute-start(bf16[2,128,640]{2,1,0:T(8,128)(2,1)} %pad_maximum_fusion.3), channel_id=1, source_target_pairs={{6,2},{10,6},{14,10},{18,14},{22,18},{26,22},{30,26},{34,30},{38,3... | collective-permute-start | bytes 983048 | tf_op jit(solution)/shard_map/ppermute | solution.py:31
  60.6 19.2 %collective-permute-start.8 = (bf16[2,128,640]{2,1,0:T(8,128)(2,1)}, bf16[2,128,640]{2,1,0:T(8,128)(2,1)S(1)}, u32[]{:S(2)}, u32[]{:S(2)}) collective-permute-start(bf16[2,128,640]{2,1,0:T(8,128)(2,1)} %pad_maximum_fusion.3), channel_id=1, source_target_pairs={{0,4},{4,8},{8,12},{12,16},{16,20},{20,24},{24,28},{28,32},{32,36}... | collective-permute-start | bytes 983048 | tf_op jit(solution)/shard_map/ppermute | solution.py:31
  62.5 19.6 %collective-permute-start.11 = (bf16[2,128,640]{2,1,0:T(8,128)(2,1)S(1)}, bf16[2,128,640]{2,1,0:T(8,128)(2,1)S(1)}, u32[]{:S(2)}, u32[]{:S(2)}) collective-permute-start(bf16[2,128,640]{2,1,0:T(8,128)(2,1)S(1)} %collective-permute-done.7.refs_1_), channel_id=1, source_target_pairs={{2,0},{6,4},{10,8},{14,12},{18,16},{22,20},{26,24},{30,28},{34,32}... | collective-permute-start | bytes 983048 | tf_op jit(solution)/shard_map/ppermute | solution.py:31
  63.8 28.2 %collective-permute-start.9 = (bf16[2,128,640]{2,1,0:T(8,128)(2,1)S(1)}, bf16[2,128,640]{2,1,0:T(8,128)(2,1)S(1)}, u32[]{:S(2)}, u32[]{:S(2)}) collective-permute-start(bf16[2,128,640]{2,1,0:T(8,128)(2,1)S(1)} %collective-permute-done.6.refs_0_), channel_id=1, source_target_pairs={{0,2},{4,6},{8,10},{12,14},{16,18},{20,22},{24,26},{28,30},{32,34}... | collective-permute-start | bytes 983048 | tf_op jit(solution)/shard_map/ppermute | solution.py:31
  74.7 28.5 %collective-permute-start.27 = (bf16[2,128,640]{2,1,0:T(8,128)(2,1)}, bf16[2,128,640]{2,1,0:T(8,128)(2,1)S(1)}, u32[]{:S(2)}, u32[]{:S(2)}) collective-permute-start(bf16[2,128,640]{2,1,0:T(8,128)(2,1)} %get-tuple-element.46), channel_id=1, source_target_pairs={{2,6},{6,10},{10,14},{14,18},{18,22},{22,26},{26,30},{30,34},{34,3... | collective-permute-start | bytes 983048 | tf_op jit(solution)/shard_map/ppermute | solution.py:31
  75.4 30.3 %collective-permute-start.28 = (bf16[2,128,640]{2,1,0:T(8,128)(2,1)}, bf16[2,128,640]{2,1,0:T(8,128)(2,1)}, u32[]{:S(2)}, u32[]{:S(2)}) collective-permute-start(bf16[2,128,640]{2,1,0:T(8,128)(2,1)} %get-tuple-element.45), channel_id=1, source_target_pairs={{4,0},{8,4},{12,8},{16,12},{20,16},{24,20},{28,24},{32,28},{36,32}... | collective-permute-start | bytes 983048 | tf_op jit(solution)/shard_map/ppermute | solution.py:31
  79.8 36.3 %collective-permute-start.25 = (bf16[2,128,640]{2,1,0:T(8,128)(2,1)}, bf16[2,128,640]{2,1,0:T(8,128)(2,1)}, u32[]{:S(2)}, u32[]{:S(2)}) collective-permute-start(bf16[2,128,640]{2,1,0:T(8,128)(2,1)} %get-tuple-element.87), channel_id=1, source_target_pairs={{0,2},{2,4},{4,6},{6,8},{8,10},{10,12},{12,14},{14,16},{16,18},{18... | collective-permute-start | bytes 983048 | tf_op jit(solution)/shard_map/ppermute | solution.py:26
  82.1 34.8 %collective-permute-start.26 = (bf16[2,128,640]{2,1,0:T(8,128)(2,1)}, bf16[2,128,640]{2,1,0:T(8,128)(2,1)}, u32[]{:S(2)}, u32[]{:S(2)}) collective-permute-start(bf16[2,128,640]{2,1,0:T(8,128)(2,1)} %get-tuple-element.88), channel_id=1, source_target_pairs={{2,0},{4,2},{6,4},{8,6},{10,8},{12,10},{14,12},{16,14},{18,16},{20... | collective-permute-start | bytes 983048 | tf_op jit(solution)/shard_map/ppermute | solution.py:26
  101.3 17.6 %collective-permute-start.29 = (bf16[2,128,640]{2,1,0:T(8,128)(2,1)S(1)}, bf16[2,128,640]{2,1,0:T(8,128)(2,1)S(1)}, u32[]{:S(2)}, u32[]{:S(2)}) collective-permute-start(bf16[2,128,640]{2,1,0:T(8,128)(2,1)S(1)} %broadcast_select_fusion.2), channel_id=1, source_target_pairs={{0,2},{2,0},{4,6},{6,4},{8,10},{10,8},{12,14},{14,12},{16,18},{18,... | collective-permute-start | bytes 983048 | tf_op jit(solution)/shard_map/ppermute | solution.py:31
  103.2 16.4 %collective-permute-start.12 = (bf16[2,128,640]{2,1,0:T(8,128)(2,1)}, bf16[2,128,640]{2,1,0:T(8,128)(2,1)S(1)}, u32[]{:S(2)}, u32[]{:S(2)}) collective-permute-start(bf16[2,128,640]{2,1,0:T(8,128)(2,1)} %pad_maximum_fusion.4), channel_id=1, source_target_pairs={{0,2},{2,4},{4,6},{6,8},{8,10},{10,12},{12,14},{14,16},{16,18},{18... | collective-permute-start | bytes 983048 | tf_op jit(solution)/shard_map/ppermute | solution.py:26
  105.7 17.8 %collective-permute-start.13 = (bf16[2,128,640]{2,1,0:T(8,128)(2,1)}, bf16[2,128,640]{2,1,0:T(8,128)(2,1)S(1)}, u32[]{:S(2)}, u32[]{:S(2)}) collective-permute-start(bf16[2,128,640]{2,1,0:T(8,128)(2,1)} %pad_maximum_fusion.4), channel_id=1, source_target_pairs={{2,0},{4,2},{6,4},{8,6},{10,8},{12,10},{14,12},{16,14},{18,16},{20... | collective-permute-start | bytes 983048 | tf_op jit(solution)/shard_map/ppermute | solution.py:26
  116.1 32.9 %collective-permute-start.32 = (bf16[2,128,640]{2,1,0:T(8,128)(2,1)S(1)}, bf16[2,128,640]{2,1,0:T(8,128)(2,1)S(1)}, u32[]{:S(2)}, u32[]{:S(2)}) collective-permute-start(bf16[2,128,640]{2,1,0:T(8,128)(2,1)S(1)} %copy-done.39), channel_id=1, source_target_pairs={{2,6},{6,10},{10,14},{14,18},{18,22},{22,26},{26,30},{30,34},{34,3... | collective-permute-start | bytes 983048 | tf_op jit(solution)/shard_map/ppermute | solution.py:31
  117.0 15.3 %collective-permute-start.14 = (bf16[2,128,640]{2,1,0:T(8,128)(2,1)S(1)}, bf16[2,128,640]{2,1,0:T(8,128)(2,1)S(1)}, u32[]{:S(2)}, u32[]{:S(2)}) collective-permute-start(bf16[2,128,640]{2,1,0:T(8,128)(2,1)S(1)} %copy-done.46), channel_id=1, source_target_pairs={{0,4},{4,8},{8,12},{12,16},{16,20},{20,24},{24,28},{28,32},{32,36}... | collective-permute-start | bytes 983048 | tf_op jit(solution)/shard_map/ppermute | solution.py:31
  118.9 16.2 %collective-permute-start.16 = (bf16[2,128,640]{2,1,0:T(8,128)(2,1)S(1)}, bf16[2,128,640]{2,1,0:T(8,128)(2,1)S(1)}, u32[]{:S(2)}, u32[]{:S(2)}) collective-permute-start(bf16[2,128,640]{2,1,0:T(8,128)(2,1)S(1)} %copy-done.46), channel_id=1, source_target_pairs={{6,2},{10,6},{14,10},{18,14},{22,18},{26,22},{30,26},{34,30},{38,3... | collective-permute-start | bytes 983048 | tf_op jit(solution)/shard_map/ppermute | solution.py:31
  119.6 17.5 %collective-permute-start.15 = (bf16[2,128,640]{2,1,0:T(8,128)(2,1)S(1)}, bf16[2,128,640]{2,1,0:T(8,128)(2,1)S(1)}, u32[]{:S(2)}, u32[]{:S(2)}) collective-permute-start(bf16[2,128,640]{2,1,0:T(8,128)(2,1)S(1)} %collective-permute-done.12.refs_0_), channel_id=1, source_target_pairs={{0,2},{4,6},{8,10},{12,14},{16,18},{20,22},{24,26},{28,30},{32,34}... | collective-permute-start | bytes 983048 | tf_op jit(solution)/shard_map/ppermute | solution.py:31
  123.5 23.6 %collective-permute-start.17 = (bf16[2,128,640]{2,1,0:T(8,128)(2,1)S(1)}, bf16[2,128,640]{2,1,0:T(8,128)(2,1)S(1)}, u32[]{:S(2)}, u32[]{:S(2)}) collective-permute-start(bf16[2,128,640]{2,1,0:T(8,128)(2,1)S(1)} %collective-permute-done.13.refs_1_), channel_id=1, source_target_pairs={{2,0},{6,4},{10,8},{14,12},{18,16},{22,20},{26,24},{30,28},{34,32}... | collective-permute-start | bytes 983048 | tf_op jit(solution)/shard_map/ppermute | solution.py:31
  132.3 36.1 %collective-permute-start.33 = (bf16[2,128,640]{2,1,0:T(8,128)(2,1)}, bf16[2,128,640]{2,1,0:T(8,128)(2,1)}, u32[]{:S(2)}, u32[]{:S(2)}) collective-permute-start(bf16[2,128,640]{2,1,0:T(8,128)(2,1)} %get-tuple-element.50), channel_id=1, source_target_pairs={{4,0},{8,4},{12,8},{16,12},{20,16},{24,20},{28,24},{32,28},{36,32}... | collective-permute-start | bytes 983048 | tf_op jit(solution)/shard_map/ppermute | solution.py:31
  135.2 35.3 %collective-permute-start.30 = (bf16[2,128,640]{2,1,0:T(8,128)(2,1)}, bf16[2,128,640]{2,1,0:T(8,128)(2,1)}, u32[]{:S(2)}, u32[]{:S(2)}) collective-permute-start(bf16[2,128,640]{2,1,0:T(8,128)(2,1)} %get-tuple-element.89), channel_id=1, source_target_pairs={{0,2},{2,4},{4,6},{6,8},{8,10},{10,12},{12,14},{14,16},{16,18},{18... | collective-permute-start | bytes 983048 | tf_op jit(solution)/shard_map/ppermute | solution.py:26
  137.1 34.0 %collective-permute-start.31 = (bf16[2,128,640]{2,1,0:T(8,128)(2,1)}, bf16[2,128,640]{2,1,0:T(8,128)(2,1)}, u32[]{:S(2)}, u32[]{:S(2)}) collective-permute-start(bf16[2,128,640]{2,1,0:T(8,128)(2,1)} %get-tuple-element.90), channel_id=1, source_target_pairs={{2,0},{4,2},{6,4},{8,6},{10,8},{12,10},{14,12},{16,14},{18,16},{20... | collective-permute-start | bytes 983048 | tf_op jit(solution)/shard_map/ppermute | solution.py:26
  147.1 26.0 %collective-permute-start.18 = (bf16[2,128,640]{2,1,0:T(8,128)(2,1)}, bf16[2,128,640]{2,1,0:T(8,128)(2,1)S(1)}, u32[]{:S(2)}, u32[]{:S(2)}) collective-permute-start(bf16[2,128,640]{2,1,0:T(8,128)(2,1)} %pad_maximum_fusion.5), channel_id=1, source_target_pairs={{0,2},{2,4},{4,6},{6,8},{8,10},{10,12},{12,14},{14,16},{16,18},{18... | collective-permute-start | bytes 983048 | tf_op jit(solution)/shard_map/ppermute | solution.py:26
  149.1 26.4 %collective-permute-start.19 = (bf16[2,128,640]{2,1,0:T(8,128)(2,1)}, bf16[2,128,640]{2,1,0:T(8,128)(2,1)}, u32[]{:S(2)}, u32[]{:S(2)}) collective-permute-start(bf16[2,128,640]{2,1,0:T(8,128)(2,1)} %pad_maximum_fusion.5), channel_id=1, source_target_pairs={{2,0},{4,2},{6,4},{8,6},{10,8},{12,10},{14,12},{16,14},{18,16},{20... | collective-permute-start | bytes 983048 | tf_op jit(solution)/shard_map/ppermute | solution.py:26
  168.4 16.5 %collective-permute-start.20 = (bf16[2,128,640]{2,1,0:T(8,128)(2,1)}, bf16[2,128,640]{2,1,0:T(8,128)(2,1)S(1)}, u32[]{:S(2)}, u32[]{:S(2)}) collective-permute-start(bf16[2,128,640]{2,1,0:T(8,128)(2,1)} %pad_maximum_fusion.5), channel_id=1, source_target_pairs={{0,4},{4,8},{8,12},{12,16},{16,20},{20,24},{24,28},{28,32},{32,36}... | collective-permute-start | bytes 983048 | tf_op jit(solution)/shard_map/ppermute | solution.py:31
  170.4 15.1 %collective-permute-start.22 = (bf16[2,128,640]{2,1,0:T(8,128)(2,1)}, bf16[2,128,640]{2,1,0:T(8,128)(2,1)S(1)}, u32[]{:S(2)}, u32[]{:S(2)}) collective-permute-start(bf16[2,128,640]{2,1,0:T(8,128)(2,1)} %pad_maximum_fusion.5), channel_id=1, source_target_pairs={{6,2},{10,6},{14,10},{18,14},{22,18},{26,22},{30,26},{34,30},{38,3... | collective-permute-start | bytes 983048 | tf_op jit(solution)/shard_map/ppermute | solution.py:31
  171.1 30.2 %collective-permute-start.34 = (bf16[2,128,640]{2,1,0:T(8,128)(2,1)}, bf16[2,128,640]{2,1,0:T(8,128)(2,1)}, u32[]{:S(2)}, u32[]{:S(2)}) collective-permute-start(bf16[2,128,640]{2,1,0:T(8,128)(2,1)} %broadcast_select_fusion.1), channel_id=1, source_target_pairs={{0,2},{2,0},{4,6},{6,4},{8,10},{10,8},{12,14},{14,12},{16,18},{18,... | collective-permute-start | bytes 983048 | tf_op jit(solution)/shard_map/ppermute | solution.py:31
  173.2 17.0 %collective-permute-start.21 = (bf16[2,128,640]{2,1,0:T(8,128)(2,1)S(1)}, bf16[2,128,640]{2,1,0:T(8,128)(2,1)S(1)}, u32[]{:S(2)}, u32[]{:S(2)}) collective-permute-start(bf16[2,128,640]{2,1,0:T(8,128)(2,1)S(1)} %collective-permute-done.18.refs_0_), channel_id=1, source_target_pairs={{0,2},{4,6},{8,10},{12,14},{16,18},{20,22},{24,26},{28,30},{32,34}... | collective-permute-start | bytes 983048 | tf_op jit(solution)/shard_map/ppermute | solution.py:31
  175.5 15.4 %collective-permute-start.23 = (bf16[2,128,640]{2,1,0:T(8,128)(2,1)}, bf16[2,128,640]{2,1,0:T(8,128)(2,1)}, u32[]{:S(2)}, u32[]{:S(2)}) collective-permute-start(bf16[2,128,640]{2,1,0:T(8,128)(2,1)} %collective-permute-done.19.refs_1_), channel_id=1, source_target_pairs={{2,0},{6,4},{10,8},{14,12},{18,16},{22,20},{26,24},{30,28},{34,32}... | collective-permute-start | bytes 983048 | tf_op jit(solution)/shard_map/ppermute | solution.py:31
  184.9 31.2 %collective-permute-start.37 = (bf16[2,128,640]{2,1,0:T(8,128)(2,1)}, bf16[2,128,640]{2,1,0:T(8,128)(2,1)S(1)}, u32[]{:S(2)}, u32[]{:S(2)}) collective-permute-start(bf16[2,128,640]{2,1,0:T(8,128)(2,1)} %get-tuple-element.56), channel_id=1, source_target_pairs={{2,6},{6,10},{10,14},{14,18},{18,22},{22,26},{26,30},{30,34},{34,3... | collective-permute-start | bytes 983048 | tf_op jit(solution)/shard_map/ppermute | solution.py:31
  185.6 32.5 %collective-permute-start.38 = (bf16[2,128,640]{2,1,0:T(8,128)(2,1)}, bf16[2,128,640]{2,1,0:T(8,128)(2,1)}, u32[]{:S(2)}, u32[]{:S(2)}) collective-permute-start(bf16[2,128,640]{2,1,0:T(8,128)(2,1)} %get-tuple-element.55), channel_id=1, source_target_pairs={{4,0},{8,4},{12,8},{16,12},{20,16},{24,20},{28,24},{32,28},{36,32}... | collective-permute-start | bytes 983048 | tf_op jit(solution)/shard_map/ppermute | solution.py:31
  199.3 15.8 %collective-permute-start.39 = (bf16[2,128,640]{2,1,0:T(8,128)(2,1)S(1)}, bf16[2,128,640]{2,1,0:T(8,128)(2,1)S(1)}, u32[]{:S(2)}, u32[]{:S(2)}) collective-permute-start(bf16[2,128,640]{2,1,0:T(8,128)(2,1)S(1)} %broadcast_select_fusion), channel_id=1, source_target_pairs={{0,2},{2,0},{4,6},{6,4},{8,10},{10,8},{12,14},{14,12},{16,18},{18,... | collective-permute-start | bytes 983048 | tf_op jit(solution)/shard_map/ppermute | solution.py:31
  203.0 17.5 %collective-permute-start.35 = (bf16[2,128,640]{2,1,0:T(8,128)(2,1)S(1)}, bf16[2,128,640]{2,1,0:T(8,128)(2,1)S(1)}, u32[]{:S(2)}, u32[]{:S(2)}) collective-permute-start(bf16[2,128,640]{2,1,0:T(8,128)(2,1)S(1)} %get-tuple-element.91), channel_id=1, source_target_pairs={{0,2},{2,4},{4,6},{6,8},{8,10},{10,12},{12,14},{14,16},{16,18},{18... | collective-permute-start | bytes 983048 | tf_op jit(solution)/shard_map/ppermute | solution.py:26
  205.5 24.9 %collective-permute-start.36 = (bf16[2,128,640]{2,1,0:T(8,128)(2,1)S(1)}, bf16[2,128,640]{2,1,0:T(8,128)(2,1)S(1)}, u32[]{:S(2)}, u32[]{:S(2)}) collective-permute-start(bf16[2,128,640]{2,1,0:T(8,128)(2,1)S(1)} %get-tuple-element.92), channel_id=1, source_target_pairs={{2,0},{4,2},{6,4},{8,6},{10,8},{12,10},{14,12},{16,14},{18,16},{20... | collective-permute-start | bytes 983048 | tf_op jit(solution)/shard_map/ppermute | solution.py:26
  215.1 16.7 %collective-permute-start.42 = (bf16[2,128,640]{2,1,0:T(8,128)(2,1)S(1)}, bf16[2,128,640]{2,1,0:T(8,128)(2,1)S(1)}, u32[]{:S(2)}, u32[]{:S(2)}) collective-permute-start(bf16[2,128,640]{2,1,0:T(8,128)(2,1)S(1)} %copy-done.45), channel_id=1, source_target_pairs={{2,6},{6,10},{10,14},{14,18},{18,22},{22,26},{26,30},{30,34},{34,3... | collective-permute-start | bytes 983048 | tf_op jit(solution)/shard_map/ppermute | solution.py:31
  216.0 15.7 %collective-permute-start.43 = (bf16[2,128,640]{2,1,0:T(8,128)(2,1)S(1)}, bf16[2,128,640]{2,1,0:T(8,128)(2,1)S(1)}, u32[]{:S(2)}, u32[]{:S(2)}) collective-permute-start(bf16[2,128,640]{2,1,0:T(8,128)(2,1)S(1)} %copy-done.44), channel_id=1, source_target_pairs={{4,0},{8,4},{12,8},{16,12},{20,16},{24,20},{28,24},{32,28},{36,32}... | collective-permute-start | bytes 983048 | tf_op jit(solution)/shard_map/ppermute | solution.py:31
  218.1 14.8 %collective-permute-start.40 = (bf16[2,128,640]{2,1,0:T(8,128)(2,1)S(1)}, bf16[2,128,640]{2,1,0:T(8,128)(2,1)S(1)}, u32[]{:S(2)}, u32[]{:S(2)}) collective-permute-start(bf16[2,128,640]{2,1,0:T(8,128)(2,1)S(1)} %get-tuple-element.93), channel_id=1, source_target_pairs={{0,2},{2,4},{4,6},{6,8},{8,10},{10,12},{12,14},{14,16},{16,18},{18... | collective-permute-start | bytes 983048 | tf_op jit(solution)/shard_map/ppermute | solution.py:26
  220.5 15.8 %collective-permute-start.41 = (bf16[2,128,640]{2,1,0:T(8,128)(2,1)S(1)}, bf16[2,128,640]{2,1,0:T(8,128)(2,1)S(1)}, u32[]{:S(2)}, u32[]{:S(2)}) collective-permute-start(bf16[2,128,640]{2,1,0:T(8,128)(2,1)S(1)} %get-tuple-element.94), channel_id=1, source_target_pairs={{2,0},{4,2},{6,4},{8,6},{10,8},{12,10},{14,12},{16,14},{18,16},{20... | collective-permute-start | bytes 983048 | tf_op jit(solution)/shard_map/ppermute | solution.py:26
  251.4 7.2 %collective-permute-start.47 = (f32[5120]{0:T(1024)S(1)}, f32[5120]{0:T(1024)S(1)}, u32[]{:S(2)}, u32[]{:S(2)}) collective-permute-start(f32[5120]{0:T(1024)S(1)} %add.216), channel_id=1, source_target_pairs={{0,8},{2,10},{4,12},{6,14},{8,0},{10,2},{12,4},{14,6},{16,24},{18,... | collective-permute-start | bytes 61448 | tf_op jit(solution)/shard_map/ppermute | solution.py:68
  264.2 6.6 %collective-permute-start.49 = (f32[5120]{0:T(1024)S(1)}, f32[5120]{0:T(1024)S(1)}, u32[]{:S(2)}, u32[]{:S(2)}) collective-permute-start(f32[5120]{0:T(1024)S(1)} %add.218), channel_id=1, source_target_pairs={{0,32},{2,34},{4,36},{6,38},{8,40},{10,42},{12,44},{14,46},{16,48}... | collective-permute-start | bytes 61448 | tf_op jit(solution)/shard_map/ppermute | solution.py:68
  270.8 9.6 %collective-permute-start.50 = (f32[5120]{0:T(1024)S(1)}, f32[5120]{0:T(1024)S(1)}, u32[]{:S(2)}, u32[]{:S(2)}) collective-permute-start(f32[5120]{0:T(1024)S(1)} %add.219), channel_id=1, source_target_pairs={{0,64},{2,66},{4,68},{6,70},{8,72},{10,74},{12,76},{14,78},{16,80}... | collective-permute-start | bytes 61448 | tf_op jit(solution)/shard_map/ppermute | solution.py:68
  280.4 6.6 %collective-permute-start.51 = (f32[5120]{0:T(1024)S(1)}, f32[5120]{0:T(1024)S(1)}, u32[]{:S(2)}, u32[]{:S(2)}) collective-permute-start(f32[5120]{0:T(1024)S(1)} %add.220), channel_id=1, source_target_pairs={{0,128},{2,130},{4,132},{6,134},{8,136},{10,138},{12,140},{14,142}... | collective-permute-start | bytes 61448 | tf_op jit(solution)/shard_map/ppermute | solution.py:68
  287.0 9.6 %collective-permute-start.52 = (f32[5120]{0:T(1024)S(1)}, f32[5120]{0:T(1024)S(1)}, u32[]{:S(2)}, u32[]{:S(2)}) collective-permute-start(f32[5120]{0:T(1024)S(1)} %add.221), channel_id=1, source_target_pairs={{0,256},{2,258},{4,260},{6,262},{8,264},{10,266},{12,268},{14,270}... | collective-permute-start | bytes 61448 | tf_op jit(solution)/shard_map/ppermute | solution.py:68
  (61 other events, 838.8 us)

commit v8 on v6

--- a/solution.py
+++ b/solution.py
@@ -35,29 +35,26 @@
     count = lax.axis_size(axis)
     behind = from_behind(value, axis, 1)
     ahead = from_behind(value, axis, -1)
-    far_behind = pairs_permute(value, axis, [(i, i + 2) for i in range(0, count, 2)])
-    far_ahead = pairs_permute(value, axis, [(i, i - 2) for i in range(1, count, 2)])
-    relay_behind = pairs_permute(behind, axis, [(i, i + 1) for i in range(0, count, 2)])
-    relay_ahead = pairs_permute(ahead, axis, [(i, i - 1) for i in range(1, count, 2)])
-    return [behind, ahead, far_behind, relay_behind, far_ahead, relay_ahead]
+    two = [(i, i + 2) for i in range(0, count, 2)] + [(i, i - 2) for i in range(1, count, 2)]
+    far2 = pairs_permute(value, axis, two)
+    odd = lax.axis_index(axis) % 2 == 1
+    relay = pairs_permute(jnp.where(odd, ahead, behind), axis, [(i, i ^ 1) for i in range(count)])
+    return [behind, ahead, far2, relay]
 
 
 def return_parts(far, axis):
     count = lax.axis_size(axis)
-    behind, ahead, far_behind, far_ahead = far
+    behind, ahead, for_partner, direct = far
     odd = lax.axis_index(axis) % 2 == 1
-    swapped = pairs_permute(
-        jnp.where(odd, far_behind, far_ahead), axis, [(i, i ^ 1) for i in range(count)]
-    )
+    swapped = pairs_permute(for_partner, axis, [(i, i ^ 1) for i in range(count)])
 
     def joined(own):
         return (own.astype(jnp.float32) + swapped.astype(jnp.float32)).astype(jnp.bfloat16)
 
     to_next = from_behind(jnp.where(odd, joined(ahead), ahead), axis, 1)
     to_previous = from_behind(jnp.where(odd, behind, joined(behind)), axis, -1)
-    two_ahead = pairs_permute(far_ahead, axis, [(i, i + 2) for i in range(1, count, 2)])
-    two_behind = pairs_permute(far_behind, axis, [(i, i - 2) for i in range(0, count, 2)])
-    return [to_next, to_previous, two_ahead, two_behind]
+    two = [(i, i + 2) for i in range(1, count, 2)] + [(i, i - 2) for i in range(0, count, 2)]
+    return [to_next, to_previous, pairs_permute(direct, axis, two)]
 
 
 def all_sum(value, axes):
@@ -87,9 +84,9 @@
 
 
 def attention_kernel(odd_ref, bias_ref, q_ref, k_ref, v_ref, g_ref, *refs):
-    behind, ahead, far_behind, relay_behind, far_ahead, relay_ahead = refs[:6]
-    dq_ref, dk_ref, dv_ref = refs[6:9]
-    far = refs[9:]
+    behind, ahead, far2, relay = refs[:4]
+    dq_ref, dk_ref, dv_ref = refs[4:7]
+    far = refs[7:]
     slots = len(far)
     rows = q_ref.shape[0]
     scale = 1.0 / math.sqrt(HEAD)
@@ -103,8 +100,8 @@
                 [
                     behind[which, :, cols],
                     ahead[which, :, cols],
-                    jnp.where(odd, relay_behind[which, :, cols], far_behind[which, :, cols]),
-                    jnp.where(odd, far_ahead[which, :, cols], relay_ahead[which, :, cols]),
+                    jnp.where(odd, relay[which, :, cols], far2[which, :, cols]),
+                    jnp.where(odd, far2[which, :, cols], relay[which, :, cols]),
                 ],
                 axis=0,
             )
@@ -127,10 +124,20 @@
         grad_v = lax.dot_general(prob, g, TN, preferred_element_type=jnp.float32)
         dk_ref[:, cols] = grad_k[:rows]
         dv_ref[:, cols] = grad_v[:rows]
-        for slot in range(slots):
-            part = slice((slot + 1) * rows, (slot + 2) * rows)
-            far[slot][0, :, cols] = grad_k[part].astype(jnp.bfloat16)
-            far[slot][1, :, cols] = grad_v[part].astype(jnp.bfloat16)
+        parts = [
+            (grad_k[(slot + 1) * rows:(slot + 2) * rows].astype(jnp.bfloat16),
+             grad_v[(slot + 1) * rows:(slot + 2) * rows].astype(jnp.bfloat16))
+            for slot in range(slots)
+        ]
+        arranged = [
+            parts[0],
+            parts[1],
+            tuple(jnp.where(odd, a, b) for a, b in zip(parts[2], parts[3])),
+            tuple(jnp.where(odd, b, a) for a, b in zip(parts[2], parts[3])),
+        ]
+        for slot, (part_k, part_v) in enumerate(arranged):
+            far[slot][0, :, cols] = part_k
+            far[slot][1, :, cols] = part_v
 
 
 def attention(odd, bias, q_norm, k_norm, value_rows, grad_rows, fetched, first=0):

time: 232 us -> 233 us (level)
  the two profiles are of different devices: /device:TPU:24 before, /device:TPU:32 now
where the time goes in v8:
time: 233 us; the launch traced here: 232 us
  waiting for transfers between devices  104 us (45%)
  starting transfers between devices  85.8 us (37%)
  Pallas kernels  22.4 us (10%)
  other arithmetic  14 us (6%)
  local copies, waits for them, and re-layouts  4.16 us (2%)
    ppermute x8, waiting for transfers between devices, from_behind(): lax.ppermute(value, axis, [(source, source + steps) for source in range(f...  62.4 us
    ppermute x8, starting transfers between devices, from_behind(): lax.ppermute(value, axis, [(source, source + steps) for source in range(f...  42.5 us
    ppermute x9, waiting for transfers between devices, all_sum(): lax.ppermute(value, axis, [(i, i ^ bit) for i in range(count)])  38.1 us
    ppermute x8, starting transfers between devices, pairs_permute(): lax.ppermute(value, axis, [(i, j) for i, j in pairs if 0 <= j < count])  25.3 us
    pallas_call x2, Pallas kernels, attention(): pl.pallas_call(attention_kernel, grid_spec=grid_spec, out_shape=[f32] * 3...  22.4 us
    ppermute x9, starting transfers between devices, all_sum(): lax.ppermute(value, axis, [(i, i ^ bit) for i in range(count)])  17.9 us
  transfers between devices with their start and end apart: 25, of which 17 were waited for; matrix products, arithmetic and copies ran while one was open for 5% of the time, Pallas kernels for 10%

profile of v8, /device:TPU:32, one launch (start us, length us, event | category | flops | bytes accessed | tf_op | source)
XLA Modules:
  0.0 231.6 jit_solution(11728773243081567812)
XLA Ops:
  0.6 1.4 fusion.25
  2.0 1.3 fusion.22.k_ref
  4.3 2.1 collective-permute-start
  6.3 12.4 %collective-permute-start.1 = (bf16[2,128,1280]{2,1,0:T(8,128)(2,1)S(1)}, bf16[2,128,1280]{2,1,0:T(8,128)(2,1)S(1)}, u32[]{:S(2)}, u32[]{:S(2)}) collective-permute-start(bf16[2,128,1280]{2,1,0:T(8,128)(2,1)S(1)} %pad_maximum_fusion.1), channel_id=1, source_target_pairs={{2,0},{4,2},{6,4},{8,6},{10,8},{12,10},{14,12},{16,14},{18,16},{20... | collective-permute-start | bytes 1966088 | tf_op jit(solution)/shard_map/ppermute | solution.py:26
  18.7 1.9 collective-permute-start.2
  20.7 8.7 %collective-permute-done.refs_0_ = bf16[2,128,1280]{2,1,0:T(8,128)(2,1)S(1)} collective-permute-done((bf16[2,128,1280]{2,1,0:T(8,128)(2,1)S(1)}, bf16[2,128,1280]{2,1,0:T(8,128)(2,1)S(1)}, u32[]{:S(2)}, u32[]{:S(2)}) %collective-permute-start) | collective-permute-done | bytes 655392 | tf_op jit(solution)/shard_map/ppermute | solution.py:26
  29.4 17.3 %collective-permute-done.1.refs_1_ = bf16[2,128,1280]{2,1,0:T(8,128)(2,1)S(1)} collective-permute-done((bf16[2,128,1280]{2,1,0:T(8,128)(2,1)S(1)}, bf16[2,128,1280]{2,1,0:T(8,128)(2,1)S(1)}, u32[]{:S(2)}, u32[]{:S(2)}) %collective-permute-start.1) | collective-permute-done | bytes 655392 | tf_op jit(solution)/shard_map/ppermute | solution.py:26
  46.8 2.1 collective-permute-start.3
  50.9 2.1 collective-permute-start.4
  53.1 9.9 %collective-permute-start.5 = (bf16[2,128,1280]{2,1,0:T(8,128)(2,1)}, bf16[2,128,1280]{2,1,0:T(8,128)(2,1)S(1)}, u32[]{:S(2)}, u32[]{:S(2)}) collective-permute-start(bf16[2,128,1280]{2,1,0:T(8,128)(2,1)} %pad_maximum_fusion.2), channel_id=1, source_target_pairs={{2,0},{4,2},{6,4},{8,6},{10,8},{12,10},{14,12},{16,14},{18,16},{20... | collective-permute-start | bytes 1966088 | tf_op jit(solution)/shard_map/ppermute | solution.py:26
  64.1 1.9 collective-permute-start.6
  66.0 9.0 %collective-permute-done.4.refs_0_ = bf16[2,128,1280]{2,1,0:T(8,128)(2,1)S(1)} collective-permute-done((bf16[2,128,1280]{2,1,0:T(8,128)(2,1)}, bf16[2,128,1280]{2,1,0:T(8,128)(2,1)S(1)}, u32[]{:S(2)}, u32[]{:S(2)}) %collective-permute-start.4) | collective-permute-done | bytes 655392 | tf_op jit(solution)/shard_map/ppermute | solution.py:26
  74.9 12.1 %collective-permute-done.5.refs_1_ = bf16[2,128,1280]{2,1,0:T(8,128)(2,1)S(1)} collective-permute-done((bf16[2,128,1280]{2,1,0:T(8,128)(2,1)}, bf16[2,128,1280]{2,1,0:T(8,128)(2,1)S(1)}, u32[]{:S(2)}, u32[]{:S(2)}) %collective-permute-start.5) | collective-permute-done | bytes 655392 | tf_op jit(solution)/shard_map/ppermute | solution.py:26
  88.1 1.9 collective-permute-start.7
  90.0 11.2 %shard_map.110 = (f32[128,1280]{1,0:T(8,128)}, f32[128,1280]{1,0:T(8,128)}, f32[128,1280]{1,0:T(8,128)}, bf16[2,128,1280]{2,1,0:T(8,128)(2,1)}, bf16[2,128,1280]...) custom-call(s32[1]{0:T(128)} %bitcast.1.odd_ref, f32[1,640]{1,0:T(1,128)} %bitcast.136, ...), custom_call_target="tpu_custom_call" | custom-call | flops 1258291200 | bytes 5898240 | tf_op jit(solution)/shard_map/pallas_call | solution.py:161
  101.2 2.4 %collective-permute-start.8 = (bf16[2,128,1280]{2,1,0:T(8,128)(2,1)}, bf16[2,128,1280]{2,1,0:T(8,128)(2,1)}, u32[]{:S(2)}, u32[]{:S(2)}) collective-permute-start(bf16[2,128,1280]{2,1,0:T(8,128)(2,1)} %get-tuple-element.25), channel_id=1, source_target_pairs={{0,2},{2,0},{4,6},{6,4},{8,10},{10,8},{12,14},{14,12},{16,18},{18,... | collective-permute-start | bytes 1966088 | tf_op jit(solution)/shard_map/ppermute | solution.py:31
  103.6 9.9 %collective-permute-start.11 = (bf16[2,128,1280]{2,1,0:T(8,128)(2,1)}, bf16[2,128,1280]{2,1,0:T(8,128)(2,1)}, u32[]{:S(2)}, u32[]{:S(2)}) collective-permute-start(bf16[2,128,1280]{2,1,0:T(8,128)(2,1)} %get-tuple-element.27), channel_id=1, source_target_pairs={{2,6},{6,10},{10,14},{14,18},{18,22},{22,26},{26,30},{30,34},{34,3... | collective-permute-start | bytes 1966088 | tf_op jit(solution)/shard_map/ppermute | solution.py:31
  114.8 11.2 %shard_map.111 = (f32[128,1280]{1,0:T(8,128)}, f32[128,1280]{1,0:T(8,128)}, f32[128,1280]{1,0:T(8,128)}, bf16[2,128,1280]{2,1,0:T(8,128)(2,1)}, bf16[2,128,1280]...) custom-call(s32[1]{0:T(128)} %bitcast.1.odd_ref, f32[1,640]{1,0:T(1,128)} %bitcast.137, ...), custom_call_target="tpu_custom_call" | custom-call | flops 1258291200 | bytes 5898240 | tf_op jit(solution)/shard_map/pallas_call | solution.py:161
  126.0 1.9 collective-permute-start.12
  128.0 1.5 fusion.33
  129.5 2.2 collective-permute-start.10
  131.7 2.3 collective-permute-start.9
  134.0 3.3 %collective-permute-start.15 = (bf16[2,128,1280]{2,1,0:T(8,128)(2,1)S(1)}, bf16[2,128,1280]{2,1,0:T(8,128)(2,1)S(1)}, u32[]{:S(2)}, u32[]{:S(2)}) collective-permute-start(bf16[2,128,1280]{2,1,0:T(8,128)(2,1)S(1)} %copy-done.21), channel_id=1, source_target_pairs={{2,6},{6,10},{10,14},{14,18},{18,22},{22,26},{26,30},{30,34},{34,3... | collective-permute-start | bytes 1966088 | tf_op jit(solution)/shard_map/ppermute | solution.py:31
  137.8 2.4 %collective-permute-start.13 = (bf16[2,128,1280]{2,1,0:T(8,128)(2,1)S(1)}, bf16[2,128,1280]{2,1,0:T(8,128)(2,1)S(1)}, u32[]{:S(2)}, u32[]{:S(2)}) collective-permute-start(bf16[2,128,1280]{2,1,0:T(8,128)(2,1)S(1)} %get-tuple-element.45), channel_id=1, source_target_pairs={{0,2},{2,4},{4,6},{6,8},{8,10},{10,12},{12,14},{14,16},{16,18},{18... | collective-permute-start | bytes 1966088 | tf_op jit(solution)/shard_map/ppermute | solution.py:26
  140.6 9.2 %collective-permute-start.14 = (bf16[2,128,1280]{2,1,0:T(8,128)(2,1)S(1)}, bf16[2,128,1280]{2,1,0:T(8,128)(2,1)S(1)}, u32[]{:S(2)}, u32[]{:S(2)}) collective-permute-start(bf16[2,128,1280]{2,1,0:T(8,128)(2,1)S(1)} %get-tuple-element.46), channel_id=1, source_target_pairs={{2,0},{4,2},{6,4},{8,6},{10,8},{12,10},{14,12},{16,14},{18,16},{20... | collective-permute-start | bytes 1966088 | tf_op jit(solution)/shard_map/ppermute | solution.py:26
  150.3 1.4 fusion.36
  151.8 2.8 %collective-permute-done.15 = bf16[2,128,1280]{2,1,0:T(8,128)(2,1)S(1)} collective-permute-done((bf16[2,128,1280]{2,1,0:T(8,128)(2,1)S(1)}, bf16[2,128,1280]{2,1,0:T(8,128)(2,1)S(1)}, u32[]{:S(2)}, u32[]{:S(2)}) %collective-permute-start.15) | collective-permute-done | bytes 655392 | tf_op jit(solution)/shard_map/ppermute | solution.py:31
  154.6 15.3 %collective-permute-done.13 = bf16[2,128,1280]{2,1,0:T(8,128)(2,1)S(1)} collective-permute-done((bf16[2,128,1280]{2,1,0:T(8,128)(2,1)S(1)}, bf16[2,128,1280]{2,1,0:T(8,128)(2,1)S(1)}, u32[]{:S(2)}, u32[]{:S(2)}) %collective-permute-start.13) | collective-permute-done | bytes 655392 | tf_op jit(solution)/shard_map/ppermute | solution.py:26
  171.4 1.9 collective-permute-start.16
  173.4 3.7 %collective-permute-done.16 = f32[5120]{0:T(1024)S(1)} collective-permute-done((f32[5120]{0:T(1024)S(1)}, f32[5120]{0:T(1024)S(1)}, u32[]{:S(2)}, u32[]{:S(2)}) %collective-permute-start.16) | collective-permute-done | bytes 20512 | tf_op jit(solution)/shard_map/ppermute | solution.py:65
  177.1 1.9 collective-permute-start.17
  179.0 1.2 collective-permute-done.17
  180.2 1.9 collective-permute-start.18
  182.1 3.7 %collective-permute-done.18 = f32[5120]{0:T(1024)S(1)} collective-permute-done((f32[5120]{0:T(1024)S(1)}, f32[5120]{0:T(1024)S(1)}, u32[]{:S(2)}, u32[]{:S(2)}) %collective-permute-start.18) | collective-permute-done | bytes 20512 | tf_op jit(solution)/shard_map/ppermute | solution.py:65
  185.9 1.9 collective-permute-start.19
  187.8 5.3 %collective-permute-done.19 = f32[5120]{0:T(1024)S(1)} collective-permute-done((f32[5120]{0:T(1024)S(1)}, f32[5120]{0:T(1024)S(1)}, u32[]{:S(2)}, u32[]{:S(2)}) %collective-permute-start.19) | collective-permute-done | bytes 20512 | tf_op jit(solution)/shard_map/ppermute | solution.py:65
  193.1 1.9 collective-permute-start.20
  195.0 3.7 %collective-permute-done.20 = f32[5120]{0:T(1024)S(1)} collective-permute-done((f32[5120]{0:T(1024)S(1)}, f32[5120]{0:T(1024)S(1)}, u32[]{:S(2)}, u32[]{:S(2)}) %collective-permute-start.20) | collective-permute-done | bytes 20512 | tf_op jit(solution)/shard_map/ppermute | solution.py:65
  198.7 1.9 collective-permute-start.21
  200.6 1.2 fusion.21
  201.9 3.4 %collective-permute-done.21 = f32[5120]{0:T(1024)S(1)} collective-permute-done((f32[5120]{0:T(1024)S(1)}, f32[5120]{0:T(1024)S(1)}, u32[]{:S(2)}, u32[]{:S(2)}) %collective-permute-start.21) | collective-permute-done | bytes 20512 | tf_op jit(solution)/shard_map/ppermute | solution.py:65
  205.3 1.9 collective-permute-start.22
  207.2 7.6 %collective-permute-done.22 = f32[5120]{0:T(1024)S(1)} collective-permute-done((f32[5120]{0:T(1024)S(1)}, f32[5120]{0:T(1024)S(1)}, u32[]{:S(2)}, u32[]{:S(2)}) %collective-permute-start.22) | collective-permute-done | bytes 20512 | tf_op jit(solution)/shard_map/ppermute | solution.py:65
  214.9 2.6 %collective-permute-start.23 = (f32[5120]{0:T(1024)S(1)}, f32[5120]{0:T(1024)S(1)}, u32[]{:S(2)}, u32[]{:S(2)}) collective-permute-start(f32[5120]{0:T(1024)S(1)} %add.124), channel_id=1, source_target_pairs={{0,128},{2,130},{4,132},{6,134},{8,136},{10,138},{12,140},{14,142}... | collective-permute-start | bytes 61448 | tf_op jit(solution)/shard_map/ppermute | solution.py:65
  217.5 1.2 fusion.29
  218.7 2.7 %collective-permute-done.23 = f32[5120]{0:T(1024)S(1)} collective-permute-done((f32[5120]{0:T(1024)S(1)}, f32[5120]{0:T(1024)S(1)}, u32[]{:S(2)}, u32[]{:S(2)}) %collective-permute-start.23) | collective-permute-done | bytes 20512 | tf_op jit(solution)/shard_map/ppermute | solution.py:65
  221.4 1.9 collective-permute-start.24
  224.2 6.8 %collective-permute-done.24 = f32[5120]{0:T(1024)S(1)} collective-permute-done((f32[5120]{0:T(1024)S(1)}, f32[5120]{0:T(1024)S(1)}, u32[]{:S(2)}, u32[]{:S(2)}) %collective-permute-start.24) | collective-permute-done | bytes 20512 | tf_op jit(solution)/shard_map/ppermute | solution.py:65
  (89 shorter events, 10.7 us)
Async XLA Ops:
  0.6 2.7 %copy-start.3 = (bf16[1,128,2560]{2,1,0:T(8,128)(2,1)S(1)}, bf16[1,128,2560]{2,1,0:T(8,128)(2,1)}, u32[]{:S(2)}) copy-start(bf16[1,128,2560]{2,1,0:T(8,128)(2,1)} %param.9) | copy-start | bytes 1966084
  3.3 0.8 copy-start.2
  4.2 16.4 %copy-start.22 = (s32[1,4]{1,0:T(1,128)S(1)}, s32[1,4]{1,0:T(1,128)}, u32[]{:S(2)}) copy-start(s32[1,4]{1,0:T(1,128)} %param.13) | copy-start | bytes 52
  4.2 45.3 %copy-start = (bf16[1,128,2560]{2,1,0:T(8,128)(2,1)S(1)}, bf16[1,128,2560]{2,1,0:T(8,128)(2,1)}, u32[]{:S(2)}) copy-start(bf16[1,128,2560]{2,1,0:T(8,128)(2,1)} %param.7) | copy-start | bytes 1966084
  4.3 25.1 %collective-permute-start = (bf16[2,128,1280]{2,1,0:T(8,128)(2,1)S(1)}, bf16[2,128,1280]{2,1,0:T(8,128)(2,1)S(1)}, u32[]{:S(2)}, u32[]{:S(2)}) collective-permute-start(bf16[2,128,1280]{2,1,0:T(8,128)(2,1)S(1)} %pad_maximum_fusion.1), channel_id=1, source_target_pairs={{0,2},{2,4},{4,6},{6,8},{8,10},{10,12},{12,14},{14,16},{16,18},{18... | collective-permute-start | bytes 1966088 | tf_op jit(solution)/shard_map/ppermute | solution.py:26
  6.3 40.4 %collective-permute-start.1 = (bf16[2,128,1280]{2,1,0:T(8,128)(2,1)S(1)}, bf16[2,128,1280]{2,1,0:T(8,128)(2,1)S(1)}, u32[]{:S(2)}, u32[]{:S(2)}) collective-permute-start(bf16[2,128,1280]{2,1,0:T(8,128)(2,1)S(1)} %pad_maximum_fusion.1), channel_id=1, source_target_pairs={{2,0},{4,2},{6,4},{8,6},{10,8},{12,10},{14,12},{16,14},{18,16},{20... | collective-permute-start | bytes 1966088 | tf_op jit(solution)/shard_map/ppermute | solution.py:26
  18.7 32.0 %collective-permute-start.2 = (bf16[2,128,1280]{2,1,0:T(8,128)(2,1)S(1)}, bf16[2,128,1280]{2,1,0:T(8,128)(2,1)}, u32[]{:S(2)}, u32[]{:S(2)}) collective-permute-start(bf16[2,128,1280]{2,1,0:T(8,128)(2,1)S(1)} %pad_maximum_fusion.1), channel_id=1, source_target_pairs={{0,4},{4,8},{8,12},{12,16},{16,20},{20,24},{24,28},{28,32},{32,36}... | collective-permute-start | bytes 1966088 | tf_op jit(solution)/shard_map/ppermute | solution.py:31
  29.4 20.3 %copy-start.6 = (bf16[2,128,1280]{2,1,0:T(8,128)(2,1)}, bf16[2,128,1280]{2,1,0:T(8,128)(2,1)S(1)}, u32[]{:S(2)}) copy-start(bf16[2,128,1280]{2,1,0:T(8,128)(2,1)S(1)} %collective-permute-done.refs_0_) | copy-start | bytes 1966084
  46.7 3.0 %copy-start.7 = (bf16[2,128,1280]{2,1,0:T(8,128)(2,1)}, bf16[2,128,1280]{2,1,0:T(8,128)(2,1)S(1)}, u32[]{:S(2)}) copy-start(bf16[2,128,1280]{2,1,0:T(8,128)(2,1)S(1)} %collective-permute-done.1.refs_1_) | copy-start | bytes 1966084
  46.8 16.2 %copy-start.19 = (f32[2560]{0:T(1024)S(1)}, f32[2560]{0:T(1024)}, u32[]{:S(2)}) copy-start(f32[2560]{0:T(1024)} %param.11) | copy-start | bytes 30724
  46.8 4.1 %collective-permute-start.3 = (bf16[2,128,1280]{2,1,0:T(8,128)(2,1)S(1)}, bf16[2,128,1280]{2,1,0:T(8,128)(2,1)S(1)}, u32[]{:S(2)}, u32[]{:S(2)}) collective-permute-start(bf16[2,128,1280]{2,1,0:T(8,128)(2,1)S(1)} %broadcast_select_fusion.1), channel_id=1, source_target_pairs={{0,2},{2,0},{4,6},{6,4},{8,10},{10,8},{12,14},{14,12},{16,18},{18,... | collective-permute-start | bytes 1966088 | tf_op jit(solution)/shard_map/ppermute | solution.py:31
  50.9 24.0 %copy-start.18 = (bf16[2,128,1280]{2,1,0:T(8,128)(2,1)}, bf16[2,128,1280]{2,1,0:T(8,128)(2,1)S(1)}, u32[]{:S(2)}) copy-start(bf16[2,128,1280]{2,1,0:T(8,128)(2,1)S(1)} %collective-permute-done.3.refs_3_) | copy-start | bytes 1966084
  50.9 24.0 %collective-permute-start.4 = (bf16[2,128,1280]{2,1,0:T(8,128)(2,1)}, bf16[2,128,1280]{2,1,0:T(8,128)(2,1)S(1)}, u32[]{:S(2)}, u32[]{:S(2)}) collective-permute-start(bf16[2,128,1280]{2,1,0:T(8,128)(2,1)} %pad_maximum_fusion.2), channel_id=1, source_target_pairs={{0,2},{2,4},{4,6},{6,8},{8,10},{10,12},{12,14},{14,16},{16,18},{18... | collective-permute-start | bytes 1966088 | tf_op jit(solution)/shard_map/ppermute | solution.py:26
  53.1 34.0 %collective-permute-start.5 = (bf16[2,128,1280]{2,1,0:T(8,128)(2,1)}, bf16[2,128,1280]{2,1,0:T(8,128)(2,1)S(1)}, u32[]{:S(2)}, u32[]{:S(2)}) collective-permute-start(bf16[2,128,1280]{2,1,0:T(8,128)(2,1)} %pad_maximum_fusion.2), channel_id=1, source_target_pairs={{2,0},{4,2},{6,4},{8,6},{10,8},{12,10},{14,12},{16,14},{18,16},{20... | collective-permute-start | bytes 1966088 | tf_op jit(solution)/shard_map/ppermute | solution.py:26
  64.1 50.7 %collective-permute-start.6 = (bf16[2,128,1280]{2,1,0:T(8,128)(2,1)}, bf16[2,128,1280]{2,1,0:T(8,128)(2,1)}, u32[]{:S(2)}, u32[]{:S(2)}) collective-permute-start(bf16[2,128,1280]{2,1,0:T(8,128)(2,1)} %pad_maximum_fusion.2), channel_id=1, source_target_pairs={{0,4},{4,8},{8,12},{12,16},{16,20},{20,24},{24,28},{28,32},{32,36}... | collective-permute-start | bytes 1966088 | tf_op jit(solution)/shard_map/ppermute | solution.py:31
  74.9 26.2 %copy-start.8 = (bf16[2,128,1280]{2,1,0:T(8,128)(2,1)}, bf16[2,128,1280]{2,1,0:T(8,128)(2,1)S(1)}, u32[]{:S(2)}) copy-start(bf16[2,128,1280]{2,1,0:T(8,128)(2,1)S(1)} %collective-permute-done.4.refs_0_) | copy-start | bytes 1966084
  87.1 14.1 %copy-start.9 = (bf16[2,128,1280]{2,1,0:T(8,128)(2,1)}, bf16[2,128,1280]{2,1,0:T(8,128)(2,1)S(1)}, u32[]{:S(2)}) copy-start(bf16[2,128,1280]{2,1,0:T(8,128)(2,1)S(1)} %collective-permute-done.5.refs_1_) | copy-start | bytes 1966084
  88.1 26.7 %collective-permute-start.7 = (bf16[2,128,1280]{2,1,0:T(8,128)(2,1)}, bf16[2,128,1280]{2,1,0:T(8,128)(2,1)}, u32[]{:S(2)}, u32[]{:S(2)}) collective-permute-start(bf16[2,128,1280]{2,1,0:T(8,128)(2,1)} %broadcast_select_fusion), channel_id=1, source_target_pairs={{0,2},{2,0},{4,6},{6,4},{8,10},{10,8},{12,14},{14,12},{16,18},{18,... | collective-permute-start | bytes 1966088 | tf_op jit(solution)/shard_map/ppermute | solution.py:31
  101.2 26.7 %collective-permute-start.8 = (bf16[2,128,1280]{2,1,0:T(8,128)(2,1)}, bf16[2,128,1280]{2,1,0:T(8,128)(2,1)}, u32[]{:S(2)}, u32[]{:S(2)}) collective-permute-start(bf16[2,128,1280]{2,1,0:T(8,128)(2,1)} %get-tuple-element.25), channel_id=1, source_target_pairs={{0,2},{2,0},{4,6},{6,4},{8,10},{10,8},{12,14},{14,12},{16,18},{18,... | collective-permute-start | bytes 1966088 | tf_op jit(solution)/shard_map/ppermute | solution.py:31
  103.6 37.0 %collective-permute-start.11 = (bf16[2,128,1280]{2,1,0:T(8,128)(2,1)}, bf16[2,128,1280]{2,1,0:T(8,128)(2,1)}, u32[]{:S(2)}, u32[]{:S(2)}) collective-permute-start(bf16[2,128,1280]{2,1,0:T(8,128)(2,1)} %get-tuple-element.27), channel_id=1, source_target_pairs={{2,6},{6,10},{10,14},{14,18},{18,22},{22,26},{26,30},{30,34},{34,3... | collective-permute-start | bytes 1966088 | tf_op jit(solution)/shard_map/ppermute | solution.py:31
  114.7 13.2 %copy-start.10 = (bf16[2,128,1280]{2,1,0:T(8,128)(2,1)S(1)}, bf16[2,128,1280]{2,1,0:T(8,128)(2,1)}, u32[]{:S(2)}) copy-start(bf16[2,128,1280]{2,1,0:T(8,128)(2,1)} %get-tuple-element.26) | copy-start | bytes 1966084
  114.7 13.2 %copy-start.11 = (bf16[2,128,1280]{2,1,0:T(8,128)(2,1)S(1)}, bf16[2,128,1280]{2,1,0:T(8,128)(2,1)}, u32[]{:S(2)}) copy-start(bf16[2,128,1280]{2,1,0:T(8,128)(2,1)} %get-tuple-element.24) | copy-start | bytes 1966084
  126.0 11.4 %collective-permute-start.12 = (bf16[2,128,1280]{2,1,0:T(8,128)(2,1)}, bf16[2,128,1280]{2,1,0:T(8,128)(2,1)S(1)}, u32[]{:S(2)}, u32[]{:S(2)}) collective-permute-start(bf16[2,128,1280]{2,1,0:T(8,128)(2,1)} %get-tuple-element.30), channel_id=1, source_target_pairs={{0,2},{2,0},{4,6},{6,4},{8,10},{10,8},{12,14},{14,12},{16,18},{18,... | collective-permute-start | bytes 1966088 | tf_op jit(solution)/shard_map/ppermute | solution.py:31
  128.0 6.1 %copy-start.21 = (bf16[2,128,1280]{2,1,0:T(8,128)(2,1)S(1)}, bf16[2,128,1280]{2,1,0:T(8,128)(2,1)}, u32[]{:S(2)}) copy-start(bf16[2,128,1280]{2,1,0:T(8,128)(2,1)} %get-tuple-element.32) | copy-start | bytes 1966084
  128.0 9.3 %copy-start.5 = (f32[128,1280]{1,0:T(8,128)S(1)}, f32[128,1280]{1,0:T(8,128)}, u32[]{:S(2)}) copy-start(f32[128,1280]{1,0:T(8,128)} %get-tuple-element.22) | copy-start | bytes 1966084
  129.5 7.9 %copy-start.12 = (bf16[2,128,1280]{2,1,0:T(8,128)(2,1)S(1)}, bf16[2,128,1280]{2,1,0:T(8,128)(2,1)}, u32[]{:S(2)}) copy-start(bf16[2,128,1280]{2,1,0:T(8,128)(2,1)} %get-tuple-element.31) | copy-start | bytes 1966084
  129.5 7.9 %copy-start.13 = (bf16[2,128,1280]{2,1,0:T(8,128)(2,1)S(1)}, bf16[2,128,1280]{2,1,0:T(8,128)(2,1)}, u32[]{:S(2)}) copy-start(bf16[2,128,1280]{2,1,0:T(8,128)(2,1)} %get-tuple-element.29) | copy-start | bytes 1966084
  129.5 20.7 %collective-permute-start.10 = (bf16[2,128,1280]{2,1,0:T(8,128)(2,1)S(1)}, bf16[2,128,1280]{2,1,0:T(8,128)(2,1)S(1)}, u32[]{:S(2)}, u32[]{:S(2)}) collective-permute-start(bf16[2,128,1280]{2,1,0:T(8,128)(2,1)S(1)} %get-tuple-element.44), channel_id=1, source_target_pairs={{2,0},{4,2},{6,4},{8,6},{10,8},{12,10},{14,12},{16,14},{18,16},{20... | collective-permute-start | bytes 1966088 | tf_op jit(solution)/shard_map/ppermute | solution.py:26
  131.7 18.6 %collective-permute-start.9 = (bf16[2,128,1280]{2,1,0:T(8,128)(2,1)S(1)}, bf16[2,128,1280]{2,1,0:T(8,128)(2,1)S(1)}, u32[]{:S(2)}, u32[]{:S(2)}) collective-permute-start(bf16[2,128,1280]{2,1,0:T(8,128)(2,1)S(1)} %get-tuple-element.43), channel_id=1, source_target_pairs={{0,2},{2,4},{4,6},{6,8},{8,10},{10,12},{12,14},{14,16},{16,18},{18... | collective-permute-start | bytes 1966088 | tf_op jit(solution)/shard_map/ppermute | solution.py:26
  134.0 20.6 %collective-permute-start.15 = (bf16[2,128,1280]{2,1,0:T(8,128)(2,1)S(1)}, bf16[2,128,1280]{2,1,0:T(8,128)(2,1)S(1)}, u32[]{:S(2)}, u32[]{:S(2)}) collective-permute-start(bf16[2,128,1280]{2,1,0:T(8,128)(2,1)S(1)} %copy-done.21), channel_id=1, source_target_pairs={{2,6},{6,10},{10,14},{14,18},{18,22},{22,26},{26,30},{30,34},{34,3... | collective-permute-start | bytes 1966088 | tf_op jit(solution)/shard_map/ppermute | solution.py:31
  137.8 12.5 %copy-start.14 = (f32[128,1280]{1,0:T(8,128)S(1)}, f32[128,1280]{1,0:T(8,128)}, u32[]{:S(2)}) copy-start(f32[128,1280]{1,0:T(8,128)} %get-tuple-element.23) | copy-start | bytes 1966084
  137.8 12.5 %copy-start.15 = (f32[128,1280]{1,0:T(8,128)S(1)}, f32[128,1280]{1,0:T(8,128)}, u32[]{:S(2)}) copy-start(f32[128,1280]{1,0:T(8,128)} %get-tuple-element.33) | copy-start | bytes 1966084
  137.8 32.1 %collective-permute-start.13 = (bf16[2,128,1280]{2,1,0:T(8,128)(2,1)S(1)}, bf16[2,128,1280]{2,1,0:T(8,128)(2,1)S(1)}, u32[]{:S(2)}, u32[]{:S(2)}) collective-permute-start(bf16[2,128,1280]{2,1,0:T(8,128)(2,1)S(1)} %get-tuple-element.45), channel_id=1, source_target_pairs={{0,2},{2,4},{4,6},{6,8},{8,10},{10,12},{12,14},{14,16},{16,18},{18... | collective-permute-start | bytes 1966088 | tf_op jit(solution)/shard_map/ppermute | solution.py:26
  140.6 29.3 %collective-permute-start.14 = (bf16[2,128,1280]{2,1,0:T(8,128)(2,1)S(1)}, bf16[2,128,1280]{2,1,0:T(8,128)(2,1)S(1)}, u32[]{:S(2)}, u32[]{:S(2)}) collective-permute-start(bf16[2,128,1280]{2,1,0:T(8,128)(2,1)S(1)} %get-tuple-element.46), channel_id=1, source_target_pairs={{2,0},{4,2},{6,4},{8,6},{10,8},{12,10},{14,12},{16,14},{18,16},{20... | collective-permute-start | bytes 1966088 | tf_op jit(solution)/shard_map/ppermute | solution.py:26
  150.3 19.6 %copy-start.16 = (f32[128,1280]{1,0:T(8,128)S(1)}, f32[128,1280]{1,0:T(8,128)}, u32[]{:S(2)}) copy-start(f32[128,1280]{1,0:T(8,128)} %get-tuple-element.28) | copy-start | bytes 1966084
  150.3 19.6 %copy-start.17 = (f32[128,1280]{1,0:T(8,128)S(1)}, f32[128,1280]{1,0:T(8,128)}, u32[]{:S(2)}) copy-start(f32[128,1280]{1,0:T(8,128)} %get-tuple-element.34) | copy-start | bytes 1966084
  169.9 1.1 copy-start.1
  169.9 1.1 copy-start.20
  170.2 30.4 %copy-start.4 = (f32[128,1280]{1,0:T(8,128)S(1)}, f32[128,1280]{1,0:T(8,128)}, u32[]{:S(2)}) copy-start(f32[128,1280]{1,0:T(8,128)} %get-tuple-element.20) | copy-start | bytes 1966084
  171.4 5.7 %collective-permute-start.16 = (f32[5120]{0:T(1024)S(1)}, f32[5120]{0:T(1024)S(1)}, u32[]{:S(2)}, u32[]{:S(2)}) collective-permute-start(f32[5120]{0:T(1024)S(1)} %pad_maximum_fusion.4), channel_id=1, source_target_pairs={{0,1},{1,0},{2,3},{3,2},{4,5},{5,4},{6,7},{7,6},{8,9},{9,8},{10,11... | collective-permute-start | bytes 61448 | tf_op jit(solution)/shard_map/ppermute | solution.py:65
  177.1 3.1 %collective-permute-start.17 = (f32[5120]{0:T(1024)S(1)}, f32[5120]{0:T(1024)S(1)}, u32[]{:S(2)}, u32[]{:S(2)}) collective-permute-start(f32[5120]{0:T(1024)S(1)} %fusion.39), channel_id=1, source_target_pairs={{0,2},{2,0},{4,6},{6,4},{8,10},{10,8},{12,14},{14,12},{16,18},{18,... | collective-permute-start | bytes 61448 | tf_op jit(solution)/shard_map/ppermute | solution.py:65
  180.2 5.7 %collective-permute-start.18 = (f32[5120]{0:T(1024)S(1)}, f32[5120]{0:T(1024)S(1)}, u32[]{:S(2)}, u32[]{:S(2)}) collective-permute-start(f32[5120]{0:T(1024)S(1)} %add.119), channel_id=1, source_target_pairs={{0,4},{2,6},{4,0},{6,2},{8,12},{10,14},{12,8},{14,10},{16,20},{18,... | collective-permute-start | bytes 61448 | tf_op jit(solution)/shard_map/ppermute | solution.py:65
  185.9 7.2 %collective-permute-start.19 = (f32[5120]{0:T(1024)S(1)}, f32[5120]{0:T(1024)S(1)}, u32[]{:S(2)}, u32[]{:S(2)}) collective-permute-start(f32[5120]{0:T(1024)S(1)} %add.120), channel_id=1, source_target_pairs={{0,8},{2,10},{4,12},{6,14},{8,0},{10,2},{12,4},{14,6},{16,24},{18,... | collective-permute-start | bytes 61448 | tf_op jit(solution)/shard_map/ppermute | solution.py:65
  193.1 5.7 %collective-permute-start.20 = (f32[5120]{0:T(1024)S(1)}, f32[5120]{0:T(1024)S(1)}, u32[]{:S(2)}, u32[]{:S(2)}) collective-permute-start(f32[5120]{0:T(1024)S(1)} %add.121), channel_id=1, source_target_pairs={{0,16},{2,18},{4,20},{6,22},{8,24},{10,26},{12,28},{14,30},{16,0},... | collective-permute-start | bytes 61448 | tf_op jit(solution)/shard_map/ppermute | solution.py:65
  198.7 6.6 %collective-permute-start.21 = (f32[5120]{0:T(1024)S(1)}, f32[5120]{0:T(1024)S(1)}, u32[]{:S(2)}, u32[]{:S(2)}) collective-permute-start(f32[5120]{0:T(1024)S(1)} %add.122), channel_id=1, source_target_pairs={{0,32},{2,34},{4,36},{6,38},{8,40},{10,42},{12,44},{14,46},{16,48}... | collective-permute-start | bytes 61448 | tf_op jit(solution)/shard_map/ppermute | solution.py:65
  205.3 9.6 %collective-permute-start.22 = (f32[5120]{0:T(1024)S(1)}, f32[5120]{0:T(1024)S(1)}, u32[]{:S(2)}, u32[]{:S(2)}) collective-permute-start(f32[5120]{0:T(1024)S(1)} %add.123), channel_id=1, source_target_pairs={{0,64},{2,66},{4,68},{6,70},{8,72},{10,74},{12,76},{14,78},{16,80}... | collective-permute-start | bytes 61448 | tf_op jit(solution)/shard_map/ppermute | solution.py:65
  214.9 6.6 %collective-permute-start.23 = (f32[5120]{0:T(1024)S(1)}, f32[5120]{0:T(1024)S(1)}, u32[]{:S(2)}, u32[]{:S(2)}) collective-permute-start(f32[5120]{0:T(1024)S(1)} %add.124), channel_id=1, source_target_pairs={{0,128},{2,130},{4,132},{6,134},{8,136},{10,138},{12,140},{14,142}... | collective-permute-start | bytes 61448 | tf_op jit(solution)/shard_map/ppermute | solution.py:65
  221.4 9.6 %collective-permute-start.24 = (f32[5120]{0:T(1024)S(1)}, f32[5120]{0:T(1024)S(1)}, u32[]{:S(2)}, u32[]{:S(2)}) collective-permute-start(f32[5120]{0:T(1024)S(1)} %add.125), channel_id=1, source_target_pairs={{0,256},{2,258},{4,260},{6,262},{8,264},{10,266},{12,268},{14,270}... | collective-permute-start | bytes 61448 | tf_op jit(solution)/shard_map/ppermute | solution.py:65

commit v9 on v8

--- a/solution.py
+++ b/solution.py
@@ -10,8 +10,8 @@
 
 HEAD = 128
 LEVELS = 2
-HEADS_PER_STEP = 2
-CHUNKS = 2
+HEADS_PER_STEP = 4
+CHUNK_HEADS = (12, 8)
 
 
 EPS = 1e-06
@@ -184,18 +184,19 @@
     live = jnp.concatenate([jnp.ones((1,), bool), entries >= 0])
     bias = jnp.repeat(jnp.where(live, 0.0, -jnp.inf).astype(jnp.float32), tile_rows)[None, :]
     odd = (lax.axis_index("seq") % 2).astype(jnp.int32)[None]
-    chunk = features // CHUNKS
     pieces = []
     fetched = None
-    for c in range(CHUNKS):
-        cols = slice(c * chunk, (c + 1) * chunk)
+    start = 0
+    for heads in CHUNK_HEADS:
+        cols = slice(start, start + heads * HEAD)
         stacked = jnp.stack([k_norm[:, cols], value_rows[:, cols]])
         if fetched is not None:
             stacked, _ = lax.optimization_barrier((stacked, fetched))
         fetched = fetch_neighbours(stacked, "seq")
         q_grad_c, k_grad_c, v_sum_c, *far = attention(
-            odd, bias, q_norm, k_norm, value_rows, grad_rows, fetched, c * chunk // (HEADS_PER_STEP * HEAD)
+            odd, bias, q_norm, k_norm, value_rows, grad_rows, fetched, start // (HEADS_PER_STEP * HEAD)
         )
+        start += heads * HEAD
         for back in return_parts(far, "seq"):
             k_grad_c = k_grad_c + back[0].astype(jnp.float32)
             v_sum_c = v_sum_c + back[1].astype(jnp.float32)

time: 233 us -> 229 us (0.983)
  waiting for transfers between devices: 104 us -> 79.3 us
  starting transfers between devices: 85.8 us -> 107 us
    ppermute x8, waiting for transfers between devices: 62.4 us -> 40.8 us  [from_behind(): lax.ppermute(value, axis, [(source, source + steps) for source in range(f...]
    ppermute x8, starting transfers between devices: 25.3 us -> 42.6 us  [pairs_permute(): lax.ppermute(value, axis, [(i, j) for i, j in pairs if 0 <= j < count])]
    ppermute x8, starting transfers between devices: 42.5 us -> 46.6 us  [from_behind(): lax.ppermute(value, axis, [(source, source + steps) for source in range(f...]
    ppermute x8, waiting for transfers between devices: 3.52 us -> 0.35 us  [pairs_permute(): lax.ppermute(value, axis, [(i, j) for i, j in pairs if 0 <= j < count])]
  transfers between devices with their start and end apart: 25 -> 25, of which waited for: 17 -> 13; matrix products, arithmetic and copies ran while one was open for 5% -> 5% of each run, Pallas kernels for 10% -> 10%
where the time goes in v9:
time: 229 us; the launch traced here: 228 us
  starting transfers between devices  107 us (47%)
  waiting for transfers between devices  79.3 us (35%)
  Pallas kernels  22.3 us (10%)
  other arithmetic  14.3 us (6%)
  local copies, waits for them, and re-layouts  3.94 us (2%)
    ppermute x8, starting transfers between devices, from_behind(): lax.ppermute(value, axis, [(source, source + steps) for source in range(f...  46.6 us
    ppermute x8, starting transfers between devices, pairs_permute(): lax.ppermute(value, axis, [(i, j) for i, j in pairs if 0 <= j < count])  42.6 us
    ppermute x8, waiting for transfers between devices, from_behind(): lax.ppermute(value, axis, [(source, source + steps) for source in range(f...  40.8 us
    ppermute x9, waiting for transfers between devices, all_sum(): lax.ppermute(value, axis, [(i, i ^ bit) for i in range(count)])  38.2 us
    pallas_call x2, Pallas kernels, attention(): pl.pallas_call(attention_kernel, grid_spec=grid_spec, out_shape=[f32] * 3...  22.3 us
    ppermute x9, starting transfers between devices, all_sum(): lax.ppermute(value, axis, [(i, i ^ bit) for i in range(count)])  17.8 us
  transfers between devices with their start and end apart: 25, of which 13 were waited for; matrix products, arithmetic and copies ran while one was open for 5% of the time, Pallas kernels for 10%

profile of v9, /device:TPU:32, one launch (start us, length us, event | category | flops | bytes accessed | tf_op | source)
XLA Modules:
  0.0 228.3 jit_solution(8107613888288713106)
XLA Ops:
  0.6 1.4 fusion.23
  2.0 1.3 fusion.20.k_ref
  3.4 1.0 pad_maximum_fusion.1
  4.4 3.4 %collective-permute-start.2 = (bf16[2,128,1536]{2,1,0:T(8,128)(2,1)}, bf16[2,128,1536]{2,1,0:T(8,128)(2,1)}, u32[]{:S(2)}, u32[]{:S(2)}) collective-permute-start(bf16[2,128,1536]{2,1,0:T(8,128)(2,1)} %pad_maximum_fusion.1), channel_id=1, source_target_pairs={{0,4},{4,8},{8,12},{12,16},{16,20},{20,24},{24,28},{28,32},{32,36}... | collective-permute-start | bytes 2359304 | tf_op jit(solution)/shard_map/ppermute | solution.py:31
  7.8 11.4 %collective-permute-start.1 = (bf16[2,128,1536]{2,1,0:T(8,128)(2,1)}, bf16[2,128,1536]{2,1,0:T(8,128)(2,1)S(1)}, u32[]{:S(2)}, u32[]{:S(2)}) collective-permute-start(bf16[2,128,1536]{2,1,0:T(8,128)(2,1)} %pad_maximum_fusion.1), channel_id=1, source_target_pairs={{2,0},{4,2},{6,4},{8,6},{10,8},{12,10},{14,12},{16,14},{18,16},{20... | collective-permute-start | bytes 2359304 | tf_op jit(solution)/shard_map/ppermute | solution.py:26
  19.2 1.9 collective-permute-start
  22.2 29.0 %collective-permute-done.1.refs_1_ = bf16[2,128,1536]{2,1,0:T(8,128)(2,1)S(1)} collective-permute-done((bf16[2,128,1536]{2,1,0:T(8,128)(2,1)}, bf16[2,128,1536]{2,1,0:T(8,128)(2,1)S(1)}, u32[]{:S(2)}, u32[]{:S(2)}) %collective-permute-start.1) | collective-permute-done | bytes 786464 | tf_op jit(solution)/shard_map/ppermute | solution.py:26
  51.3 2.7 %collective-permute-done.refs_0_ = bf16[2,128,1536]{2,1,0:T(8,128)(2,1)S(1)} collective-permute-done((bf16[2,128,1536]{2,1,0:T(8,128)(2,1)}, bf16[2,128,1536]{2,1,0:T(8,128)(2,1)S(1)}, u32[]{:S(2)}, u32[]{:S(2)}) %collective-permute-start) | collective-permute-done | bytes 786464 | tf_op jit(solution)/shard_map/ppermute | solution.py:26
  54.1 1.9 collective-permute-start.3
  56.8 1.1 fusion.12.q_ref
  58.2 1.0 copy-done.14
  59.2 7.3 %collective-permute-start.5 = (bf16[2,128,1024]{2,1,0:T(8,128)(2,1)}, bf16[2,128,1024]{2,1,0:T(8,128)(2,1)S(1)}, u32[]{:S(2)}, u32[]{:S(2)}) collective-permute-start(bf16[2,128,1024]{2,1,0:T(8,128)(2,1)} %pad_maximum_fusion.3), channel_id=1, source_target_pairs={{2,0},{4,2},{6,4},{8,6},{10,8},{12,10},{14,12},{16,14},{18,16},{20... | collective-permute-start | bytes 1572872 | tf_op jit(solution)/shard_map/ppermute | solution.py:26
  66.5 1.9 collective-permute-start.4
  68.5 12.9 %shard_map.110 = (f32[128,1536]{1,0:T(8,128)}, f32[128,1536]{1,0:T(8,128)}, f32[128,1536]{1,0:T(8,128)}, bf16[2,128,1536]{2,1,0:T(8,128)(2,1)}, bf16[2,128,1536]...) custom-call(s32[1]{0:T(128)} %bitcast.1.odd_ref, f32[1,640]{1,0:T(1,128)} %bitcast.137, ...), custom_call_target="tpu_custom_call" | custom-call | flops 1509949440 | bytes 7077888 | tf_op jit(solution)/shard_map/pallas_call | solution.py:161
  81.3 2.1 collective-permute-start.8
  83.4 1.9 collective-permute-start.6
  85.3 10.4 %collective-permute-start.11 = (bf16[2,128,1536]{2,1,0:T(8,128)(2,1)}, bf16[2,128,1536]{2,1,0:T(8,128)(2,1)S(1)}, u32[]{:S(2)}, u32[]{:S(2)}) collective-permute-start(bf16[2,128,1536]{2,1,0:T(8,128)(2,1)} %get-tuple-element.27), channel_id=1, source_target_pairs={{2,6},{6,10},{10,14},{14,18},{18,22},{22,26},{26,30},{30,34},{34,3... | collective-permute-start | bytes 2359304 | tf_op jit(solution)/shard_map/ppermute | solution.py:31
  95.8 1.9 collective-permute-start.7
  97.8 1.6 fusion.29
  99.4 2.4 %collective-permute-start.9 = (bf16[2,128,1536]{2,1,0:T(8,128)(2,1)}, bf16[2,128,1536]{2,1,0:T(8,128)(2,1)S(1)}, u32[]{:S(2)}, u32[]{:S(2)}) collective-permute-start(bf16[2,128,1536]{2,1,0:T(8,128)(2,1)} %get-tuple-element.43), channel_id=1, source_target_pairs={{0,2},{2,4},{4,6},{6,8},{8,10},{10,12},{12,14},{14,16},{16,18},{18... | collective-permute-start | bytes 2359304 | tf_op jit(solution)/shard_map/ppermute | solution.py:26
  101.8 9.6 %collective-permute-start.10 = (bf16[2,128,1536]{2,1,0:T(8,128)(2,1)}, bf16[2,128,1536]{2,1,0:T(8,128)(2,1)}, u32[]{:S(2)}, u32[]{:S(2)}) collective-permute-start(bf16[2,128,1536]{2,1,0:T(8,128)(2,1)} %get-tuple-element.44), channel_id=1, source_target_pairs={{2,0},{4,2},{6,4},{8,6},{10,8},{12,10},{14,12},{16,14},{18,16},{20... | collective-permute-start | bytes 2359304 | tf_op jit(solution)/shard_map/ppermute | solution.py:26
  111.4 9.5 %shard_map.111 = (f32[128,1024]{1,0:T(8,128)}, f32[128,1024]{1,0:T(8,128)}, f32[128,1024]{1,0:T(8,128)}, bf16[2,128,1024]{2,1,0:T(8,128)(2,1)}, bf16[2,128,1024]...) custom-call(s32[1]{0:T(128)} %bitcast.1.odd_ref, f32[1,640]{1,0:T(1,128)} %bitcast.138, ...), custom_call_target="tpu_custom_call" | custom-call | flops 1006632960 | bytes 4718592 | tf_op jit(solution)/shard_map/pallas_call | solution.py:161
  120.9 10.5 %collective-permute-start.12 = (bf16[2,128,1024]{2,1,0:T(8,128)(2,1)}, bf16[2,128,1024]{2,1,0:T(8,128)(2,1)S(1)}, u32[]{:S(2)}, u32[]{:S(2)}) collective-permute-start(bf16[2,128,1024]{2,1,0:T(8,128)(2,1)} %get-tuple-element.30), channel_id=1, source_target_pairs={{0,2},{2,0},{4,6},{6,4},{8,10},{10,8},{12,14},{14,12},{16,18},{18,... | collective-permute-start | bytes 1572872 | tf_op jit(solution)/shard_map/ppermute | solution.py:31
  131.5 10.6 %collective-permute-start.15 = (bf16[2,128,1024]{2,1,0:T(8,128)(2,1)S(1)}, bf16[2,128,1024]{2,1,0:T(8,128)(2,1)S(1)}, u32[]{:S(2)}, u32[]{:S(2)}) collective-permute-start(bf16[2,128,1024]{2,1,0:T(8,128)(2,1)S(1)} %copy-done.23), channel_id=1, source_target_pairs={{2,6},{6,10},{10,14},{14,18},{18,22},{22,26},{26,30},{30,34},{34,3... | collective-permute-start | bytes 1572872 | tf_op jit(solution)/shard_map/ppermute | solution.py:31
  143.7 2.1 collective-permute-start.13
  145.7 10.0 %collective-permute-start.14 = (bf16[2,128,1024]{2,1,0:T(8,128)(2,1)S(1)}, bf16[2,128,1024]{2,1,0:T(8,128)(2,1)S(1)}, u32[]{:S(2)}, u32[]{:S(2)}) collective-permute-start(bf16[2,128,1024]{2,1,0:T(8,128)(2,1)S(1)} %get-tuple-element.46), channel_id=1, source_target_pairs={{2,0},{4,2},{6,4},{8,6},{10,8},{12,10},{14,12},{16,14},{18,16},{20... | collective-permute-start | bytes 1572872 | tf_op jit(solution)/shard_map/ppermute | solution.py:26
  155.8 1.7 fusion.36
  157.5 9.0 %collective-permute-done.13 = bf16[2,128,1024]{2,1,0:T(8,128)(2,1)S(1)} collective-permute-done((bf16[2,128,1024]{2,1,0:T(8,128)(2,1)S(1)}, bf16[2,128,1024]{2,1,0:T(8,128)(2,1)S(1)}, u32[]{:S(2)}, u32[]{:S(2)}) %collective-permute-start.13) | collective-permute-done | bytes 524320 | tf_op jit(solution)/shard_map/ppermute | solution.py:26
  168.1 1.9 collective-permute-start.16
  170.0 3.7 %collective-permute-done.16 = f32[5120]{0:T(1024)S(1)} collective-permute-done((f32[5120]{0:T(1024)S(1)}, f32[5120]{0:T(1024)S(1)}, u32[]{:S(2)}, u32[]{:S(2)}) %collective-permute-start.16) | collective-permute-done | bytes 20512 | tf_op jit(solution)/shard_map/ppermute | solution.py:65
  173.8 1.9 collective-permute-start.17
  175.7 1.2 collective-permute-done.17
  176.8 1.9 collective-permute-start.18
  178.8 3.7 %collective-permute-done.18 = f32[5120]{0:T(1024)S(1)} collective-permute-done((f32[5120]{0:T(1024)S(1)}, f32[5120]{0:T(1024)S(1)}, u32[]{:S(2)}, u32[]{:S(2)}) %collective-permute-start.18) | collective-permute-done | bytes 20512 | tf_op jit(solution)/shard_map/ppermute | solution.py:65
  182.5 1.9 collective-permute-start.19
  184.4 5.3 %collective-permute-done.19 = f32[5120]{0:T(1024)S(1)} collective-permute-done((f32[5120]{0:T(1024)S(1)}, f32[5120]{0:T(1024)S(1)}, u32[]{:S(2)}, u32[]{:S(2)}) %collective-permute-start.19) | collective-permute-done | bytes 20512 | tf_op jit(solution)/shard_map/ppermute | solution.py:65
  189.7 1.9 collective-permute-start.20
  191.6 3.7 %collective-permute-done.20 = f32[5120]{0:T(1024)S(1)} collective-permute-done((f32[5120]{0:T(1024)S(1)}, f32[5120]{0:T(1024)S(1)}, u32[]{:S(2)}, u32[]{:S(2)}) %collective-permute-start.20) | collective-permute-done | bytes 20512 | tf_op jit(solution)/shard_map/ppermute | solution.py:65
  195.3 1.9 collective-permute-start.21
  197.3 1.3 fusion.19
  198.5 3.4 %collective-permute-done.21 = f32[5120]{0:T(1024)S(1)} collective-permute-done((f32[5120]{0:T(1024)S(1)}, f32[5120]{0:T(1024)S(1)}, u32[]{:S(2)}, u32[]{:S(2)}) %collective-permute-start.21) | collective-permute-done | bytes 20512 | tf_op jit(solution)/shard_map/ppermute | solution.py:65
  201.9 1.9 collective-permute-start.22
  203.8 7.6 %collective-permute-done.22 = f32[5120]{0:T(1024)S(1)} collective-permute-done((f32[5120]{0:T(1024)S(1)}, f32[5120]{0:T(1024)S(1)}, u32[]{:S(2)}, u32[]{:S(2)}) %collective-permute-start.22) | collective-permute-done | bytes 20512 | tf_op jit(solution)/shard_map/ppermute | solution.py:65
  211.5 2.6 %collective-permute-start.23 = (f32[5120]{0:T(1024)S(1)}, f32[5120]{0:T(1024)S(1)}, u32[]{:S(2)}, u32[]{:S(2)}) collective-permute-start(f32[5120]{0:T(1024)S(1)} %add.124), channel_id=1, source_target_pairs={{0,128},{2,130},{4,132},{6,134},{8,136},{10,138},{12,140},{14,142}... | collective-permute-start | bytes 61448 | tf_op jit(solution)/shard_map/ppermute | solution.py:65
  214.1 1.2 fusion.27
  215.3 2.8 %collective-permute-done.23 = f32[5120]{0:T(1024)S(1)} collective-permute-done((f32[5120]{0:T(1024)S(1)}, f32[5120]{0:T(1024)S(1)}, u32[]{:S(2)}, u32[]{:S(2)}) %collective-permute-start.23) | collective-permute-done | bytes 20512 | tf_op jit(solution)/shard_map/ppermute | solution.py:65
  218.1 1.9 collective-permute-start.24
  220.9 6.8 %collective-permute-done.24 = f32[5120]{0:T(1024)S(1)} collective-permute-done((f32[5120]{0:T(1024)S(1)}, f32[5120]{0:T(1024)S(1)}, u32[]{:S(2)}, u32[]{:S(2)}) %collective-permute-start.24) | collective-permute-done | bytes 20512 | tf_op jit(solution)/shard_map/ppermute | solution.py:65
  (94 shorter events, 7.1 us)
Async XLA Ops:
  0.6 2.7 %copy-start.3 = (bf16[1,128,2560]{2,1,0:T(8,128)(2,1)S(1)}, bf16[1,128,2560]{2,1,0:T(8,128)(2,1)}, u32[]{:S(2)}) copy-start(bf16[1,128,2560]{2,1,0:T(8,128)(2,1)} %param.9) | copy-start | bytes 1966084
  3.3 18.8 %copy-start.2 = (bf16[128,2560]{1,0:T(8,128)(2,1)}, bf16[128,2560]{1,0:T(8,128)(2,1)S(1)}, u32[]{:S(2)}) copy-start(bf16[128,2560]{1,0:T(8,128)(2,1)S(1)} %fusion.20.k_ref) | copy-start | bytes 1966084
  3.4 17.8 %copy-start.24 = (s32[1,4]{1,0:T(1,128)S(1)}, s32[1,4]{1,0:T(1,128)}, u32[]{:S(2)}) copy-start(s32[1,4]{1,0:T(1,128)} %param.13) | copy-start | bytes 52
  3.4 18.6 %copy-start = (bf16[1,128,2560]{2,1,0:T(8,128)(2,1)S(1)}, bf16[1,128,2560]{2,1,0:T(8,128)(2,1)}, u32[]{:S(2)}) copy-start(bf16[1,128,2560]{2,1,0:T(8,128)(2,1)} %param.7) | copy-start | bytes 1966084
  4.4 53.5 %collective-permute-start.2 = (bf16[2,128,1536]{2,1,0:T(8,128)(2,1)}, bf16[2,128,1536]{2,1,0:T(8,128)(2,1)}, u32[]{:S(2)}, u32[]{:S(2)}) collective-permute-start(bf16[2,128,1536]{2,1,0:T(8,128)(2,1)} %pad_maximum_fusion.1), channel_id=1, source_target_pairs={{0,4},{4,8},{8,12},{12,16},{16,20},{20,24},{24,28},{28,32},{32,36}... | collective-permute-start | bytes 2359304 | tf_op jit(solution)/shard_map/ppermute | solution.py:31
  7.8 43.5 %collective-permute-start.1 = (bf16[2,128,1536]{2,1,0:T(8,128)(2,1)}, bf16[2,128,1536]{2,1,0:T(8,128)(2,1)S(1)}, u32[]{:S(2)}, u32[]{:S(2)}) collective-permute-start(bf16[2,128,1536]{2,1,0:T(8,128)(2,1)} %pad_maximum_fusion.1), channel_id=1, source_target_pairs={{2,0},{4,2},{6,4},{8,6},{10,8},{12,10},{14,12},{16,14},{18,16},{20... | collective-permute-start | bytes 2359304 | tf_op jit(solution)/shard_map/ppermute | solution.py:26
  19.2 34.7 %collective-permute-start = (bf16[2,128,1536]{2,1,0:T(8,128)(2,1)}, bf16[2,128,1536]{2,1,0:T(8,128)(2,1)S(1)}, u32[]{:S(2)}, u32[]{:S(2)}) collective-permute-start(bf16[2,128,1536]{2,1,0:T(8,128)(2,1)} %pad_maximum_fusion.1), channel_id=1, source_target_pairs={{0,2},{2,4},{4,6},{6,8},{8,10},{10,12},{12,14},{14,16},{16,18},{18... | collective-permute-start | bytes 2359304 | tf_op jit(solution)/shard_map/ppermute | solution.py:26
  22.2 34.7 %copy-start.21 = (f32[128]{0:T(128)}, f32[128]{0:T(128)S(1)}, u32[]{:S(2)}) copy-start(f32[128]{0:T(128)S(1)} %add_rsqrt_fusion.1) | copy-start | bytes 1540
  22.2 34.6 %copy-start.19 = (f32[2560]{0:T(1024)S(1)}, f32[2560]{0:T(1024)}, u32[]{:S(2)}) copy-start(f32[2560]{0:T(1024)} %param.11) | copy-start | bytes 30724
  51.3 5.6 %copy-start.5 = (bf16[2,128,1536]{2,1,0:T(8,128)(2,1)}, bf16[2,128,1536]{2,1,0:T(8,128)(2,1)S(1)}, u32[]{:S(2)}) copy-start(bf16[2,128,1536]{2,1,0:T(8,128)(2,1)S(1)} %collective-permute-done.1.refs_1_) | copy-start | bytes 2359300
  54.0 2.9 %copy-start.6 = (bf16[2,128,1536]{2,1,0:T(8,128)(2,1)}, bf16[2,128,1536]{2,1,0:T(8,128)(2,1)S(1)}, u32[]{:S(2)}) copy-start(bf16[2,128,1536]{2,1,0:T(8,128)(2,1)S(1)} %collective-permute-done.refs_0_) | copy-start | bytes 2359300
  54.1 4.2 %collective-permute-start.3 = (bf16[2,128,1536]{2,1,0:T(8,128)(2,1)S(1)}, bf16[2,128,1536]{2,1,0:T(8,128)(2,1)S(1)}, u32[]{:S(2)}, u32[]{:S(2)}) collective-permute-start(bf16[2,128,1536]{2,1,0:T(8,128)(2,1)S(1)} %broadcast_select_fusion), channel_id=1, source_target_pairs={{0,2},{2,0},{4,6},{6,4},{8,10},{10,8},{12,14},{14,12},{16,18},{18,... | collective-permute-start | bytes 2359304 | tf_op jit(solution)/shard_map/ppermute | solution.py:31
  59.2 36.5 %collective-permute-start.5 = (bf16[2,128,1024]{2,1,0:T(8,128)(2,1)}, bf16[2,128,1024]{2,1,0:T(8,128)(2,1)S(1)}, u32[]{:S(2)}, u32[]{:S(2)}) collective-permute-start(bf16[2,128,1024]{2,1,0:T(8,128)(2,1)} %pad_maximum_fusion.3), channel_id=1, source_target_pairs={{2,0},{4,2},{6,4},{8,6},{10,8},{12,10},{14,12},{16,14},{18,16},{20... | collective-permute-start | bytes 1572872 | tf_op jit(solution)/shard_map/ppermute | solution.py:26
  66.5 29.2 %collective-permute-start.4 = (bf16[2,128,1024]{2,1,0:T(8,128)(2,1)}, bf16[2,128,1024]{2,1,0:T(8,128)(2,1)S(1)}, u32[]{:S(2)}, u32[]{:S(2)}) collective-permute-start(bf16[2,128,1024]{2,1,0:T(8,128)(2,1)} %pad_maximum_fusion.3), channel_id=1, source_target_pairs={{0,2},{2,4},{4,6},{6,8},{8,10},{10,12},{12,14},{14,16},{16,18},{18... | collective-permute-start | bytes 1572872 | tf_op jit(solution)/shard_map/ppermute | solution.py:26
  81.3 16.4 %copy-start.12 = (bf16[2,128,1536]{2,1,0:T(8,128)(2,1)S(1)}, bf16[2,128,1536]{2,1,0:T(8,128)(2,1)}, u32[]{:S(2)}) copy-start(bf16[2,128,1536]{2,1,0:T(8,128)(2,1)} %get-tuple-element.26) | copy-start | bytes 2359300
  81.3 16.4 %copy-start.13 = (bf16[2,128,1536]{2,1,0:T(8,128)(2,1)S(1)}, bf16[2,128,1536]{2,1,0:T(8,128)(2,1)}, u32[]{:S(2)}) copy-start(bf16[2,128,1536]{2,1,0:T(8,128)(2,1)} %get-tuple-element.24) | copy-start | bytes 2359300
  81.3 16.4 %collective-permute-start.8 = (bf16[2,128,1536]{2,1,0:T(8,128)(2,1)}, bf16[2,128,1536]{2,1,0:T(8,128)(2,1)S(1)}, u32[]{:S(2)}, u32[]{:S(2)}) collective-permute-start(bf16[2,128,1536]{2,1,0:T(8,128)(2,1)} %get-tuple-element.25), channel_id=1, source_target_pairs={{0,2},{2,0},{4,6},{6,4},{8,10},{10,8},{12,14},{14,12},{16,18},{18,... | collective-permute-start | bytes 2359304 | tf_op jit(solution)/shard_map/ppermute | solution.py:31
  83.4 28.0 %collective-permute-start.6 = (bf16[2,128,1024]{2,1,0:T(8,128)(2,1)}, bf16[2,128,1024]{2,1,0:T(8,128)(2,1)}, u32[]{:S(2)}, u32[]{:S(2)}) collective-permute-start(bf16[2,128,1024]{2,1,0:T(8,128)(2,1)} %pad_maximum_fusion.3), channel_id=1, source_target_pairs={{0,4},{4,8},{8,12},{12,16},{16,20},{20,24},{24,28},{28,32},{32,36}... | collective-permute-start | bytes 1572872 | tf_op jit(solution)/shard_map/ppermute | solution.py:31
  85.3 60.4 %collective-permute-start.11 = (bf16[2,128,1536]{2,1,0:T(8,128)(2,1)}, bf16[2,128,1536]{2,1,0:T(8,128)(2,1)S(1)}, u32[]{:S(2)}, u32[]{:S(2)}) collective-permute-start(bf16[2,128,1536]{2,1,0:T(8,128)(2,1)} %get-tuple-element.27), channel_id=1, source_target_pairs={{2,6},{6,10},{10,14},{14,18},{18,22},{22,26},{26,30},{30,34},{34,3... | collective-permute-start | bytes 2359304 | tf_op jit(solution)/shard_map/ppermute | solution.py:31
  95.7 3.7 %copy-start.8 = (bf16[2,128,1024]{2,1,0:T(8,128)(2,1)}, bf16[2,128,1024]{2,1,0:T(8,128)(2,1)S(1)}, u32[]{:S(2)}) copy-start(bf16[2,128,1024]{2,1,0:T(8,128)(2,1)S(1)} %collective-permute-done.5.refs_1_) | copy-start | bytes 1572868
  95.7 3.7 %copy-start.9 = (bf16[2,128,1024]{2,1,0:T(8,128)(2,1)}, bf16[2,128,1024]{2,1,0:T(8,128)(2,1)S(1)}, u32[]{:S(2)}) copy-start(bf16[2,128,1024]{2,1,0:T(8,128)(2,1)S(1)} %collective-permute-done.4.refs_0_) | copy-start | bytes 1572868
  95.8 15.6 %collective-permute-start.7 = (bf16[2,128,1024]{2,1,0:T(8,128)(2,1)S(1)}, bf16[2,128,1024]{2,1,0:T(8,128)(2,1)}, u32[]{:S(2)}, u32[]{:S(2)}) collective-permute-start(bf16[2,128,1024]{2,1,0:T(8,128)(2,1)S(1)} %broadcast_select_fusion.1), channel_id=1, source_target_pairs={{0,2},{2,0},{4,6},{6,4},{8,10},{10,8},{12,14},{14,12},{16,18},{18,... | collective-permute-start | bytes 1572872 | tf_op jit(solution)/shard_map/ppermute | solution.py:31
  99.4 56.3 %collective-permute-start.9 = (bf16[2,128,1536]{2,1,0:T(8,128)(2,1)}, bf16[2,128,1536]{2,1,0:T(8,128)(2,1)S(1)}, u32[]{:S(2)}, u32[]{:S(2)}) collective-permute-start(bf16[2,128,1536]{2,1,0:T(8,128)(2,1)} %get-tuple-element.43), channel_id=1, source_target_pairs={{0,2},{2,4},{4,6},{6,8},{8,10},{10,12},{12,14},{14,16},{16,18},{18... | collective-permute-start | bytes 2359304 | tf_op jit(solution)/shard_map/ppermute | solution.py:26
  101.8 29.6 %copy-start.4 = (f32[128,1536]{1,0:T(8,128)S(1)}, f32[128,1536]{1,0:T(8,128)}, u32[]{:S(2)}) copy-start(f32[128,1536]{1,0:T(8,128)} %get-tuple-element.20) | copy-start | bytes 2359300
  101.8 53.9 %collective-permute-start.10 = (bf16[2,128,1536]{2,1,0:T(8,128)(2,1)}, bf16[2,128,1536]{2,1,0:T(8,128)(2,1)}, u32[]{:S(2)}, u32[]{:S(2)}) collective-permute-start(bf16[2,128,1536]{2,1,0:T(8,128)(2,1)} %get-tuple-element.44), channel_id=1, source_target_pairs={{2,0},{4,2},{6,4},{8,6},{10,8},{12,10},{14,12},{16,14},{18,16},{20... | collective-permute-start | bytes 2359304 | tf_op jit(solution)/shard_map/ppermute | solution.py:26
  120.9 10.6 %copy-start.23 = (bf16[2,128,1024]{2,1,0:T(8,128)(2,1)S(1)}, bf16[2,128,1024]{2,1,0:T(8,128)(2,1)}, u32[]{:S(2)}) copy-start(bf16[2,128,1024]{2,1,0:T(8,128)(2,1)} %get-tuple-element.32) | copy-start | bytes 1572868
  120.9 21.2 %copy-start.7 = (f32[128,1024]{1,0:T(8,128)S(1)}, f32[128,1024]{1,0:T(8,128)}, u32[]{:S(2)}) copy-start(f32[128,1024]{1,0:T(8,128)} %get-tuple-element.22) | copy-start | bytes 1572868
  120.9 21.7 %collective-permute-start.12 = (bf16[2,128,1024]{2,1,0:T(8,128)(2,1)}, bf16[2,128,1024]{2,1,0:T(8,128)(2,1)S(1)}, u32[]{:S(2)}, u32[]{:S(2)}) collective-permute-start(bf16[2,128,1024]{2,1,0:T(8,128)(2,1)} %get-tuple-element.30), channel_id=1, source_target_pairs={{0,2},{2,0},{4,6},{6,4},{8,10},{10,8},{12,14},{14,12},{16,18},{18,... | collective-permute-start | bytes 1572872 | tf_op jit(solution)/shard_map/ppermute | solution.py:31
  131.4 10.8 %copy-start.22 = (f32[128]{0:T(128)S(1)}, f32[128]{0:T(128)}, u32[]{:S(2)}) copy-start(f32[128]{0:T(128)} %copy-done.21) | copy-start | bytes 1540
  131.5 26.0 %collective-permute-start.15 = (bf16[2,128,1024]{2,1,0:T(8,128)(2,1)S(1)}, bf16[2,128,1024]{2,1,0:T(8,128)(2,1)S(1)}, u32[]{:S(2)}, u32[]{:S(2)}) collective-permute-start(bf16[2,128,1024]{2,1,0:T(8,128)(2,1)S(1)} %copy-done.23), channel_id=1, source_target_pairs={{2,6},{6,10},{10,14},{14,18},{18,22},{22,26},{26,30},{30,34},{34,3... | collective-permute-start | bytes 1572872 | tf_op jit(solution)/shard_map/ppermute | solution.py:31
  142.1 1.2 copy-start.18
  143.3 12.4 %copy-start.10 = (f32[128,1536]{1,0:T(8,128)S(1)}, f32[128,1536]{1,0:T(8,128)}, u32[]{:S(2)}) copy-start(f32[128,1536]{1,0:T(8,128)} %get-tuple-element.23) | copy-start | bytes 2359300
  143.3 12.4 %copy-start.11 = (f32[128,1536]{1,0:T(8,128)S(1)}, f32[128,1536]{1,0:T(8,128)}, u32[]{:S(2)}) copy-start(f32[128,1536]{1,0:T(8,128)} %get-tuple-element.33) | copy-start | bytes 2359300
  143.7 22.8 %collective-permute-start.13 = (bf16[2,128,1024]{2,1,0:T(8,128)(2,1)S(1)}, bf16[2,128,1024]{2,1,0:T(8,128)(2,1)S(1)}, u32[]{:S(2)}, u32[]{:S(2)}) collective-permute-start(bf16[2,128,1024]{2,1,0:T(8,128)(2,1)S(1)} %get-tuple-element.45), channel_id=1, source_target_pairs={{0,2},{2,4},{4,6},{6,8},{8,10},{10,12},{12,14},{14,16},{16,18},{18... | collective-permute-start | bytes 1572872 | tf_op jit(solution)/shard_map/ppermute | solution.py:26
  145.7 20.8 %collective-permute-start.14 = (bf16[2,128,1024]{2,1,0:T(8,128)(2,1)S(1)}, bf16[2,128,1024]{2,1,0:T(8,128)(2,1)S(1)}, u32[]{:S(2)}, u32[]{:S(2)}) collective-permute-start(bf16[2,128,1024]{2,1,0:T(8,128)(2,1)S(1)} %get-tuple-element.46), channel_id=1, source_target_pairs={{2,0},{4,2},{6,4},{8,6},{10,8},{12,10},{14,12},{16,14},{18,16},{20... | collective-permute-start | bytes 1572872 | tf_op jit(solution)/shard_map/ppermute | solution.py:26
  155.8 10.8 %copy-start.15 = (f32[128,1024]{1,0:T(8,128)S(1)}, f32[128,1024]{1,0:T(8,128)}, u32[]{:S(2)}) copy-start(f32[128,1024]{1,0:T(8,128)} %get-tuple-element.28) | copy-start | bytes 1572868
  155.8 10.7 %copy-start.16 = (f32[128,1024]{1,0:T(8,128)S(1)}, f32[128,1024]{1,0:T(8,128)}, u32[]{:S(2)}) copy-start(f32[128,1024]{1,0:T(8,128)} %get-tuple-element.34) | copy-start | bytes 1572868
  166.5 1.1 copy-start.1
  166.5 1.1 copy-start.20
  168.1 5.7 %collective-permute-start.16 = (f32[5120]{0:T(1024)S(1)}, f32[5120]{0:T(1024)S(1)}, u32[]{:S(2)}, u32[]{:S(2)}) collective-permute-start(f32[5120]{0:T(1024)S(1)} %pad_maximum_fusion.4), channel_id=1, source_target_pairs={{0,1},{1,0},{2,3},{3,2},{4,5},{5,4},{6,7},{7,6},{8,9},{9,8},{10,11... | collective-permute-start | bytes 61448 | tf_op jit(solution)/shard_map/ppermute | solution.py:65
  173.8 3.1 %collective-permute-start.17 = (f32[5120]{0:T(1024)S(1)}, f32[5120]{0:T(1024)S(1)}, u32[]{:S(2)}, u32[]{:S(2)}) collective-permute-start(f32[5120]{0:T(1024)S(1)} %fusion.39), channel_id=1, source_target_pairs={{0,2},{2,0},{4,6},{6,4},{8,10},{10,8},{12,14},{14,12},{16,18},{18,... | collective-permute-start | bytes 61448 | tf_op jit(solution)/shard_map/ppermute | solution.py:65
  176.8 5.7 %collective-permute-start.18 = (f32[5120]{0:T(1024)S(1)}, f32[5120]{0:T(1024)S(1)}, u32[]{:S(2)}, u32[]{:S(2)}) collective-permute-start(f32[5120]{0:T(1024)S(1)} %add.119), channel_id=1, source_target_pairs={{0,4},{2,6},{4,0},{6,2},{8,12},{10,14},{12,8},{14,10},{16,20},{18,... | collective-permute-start | bytes 61448 | tf_op jit(solution)/shard_map/ppermute | solution.py:65
  182.5 7.2 %collective-permute-start.19 = (f32[5120]{0:T(1024)S(1)}, f32[5120]{0:T(1024)S(1)}, u32[]{:S(2)}, u32[]{:S(2)}) collective-permute-start(f32[5120]{0:T(1024)S(1)} %add.120), channel_id=1, source_target_pairs={{0,8},{2,10},{4,12},{6,14},{8,0},{10,2},{12,4},{14,6},{16,24},{18,... | collective-permute-start | bytes 61448 | tf_op jit(solution)/shard_map/ppermute | solution.py:65
  189.7 5.7 %collective-permute-start.20 = (f32[5120]{0:T(1024)S(1)}, f32[5120]{0:T(1024)S(1)}, u32[]{:S(2)}, u32[]{:S(2)}) collective-permute-start(f32[5120]{0:T(1024)S(1)} %add.121), channel_id=1, source_target_pairs={{0,16},{2,18},{4,20},{6,22},{8,24},{10,26},{12,28},{14,30},{16,0},... | collective-permute-start | bytes 61448 | tf_op jit(solution)/shard_map/ppermute | solution.py:65
  195.3 6.6 %collective-permute-start.21 = (f32[5120]{0:T(1024)S(1)}, f32[5120]{0:T(1024)S(1)}, u32[]{:S(2)}, u32[]{:S(2)}) collective-permute-start(f32[5120]{0:T(1024)S(1)} %add.122), channel_id=1, source_target_pairs={{0,32},{2,34},{4,36},{6,38},{8,40},{10,42},{12,44},{14,46},{16,48}... | collective-permute-start | bytes 61448 | tf_op jit(solution)/shard_map/ppermute | solution.py:65
  201.9 9.6 %collective-permute-start.22 = (f32[5120]{0:T(1024)S(1)}, f32[5120]{0:T(1024)S(1)}, u32[]{:S(2)}, u32[]{:S(2)}) collective-permute-start(f32[5120]{0:T(1024)S(1)} %add.123), channel_id=1, source_target_pairs={{0,64},{2,66},{4,68},{6,70},{8,72},{10,74},{12,76},{14,78},{16,80}... | collective-permute-start | bytes 61448 | tf_op jit(solution)/shard_map/ppermute | solution.py:65
  211.5 6.6 %collective-permute-start.23 = (f32[5120]{0:T(1024)S(1)}, f32[5120]{0:T(1024)S(1)}, u32[]{:S(2)}, u32[]{:S(2)}) collective-permute-start(f32[5120]{0:T(1024)S(1)} %add.124), channel_id=1, source_target_pairs={{0,128},{2,130},{4,132},{6,134},{8,136},{10,138},{12,140},{14,142}... | collective-permute-start | bytes 61448 | tf_op jit(solution)/shard_map/ppermute | solution.py:65
  218.1 9.6 %collective-permute-start.24 = (f32[5120]{0:T(1024)S(1)}, f32[5120]{0:T(1024)S(1)}, u32[]{:S(2)}, u32[]{:S(2)}) collective-permute-start(f32[5120]{0:T(1024)S(1)} %add.125), channel_id=1, source_target_pairs={{0,256},{2,258},{4,260},{6,262},{8,264},{10,266},{12,268},{14,270}... | collective-permute-start | bytes 61448 | tf_op jit(solution)/shard_map/ppermute | solution.py:65
  (2 other events, 2.0 us)

commit v10 on v9

--- a/solution.py
+++ b/solution.py
@@ -10,8 +10,8 @@
 
 HEAD = 128
 LEVELS = 2
-HEADS_PER_STEP = 4
-CHUNK_HEADS = (12, 8)
+HEADS_PER_STEP = 2
+CHUNK_HEADS = (14, 6)
 
 
 EPS = 1e-06

time: 229 us -> 242 us (1.057)
  the two profiles are of different devices: /device:TPU:32 before, /device:TPU:40 now
where the time goes in v10:
time: 242 us; the launch traced here: 241 us
  waiting for transfers between devices  109 us (45%)
  starting transfers between devices  92.6 us (38%)
  Pallas kernels  22.3 us (9%)
  other arithmetic  14.4 us (6%)
    ppermute x8, waiting for transfers between devices, from_behind(): lax.ppermute(value, axis, [(source, source + steps) for source in range(f...  64.9 us
    ppermute x8, starting transfers between devices, from_behind(): lax.ppermute(value, axis, [(source, source + steps) for source in range(f...  43.7 us
    ppermute x9, waiting for transfers between devices, all_sum(): lax.ppermute(value, axis, [(i, i ^ bit) for i in range(count)])  38.9 us
    ppermute x8, starting transfers between devices, pairs_permute(): lax.ppermute(value, axis, [(i, j) for i, j in pairs if 0 <= j < count])  31.7 us
    pallas_call x2, Pallas kernels, attention(): pl.pallas_call(attention_kernel, grid_spec=grid_spec, out_shape=[f32] * 3...  22.3 us
    ppermute x9, starting transfers between devices, all_sum(): lax.ppermute(value, axis, [(i, i ^ bit) for i in range(count)])  17.2 us
    ppermute x8, waiting for transfers between devices, pairs_permute(): lax.ppermute(value, axis, [(i, j) for i, j in pairs if 0 <= j < count])  4.94 us
  transfers between devices with their start and end apart: 25, of which 15 were waited for; matrix products, arithmetic and copies ran while one was open for 4% of the time, Pallas kernels for 9%

profile of v10, /device:TPU:40, one launch (start us, length us, event | category | flops | bytes accessed | tf_op | source)
XLA Modules:
  0.0 240.8 jit_solution(1738901347780806342)
XLA Ops:
  0.6 1.4 fusion.25
  2.0 1.3 fusion.22.k_ref
  3.5 13.4 %collective-permute-start.1 = (bf16[2,128,1792]{2,1,0:T(8,128)(2,1)S(1)}, bf16[2,128,1792]{2,1,0:T(8,128)(2,1)}, u32[]{:S(2)}, u32[]{:S(2)}) collective-permute-start(bf16[2,128,1792]{2,1,0:T(8,128)(2,1)S(1)} %pad_maximum_fusion.1), channel_id=1, source_target_pairs={{2,0},{4,2},{6,4},{8,6},{10,8},{12,10},{14,12},{16,14},{18,16},{20... | collective-permute-start | bytes 2752520 | tf_op jit(solution)/shard_map/ppermute | solution.py:26
  16.9 1.9 collective-permute-start
  18.9 1.9 collective-permute-start.2
  21.9 6.1 %collective-permute-done.1.refs_1_ = bf16[2,128,1792]{2,1,0:T(8,128)(2,1)} collective-permute-done((bf16[2,128,1792]{2,1,0:T(8,128)(2,1)S(1)}, bf16[2,128,1792]{2,1,0:T(8,128)(2,1)}, u32[]{:S(2)}, u32[]{:S(2)}) %collective-permute-start.1) | collective-permute-done | bytes 917536 | tf_op jit(solution)/shard_map/ppermute | solution.py:26
  28.1 38.1 %collective-permute-done.refs_0_ = bf16[2,128,1792]{2,1,0:T(8,128)(2,1)} collective-permute-done((bf16[2,128,1792]{2,1,0:T(8,128)(2,1)S(1)}, bf16[2,128,1792]{2,1,0:T(8,128)(2,1)}, u32[]{:S(2)}, u32[]{:S(2)}) %collective-permute-start) | collective-permute-done | bytes 917536 | tf_op jit(solution)/shard_map/ppermute | solution.py:26
  66.2 1.3 broadcast_select_fusion
  67.5 1.9 collective-permute-start.3
  70.5 1.4 collective-permute-done.3.refs_3_
  71.8 1.9 collective-permute-start.5
  73.8 2.4 collective-permute-start.4
  76.8 14.8 %shard_map.110 = (f32[128,1792]{1,0:T(8,128)}, f32[128,1792]{1,0:T(8,128)}, f32[128,1792]{1,0:T(8,128)}, bf16[2,128,1792]{2,1,0:T(8,128)(2,1)}, bf16[2,128,1792]...) custom-call(s32[1]{0:T(128)} %bitcast.1.odd_ref, f32[1,640]{1,0:T(1,128)} %bitcast.137, ...), custom_call_target="tpu_custom_call" | custom-call | flops 1761607680 | bytes 8257536 | tf_op jit(solution)/shard_map/pallas_call | solution.py:161
  91.6 3.3 %collective-permute-start.8 = (bf16[2,128,1792]{2,1,0:T(8,128)(2,1)}, bf16[2,128,1792]{2,1,0:T(8,128)(2,1)}, u32[]{:S(2)}, u32[]{:S(2)}) collective-permute-start(bf16[2,128,1792]{2,1,0:T(8,128)(2,1)} %get-tuple-element.25), channel_id=1, source_target_pairs={{0,2},{2,0},{4,6},{6,4},{8,10},{10,8},{12,14},{14,12},{16,18},{18,... | collective-permute-start | bytes 2752520 | tf_op jit(solution)/shard_map/ppermute | solution.py:31
  94.9 1.9 collective-permute-start.6
  96.9 8.2 %collective-permute-start.7 = (bf16[2,128,768]{2,1,0:T(8,128)(2,1)S(1)}, bf16[2,128,768]{2,1,0:T(8,128)(2,1)}, u32[]{:S(2)}, u32[]{:S(2)}) collective-permute-start(bf16[2,128,768]{2,1,0:T(8,128)(2,1)S(1)} %broadcast_select_fusion.1), channel_id=1, source_target_pairs={{0,2},{2,0},{4,6},{6,4},{8,10},{10,8},{12,14},{14,12},{16,18},{18,... | collective-permute-start | bytes 1179656 | tf_op jit(solution)/shard_map/ppermute | solution.py:31
  105.2 4.1 %collective-permute-start.11 = (bf16[2,128,1792]{2,1,0:T(8,128)(2,1)}, bf16[2,128,1792]{2,1,0:T(8,128)(2,1)}, u32[]{:S(2)}, u32[]{:S(2)}) collective-permute-start(bf16[2,128,1792]{2,1,0:T(8,128)(2,1)} %get-tuple-element.27), channel_id=1, source_target_pairs={{2,6},{6,10},{10,14},{14,18},{18,22},{22,26},{26,30},{30,34},{34,3... | collective-permute-start | bytes 2752520 | tf_op jit(solution)/shard_map/ppermute | solution.py:31
  109.3 3.6 %collective-permute-done.6.refs_2_ = bf16[2,128,768]{2,1,0:T(8,128)(2,1)} collective-permute-done((bf16[2,128,768]{2,1,0:T(8,128)(2,1)}, bf16[2,128,768]{2,1,0:T(8,128)(2,1)}, u32[]{:S(2)}, u32[]{:S(2)}) %collective-permute-start.6) | collective-permute-done | bytes 393248 | tf_op jit(solution)/shard_map/ppermute | solution.py:31
  112.9 7.5 %shard_map.111 = (f32[128,768]{1,0:T(8,128)}, f32[128,768]{1,0:T(8,128)}, f32[128,768]{1,0:T(8,128)}, bf16[2,128,768]{2,1,0:T(8,128)(2,1)}, bf16[2,128,768]{2,1,...) custom-call(s32[1]{0:T(128)} %bitcast.1.odd_ref, f32[1,640]{1,0:T(1,128)} %bitcast.138, ...), custom_call_target="tpu_custom_call" | custom-call | flops 754974720 | bytes 3538944 | tf_op jit(solution)/shard_map/pallas_call | solution.py:161
  120.4 1.9 collective-permute-start.12
  122.3 8.4 %collective-permute-start.15 = (bf16[2,128,768]{2,1,0:T(8,128)(2,1)}, bf16[2,128,768]{2,1,0:T(8,128)(2,1)S(1)}, u32[]{:S(2)}, u32[]{:S(2)}) collective-permute-start(bf16[2,128,768]{2,1,0:T(8,128)(2,1)} %get-tuple-element.32), channel_id=1, source_target_pairs={{2,6},{6,10},{10,14},{14,18},{18,22},{22,26},{26,30},{30,34},{34,3... | collective-permute-start | bytes 1179656 | tf_op jit(solution)/shard_map/ppermute | solution.py:31
  130.8 1.7 fusion.13
  132.5 2.1 collective-permute-start.9
  134.6 10.0 %collective-permute-start.10 = (bf16[2,128,1792]{2,1,0:T(8,128)(2,1)S(1)}, bf16[2,128,1792]{2,1,0:T(8,128)(2,1)S(1)}, u32[]{:S(2)}, u32[]{:S(2)}) collective-permute-start(bf16[2,128,1792]{2,1,0:T(8,128)(2,1)S(1)} %get-tuple-element.44), channel_id=1, source_target_pairs={{2,0},{4,2},{6,4},{8,6},{10,8},{12,10},{14,12},{16,14},{18,16},{20... | collective-permute-start | bytes 2752520 | tf_op jit(solution)/shard_map/ppermute | solution.py:26
  144.8 2.1 collective-permute-start.13
  146.9 10.0 %collective-permute-start.14 = (bf16[2,128,768]{2,1,0:T(8,128)(2,1)S(1)}, bf16[2,128,768]{2,1,0:T(8,128)(2,1)S(1)}, u32[]{:S(2)}, u32[]{:S(2)}) collective-permute-start(bf16[2,128,768]{2,1,0:T(8,128)(2,1)S(1)} %get-tuple-element.46), channel_id=1, source_target_pairs={{2,0},{4,2},{6,4},{8,6},{10,8},{12,10},{14,12},{16,14},{18,16},{20... | collective-permute-start | bytes 1179656 | tf_op jit(solution)/shard_map/ppermute | solution.py:26
  157.5 4.8 %collective-permute-done.13 = bf16[2,128,768]{2,1,0:T(8,128)(2,1)S(1)} collective-permute-done((bf16[2,128,768]{2,1,0:T(8,128)(2,1)S(1)}, bf16[2,128,768]{2,1,0:T(8,128)(2,1)S(1)}, u32[]{:S(2)}, u32[]{:S(2)}) %collective-permute-start.13) | collective-permute-done | bytes 393248 | tf_op jit(solution)/shard_map/ppermute | solution.py:26
  162.3 15.9 %collective-permute-done.14 = bf16[2,128,768]{2,1,0:T(8,128)(2,1)S(1)} collective-permute-done((bf16[2,128,768]{2,1,0:T(8,128)(2,1)S(1)}, bf16[2,128,768]{2,1,0:T(8,128)(2,1)S(1)}, u32[]{:S(2)}, u32[]{:S(2)}) %collective-permute-start.14) | collective-permute-done | bytes 393248 | tf_op jit(solution)/shard_map/ppermute | solution.py:26
  178.4 1.7 fusion.35
  180.6 1.9 collective-permute-start.16
  182.5 3.7 %collective-permute-done.16 = f32[5120]{0:T(1024)S(1)} collective-permute-done((f32[5120]{0:T(1024)S(1)}, f32[5120]{0:T(1024)S(1)}, u32[]{:S(2)}, u32[]{:S(2)}) %collective-permute-start.16) | collective-permute-done | bytes 20512 | tf_op jit(solution)/shard_map/ppermute | solution.py:65
  186.3 1.9 collective-permute-start.17
  189.4 1.9 collective-permute-start.18
  191.3 3.7 %collective-permute-done.18 = f32[5120]{0:T(1024)S(1)} collective-permute-done((f32[5120]{0:T(1024)S(1)}, f32[5120]{0:T(1024)S(1)}, u32[]{:S(2)}, u32[]{:S(2)}) %collective-permute-start.18) | collective-permute-done | bytes 20512 | tf_op jit(solution)/shard_map/ppermute | solution.py:65
  195.0 1.9 collective-permute-start.19
  197.0 5.3 %collective-permute-done.19 = f32[5120]{0:T(1024)S(1)} collective-permute-done((f32[5120]{0:T(1024)S(1)}, f32[5120]{0:T(1024)S(1)}, u32[]{:S(2)}, u32[]{:S(2)}) %collective-permute-start.19) | collective-permute-done | bytes 20512 | tf_op jit(solution)/shard_map/ppermute | solution.py:65
  202.2 1.9 collective-permute-start.20
  204.1 3.7 %collective-permute-done.20 = f32[5120]{0:T(1024)S(1)} collective-permute-done((f32[5120]{0:T(1024)S(1)}, f32[5120]{0:T(1024)S(1)}, u32[]{:S(2)}, u32[]{:S(2)}) %collective-permute-start.20) | collective-permute-done | bytes 20512 | tf_op jit(solution)/shard_map/ppermute | solution.py:65
  207.9 1.9 collective-permute-start.21
  209.8 1.2 fusion.21
  211.0 3.4 %collective-permute-done.21 = f32[5120]{0:T(1024)S(1)} collective-permute-done((f32[5120]{0:T(1024)S(1)}, f32[5120]{0:T(1024)S(1)}, u32[]{:S(2)}, u32[]{:S(2)}) %collective-permute-start.21) | collective-permute-done | bytes 20512 | tf_op jit(solution)/shard_map/ppermute | solution.py:65
  214.4 1.9 collective-permute-start.22
  216.4 7.6 %collective-permute-done.22 = f32[5120]{0:T(1024)S(1)} collective-permute-done((f32[5120]{0:T(1024)S(1)}, f32[5120]{0:T(1024)S(1)}, u32[]{:S(2)}, u32[]{:S(2)}) %collective-permute-start.22) | collective-permute-done | bytes 20512 | tf_op jit(solution)/shard_map/ppermute | solution.py:65
  224.0 1.9 collective-permute-start.23
  225.9 1.2 fusion.29
  227.2 3.4 %collective-permute-done.23 = f32[5120]{0:T(1024)S(1)} collective-permute-done((f32[5120]{0:T(1024)S(1)}, f32[5120]{0:T(1024)S(1)}, u32[]{:S(2)}, u32[]{:S(2)}) %collective-permute-start.23) | collective-permute-done | bytes 20512 | tf_op jit(solution)/shard_map/ppermute | solution.py:65
  230.6 1.9 collective-permute-start.24
  233.4 6.8 %collective-permute-done.24 = f32[5120]{0:T(1024)S(1)} collective-permute-done((f32[5120]{0:T(1024)S(1)}, f32[5120]{0:T(1024)S(1)}, u32[]{:S(2)}, u32[]{:S(2)}) %collective-permute-start.24) | collective-permute-done | bytes 20512 | tf_op jit(solution)/shard_map/ppermute | solution.py:65
  (84 shorter events, 7.3 us)
Async XLA Ops:
  0.6 2.7 %copy-start.4 = (bf16[1,128,2560]{2,1,0:T(8,128)(2,1)S(1)}, bf16[1,128,2560]{2,1,0:T(8,128)(2,1)}, u32[]{:S(2)}) copy-start(bf16[1,128,2560]{2,1,0:T(8,128)(2,1)} %param.9) | copy-start | bytes 1966084
  3.3 17.6 %copy-start.2 = (bf16[128,2560]{1,0:T(8,128)(2,1)}, bf16[128,2560]{1,0:T(8,128)(2,1)S(1)}, u32[]{:S(2)}) copy-start(bf16[128,2560]{1,0:T(8,128)(2,1)S(1)} %fusion.22.k_ref) | copy-start | bytes 1966084
  3.4 17.4 %copy-start.19 = (s32[1,4]{1,0:T(1,128)S(1)}, s32[1,4]{1,0:T(1,128)}, u32[]{:S(2)}) copy-start(s32[1,4]{1,0:T(1,128)} %param.13) | copy-start | bytes 52
  3.4 18.3 %copy-start = (bf16[1,128,2560]{2,1,0:T(8,128)(2,1)S(1)}, bf16[1,128,2560]{2,1,0:T(8,128)(2,1)}, u32[]{:S(2)}) copy-start(bf16[1,128,2560]{2,1,0:T(8,128)(2,1)} %param.7) | copy-start | bytes 1966084
  3.5 24.5 %collective-permute-start.1 = (bf16[2,128,1792]{2,1,0:T(8,128)(2,1)S(1)}, bf16[2,128,1792]{2,1,0:T(8,128)(2,1)}, u32[]{:S(2)}, u32[]{:S(2)}) collective-permute-start(bf16[2,128,1792]{2,1,0:T(8,128)(2,1)S(1)} %pad_maximum_fusion.1), channel_id=1, source_target_pairs={{2,0},{4,2},{6,4},{8,6},{10,8},{12,10},{14,12},{16,14},{18,16},{20... | collective-permute-start | bytes 2752520 | tf_op jit(solution)/shard_map/ppermute | solution.py:26
  16.9 49.3 %collective-permute-start = (bf16[2,128,1792]{2,1,0:T(8,128)(2,1)S(1)}, bf16[2,128,1792]{2,1,0:T(8,128)(2,1)}, u32[]{:S(2)}, u32[]{:S(2)}) collective-permute-start(bf16[2,128,1792]{2,1,0:T(8,128)(2,1)S(1)} %pad_maximum_fusion.1), channel_id=1, source_target_pairs={{0,2},{2,4},{4,6},{6,8},{8,10},{10,12},{12,14},{14,16},{16,18},{18... | collective-permute-start | bytes 2752520 | tf_op jit(solution)/shard_map/ppermute | solution.py:26
  18.9 51.6 %collective-permute-start.2 = (bf16[2,128,1792]{2,1,0:T(8,128)(2,1)S(1)}, bf16[2,128,1792]{2,1,0:T(8,128)(2,1)}, u32[]{:S(2)}, u32[]{:S(2)}) collective-permute-start(bf16[2,128,1792]{2,1,0:T(8,128)(2,1)S(1)} %pad_maximum_fusion.1), channel_id=1, source_target_pairs={{0,4},{4,8},{8,12},{12,16},{16,20},{20,24},{24,28},{28,32},{32,36}... | collective-permute-start | bytes 2752520 | tf_op jit(solution)/shard_map/ppermute | solution.py:31
  21.9 47.5 %copy-start.16 = (f32[2560]{0:T(1024)S(1)}, f32[2560]{0:T(1024)}, u32[]{:S(2)}) copy-start(f32[2560]{0:T(1024)} %param.11) | copy-start | bytes 30724
  67.5 4.4 %collective-permute-start.3 = (bf16[2,128,1792]{2,1,0:T(8,128)(2,1)S(1)}, bf16[2,128,1792]{2,1,0:T(8,128)(2,1)S(1)}, u32[]{:S(2)}, u32[]{:S(2)}) collective-permute-start(bf16[2,128,1792]{2,1,0:T(8,128)(2,1)S(1)} %broadcast_select_fusion), channel_id=1, source_target_pairs={{0,2},{2,0},{4,6},{6,4},{8,10},{10,8},{12,14},{14,12},{16,18},{18,... | collective-permute-start | bytes 2752520 | tf_op jit(solution)/shard_map/ppermute | solution.py:31
  71.8 5.0 %copy-start.18 = (bf16[2,128,1792]{2,1,0:T(8,128)(2,1)}, bf16[2,128,1792]{2,1,0:T(8,128)(2,1)S(1)}, u32[]{:S(2)}) copy-start(bf16[2,128,1792]{2,1,0:T(8,128)(2,1)S(1)} %collective-permute-done.3.refs_3_) | copy-start | bytes 2752516
  71.8 25.0 %collective-permute-start.5 = (bf16[2,128,768]{2,1,0:T(8,128)(2,1)}, bf16[2,128,768]{2,1,0:T(8,128)(2,1)S(1)}, u32[]{:S(2)}, u32[]{:S(2)}) collective-permute-start(bf16[2,128,768]{2,1,0:T(8,128)(2,1)} %pad_maximum_fusion.3), channel_id=1, source_target_pairs={{2,0},{4,2},{6,4},{8,6},{10,8},{12,10},{14,12},{16,14},{18,16},{20... | collective-permute-start | bytes 1179656 | tf_op jit(solution)/shard_map/ppermute | solution.py:26
  73.8 23.1 %collective-permute-start.4 = (bf16[2,128,768]{2,1,0:T(8,128)(2,1)}, bf16[2,128,768]{2,1,0:T(8,128)(2,1)S(1)}, u32[]{:S(2)}, u32[]{:S(2)}) collective-permute-start(bf16[2,128,768]{2,1,0:T(8,128)(2,1)} %pad_maximum_fusion.3), channel_id=1, source_target_pairs={{0,2},{2,4},{4,6},{6,8},{8,10},{10,12},{12,14},{14,16},{16,18},{18... | collective-permute-start | bytes 1179656 | tf_op jit(solution)/shard_map/ppermute | solution.py:26
  91.6 39.1 %collective-permute-start.8 = (bf16[2,128,1792]{2,1,0:T(8,128)(2,1)}, bf16[2,128,1792]{2,1,0:T(8,128)(2,1)}, u32[]{:S(2)}, u32[]{:S(2)}) collective-permute-start(bf16[2,128,1792]{2,1,0:T(8,128)(2,1)} %get-tuple-element.25), channel_id=1, source_target_pairs={{0,2},{2,0},{4,6},{6,4},{8,10},{10,8},{12,14},{14,12},{16,18},{18,... | collective-permute-start | bytes 2752520 | tf_op jit(solution)/shard_map/ppermute | solution.py:31
  94.9 17.9 %collective-permute-start.6 = (bf16[2,128,768]{2,1,0:T(8,128)(2,1)}, bf16[2,128,768]{2,1,0:T(8,128)(2,1)}, u32[]{:S(2)}, u32[]{:S(2)}) collective-permute-start(bf16[2,128,768]{2,1,0:T(8,128)(2,1)} %pad_maximum_fusion.3), channel_id=1, source_target_pairs={{0,4},{4,8},{8,12},{12,16},{16,20},{20,24},{24,28},{28,32},{32,36}... | collective-permute-start | bytes 1179656 | tf_op jit(solution)/shard_map/ppermute | solution.py:31
  96.8 16.0 %copy-start.6 = (bf16[2,128,768]{2,1,0:T(8,128)(2,1)}, bf16[2,128,768]{2,1,0:T(8,128)(2,1)S(1)}, u32[]{:S(2)}) copy-start(bf16[2,128,768]{2,1,0:T(8,128)(2,1)S(1)} %collective-permute-done.5.refs_1_) | copy-start | bytes 1179652
  96.9 16.0 %copy-start.7 = (bf16[2,128,768]{2,1,0:T(8,128)(2,1)}, bf16[2,128,768]{2,1,0:T(8,128)(2,1)S(1)}, u32[]{:S(2)}) copy-start(bf16[2,128,768]{2,1,0:T(8,128)(2,1)S(1)} %collective-permute-done.4.refs_0_) | copy-start | bytes 1179652
  96.9 15.9 %collective-permute-start.7 = (bf16[2,128,768]{2,1,0:T(8,128)(2,1)S(1)}, bf16[2,128,768]{2,1,0:T(8,128)(2,1)}, u32[]{:S(2)}, u32[]{:S(2)}) collective-permute-start(bf16[2,128,768]{2,1,0:T(8,128)(2,1)S(1)} %broadcast_select_fusion.1), channel_id=1, source_target_pairs={{0,2},{2,0},{4,6},{6,4},{8,10},{10,8},{12,14},{14,12},{16,18},{18,... | collective-permute-start | bytes 1179656 | tf_op jit(solution)/shard_map/ppermute | solution.py:31
  105.2 25.6 %copy-start.8 = (bf16[2,128,1792]{2,1,0:T(8,128)(2,1)S(1)}, bf16[2,128,1792]{2,1,0:T(8,128)(2,1)}, u32[]{:S(2)}) copy-start(bf16[2,128,1792]{2,1,0:T(8,128)(2,1)} %get-tuple-element.26) | copy-start | bytes 2752516
  105.2 25.6 %copy-start.9 = (bf16[2,128,1792]{2,1,0:T(8,128)(2,1)S(1)}, bf16[2,128,1792]{2,1,0:T(8,128)(2,1)}, u32[]{:S(2)}) copy-start(bf16[2,128,1792]{2,1,0:T(8,128)(2,1)} %get-tuple-element.24) | copy-start | bytes 2752516
  105.2 73.2 %collective-permute-start.11 = (bf16[2,128,1792]{2,1,0:T(8,128)(2,1)}, bf16[2,128,1792]{2,1,0:T(8,128)(2,1)}, u32[]{:S(2)}, u32[]{:S(2)}) collective-permute-start(bf16[2,128,1792]{2,1,0:T(8,128)(2,1)} %get-tuple-element.27), channel_id=1, source_target_pairs={{2,6},{6,10},{10,14},{14,18},{18,22},{22,26},{26,30},{30,34},{34,3... | collective-permute-start | bytes 2752520 | tf_op jit(solution)/shard_map/ppermute | solution.py:31
  120.4 24.2 %collective-permute-start.12 = (bf16[2,128,768]{2,1,0:T(8,128)(2,1)}, bf16[2,128,768]{2,1,0:T(8,128)(2,1)S(1)}, u32[]{:S(2)}, u32[]{:S(2)}) collective-permute-start(bf16[2,128,768]{2,1,0:T(8,128)(2,1)} %get-tuple-element.30), channel_id=1, source_target_pairs={{0,2},{2,0},{4,6},{6,4},{8,10},{10,8},{12,14},{14,12},{16,18},{18,... | collective-permute-start | bytes 1179656 | tf_op jit(solution)/shard_map/ppermute | solution.py:31
  122.3 24.6 %collective-permute-start.15 = (bf16[2,128,768]{2,1,0:T(8,128)(2,1)}, bf16[2,128,768]{2,1,0:T(8,128)(2,1)S(1)}, u32[]{:S(2)}, u32[]{:S(2)}) collective-permute-start(bf16[2,128,768]{2,1,0:T(8,128)(2,1)} %get-tuple-element.32), channel_id=1, source_target_pairs={{2,6},{6,10},{10,14},{14,18},{18,22},{22,26},{26,30},{30,34},{34,3... | collective-permute-start | bytes 1179656 | tf_op jit(solution)/shard_map/ppermute | solution.py:31
  130.8 13.8 %copy-start.14 = (bf16[2,128,768]{2,1,0:T(8,128)(2,1)S(1)}, bf16[2,128,768]{2,1,0:T(8,128)(2,1)}, u32[]{:S(2)}) copy-start(bf16[2,128,768]{2,1,0:T(8,128)(2,1)} %get-tuple-element.31) | copy-start | bytes 1179652
  130.8 13.8 %copy-start.15 = (bf16[2,128,768]{2,1,0:T(8,128)(2,1)S(1)}, bf16[2,128,768]{2,1,0:T(8,128)(2,1)}, u32[]{:S(2)}) copy-start(bf16[2,128,768]{2,1,0:T(8,128)(2,1)} %get-tuple-element.29) | copy-start | bytes 1179652
  132.5 24.4 %copy-start.3 = (f32[128,1792]{1,0:T(8,128)S(1)}, f32[128,1792]{1,0:T(8,128)}, u32[]{:S(2)}) copy-start(f32[128,1792]{1,0:T(8,128)} %get-tuple-element.20) | copy-start | bytes 2752516
  132.5 45.8 %collective-permute-start.9 = (bf16[2,128,1792]{2,1,0:T(8,128)(2,1)S(1)}, bf16[2,128,1792]{2,1,0:T(8,128)(2,1)S(1)}, u32[]{:S(2)}, u32[]{:S(2)}) collective-permute-start(bf16[2,128,1792]{2,1,0:T(8,128)(2,1)S(1)} %get-tuple-element.43), channel_id=1, source_target_pairs={{0,2},{2,4},{4,6},{6,8},{8,10},{10,12},{12,14},{14,16},{16,18},{18... | collective-permute-start | bytes 2752520 | tf_op jit(solution)/shard_map/ppermute | solution.py:26
  134.6 43.8 %collective-permute-start.10 = (bf16[2,128,1792]{2,1,0:T(8,128)(2,1)S(1)}, bf16[2,128,1792]{2,1,0:T(8,128)(2,1)S(1)}, u32[]{:S(2)}, u32[]{:S(2)}) collective-permute-start(bf16[2,128,1792]{2,1,0:T(8,128)(2,1)S(1)} %get-tuple-element.44), channel_id=1, source_target_pairs={{2,0},{4,2},{6,4},{8,6},{10,8},{12,10},{14,12},{16,14},{18,16},{20... | collective-permute-start | bytes 2752520 | tf_op jit(solution)/shard_map/ppermute | solution.py:26
  144.8 12.2 %copy-start.5 = (f32[128,768]{1,0:T(8,128)S(1)}, f32[128,768]{1,0:T(8,128)}, u32[]{:S(2)}) copy-start(f32[128,768]{1,0:T(8,128)} %get-tuple-element.22) | copy-start | bytes 1179652
  144.8 17.4 %collective-permute-start.13 = (bf16[2,128,768]{2,1,0:T(8,128)(2,1)S(1)}, bf16[2,128,768]{2,1,0:T(8,128)(2,1)S(1)}, u32[]{:S(2)}, u32[]{:S(2)}) collective-permute-start(bf16[2,128,768]{2,1,0:T(8,128)(2,1)S(1)} %get-tuple-element.45), channel_id=1, source_target_pairs={{0,2},{2,4},{4,6},{6,8},{8,10},{10,12},{12,14},{14,16},{16,18},{18... | collective-permute-start | bytes 1179656 | tf_op jit(solution)/shard_map/ppermute | solution.py:26
  146.9 31.2 %collective-permute-start.14 = (bf16[2,128,768]{2,1,0:T(8,128)(2,1)S(1)}, bf16[2,128,768]{2,1,0:T(8,128)(2,1)S(1)}, u32[]{:S(2)}, u32[]{:S(2)}) collective-permute-start(bf16[2,128,768]{2,1,0:T(8,128)(2,1)S(1)} %get-tuple-element.46), channel_id=1, source_target_pairs={{2,0},{4,2},{6,4},{8,6},{10,8},{12,10},{14,12},{16,14},{18,16},{20... | collective-permute-start | bytes 1179656 | tf_op jit(solution)/shard_map/ppermute | solution.py:26
  157.0 21.1 %copy-start.12 = (f32[128,768]{1,0:T(8,128)S(1)}, f32[128,768]{1,0:T(8,128)}, u32[]{:S(2)}) copy-start(f32[128,768]{1,0:T(8,128)} %get-tuple-element.28) | copy-start | bytes 1179652
  157.0 21.1 %copy-start.13 = (f32[128,768]{1,0:T(8,128)S(1)}, f32[128,768]{1,0:T(8,128)}, u32[]{:S(2)}) copy-start(f32[128,768]{1,0:T(8,128)} %get-tuple-element.34) | copy-start | bytes 1179652
  157.5 20.9 %copy-start.10 = (f32[128,1792]{1,0:T(8,128)S(1)}, f32[128,1792]{1,0:T(8,128)}, u32[]{:S(2)}) copy-start(f32[128,1792]{1,0:T(8,128)} %get-tuple-element.23) | copy-start | bytes 2752516
  157.5 20.9 %copy-start.11 = (f32[128,1792]{1,0:T(8,128)S(1)}, f32[128,1792]{1,0:T(8,128)}, u32[]{:S(2)}) copy-start(f32[128,1792]{1,0:T(8,128)} %get-tuple-element.33) | copy-start | bytes 2752516
  178.4 1.7 copy-start.1
  178.4 1.7 copy-start.17
  180.6 5.7 %collective-permute-start.16 = (f32[5120]{0:T(1024)S(1)}, f32[5120]{0:T(1024)S(1)}, u32[]{:S(2)}, u32[]{:S(2)}) collective-permute-start(f32[5120]{0:T(1024)S(1)} %pad_maximum_fusion.4), channel_id=1, source_target_pairs={{0,1},{1,0},{2,3},{3,2},{4,5},{5,4},{6,7},{7,6},{8,9},{9,8},{10,11... | collective-permute-start | bytes 61448 | tf_op jit(solution)/shard_map/ppermute | solution.py:65
  186.3 3.1 %collective-permute-start.17 = (f32[5120]{0:T(1024)S(1)}, f32[5120]{0:T(1024)S(1)}, u32[]{:S(2)}, u32[]{:S(2)}) collective-permute-start(f32[5120]{0:T(1024)S(1)} %fusion.39), channel_id=1, source_target_pairs={{0,2},{2,0},{4,6},{6,4},{8,10},{10,8},{12,14},{14,12},{16,18},{18,... | collective-permute-start | bytes 61448 | tf_op jit(solution)/shard_map/ppermute | solution.py:65
  189.4 5.7 %collective-permute-start.18 = (f32[5120]{0:T(1024)S(1)}, f32[5120]{0:T(1024)S(1)}, u32[]{:S(2)}, u32[]{:S(2)}) collective-permute-start(f32[5120]{0:T(1024)S(1)} %add.119), channel_id=1, source_target_pairs={{0,4},{2,6},{4,0},{6,2},{8,12},{10,14},{12,8},{14,10},{16,20},{18,... | collective-permute-start | bytes 61448 | tf_op jit(solution)/shard_map/ppermute | solution.py:65
  195.0 7.2 %collective-permute-start.19 = (f32[5120]{0:T(1024)S(1)}, f32[5120]{0:T(1024)S(1)}, u32[]{:S(2)}, u32[]{:S(2)}) collective-permute-start(f32[5120]{0:T(1024)S(1)} %add.120), channel_id=1, source_target_pairs={{0,8},{2,10},{4,12},{6,14},{8,0},{10,2},{12,4},{14,6},{16,24},{18,... | collective-permute-start | bytes 61448 | tf_op jit(solution)/shard_map/ppermute | solution.py:65
  202.2 5.7 %collective-permute-start.20 = (f32[5120]{0:T(1024)S(1)}, f32[5120]{0:T(1024)S(1)}, u32[]{:S(2)}, u32[]{:S(2)}) collective-permute-start(f32[5120]{0:T(1024)S(1)} %add.121), channel_id=1, source_target_pairs={{0,16},{2,18},{4,20},{6,22},{8,24},{10,26},{12,28},{14,30},{16,0},... | collective-permute-start | bytes 61448 | tf_op jit(solution)/shard_map/ppermute | solution.py:65
  207.9 6.6 %collective-permute-start.21 = (f32[5120]{0:T(1024)S(1)}, f32[5120]{0:T(1024)S(1)}, u32[]{:S(2)}, u32[]{:S(2)}) collective-permute-start(f32[5120]{0:T(1024)S(1)} %add.122), channel_id=1, source_target_pairs={{0,32},{2,34},{4,36},{6,38},{8,40},{10,42},{12,44},{14,46},{16,48}... | collective-permute-start | bytes 61448 | tf_op jit(solution)/shard_map/ppermute | solution.py:65
  214.4 9.6 %collective-permute-start.22 = (f32[5120]{0:T(1024)S(1)}, f32[5120]{0:T(1024)S(1)}, u32[]{:S(2)}, u32[]{:S(2)}) collective-permute-start(f32[5120]{0:T(1024)S(1)} %add.123), channel_id=1, source_target_pairs={{0,64},{2,66},{4,68},{6,70},{8,72},{10,74},{12,76},{14,78},{16,80}... | collective-permute-start | bytes 61448 | tf_op jit(solution)/shard_map/ppermute | solution.py:65
  224.0 6.6 %collective-permute-start.23 = (f32[5120]{0:T(1024)S(1)}, f32[5120]{0:T(1024)S(1)}, u32[]{:S(2)}, u32[]{:S(2)}) collective-permute-start(f32[5120]{0:T(1024)S(1)} %add.124), channel_id=1, source_target_pairs={{0,128},{2,130},{4,132},{6,134},{8,136},{10,138},{12,140},{14,142}... | collective-permute-start | bytes 61448 | tf_op jit(solution)/shard_map/ppermute | solution.py:65
  230.6 9.6 %collective-permute-start.24 = (f32[5120]{0:T(1024)S(1)}, f32[5120]{0:T(1024)S(1)}, u32[]{:S(2)}, u32[]{:S(2)}) collective-permute-start(f32[5120]{0:T(1024)S(1)} %add.125), channel_id=1, source_target_pairs={{0,256},{2,258},{4,260},{6,262},{8,264},{10,266},{12,268},{14,270}... | collective-permute-start | bytes 61448 | tf_op jit(solution)/shard_map/ppermute | solution.py:65

commit v11 on v9

--- a/solution.py
+++ b/solution.py
@@ -174,9 +174,7 @@
     tile_rows = q_raw.shape[1]
     features = q_raw.shape[2]
     offsets = level_offsets(LEVELS)
-    q_hat, q_inv = normalize(q_raw[0])
     k_hat, k_inv = normalize(k_raw[0])
-    q_norm = (q_hat * q_gain).astype(jnp.bfloat16)
     k_norm = (k_hat * k_gain).astype(jnp.bfloat16)
     value_rows = values[0]
     grad_rows = cotangent[0]
@@ -193,6 +191,10 @@
         if fetched is not None:
             stacked, _ = lax.optimization_barrier((stacked, fetched))
         fetched = fetch_neighbours(stacked, "seq")
+        if start == 0:
+            q_in, _ = lax.optimization_barrier((q_raw[0], fetched))
+            q_hat, q_inv = normalize(q_in)
+            q_norm = (q_hat * q_gain).astype(jnp.bfloat16)
         q_grad_c, k_grad_c, v_sum_c, *far = attention(
             odd, bias, q_norm, k_norm, value_rows, grad_rows, fetched, start // (HEADS_PER_STEP * HEAD)
         )

time: 229 us -> 234 us (1.022)
  the two profiles are of different devices: /device:TPU:32 before, /device:TPU:40 now
where the time goes in v11:
time: 234 us; the launch traced here: 233 us
  waiting for transfers between devices  104 us (44%)
  starting transfers between devices  86.4 us (37%)
  Pallas kernels  22.3 us (10%)
  other arithmetic  13.1 us (6%)
  local copies, waits for them, and re-layouts  5.84 us (2%)
    ppermute x8, waiting for transfers between devices, from_behind(): lax.ppermute(value, axis, [(source, source + steps) for source in range(f...  55.6 us
    ppermute x8, starting transfers between devices, from_behind(): lax.ppermute(value, axis, [(source, source + steps) for source in range(f...  43.6 us
    ppermute x9, waiting for transfers between devices, all_sum(): lax.ppermute(value, axis, [(i, i ^ bit) for i in range(count)])  38.7 us
    ppermute x8, starting transfers between devices, pairs_permute(): lax.ppermute(value, axis, [(i, j) for i, j in pairs if 0 <= j < count])  25.4 us
    pallas_call x2, Pallas kernels, attention(): pl.pallas_call(attention_kernel, grid_spec=grid_spec, out_shape=[f32] * 3...  22.3 us
    ppermute x9, starting transfers between devices, all_sum(): lax.ppermute(value, axis, [(i, i ^ bit) for i in range(count)])  17.4 us
    ppermute x8, waiting for transfers between devices, pairs_permute(): lax.ppermute(value, axis, [(i, j) for i, j in pairs if 0 <= j < count])  10 us
    unnamed x53, local copies, waits for them, and re-layouts  5.09 us
  transfers between devices with their start and end apart: 25, of which 14 were waited for; matrix products, arithmetic and copies ran while one was open for 5% of the time, Pallas kernels for 10%

profile of v11, /device:TPU:40, one launch (start us, length us, event | category | flops | bytes accessed | tf_op | source)
XLA Modules:
  0.0 233.2 jit_solution(9496276316149300313)
XLA Ops:
  0.6 1.4 fusion.21
  2.0 1.3 fusion.18.k_ref
  3.4 1.0 pad_maximum_fusion.1
  4.5 13.4 %collective-permute-start.1 = (bf16[2,128,1536]{2,1,0:T(8,128)(2,1)}, bf16[2,128,1536]{2,1,0:T(8,128)(2,1)S(1)}, u32[]{:S(2)}, u32[]{:S(2)}) collective-permute-start(bf16[2,128,1536]{2,1,0:T(8,128)(2,1)} %pad_maximum_fusion.1), channel_id=1, source_target_pairs={{2,0},{4,2},{6,4},{8,6},{10,8},{12,10},{14,12},{16,14},{18,16},{20... | collective-permute-start | bytes 2359304 | tf_op jit(solution)/shard_map/ppermute | solution.py:26
  17.8 1.9 collective-permute-start
  19.8 1.9 collective-permute-start.2
  21.7 6.2 %collective-permute-done.1.refs_1_ = bf16[2,128,1536]{2,1,0:T(8,128)(2,1)S(1)} collective-permute-done((bf16[2,128,1536]{2,1,0:T(8,128)(2,1)}, bf16[2,128,1536]{2,1,0:T(8,128)(2,1)S(1)}, u32[]{:S(2)}, u32[]{:S(2)}) %collective-permute-start.1) | collective-permute-done | bytes 786464 | tf_op jit(solution)/shard_map/ppermute | solution.py:26
  27.9 33.7 %collective-permute-done.refs_0_ = bf16[2,128,1536]{2,1,0:T(8,128)(2,1)S(1)} collective-permute-done((bf16[2,128,1536]{2,1,0:T(8,128)(2,1)}, bf16[2,128,1536]{2,1,0:T(8,128)(2,1)S(1)}, u32[]{:S(2)}, u32[]{:S(2)}) %collective-permute-start) | collective-permute-done | bytes 786464 | tf_op jit(solution)/shard_map/ppermute | solution.py:26
  61.7 2.1 collective-permute-start.3
  66.9 1.9 collective-permute-start.5
  68.9 2.4 %collective-permute-start.4 = (bf16[2,128,1024]{2,1,0:T(8,128)(2,1)}, bf16[2,128,1024]{2,1,0:T(8,128)(2,1)S(1)}, u32[]{:S(2)}, u32[]{:S(2)}) collective-permute-start(bf16[2,128,1024]{2,1,0:T(8,128)(2,1)} %pad_maximum_fusion.3), channel_id=1, source_target_pairs={{0,2},{2,4},{4,6},{6,8},{8,10},{10,12},{12,14},{14,16},{16,18},{18... | collective-permute-start | bytes 1572872 | tf_op jit(solution)/shard_map/ppermute | solution.py:26
  71.5 1.1 fusion.11.q_ref
  72.6 12.8 %shard_map.110 = (f32[128,1536]{1,0:T(8,128)}, f32[128,1536]{1,0:T(8,128)}, f32[128,1536]{1,0:T(8,128)}, bf16[2,128,1536]{2,1,0:T(8,128)(2,1)}, bf16[2,128,1536]...) custom-call(s32[1]{0:T(128)} %bitcast.5.odd_ref, f32[1,640]{1,0:T(1,128)} %bitcast.120, ...), custom_call_target="tpu_custom_call" | custom-call | flops 1509949440 | bytes 7077888 | tf_op jit(solution)/shard_map/pallas_call | solution.py:161
  85.5 3.4 %collective-permute-start.8 = (bf16[2,128,1536]{2,1,0:T(8,128)(2,1)}, bf16[2,128,1536]{2,1,0:T(8,128)(2,1)S(1)}, u32[]{:S(2)}, u32[]{:S(2)}) collective-permute-start(bf16[2,128,1536]{2,1,0:T(8,128)(2,1)} %get-tuple-element.27), channel_id=1, source_target_pairs={{0,2},{2,0},{4,6},{6,4},{8,10},{10,8},{12,14},{14,12},{16,18},{18,... | collective-permute-start | bytes 2359304 | tf_op jit(solution)/shard_map/ppermute | solution.py:31
  88.9 1.9 collective-permute-start.6
  90.8 10.2 %collective-permute-start.11 = (bf16[2,128,1536]{2,1,0:T(8,128)(2,1)}, bf16[2,128,1536]{2,1,0:T(8,128)(2,1)S(1)}, u32[]{:S(2)}, u32[]{:S(2)}) collective-permute-start(bf16[2,128,1536]{2,1,0:T(8,128)(2,1)} %get-tuple-element.29), channel_id=1, source_target_pairs={{2,6},{6,10},{10,14},{14,18},{18,22},{22,26},{26,30},{30,34},{34,3... | collective-permute-start | bytes 2359304 | tf_op jit(solution)/shard_map/ppermute | solution.py:31
  101.2 1.9 collective-permute-start.7
  103.1 1.6 fusion.27
  104.7 2.4 %collective-permute-start.9 = (bf16[2,128,1536]{2,1,0:T(8,128)(2,1)}, bf16[2,128,1536]{2,1,0:T(8,128)(2,1)S(1)}, u32[]{:S(2)}, u32[]{:S(2)}) collective-permute-start(bf16[2,128,1536]{2,1,0:T(8,128)(2,1)} %get-tuple-element.45), channel_id=1, source_target_pairs={{0,2},{2,4},{4,6},{6,8},{8,10},{10,12},{12,14},{14,16},{16,18},{18... | collective-permute-start | bytes 2359304 | tf_op jit(solution)/shard_map/ppermute | solution.py:26
  107.1 9.5 %collective-permute-start.10 = (bf16[2,128,1536]{2,1,0:T(8,128)(2,1)}, bf16[2,128,1536]{2,1,0:T(8,128)(2,1)S(1)}, u32[]{:S(2)}, u32[]{:S(2)}) collective-permute-start(bf16[2,128,1536]{2,1,0:T(8,128)(2,1)} %get-tuple-element.46), channel_id=1, source_target_pairs={{2,0},{4,2},{6,4},{8,6},{10,8},{12,10},{14,12},{16,14},{18,16},{20... | collective-permute-start | bytes 2359304 | tf_op jit(solution)/shard_map/ppermute | solution.py:26
  116.6 9.4 %collective-permute-done.6.refs_2_ = bf16[2,128,1024]{2,1,0:T(8,128)(2,1)S(1)} collective-permute-done((bf16[2,128,1024]{2,1,0:T(8,128)(2,1)}, bf16[2,128,1024]{2,1,0:T(8,128)(2,1)S(1)}, u32[]{:S(2)}, u32[]{:S(2)}) %collective-permute-start.6) | collective-permute-done | bytes 524320 | tf_op jit(solution)/shard_map/ppermute | solution.py:31
  126.8 9.4 %shard_map.111 = (f32[128,1024]{1,0:T(8,128)}, f32[128,1024]{1,0:T(8,128)}, f32[128,1024]{1,0:T(8,128)}, bf16[2,128,1024]{2,1,0:T(8,128)(2,1)}, bf16[2,128,1024]...) custom-call(s32[1]{0:T(128)} %bitcast.5.odd_ref, f32[1,640]{1,0:T(1,128)} %bitcast.121, ...), custom_call_target="tpu_custom_call" | custom-call | flops 1006632960 | bytes 4718592 | tf_op jit(solution)/shard_map/pallas_call | solution.py:161
  136.3 2.1 collective-permute-start.12
  138.3 1.2 constant_dynamic-update-slice_fusion.1
  139.5 1.9 collective-permute-start.15
  143.0 2.5 %collective-permute-start.13 = (bf16[2,128,1024]{2,1,0:T(8,128)(2,1)S(1)}, bf16[2,128,1024]{2,1,0:T(8,128)(2,1)S(1)}, u32[]{:S(2)}, u32[]{:S(2)}) collective-permute-start(bf16[2,128,1024]{2,1,0:T(8,128)(2,1)S(1)} %get-tuple-element.47), channel_id=1, source_target_pairs={{0,2},{2,4},{4,6},{6,8},{8,10},{10,12},{12,14},{14,16},{16,18},{18... | collective-permute-start | bytes 1572872 | tf_op jit(solution)/shard_map/ppermute | solution.py:26
  145.6 9.6 %collective-permute-start.14 = (bf16[2,128,1024]{2,1,0:T(8,128)(2,1)S(1)}, bf16[2,128,1024]{2,1,0:T(8,128)(2,1)S(1)}, u32[]{:S(2)}, u32[]{:S(2)}) collective-permute-start(bf16[2,128,1024]{2,1,0:T(8,128)(2,1)S(1)} %get-tuple-element.48), channel_id=1, source_target_pairs={{2,0},{4,2},{6,4},{8,6},{10,8},{12,10},{14,12},{16,14},{18,16},{20... | collective-permute-start | bytes 1572872 | tf_op jit(solution)/shard_map/ppermute | solution.py:26
  155.8 15.8 %collective-permute-done.13 = bf16[2,128,1024]{2,1,0:T(8,128)(2,1)S(1)} collective-permute-done((bf16[2,128,1024]{2,1,0:T(8,128)(2,1)S(1)}, bf16[2,128,1024]{2,1,0:T(8,128)(2,1)S(1)}, u32[]{:S(2)}, u32[]{:S(2)}) %collective-permute-start.13) | collective-permute-done | bytes 524320 | tf_op jit(solution)/shard_map/ppermute | solution.py:26
  173.1 2.1 collective-permute-start.16
  175.2 3.6 %collective-permute-done.16 = f32[5120]{0:T(1024)S(1)} collective-permute-done((f32[5120]{0:T(1024)S(1)}, f32[5120]{0:T(1024)S(1)}, u32[]{:S(2)}, u32[]{:S(2)}) %collective-permute-start.16) | collective-permute-done | bytes 20512 | tf_op jit(solution)/shard_map/ppermute | solution.py:65
  178.8 1.9 collective-permute-start.17
  180.7 1.2 collective-permute-done.17
  181.8 1.9 collective-permute-start.18
  183.7 3.7 %collective-permute-done.18 = f32[5120]{0:T(1024)S(1)} collective-permute-done((f32[5120]{0:T(1024)S(1)}, f32[5120]{0:T(1024)S(1)}, u32[]{:S(2)}, u32[]{:S(2)}) %collective-permute-start.18) | collective-permute-done | bytes 20512 | tf_op jit(solution)/shard_map/ppermute | solution.py:65
  187.5 1.9 collective-permute-start.19
  189.4 5.3 %collective-permute-done.19 = f32[5120]{0:T(1024)S(1)} collective-permute-done((f32[5120]{0:T(1024)S(1)}, f32[5120]{0:T(1024)S(1)}, u32[]{:S(2)}, u32[]{:S(2)}) %collective-permute-start.19) | collective-permute-done | bytes 20512 | tf_op jit(solution)/shard_map/ppermute | solution.py:65
  194.7 1.9 collective-permute-start.20
  196.6 3.7 %collective-permute-done.20 = f32[5120]{0:T(1024)S(1)} collective-permute-done((f32[5120]{0:T(1024)S(1)}, f32[5120]{0:T(1024)S(1)}, u32[]{:S(2)}, u32[]{:S(2)}) %collective-permute-start.20) | collective-permute-done | bytes 20512 | tf_op jit(solution)/shard_map/ppermute | solution.py:65
  200.3 1.9 collective-permute-start.21
  202.3 1.2 fusion.33
  203.5 3.4 %collective-permute-done.21 = f32[5120]{0:T(1024)S(1)} collective-permute-done((f32[5120]{0:T(1024)S(1)}, f32[5120]{0:T(1024)S(1)}, u32[]{:S(2)}, u32[]{:S(2)}) %collective-permute-start.21) | collective-permute-done | bytes 20512 | tf_op jit(solution)/shard_map/ppermute | solution.py:65
  206.9 1.9 collective-permute-start.22
  208.8 7.6 %collective-permute-done.22 = f32[5120]{0:T(1024)S(1)} collective-permute-done((f32[5120]{0:T(1024)S(1)}, f32[5120]{0:T(1024)S(1)}, u32[]{:S(2)}, u32[]{:S(2)}) %collective-permute-start.22) | collective-permute-done | bytes 20512 | tf_op jit(solution)/shard_map/ppermute | solution.py:65
  216.5 1.9 collective-permute-start.23
  218.4 1.2 fusion.25
  219.6 3.4 %collective-permute-done.23 = f32[5120]{0:T(1024)S(1)} collective-permute-done((f32[5120]{0:T(1024)S(1)}, f32[5120]{0:T(1024)S(1)}, u32[]{:S(2)}, u32[]{:S(2)}) %collective-permute-start.23) | collective-permute-done | bytes 20512 | tf_op jit(solution)/shard_map/ppermute | solution.py:65
  223.1 1.9 collective-permute-start.24
  225.9 6.8 %collective-permute-done.24 = f32[5120]{0:T(1024)S(1)} collective-permute-done((f32[5120]{0:T(1024)S(1)}, f32[5120]{0:T(1024)S(1)}, u32[]{:S(2)}, u32[]{:S(2)}) %collective-permute-start.24) | collective-permute-done | bytes 20512 | tf_op jit(solution)/shard_map/ppermute | solution.py:65
  (94 shorter events, 9.5 us)
Async XLA Ops:
  0.6 2.7 %copy-start.3 = (bf16[1,128,2560]{2,1,0:T(8,128)(2,1)S(1)}, bf16[1,128,2560]{2,1,0:T(8,128)(2,1)}, u32[]{:S(2)}) copy-start(bf16[1,128,2560]{2,1,0:T(8,128)(2,1)} %param.9) | copy-start | bytes 1966084
  3.3 61.2 %copy-start.2 = (bf16[128,2560]{1,0:T(8,128)(2,1)}, bf16[128,2560]{1,0:T(8,128)(2,1)S(1)}, u32[]{:S(2)}) copy-start(bf16[128,2560]{1,0:T(8,128)(2,1)S(1)} %fusion.18.k_ref) | copy-start | bytes 1966084
  4.5 59.3 %copy-start.24 = (s32[1,4]{1,0:T(1,128)S(1)}, s32[1,4]{1,0:T(1,128)}, u32[]{:S(2)}) copy-start(s32[1,4]{1,0:T(1,128)} %param.13) | copy-start | bytes 52
  4.5 23.4 %collective-permute-start.1 = (bf16[2,128,1536]{2,1,0:T(8,128)(2,1)}, bf16[2,128,1536]{2,1,0:T(8,128)(2,1)S(1)}, u32[]{:S(2)}, u32[]{:S(2)}) collective-permute-start(bf16[2,128,1536]{2,1,0:T(8,128)(2,1)} %pad_maximum_fusion.1), channel_id=1, source_target_pairs={{2,0},{4,2},{6,4},{8,6},{10,8},{12,10},{14,12},{16,14},{18,16},{20... | collective-permute-start | bytes 2359304 | tf_op jit(solution)/shard_map/ppermute | solution.py:26
  17.8 43.7 %collective-permute-start = (bf16[2,128,1536]{2,1,0:T(8,128)(2,1)}, bf16[2,128,1536]{2,1,0:T(8,128)(2,1)S(1)}, u32[]{:S(2)}, u32[]{:S(2)}) collective-permute-start(bf16[2,128,1536]{2,1,0:T(8,128)(2,1)} %pad_maximum_fusion.1), channel_id=1, source_target_pairs={{0,2},{2,4},{4,6},{6,8},{8,10},{10,12},{12,14},{14,16},{16,18},{18... | collective-permute-start | bytes 2359304 | tf_op jit(solution)/shard_map/ppermute | solution.py:26
  19.8 45.7 %collective-permute-start.2 = (bf16[2,128,1536]{2,1,0:T(8,128)(2,1)}, bf16[2,128,1536]{2,1,0:T(8,128)(2,1)}, u32[]{:S(2)}, u32[]{:S(2)}) collective-permute-start(bf16[2,128,1536]{2,1,0:T(8,128)(2,1)} %pad_maximum_fusion.1), channel_id=1, source_target_pairs={{0,4},{4,8},{8,12},{12,16},{16,20},{20,24},{24,28},{28,32},{32,36}... | collective-permute-start | bytes 2359304 | tf_op jit(solution)/shard_map/ppermute | solution.py:31
  27.9 36.7 %copy-start.4 = (bf16[2,128,1536]{2,1,0:T(8,128)(2,1)}, bf16[2,128,1536]{2,1,0:T(8,128)(2,1)S(1)}, u32[]{:S(2)}) copy-start(bf16[2,128,1536]{2,1,0:T(8,128)(2,1)S(1)} %collective-permute-done.1.refs_1_) | copy-start | bytes 2359300
  61.6 3.0 %copy-start.5 = (bf16[2,128,1536]{2,1,0:T(8,128)(2,1)}, bf16[2,128,1536]{2,1,0:T(8,128)(2,1)S(1)}, u32[]{:S(2)}) copy-start(bf16[2,128,1536]{2,1,0:T(8,128)(2,1)S(1)} %collective-permute-done.refs_0_) | copy-start | bytes 2359300
  61.7 9.6 %copy-start = (bf16[1,128,2560]{2,1,0:T(8,128)(2,1)S(1)}, bf16[1,128,2560]{2,1,0:T(8,128)(2,1)}, u32[]{:S(2)}) copy-start(bf16[1,128,2560]{2,1,0:T(8,128)(2,1)} %param.7) | copy-start | bytes 1966084
  61.7 4.3 %collective-permute-start.3 = (bf16[2,128,1536]{2,1,0:T(8,128)(2,1)S(1)}, bf16[2,128,1536]{2,1,0:T(8,128)(2,1)S(1)}, u32[]{:S(2)}, u32[]{:S(2)}) collective-permute-start(bf16[2,128,1536]{2,1,0:T(8,128)(2,1)S(1)} %broadcast_select_fusion), channel_id=1, source_target_pairs={{0,2},{2,0},{4,6},{6,4},{8,10},{10,8},{12,14},{14,12},{16,18},{18,... | collective-permute-start | bytes 2359304 | tf_op jit(solution)/shard_map/ppermute | solution.py:31
  64.5 7.0 %copy-start.19 = (f32[2560]{0:T(1024)S(1)}, f32[2560]{0:T(1024)}, u32[]{:S(2)}) copy-start(f32[2560]{0:T(1024)} %param.11) | copy-start | bytes 30724
  66.9 34.1 %collective-permute-start.5 = (bf16[2,128,1024]{2,1,0:T(8,128)(2,1)}, bf16[2,128,1024]{2,1,0:T(8,128)(2,1)S(1)}, u32[]{:S(2)}, u32[]{:S(2)}) collective-permute-start(bf16[2,128,1024]{2,1,0:T(8,128)(2,1)} %pad_maximum_fusion.3), channel_id=1, source_target_pairs={{2,0},{4,2},{6,4},{8,6},{10,8},{12,10},{14,12},{16,14},{18,16},{20... | collective-permute-start | bytes 1572872 | tf_op jit(solution)/shard_map/ppermute | solution.py:26
  68.9 32.2 %collective-permute-start.4 = (bf16[2,128,1024]{2,1,0:T(8,128)(2,1)}, bf16[2,128,1024]{2,1,0:T(8,128)(2,1)S(1)}, u32[]{:S(2)}, u32[]{:S(2)}) collective-permute-start(bf16[2,128,1024]{2,1,0:T(8,128)(2,1)} %pad_maximum_fusion.3), channel_id=1, source_target_pairs={{0,2},{2,4},{4,6},{6,8},{8,10},{10,12},{12,14},{14,16},{16,18},{18... | collective-permute-start | bytes 1572872 | tf_op jit(solution)/shard_map/ppermute | solution.py:26
  71.5 13.9 %copy-start.21 = (f32[128]{0:T(128)}, f32[128]{0:T(128)S(1)}, u32[]{:S(2)}) copy-start(f32[128]{0:T(128)S(1)} %add_rsqrt_fusion) | copy-start | bytes 1540
  85.4 17.7 %copy-start.10 = (bf16[2,128,1536]{2,1,0:T(8,128)(2,1)S(1)}, bf16[2,128,1536]{2,1,0:T(8,128)(2,1)}, u32[]{:S(2)}) copy-start(bf16[2,128,1536]{2,1,0:T(8,128)(2,1)} %get-tuple-element.28) | copy-start | bytes 2359300
  85.4 17.7 %copy-start.11 = (bf16[2,128,1536]{2,1,0:T(8,128)(2,1)S(1)}, bf16[2,128,1536]{2,1,0:T(8,128)(2,1)}, u32[]{:S(2)}) copy-start(bf16[2,128,1536]{2,1,0:T(8,128)(2,1)} %get-tuple-element.26) | copy-start | bytes 2359300
  85.5 17.6 %collective-permute-start.8 = (bf16[2,128,1536]{2,1,0:T(8,128)(2,1)}, bf16[2,128,1536]{2,1,0:T(8,128)(2,1)S(1)}, u32[]{:S(2)}, u32[]{:S(2)}) collective-permute-start(bf16[2,128,1536]{2,1,0:T(8,128)(2,1)} %get-tuple-element.27), channel_id=1, source_target_pairs={{0,2},{2,0},{4,6},{6,4},{8,10},{10,8},{12,14},{14,12},{16,18},{18,... | collective-permute-start | bytes 2359304 | tf_op jit(solution)/shard_map/ppermute | solution.py:31
  88.9 37.2 %collective-permute-start.6 = (bf16[2,128,1024]{2,1,0:T(8,128)(2,1)}, bf16[2,128,1024]{2,1,0:T(8,128)(2,1)S(1)}, u32[]{:S(2)}, u32[]{:S(2)}) collective-permute-start(bf16[2,128,1024]{2,1,0:T(8,128)(2,1)} %pad_maximum_fusion.3), channel_id=1, source_target_pairs={{0,4},{4,8},{8,12},{12,16},{16,20},{20,24},{24,28},{28,32},{32,36}... | collective-permute-start | bytes 1572872 | tf_op jit(solution)/shard_map/ppermute | solution.py:31
  90.8 54.8 %collective-permute-start.11 = (bf16[2,128,1536]{2,1,0:T(8,128)(2,1)}, bf16[2,128,1536]{2,1,0:T(8,128)(2,1)S(1)}, u32[]{:S(2)}, u32[]{:S(2)}) collective-permute-start(bf16[2,128,1536]{2,1,0:T(8,128)(2,1)} %get-tuple-element.29), channel_id=1, source_target_pairs={{2,6},{6,10},{10,14},{14,18},{18,22},{22,26},{26,30},{30,34},{34,3... | collective-permute-start | bytes 2359304 | tf_op jit(solution)/shard_map/ppermute | solution.py:31
  101.1 3.6 %copy-start.6 = (bf16[2,128,1024]{2,1,0:T(8,128)(2,1)}, bf16[2,128,1024]{2,1,0:T(8,128)(2,1)S(1)}, u32[]{:S(2)}) copy-start(bf16[2,128,1024]{2,1,0:T(8,128)(2,1)S(1)} %collective-permute-done.5.refs_1_) | copy-start | bytes 1572868
  101.1 3.6 %copy-start.7 = (bf16[2,128,1024]{2,1,0:T(8,128)(2,1)}, bf16[2,128,1024]{2,1,0:T(8,128)(2,1)S(1)}, u32[]{:S(2)}) copy-start(bf16[2,128,1024]{2,1,0:T(8,128)(2,1)S(1)} %collective-permute-done.4.refs_0_) | copy-start | bytes 1572868
  101.2 24.9 %collective-permute-start.7 = (bf16[2,128,1024]{2,1,0:T(8,128)(2,1)S(1)}, bf16[2,128,1024]{2,1,0:T(8,128)(2,1)}, u32[]{:S(2)}, u32[]{:S(2)}) collective-permute-start(bf16[2,128,1024]{2,1,0:T(8,128)(2,1)S(1)} %broadcast_select_fusion.1), channel_id=1, source_target_pairs={{0,2},{2,0},{4,6},{6,4},{8,10},{10,8},{12,14},{14,12},{16,18},{18,... | collective-permute-start | bytes 1572872 | tf_op jit(solution)/shard_map/ppermute | solution.py:31
  104.7 50.5 %collective-permute-start.9 = (bf16[2,128,1536]{2,1,0:T(8,128)(2,1)}, bf16[2,128,1536]{2,1,0:T(8,128)(2,1)S(1)}, u32[]{:S(2)}, u32[]{:S(2)}) collective-permute-start(bf16[2,128,1536]{2,1,0:T(8,128)(2,1)} %get-tuple-element.45), channel_id=1, source_target_pairs={{0,2},{2,4},{4,6},{6,8},{8,10},{10,12},{12,14},{14,16},{16,18},{18... | collective-permute-start | bytes 2359304 | tf_op jit(solution)/shard_map/ppermute | solution.py:26
  107.1 48.1 %collective-permute-start.10 = (bf16[2,128,1536]{2,1,0:T(8,128)(2,1)}, bf16[2,128,1536]{2,1,0:T(8,128)(2,1)S(1)}, u32[]{:S(2)}, u32[]{:S(2)}) collective-permute-start(bf16[2,128,1536]{2,1,0:T(8,128)(2,1)} %get-tuple-element.46), channel_id=1, source_target_pairs={{2,0},{4,2},{6,4},{8,6},{10,8},{12,10},{14,12},{16,14},{18,16},{20... | collective-permute-start | bytes 2359304 | tf_op jit(solution)/shard_map/ppermute | solution.py:26
  136.3 3.3 %copy-start.23 = (bf16[2,128,1024]{2,1,0:T(8,128)(2,1)S(1)}, bf16[2,128,1024]{2,1,0:T(8,128)(2,1)}, u32[]{:S(2)}) copy-start(bf16[2,128,1024]{2,1,0:T(8,128)(2,1)} %get-tuple-element.34) | copy-start | bytes 1572868
  136.3 5.2 %copy-start.14 = (f32[128,1024]{1,0:T(8,128)S(1)}, f32[128,1024]{1,0:T(8,128)}, u32[]{:S(2)}) copy-start(f32[128,1024]{1,0:T(8,128)} %get-tuple-element.24) | copy-start | bytes 1572868
  136.3 5.8 %collective-permute-start.12 = (bf16[2,128,1024]{2,1,0:T(8,128)(2,1)}, bf16[2,128,1024]{2,1,0:T(8,128)(2,1)S(1)}, u32[]{:S(2)}, u32[]{:S(2)}) collective-permute-start(bf16[2,128,1024]{2,1,0:T(8,128)(2,1)} %get-tuple-element.32), channel_id=1, source_target_pairs={{0,2},{2,0},{4,6},{6,4},{8,10},{10,8},{12,14},{14,12},{16,18},{18,... | collective-permute-start | bytes 1572872 | tf_op jit(solution)/shard_map/ppermute | solution.py:31
  138.3 3.2 %copy-start.22 = (f32[128]{0:T(128)S(1)}, f32[128]{0:T(128)}, u32[]{:S(2)}) copy-start(f32[128]{0:T(128)} %copy-done.21) | copy-start | bytes 1540
  139.5 16.2 %collective-permute-start.15 = (bf16[2,128,1024]{2,1,0:T(8,128)(2,1)S(1)}, bf16[2,128,1024]{2,1,0:T(8,128)(2,1)S(1)}, u32[]{:S(2)}, u32[]{:S(2)}) collective-permute-start(bf16[2,128,1024]{2,1,0:T(8,128)(2,1)S(1)} %copy-done.23), channel_id=1, source_target_pairs={{2,6},{6,10},{10,14},{14,18},{18,22},{22,26},{26,30},{30,34},{34,3... | collective-permute-start | bytes 1572872 | tf_op jit(solution)/shard_map/ppermute | solution.py:31
  141.5 1.0 copy-start.17
  141.5 1.2 copy-start.18
  142.7 12.5 %copy-start.8 = (f32[128,1536]{1,0:T(8,128)S(1)}, f32[128,1536]{1,0:T(8,128)}, u32[]{:S(2)}) copy-start(f32[128,1536]{1,0:T(8,128)} %get-tuple-element.25) | copy-start | bytes 2359300
  142.7 12.5 %copy-start.9 = (f32[128,1536]{1,0:T(8,128)S(1)}, f32[128,1536]{1,0:T(8,128)}, u32[]{:S(2)}) copy-start(f32[128,1536]{1,0:T(8,128)} %get-tuple-element.35) | copy-start | bytes 2359300
  143.0 28.5 %collective-permute-start.13 = (bf16[2,128,1024]{2,1,0:T(8,128)(2,1)S(1)}, bf16[2,128,1024]{2,1,0:T(8,128)(2,1)S(1)}, u32[]{:S(2)}, u32[]{:S(2)}) collective-permute-start(bf16[2,128,1024]{2,1,0:T(8,128)(2,1)S(1)} %get-tuple-element.47), channel_id=1, source_target_pairs={{0,2},{2,4},{4,6},{6,8},{8,10},{10,12},{12,14},{14,16},{16,18},{18... | collective-permute-start | bytes 1572872 | tf_op jit(solution)/shard_map/ppermute | solution.py:26
  145.6 25.9 %collective-permute-start.14 = (bf16[2,128,1024]{2,1,0:T(8,128)(2,1)S(1)}, bf16[2,128,1024]{2,1,0:T(8,128)(2,1)S(1)}, u32[]{:S(2)}, u32[]{:S(2)}) collective-permute-start(bf16[2,128,1024]{2,1,0:T(8,128)(2,1)S(1)} %get-tuple-element.48), channel_id=1, source_target_pairs={{2,0},{4,2},{6,4},{8,6},{10,8},{12,10},{14,12},{16,14},{18,16},{20... | collective-permute-start | bytes 1572872 | tf_op jit(solution)/shard_map/ppermute | solution.py:26
  155.2 16.3 %copy-start.15 = (f32[128,1024]{1,0:T(8,128)S(1)}, f32[128,1024]{1,0:T(8,128)}, u32[]{:S(2)}) copy-start(f32[128,1024]{1,0:T(8,128)} %get-tuple-element.30) | copy-start | bytes 1572868
  155.2 16.3 %copy-start.16 = (f32[128,1024]{1,0:T(8,128)S(1)}, f32[128,1024]{1,0:T(8,128)}, u32[]{:S(2)}) copy-start(f32[128,1024]{1,0:T(8,128)} %get-tuple-element.36) | copy-start | bytes 1572868
  171.5 1.1 copy-start.1
  171.5 1.1 copy-start.20
  173.1 5.7 %collective-permute-start.16 = (f32[5120]{0:T(1024)S(1)}, f32[5120]{0:T(1024)S(1)}, u32[]{:S(2)}, u32[]{:S(2)}) collective-permute-start(f32[5120]{0:T(1024)S(1)} %pad_maximum_fusion.4), channel_id=1, source_target_pairs={{0,1},{1,0},{2,3},{3,2},{4,5},{5,4},{6,7},{7,6},{8,9},{9,8},{10,11... | collective-permute-start | bytes 61448 | tf_op jit(solution)/shard_map/ppermute | solution.py:65
  178.8 3.1 %collective-permute-start.17 = (f32[5120]{0:T(1024)S(1)}, f32[5120]{0:T(1024)S(1)}, u32[]{:S(2)}, u32[]{:S(2)}) collective-permute-start(f32[5120]{0:T(1024)S(1)} %fusion.38), channel_id=1, source_target_pairs={{0,2},{2,0},{4,6},{6,4},{8,10},{10,8},{12,14},{14,12},{16,18},{18,... | collective-permute-start | bytes 61448 | tf_op jit(solution)/shard_map/ppermute | solution.py:65
  181.8 5.7 %collective-permute-start.18 = (f32[5120]{0:T(1024)S(1)}, f32[5120]{0:T(1024)S(1)}, u32[]{:S(2)}, u32[]{:S(2)}) collective-permute-start(f32[5120]{0:T(1024)S(1)} %add.119), channel_id=1, source_target_pairs={{0,4},{2,6},{4,0},{6,2},{8,12},{10,14},{12,8},{14,10},{16,20},{18,... | collective-permute-start | bytes 61448 | tf_op jit(solution)/shard_map/ppermute | solution.py:65
  187.5 7.2 %collective-permute-start.19 = (f32[5120]{0:T(1024)S(1)}, f32[5120]{0:T(1024)S(1)}, u32[]{:S(2)}, u32[]{:S(2)}) collective-permute-start(f32[5120]{0:T(1024)S(1)} %add.120), channel_id=1, source_target_pairs={{0,8},{2,10},{4,12},{6,14},{8,0},{10,2},{12,4},{14,6},{16,24},{18,... | collective-permute-start | bytes 61448 | tf_op jit(solution)/shard_map/ppermute | solution.py:65
  194.7 5.7 %collective-permute-start.20 = (f32[5120]{0:T(1024)S(1)}, f32[5120]{0:T(1024)S(1)}, u32[]{:S(2)}, u32[]{:S(2)}) collective-permute-start(f32[5120]{0:T(1024)S(1)} %add.121), channel_id=1, source_target_pairs={{0,16},{2,18},{4,20},{6,22},{8,24},{10,26},{12,28},{14,30},{16,0},... | collective-permute-start | bytes 61448 | tf_op jit(solution)/shard_map/ppermute | solution.py:65
  200.3 6.6 %collective-permute-start.21 = (f32[5120]{0:T(1024)S(1)}, f32[5120]{0:T(1024)S(1)}, u32[]{:S(2)}, u32[]{:S(2)}) collective-permute-start(f32[5120]{0:T(1024)S(1)} %add.122), channel_id=1, source_target_pairs={{0,32},{2,34},{4,36},{6,38},{8,40},{10,42},{12,44},{14,46},{16,48}... | collective-permute-start | bytes 61448 | tf_op jit(solution)/shard_map/ppermute | solution.py:65
  206.9 9.6 %collective-permute-start.22 = (f32[5120]{0:T(1024)S(1)}, f32[5120]{0:T(1024)S(1)}, u32[]{:S(2)}, u32[]{:S(2)}) collective-permute-start(f32[5120]{0:T(1024)S(1)} %add.123), channel_id=1, source_target_pairs={{0,64},{2,66},{4,68},{6,70},{8,72},{10,74},{12,76},{14,78},{16,80}... | collective-permute-start | bytes 61448 | tf_op jit(solution)/shard_map/ppermute | solution.py:65
  216.5 6.6 %collective-permute-start.23 = (f32[5120]{0:T(1024)S(1)}, f32[5120]{0:T(1024)S(1)}, u32[]{:S(2)}, u32[]{:S(2)}) collective-permute-start(f32[5120]{0:T(1024)S(1)} %add.124), channel_id=1, source_target_pairs={{0,128},{2,130},{4,132},{6,134},{8,136},{10,138},{12,140},{14,142}... | collective-permute-start | bytes 61448 | tf_op jit(solution)/shard_map/ppermute | solution.py:65
  223.1 9.6 %collective-permute-start.24 = (f32[5120]{0:T(1024)S(1)}, f32[5120]{0:T(1024)S(1)}, u32[]{:S(2)}, u32[]{:S(2)}) collective-permute-start(f32[5120]{0:T(1024)S(1)} %add.125), channel_id=1, source_target_pairs={{0,256},{2,258},{4,260},{6,262},{8,264},{10,266},{12,268},{14,270}... | collective-permute-start | bytes 61448 | tf_op jit(solution)/shard_map/ppermute | solution.py:65
  (2 other events, 1.7 us)

commit v12 on v9

--- a/solution.py
+++ b/solution.py
@@ -112,9 +112,9 @@
         vals = jnp.concatenate([v_ref[:, cols], pick(1)], axis=0)
         scores = lax.dot_general(q, keys, NT, preferred_element_type=jnp.float32) * scale + bias
         highest = jnp.max(scores, axis=1, keepdims=True)
-        total = jnp.sum(jnp.exp(scores - highest), axis=1, keepdims=True)
-        log_total = highest + jnp.log(total)
-        prob = jnp.exp(scores - log_total).astype(jnp.bfloat16)
+        shifted = jnp.exp(scores - highest)
+        total = jnp.sum(shifted, axis=1, keepdims=True)
+        prob = (shifted * (1.0 / total)).astype(jnp.bfloat16)
         attended = jnp.dot(prob, vals, preferred_element_type=jnp.float32)
         delta = jnp.sum(g.astype(jnp.float32) * attended, axis=1, keepdims=True)
         prob_grad = lax.dot_general(g, vals, NT, preferred_element_type=jnp.float32)

time: 229 us -> 229 us (level)
  no operation moved by 1% of the time
where the time goes in v12:
time: 229 us; the launch traced here: 228 us
  starting transfers between devices  107 us (47%)
  waiting for transfers between devices  79.2 us (35%)
  Pallas kernels  21.9 us (10%)
  other arithmetic  14.3 us (6%)
  local copies, waits for them, and re-layouts  3.94 us (2%)
    ppermute x8, starting transfers between devices, from_behind(): lax.ppermute(value, axis, [(source, source + steps) for source in range(f...  46.6 us
    ppermute x8, starting transfers between devices, pairs_permute(): lax.ppermute(value, axis, [(i, j) for i, j in pairs if 0 <= j < count])  42.6 us
    ppermute x8, waiting for transfers between devices, from_behind(): lax.ppermute(value, axis, [(source, source + steps) for source in range(f...  40.7 us
    ppermute x9, waiting for transfers between devices, all_sum(): lax.ppermute(value, axis, [(i, i ^ bit) for i in range(count)])  38.2 us
    pallas_call x2, Pallas kernels, attention(): pl.pallas_call(attention_kernel, grid_spec=grid_spec, out_shape=[f32] * 3...  21.9 us
    ppermute x9, starting transfers between devices, all_sum(): lax.ppermute(value, axis, [(i, i ^ bit) for i in range(count)])  17.9 us
  transfers between devices with their start and end apart: 25, of which 13 were waited for; matrix products, arithmetic and copies ran while one was open for 5% of the time, Pallas kernels for 10%

profile of v12, /device:TPU:32, one launch (start us, length us, event | category | flops | bytes accessed | tf_op | source)
XLA Modules:
  0.0 227.7 jit_solution(15557530049073092693)
XLA Ops:
  0.6 1.4 fusion.23
  2.0 1.3 fusion.20.k_ref
  3.4 1.0 pad_maximum_fusion.1
  4.4 3.4 %collective-permute-start.2 = (bf16[2,128,1536]{2,1,0:T(8,128)(2,1)}, bf16[2,128,1536]{2,1,0:T(8,128)(2,1)}, u32[]{:S(2)}, u32[]{:S(2)}) collective-permute-start(bf16[2,128,1536]{2,1,0:T(8,128)(2,1)} %pad_maximum_fusion.1), channel_id=1, source_target_pairs={{0,4},{4,8},{8,12},{12,16},{16,20},{20,24},{24,28},{28,32},{32,36}... | collective-permute-start | bytes 2359304 | tf_op jit(solution)/shard_map/ppermute | solution.py:31
  7.8 11.4 %collective-permute-start.1 = (bf16[2,128,1536]{2,1,0:T(8,128)(2,1)}, bf16[2,128,1536]{2,1,0:T(8,128)(2,1)S(1)}, u32[]{:S(2)}, u32[]{:S(2)}) collective-permute-start(bf16[2,128,1536]{2,1,0:T(8,128)(2,1)} %pad_maximum_fusion.1), channel_id=1, source_target_pairs={{2,0},{4,2},{6,4},{8,6},{10,8},{12,10},{14,12},{16,14},{18,16},{20... | collective-permute-start | bytes 2359304 | tf_op jit(solution)/shard_map/ppermute | solution.py:26
  19.2 1.9 collective-permute-start
  22.2 29.0 %collective-permute-done.1.refs_1_ = bf16[2,128,1536]{2,1,0:T(8,128)(2,1)S(1)} collective-permute-done((bf16[2,128,1536]{2,1,0:T(8,128)(2,1)}, bf16[2,128,1536]{2,1,0:T(8,128)(2,1)S(1)}, u32[]{:S(2)}, u32[]{:S(2)}) %collective-permute-start.1) | collective-permute-done | bytes 786464 | tf_op jit(solution)/shard_map/ppermute | solution.py:26
  51.3 2.7 %collective-permute-done.refs_0_ = bf16[2,128,1536]{2,1,0:T(8,128)(2,1)S(1)} collective-permute-done((bf16[2,128,1536]{2,1,0:T(8,128)(2,1)}, bf16[2,128,1536]{2,1,0:T(8,128)(2,1)S(1)}, u32[]{:S(2)}, u32[]{:S(2)}) %collective-permute-start) | collective-permute-done | bytes 786464 | tf_op jit(solution)/shard_map/ppermute | solution.py:26
  54.1 1.9 collective-permute-start.3
  56.8 1.1 fusion.12.q_ref
  58.2 1.0 copy-done.14
  59.2 7.3 %collective-permute-start.5 = (bf16[2,128,1024]{2,1,0:T(8,128)(2,1)}, bf16[2,128,1024]{2,1,0:T(8,128)(2,1)S(1)}, u32[]{:S(2)}, u32[]{:S(2)}) collective-permute-start(bf16[2,128,1024]{2,1,0:T(8,128)(2,1)} %pad_maximum_fusion.3), channel_id=1, source_target_pairs={{2,0},{4,2},{6,4},{8,6},{10,8},{12,10},{14,12},{16,14},{18,16},{20... | collective-permute-start | bytes 1572872 | tf_op jit(solution)/shard_map/ppermute | solution.py:26
  66.5 1.9 collective-permute-start.4
  68.5 12.6 %shard_map.110 = (f32[128,1536]{1,0:T(8,128)}, f32[128,1536]{1,0:T(8,128)}, f32[128,1536]{1,0:T(8,128)}, bf16[2,128,1536]{2,1,0:T(8,128)(2,1)}, bf16[2,128,1536]...) custom-call(s32[1]{0:T(128)} %bitcast.1.odd_ref, f32[1,640]{1,0:T(1,128)} %bitcast.137, ...), custom_call_target="tpu_custom_call" | custom-call | flops 1509949440 | bytes 7077888 | tf_op jit(solution)/shard_map/pallas_call | solution.py:161
  81.1 2.1 collective-permute-start.8
  83.2 1.9 collective-permute-start.6
  85.1 10.4 %collective-permute-start.11 = (bf16[2,128,1536]{2,1,0:T(8,128)(2,1)}, bf16[2,128,1536]{2,1,0:T(8,128)(2,1)S(1)}, u32[]{:S(2)}, u32[]{:S(2)}) collective-permute-start(bf16[2,128,1536]{2,1,0:T(8,128)(2,1)} %get-tuple-element.27), channel_id=1, source_target_pairs={{2,6},{6,10},{10,14},{14,18},{18,22},{22,26},{26,30},{30,34},{34,3... | collective-permute-start | bytes 2359304 | tf_op jit(solution)/shard_map/ppermute | solution.py:31
  95.6 1.9 collective-permute-start.7
  97.5 1.6 fusion.29
  99.2 2.4 %collective-permute-start.9 = (bf16[2,128,1536]{2,1,0:T(8,128)(2,1)}, bf16[2,128,1536]{2,1,0:T(8,128)(2,1)S(1)}, u32[]{:S(2)}, u32[]{:S(2)}) collective-permute-start(bf16[2,128,1536]{2,1,0:T(8,128)(2,1)} %get-tuple-element.43), channel_id=1, source_target_pairs={{0,2},{2,4},{4,6},{6,8},{8,10},{10,12},{12,14},{14,16},{16,18},{18... | collective-permute-start | bytes 2359304 | tf_op jit(solution)/shard_map/ppermute | solution.py:26
  101.6 9.6 %collective-permute-start.10 = (bf16[2,128,1536]{2,1,0:T(8,128)(2,1)}, bf16[2,128,1536]{2,1,0:T(8,128)(2,1)}, u32[]{:S(2)}, u32[]{:S(2)}) collective-permute-start(bf16[2,128,1536]{2,1,0:T(8,128)(2,1)} %get-tuple-element.44), channel_id=1, source_target_pairs={{2,0},{4,2},{6,4},{8,6},{10,8},{12,10},{14,12},{16,14},{18,16},{20... | collective-permute-start | bytes 2359304 | tf_op jit(solution)/shard_map/ppermute | solution.py:26
  111.2 9.2 %shard_map.111 = (f32[128,1024]{1,0:T(8,128)}, f32[128,1024]{1,0:T(8,128)}, f32[128,1024]{1,0:T(8,128)}, bf16[2,128,1024]{2,1,0:T(8,128)(2,1)}, bf16[2,128,1024]...) custom-call(s32[1]{0:T(128)} %bitcast.1.odd_ref, f32[1,640]{1,0:T(1,128)} %bitcast.138, ...), custom_call_target="tpu_custom_call" | custom-call | flops 1006632960 | bytes 4718592 | tf_op jit(solution)/shard_map/pallas_call | solution.py:161
  120.5 10.5 %collective-permute-start.12 = (bf16[2,128,1024]{2,1,0:T(8,128)(2,1)}, bf16[2,128,1024]{2,1,0:T(8,128)(2,1)S(1)}, u32[]{:S(2)}, u32[]{:S(2)}) collective-permute-start(bf16[2,128,1024]{2,1,0:T(8,128)(2,1)} %get-tuple-element.30), channel_id=1, source_target_pairs={{0,2},{2,0},{4,6},{6,4},{8,10},{10,8},{12,14},{14,12},{16,18},{18,... | collective-permute-start | bytes 1572872 | tf_op jit(solution)/shard_map/ppermute | solution.py:31
  131.0 10.6 %collective-permute-start.15 = (bf16[2,128,1024]{2,1,0:T(8,128)(2,1)S(1)}, bf16[2,128,1024]{2,1,0:T(8,128)(2,1)S(1)}, u32[]{:S(2)}, u32[]{:S(2)}) collective-permute-start(bf16[2,128,1024]{2,1,0:T(8,128)(2,1)S(1)} %copy-done.23), channel_id=1, source_target_pairs={{2,6},{6,10},{10,14},{14,18},{18,22},{22,26},{26,30},{30,34},{34,3... | collective-permute-start | bytes 1572872 | tf_op jit(solution)/shard_map/ppermute | solution.py:31
  143.2 2.1 collective-permute-start.13
  145.3 10.0 %collective-permute-start.14 = (bf16[2,128,1024]{2,1,0:T(8,128)(2,1)S(1)}, bf16[2,128,1024]{2,1,0:T(8,128)(2,1)S(1)}, u32[]{:S(2)}, u32[]{:S(2)}) collective-permute-start(bf16[2,128,1024]{2,1,0:T(8,128)(2,1)S(1)} %get-tuple-element.46), channel_id=1, source_target_pairs={{2,0},{4,2},{6,4},{8,6},{10,8},{12,10},{14,12},{16,14},{18,16},{20... | collective-permute-start | bytes 1572872 | tf_op jit(solution)/shard_map/ppermute | solution.py:26
  155.3 1.7 fusion.36
  157.0 9.0 %collective-permute-done.13 = bf16[2,128,1024]{2,1,0:T(8,128)(2,1)S(1)} collective-permute-done((bf16[2,128,1024]{2,1,0:T(8,128)(2,1)S(1)}, bf16[2,128,1024]{2,1,0:T(8,128)(2,1)S(1)}, u32[]{:S(2)}, u32[]{:S(2)}) %collective-permute-start.13) | collective-permute-done | bytes 524320 | tf_op jit(solution)/shard_map/ppermute | solution.py:26
  167.6 1.9 collective-permute-start.16
  169.5 3.7 %collective-permute-done.16 = f32[5120]{0:T(1024)S(1)} collective-permute-done((f32[5120]{0:T(1024)S(1)}, f32[5120]{0:T(1024)S(1)}, u32[]{:S(2)}, u32[]{:S(2)}) %collective-permute-start.16) | collective-permute-done | bytes 20512 | tf_op jit(solution)/shard_map/ppermute | solution.py:65
  173.2 1.9 collective-permute-start.17
  175.2 1.2 collective-permute-done.17
  176.3 1.9 collective-permute-start.18
  178.2 3.7 %collective-permute-done.18 = f32[5120]{0:T(1024)S(1)} collective-permute-done((f32[5120]{0:T(1024)S(1)}, f32[5120]{0:T(1024)S(1)}, u32[]{:S(2)}, u32[]{:S(2)}) %collective-permute-start.18) | collective-permute-done | bytes 20512 | tf_op jit(solution)/shard_map/ppermute | solution.py:65
  182.0 1.9 collective-permute-start.19
  183.9 5.3 %collective-permute-done.19 = f32[5120]{0:T(1024)S(1)} collective-permute-done((f32[5120]{0:T(1024)S(1)}, f32[5120]{0:T(1024)S(1)}, u32[]{:S(2)}, u32[]{:S(2)}) %collective-permute-start.19) | collective-permute-done | bytes 20512 | tf_op jit(solution)/shard_map/ppermute | solution.py:65
  189.2 1.9 collective-permute-start.20
  191.1 3.7 %collective-permute-done.20 = f32[5120]{0:T(1024)S(1)} collective-permute-done((f32[5120]{0:T(1024)S(1)}, f32[5120]{0:T(1024)S(1)}, u32[]{:S(2)}, u32[]{:S(2)}) %collective-permute-start.20) | collective-permute-done | bytes 20512 | tf_op jit(solution)/shard_map/ppermute | solution.py:65
  194.8 1.9 collective-permute-start.21
  196.8 1.3 fusion.19
  198.0 3.4 %collective-permute-done.21 = f32[5120]{0:T(1024)S(1)} collective-permute-done((f32[5120]{0:T(1024)S(1)}, f32[5120]{0:T(1024)S(1)}, u32[]{:S(2)}, u32[]{:S(2)}) %collective-permute-start.21) | collective-permute-done | bytes 20512 | tf_op jit(solution)/shard_map/ppermute | solution.py:65
  201.4 1.9 collective-permute-start.22
  203.3 7.6 %collective-permute-done.22 = f32[5120]{0:T(1024)S(1)} collective-permute-done((f32[5120]{0:T(1024)S(1)}, f32[5120]{0:T(1024)S(1)}, u32[]{:S(2)}, u32[]{:S(2)}) %collective-permute-start.22) | collective-permute-done | bytes 20512 | tf_op jit(solution)/shard_map/ppermute | solution.py:65
  211.0 2.6 %collective-permute-start.23 = (f32[5120]{0:T(1024)S(1)}, f32[5120]{0:T(1024)S(1)}, u32[]{:S(2)}, u32[]{:S(2)}) collective-permute-start(f32[5120]{0:T(1024)S(1)} %add.124), channel_id=1, source_target_pairs={{0,128},{2,130},{4,132},{6,134},{8,136},{10,138},{12,140},{14,142}... | collective-permute-start | bytes 61448 | tf_op jit(solution)/shard_map/ppermute | solution.py:65
  213.6 1.2 fusion.27
  214.8 2.7 %collective-permute-done.23 = f32[5120]{0:T(1024)S(1)} collective-permute-done((f32[5120]{0:T(1024)S(1)}, f32[5120]{0:T(1024)S(1)}, u32[]{:S(2)}, u32[]{:S(2)}) %collective-permute-start.23) | collective-permute-done | bytes 20512 | tf_op jit(solution)/shard_map/ppermute | solution.py:65
  217.6 1.9 collective-permute-start.24
  220.4 6.8 %collective-permute-done.24 = f32[5120]{0:T(1024)S(1)} collective-permute-done((f32[5120]{0:T(1024)S(1)}, f32[5120]{0:T(1024)S(1)}, u32[]{:S(2)}, u32[]{:S(2)}) %collective-permute-start.24) | collective-permute-done | bytes 20512 | tf_op jit(solution)/shard_map/ppermute | solution.py:65
  (94 shorter events, 7.1 us)
Async XLA Ops:
  0.6 2.7 %copy-start.3 = (bf16[1,128,2560]{2,1,0:T(8,128)(2,1)S(1)}, bf16[1,128,2560]{2,1,0:T(8,128)(2,1)}, u32[]{:S(2)}) copy-start(bf16[1,128,2560]{2,1,0:T(8,128)(2,1)} %param.9) | copy-start | bytes 1966084
  3.3 18.8 %copy-start.2 = (bf16[128,2560]{1,0:T(8,128)(2,1)}, bf16[128,2560]{1,0:T(8,128)(2,1)S(1)}, u32[]{:S(2)}) copy-start(bf16[128,2560]{1,0:T(8,128)(2,1)S(1)} %fusion.20.k_ref) | copy-start | bytes 1966084
  3.4 17.8 %copy-start.24 = (s32[1,4]{1,0:T(1,128)S(1)}, s32[1,4]{1,0:T(1,128)}, u32[]{:S(2)}) copy-start(s32[1,4]{1,0:T(1,128)} %param.13) | copy-start | bytes 52
  3.4 18.6 %copy-start = (bf16[1,128,2560]{2,1,0:T(8,128)(2,1)S(1)}, bf16[1,128,2560]{2,1,0:T(8,128)(2,1)}, u32[]{:S(2)}) copy-start(bf16[1,128,2560]{2,1,0:T(8,128)(2,1)} %param.7) | copy-start | bytes 1966084
  4.4 53.5 %collective-permute-start.2 = (bf16[2,128,1536]{2,1,0:T(8,128)(2,1)}, bf16[2,128,1536]{2,1,0:T(8,128)(2,1)}, u32[]{:S(2)}, u32[]{:S(2)}) collective-permute-start(bf16[2,128,1536]{2,1,0:T(8,128)(2,1)} %pad_maximum_fusion.1), channel_id=1, source_target_pairs={{0,4},{4,8},{8,12},{12,16},{16,20},{20,24},{24,28},{28,32},{32,36}... | collective-permute-start | bytes 2359304 | tf_op jit(solution)/shard_map/ppermute | solution.py:31
  7.8 43.5 %collective-permute-start.1 = (bf16[2,128,1536]{2,1,0:T(8,128)(2,1)}, bf16[2,128,1536]{2,1,0:T(8,128)(2,1)S(1)}, u32[]{:S(2)}, u32[]{:S(2)}) collective-permute-start(bf16[2,128,1536]{2,1,0:T(8,128)(2,1)} %pad_maximum_fusion.1), channel_id=1, source_target_pairs={{2,0},{4,2},{6,4},{8,6},{10,8},{12,10},{14,12},{16,14},{18,16},{20... | collective-permute-start | bytes 2359304 | tf_op jit(solution)/shard_map/ppermute | solution.py:26
  19.2 34.7 %collective-permute-start = (bf16[2,128,1536]{2,1,0:T(8,128)(2,1)}, bf16[2,128,1536]{2,1,0:T(8,128)(2,1)S(1)}, u32[]{:S(2)}, u32[]{:S(2)}) collective-permute-start(bf16[2,128,1536]{2,1,0:T(8,128)(2,1)} %pad_maximum_fusion.1), channel_id=1, source_target_pairs={{0,2},{2,4},{4,6},{6,8},{8,10},{10,12},{12,14},{14,16},{16,18},{18... | collective-permute-start | bytes 2359304 | tf_op jit(solution)/shard_map/ppermute | solution.py:26
  22.2 34.7 %copy-start.21 = (f32[128]{0:T(128)}, f32[128]{0:T(128)S(1)}, u32[]{:S(2)}) copy-start(f32[128]{0:T(128)S(1)} %add_rsqrt_fusion.1) | copy-start | bytes 1540
  22.2 34.6 %copy-start.19 = (f32[2560]{0:T(1024)S(1)}, f32[2560]{0:T(1024)}, u32[]{:S(2)}) copy-start(f32[2560]{0:T(1024)} %param.11) | copy-start | bytes 30724
  51.3 5.6 %copy-start.5 = (bf16[2,128,1536]{2,1,0:T(8,128)(2,1)}, bf16[2,128,1536]{2,1,0:T(8,128)(2,1)S(1)}, u32[]{:S(2)}) copy-start(bf16[2,128,1536]{2,1,0:T(8,128)(2,1)S(1)} %collective-permute-done.1.refs_1_) | copy-start | bytes 2359300
  54.0 2.9 %copy-start.6 = (bf16[2,128,1536]{2,1,0:T(8,128)(2,1)}, bf16[2,128,1536]{2,1,0:T(8,128)(2,1)S(1)}, u32[]{:S(2)}) copy-start(bf16[2,128,1536]{2,1,0:T(8,128)(2,1)S(1)} %collective-permute-done.refs_0_) | copy-start | bytes 2359300
  54.1 4.2 %collective-permute-start.3 = (bf16[2,128,1536]{2,1,0:T(8,128)(2,1)S(1)}, bf16[2,128,1536]{2,1,0:T(8,128)(2,1)S(1)}, u32[]{:S(2)}, u32[]{:S(2)}) collective-permute-start(bf16[2,128,1536]{2,1,0:T(8,128)(2,1)S(1)} %broadcast_select_fusion), channel_id=1, source_target_pairs={{0,2},{2,0},{4,6},{6,4},{8,10},{10,8},{12,14},{14,12},{16,18},{18,... | collective-permute-start | bytes 2359304 | tf_op jit(solution)/shard_map/ppermute | solution.py:31
  59.2 36.3 %collective-permute-start.5 = (bf16[2,128,1024]{2,1,0:T(8,128)(2,1)}, bf16[2,128,1024]{2,1,0:T(8,128)(2,1)S(1)}, u32[]{:S(2)}, u32[]{:S(2)}) collective-permute-start(bf16[2,128,1024]{2,1,0:T(8,128)(2,1)} %pad_maximum_fusion.3), channel_id=1, source_target_pairs={{2,0},{4,2},{6,4},{8,6},{10,8},{12,10},{14,12},{16,14},{18,16},{20... | collective-permute-start | bytes 1572872 | tf_op jit(solution)/shard_map/ppermute | solution.py:26
  66.5 29.0 %collective-permute-start.4 = (bf16[2,128,1024]{2,1,0:T(8,128)(2,1)}, bf16[2,128,1024]{2,1,0:T(8,128)(2,1)S(1)}, u32[]{:S(2)}, u32[]{:S(2)}) collective-permute-start(bf16[2,128,1024]{2,1,0:T(8,128)(2,1)} %pad_maximum_fusion.3), channel_id=1, source_target_pairs={{0,2},{2,4},{4,6},{6,8},{8,10},{10,12},{12,14},{14,16},{16,18},{18... | collective-permute-start | bytes 1572872 | tf_op jit(solution)/shard_map/ppermute | solution.py:26
  81.1 16.4 %copy-start.12 = (bf16[2,128,1536]{2,1,0:T(8,128)(2,1)S(1)}, bf16[2,128,1536]{2,1,0:T(8,128)(2,1)}, u32[]{:S(2)}) copy-start(bf16[2,128,1536]{2,1,0:T(8,128)(2,1)} %get-tuple-element.26) | copy-start | bytes 2359300
  81.1 16.4 %copy-start.13 = (bf16[2,128,1536]{2,1,0:T(8,128)(2,1)S(1)}, bf16[2,128,1536]{2,1,0:T(8,128)(2,1)}, u32[]{:S(2)}) copy-start(bf16[2,128,1536]{2,1,0:T(8,128)(2,1)} %get-tuple-element.24) | copy-start | bytes 2359300
  81.1 16.4 %collective-permute-start.8 = (bf16[2,128,1536]{2,1,0:T(8,128)(2,1)}, bf16[2,128,1536]{2,1,0:T(8,128)(2,1)S(1)}, u32[]{:S(2)}, u32[]{:S(2)}) collective-permute-start(bf16[2,128,1536]{2,1,0:T(8,128)(2,1)} %get-tuple-element.25), channel_id=1, source_target_pairs={{0,2},{2,0},{4,6},{6,4},{8,10},{10,8},{12,14},{14,12},{16,18},{18,... | collective-permute-start | bytes 2359304 | tf_op jit(solution)/shard_map/ppermute | solution.py:31
  83.2 28.0 %collective-permute-start.6 = (bf16[2,128,1024]{2,1,0:T(8,128)(2,1)}, bf16[2,128,1024]{2,1,0:T(8,128)(2,1)}, u32[]{:S(2)}, u32[]{:S(2)}) collective-permute-start(bf16[2,128,1024]{2,1,0:T(8,128)(2,1)} %pad_maximum_fusion.3), channel_id=1, source_target_pairs={{0,4},{4,8},{8,12},{12,16},{16,20},{20,24},{24,28},{28,32},{32,36}... | collective-permute-start | bytes 1572872 | tf_op jit(solution)/shard_map/ppermute | solution.py:31
  85.1 60.2 %collective-permute-start.11 = (bf16[2,128,1536]{2,1,0:T(8,128)(2,1)}, bf16[2,128,1536]{2,1,0:T(8,128)(2,1)S(1)}, u32[]{:S(2)}, u32[]{:S(2)}) collective-permute-start(bf16[2,128,1536]{2,1,0:T(8,128)(2,1)} %get-tuple-element.27), channel_id=1, source_target_pairs={{2,6},{6,10},{10,14},{14,18},{18,22},{22,26},{26,30},{30,34},{34,3... | collective-permute-start | bytes 2359304 | tf_op jit(solution)/shard_map/ppermute | solution.py:31
  95.5 3.7 %copy-start.8 = (bf16[2,128,1024]{2,1,0:T(8,128)(2,1)}, bf16[2,128,1024]{2,1,0:T(8,128)(2,1)S(1)}, u32[]{:S(2)}) copy-start(bf16[2,128,1024]{2,1,0:T(8,128)(2,1)S(1)} %collective-permute-done.5.refs_1_) | copy-start | bytes 1572868
  95.5 3.7 %copy-start.9 = (bf16[2,128,1024]{2,1,0:T(8,128)(2,1)}, bf16[2,128,1024]{2,1,0:T(8,128)(2,1)S(1)}, u32[]{:S(2)}) copy-start(bf16[2,128,1024]{2,1,0:T(8,128)(2,1)S(1)} %collective-permute-done.4.refs_0_) | copy-start | bytes 1572868
  95.6 15.6 %collective-permute-start.7 = (bf16[2,128,1024]{2,1,0:T(8,128)(2,1)S(1)}, bf16[2,128,1024]{2,1,0:T(8,128)(2,1)}, u32[]{:S(2)}, u32[]{:S(2)}) collective-permute-start(bf16[2,128,1024]{2,1,0:T(8,128)(2,1)S(1)} %broadcast_select_fusion.1), channel_id=1, source_target_pairs={{0,2},{2,0},{4,6},{6,4},{8,10},{10,8},{12,14},{14,12},{16,18},{18,... | collective-permute-start | bytes 1572872 | tf_op jit(solution)/shard_map/ppermute | solution.py:31
  99.2 56.1 %collective-permute-start.9 = (bf16[2,128,1536]{2,1,0:T(8,128)(2,1)}, bf16[2,128,1536]{2,1,0:T(8,128)(2,1)S(1)}, u32[]{:S(2)}, u32[]{:S(2)}) collective-permute-start(bf16[2,128,1536]{2,1,0:T(8,128)(2,1)} %get-tuple-element.43), channel_id=1, source_target_pairs={{0,2},{2,4},{4,6},{6,8},{8,10},{10,12},{12,14},{14,16},{16,18},{18... | collective-permute-start | bytes 2359304 | tf_op jit(solution)/shard_map/ppermute | solution.py:26
  101.6 29.4 %copy-start.4 = (f32[128,1536]{1,0:T(8,128)S(1)}, f32[128,1536]{1,0:T(8,128)}, u32[]{:S(2)}) copy-start(f32[128,1536]{1,0:T(8,128)} %get-tuple-element.20) | copy-start | bytes 2359300
  101.6 53.7 %collective-permute-start.10 = (bf16[2,128,1536]{2,1,0:T(8,128)(2,1)}, bf16[2,128,1536]{2,1,0:T(8,128)(2,1)}, u32[]{:S(2)}, u32[]{:S(2)}) collective-permute-start(bf16[2,128,1536]{2,1,0:T(8,128)(2,1)} %get-tuple-element.44), channel_id=1, source_target_pairs={{2,0},{4,2},{6,4},{8,6},{10,8},{12,10},{14,12},{16,14},{18,16},{20... | collective-permute-start | bytes 2359304 | tf_op jit(solution)/shard_map/ppermute | solution.py:26
  120.4 10.6 %copy-start.23 = (bf16[2,128,1024]{2,1,0:T(8,128)(2,1)S(1)}, bf16[2,128,1024]{2,1,0:T(8,128)(2,1)}, u32[]{:S(2)}) copy-start(bf16[2,128,1024]{2,1,0:T(8,128)(2,1)} %get-tuple-element.32) | copy-start | bytes 1572868
  120.5 21.2 %copy-start.7 = (f32[128,1024]{1,0:T(8,128)S(1)}, f32[128,1024]{1,0:T(8,128)}, u32[]{:S(2)}) copy-start(f32[128,1024]{1,0:T(8,128)} %get-tuple-element.22) | copy-start | bytes 1572868
  120.5 21.7 %collective-permute-start.12 = (bf16[2,128,1024]{2,1,0:T(8,128)(2,1)}, bf16[2,128,1024]{2,1,0:T(8,128)(2,1)S(1)}, u32[]{:S(2)}, u32[]{:S(2)}) collective-permute-start(bf16[2,128,1024]{2,1,0:T(8,128)(2,1)} %get-tuple-element.30), channel_id=1, source_target_pairs={{0,2},{2,0},{4,6},{6,4},{8,10},{10,8},{12,14},{14,12},{16,18},{18,... | collective-permute-start | bytes 1572872 | tf_op jit(solution)/shard_map/ppermute | solution.py:31
  130.9 10.8 %copy-start.22 = (f32[128]{0:T(128)S(1)}, f32[128]{0:T(128)}, u32[]{:S(2)}) copy-start(f32[128]{0:T(128)} %copy-done.21) | copy-start | bytes 1540
  131.0 26.0 %collective-permute-start.15 = (bf16[2,128,1024]{2,1,0:T(8,128)(2,1)S(1)}, bf16[2,128,1024]{2,1,0:T(8,128)(2,1)S(1)}, u32[]{:S(2)}, u32[]{:S(2)}) collective-permute-start(bf16[2,128,1024]{2,1,0:T(8,128)(2,1)S(1)} %copy-done.23), channel_id=1, source_target_pairs={{2,6},{6,10},{10,14},{14,18},{18,22},{22,26},{26,30},{30,34},{34,3... | collective-permute-start | bytes 1572872 | tf_op jit(solution)/shard_map/ppermute | solution.py:31
  141.7 1.2 copy-start.18
  142.9 12.4 %copy-start.10 = (f32[128,1536]{1,0:T(8,128)S(1)}, f32[128,1536]{1,0:T(8,128)}, u32[]{:S(2)}) copy-start(f32[128,1536]{1,0:T(8,128)} %get-tuple-element.23) | copy-start | bytes 2359300
  142.9 12.4 %copy-start.11 = (f32[128,1536]{1,0:T(8,128)S(1)}, f32[128,1536]{1,0:T(8,128)}, u32[]{:S(2)}) copy-start(f32[128,1536]{1,0:T(8,128)} %get-tuple-element.33) | copy-start | bytes 2359300
  143.2 22.8 %collective-permute-start.13 = (bf16[2,128,1024]{2,1,0:T(8,128)(2,1)S(1)}, bf16[2,128,1024]{2,1,0:T(8,128)(2,1)S(1)}, u32[]{:S(2)}, u32[]{:S(2)}) collective-permute-start(bf16[2,128,1024]{2,1,0:T(8,128)(2,1)S(1)} %get-tuple-element.45), channel_id=1, source_target_pairs={{0,2},{2,4},{4,6},{6,8},{8,10},{10,12},{12,14},{14,16},{16,18},{18... | collective-permute-start | bytes 1572872 | tf_op jit(solution)/shard_map/ppermute | solution.py:26
  145.3 20.7 %collective-permute-start.14 = (bf16[2,128,1024]{2,1,0:T(8,128)(2,1)S(1)}, bf16[2,128,1024]{2,1,0:T(8,128)(2,1)S(1)}, u32[]{:S(2)}, u32[]{:S(2)}) collective-permute-start(bf16[2,128,1024]{2,1,0:T(8,128)(2,1)S(1)} %get-tuple-element.46), channel_id=1, source_target_pairs={{2,0},{4,2},{6,4},{8,6},{10,8},{12,10},{14,12},{16,14},{18,16},{20... | collective-permute-start | bytes 1572872 | tf_op jit(solution)/shard_map/ppermute | solution.py:26
  155.3 10.7 %copy-start.15 = (f32[128,1024]{1,0:T(8,128)S(1)}, f32[128,1024]{1,0:T(8,128)}, u32[]{:S(2)}) copy-start(f32[128,1024]{1,0:T(8,128)} %get-tuple-element.28) | copy-start | bytes 1572868
  155.3 10.7 %copy-start.16 = (f32[128,1024]{1,0:T(8,128)S(1)}, f32[128,1024]{1,0:T(8,128)}, u32[]{:S(2)}) copy-start(f32[128,1024]{1,0:T(8,128)} %get-tuple-element.34) | copy-start | bytes 1572868
  166.0 1.1 copy-start.1
  166.0 1.1 copy-start.20
  167.6 5.7 %collective-permute-start.16 = (f32[5120]{0:T(1024)S(1)}, f32[5120]{0:T(1024)S(1)}, u32[]{:S(2)}, u32[]{:S(2)}) collective-permute-start(f32[5120]{0:T(1024)S(1)} %pad_maximum_fusion.4), channel_id=1, source_target_pairs={{0,1},{1,0},{2,3},{3,2},{4,5},{5,4},{6,7},{7,6},{8,9},{9,8},{10,11... | collective-permute-start | bytes 61448 | tf_op jit(solution)/shard_map/ppermute | solution.py:65
  173.2 3.1 %collective-permute-start.17 = (f32[5120]{0:T(1024)S(1)}, f32[5120]{0:T(1024)S(1)}, u32[]{:S(2)}, u32[]{:S(2)}) collective-permute-start(f32[5120]{0:T(1024)S(1)} %fusion.39), channel_id=1, source_target_pairs={{0,2},{2,0},{4,6},{6,4},{8,10},{10,8},{12,14},{14,12},{16,18},{18,... | collective-permute-start | bytes 61448 | tf_op jit(solution)/shard_map/ppermute | solution.py:65
  176.3 5.7 %collective-permute-start.18 = (f32[5120]{0:T(1024)S(1)}, f32[5120]{0:T(1024)S(1)}, u32[]{:S(2)}, u32[]{:S(2)}) collective-permute-start(f32[5120]{0:T(1024)S(1)} %add.119), channel_id=1, source_target_pairs={{0,4},{2,6},{4,0},{6,2},{8,12},{10,14},{12,8},{14,10},{16,20},{18,... | collective-permute-start | bytes 61448 | tf_op jit(solution)/shard_map/ppermute | solution.py:65
  182.0 7.2 %collective-permute-start.19 = (f32[5120]{0:T(1024)S(1)}, f32[5120]{0:T(1024)S(1)}, u32[]{:S(2)}, u32[]{:S(2)}) collective-permute-start(f32[5120]{0:T(1024)S(1)} %add.120), channel_id=1, source_target_pairs={{0,8},{2,10},{4,12},{6,14},{8,0},{10,2},{12,4},{14,6},{16,24},{18,... | collective-permute-start | bytes 61448 | tf_op jit(solution)/shard_map/ppermute | solution.py:65
  189.2 5.7 %collective-permute-start.20 = (f32[5120]{0:T(1024)S(1)}, f32[5120]{0:T(1024)S(1)}, u32[]{:S(2)}, u32[]{:S(2)}) collective-permute-start(f32[5120]{0:T(1024)S(1)} %add.121), channel_id=1, source_target_pairs={{0,16},{2,18},{4,20},{6,22},{8,24},{10,26},{12,28},{14,30},{16,0},... | collective-permute-start | bytes 61448 | tf_op jit(solution)/shard_map/ppermute | solution.py:65
  194.8 6.6 %collective-permute-start.21 = (f32[5120]{0:T(1024)S(1)}, f32[5120]{0:T(1024)S(1)}, u32[]{:S(2)}, u32[]{:S(2)}) collective-permute-start(f32[5120]{0:T(1024)S(1)} %add.122), channel_id=1, source_target_pairs={{0,32},{2,34},{4,36},{6,38},{8,40},{10,42},{12,44},{14,46},{16,48}... | collective-permute-start | bytes 61448 | tf_op jit(solution)/shard_map/ppermute | solution.py:65
  201.4 9.6 %collective-permute-start.22 = (f32[5120]{0:T(1024)S(1)}, f32[5120]{0:T(1024)S(1)}, u32[]{:S(2)}, u32[]{:S(2)}) collective-permute-start(f32[5120]{0:T(1024)S(1)} %add.123), channel_id=1, source_target_pairs={{0,64},{2,66},{4,68},{6,70},{8,72},{10,74},{12,76},{14,78},{16,80}... | collective-permute-start | bytes 61448 | tf_op jit(solution)/shard_map/ppermute | solution.py:65
  211.0 6.6 %collective-permute-start.23 = (f32[5120]{0:T(1024)S(1)}, f32[5120]{0:T(1024)S(1)}, u32[]{:S(2)}, u32[]{:S(2)}) collective-permute-start(f32[5120]{0:T(1024)S(1)} %add.124), channel_id=1, source_target_pairs={{0,128},{2,130},{4,132},{6,134},{8,136},{10,138},{12,140},{14,142}... | collective-permute-start | bytes 61448 | tf_op jit(solution)/shard_map/ppermute | solution.py:65
  217.6 9.6 %collective-permute-start.24 = (f32[5120]{0:T(1024)S(1)}, f32[5120]{0:T(1024)S(1)}, u32[]{:S(2)}, u32[]{:S(2)}) collective-permute-start(f32[5120]{0:T(1024)S(1)} %add.125), channel_id=1, source_target_pairs={{0,256},{2,258},{4,260},{6,262},{8,264},{10,266},{12,268},{14,270}... | collective-permute-start | bytes 61448 | tf_op jit(solution)/shard_map/ppermute | solution.py:65
  (2 other events, 2.0 us)
